TPU v7x, 32 devices: a whole 2x2x4 slice. The times are simulated.
32 devices in a mesh: grp: 8 (over z, y), band: 4 (over x, core).
Axes of the slice: x: 2, y: 2, z: 4, core: 2. Of those that a mesh axis runs over, the one named last changes fastest.
Arguments:
- x_blocks: bfloat16 [4, 4, 64, 8192], P('band', None, None, 'grp'), may hold values from -6 to 6
- pair_ids: int32 [8, 4, 4], P('grp', 'band'), may hold values from 0 to 15, as said below
- live_count: int32 [8, 4], P('grp', 'band'), may hold values from 2 to 4, as said below
- green_occ: bfloat16 [512, 512], replicated, may hold values from -0.0234375 to 0.0234375
- green_virt: bfloat16 [512, 512], replicated, may hold values from -0.0234375 to 0.0234375
Outputs:
- chi: float32 [128, 128], P(('grp', 'band'))
Inputs may be any that keep to these rules, and one draw needn't show every extreme that they name: On each device the 4 codes pair_ids[g, b, :] are distinct; code e names mu block e // 2 and nu block 2 * b + e % 2. `live_count`: in every draw some device has all 4 slots live.
All inputs are finite; a program needn't handle non-finite values.
Results may differ from a plain program's by a relative error of at most 0.0041.
Values may be sent and summed in bfloat16 or wider, within the bound.
No kernel may reach another device: no remote copies, remote signals or barrier semaphores. Data moves between devices by JAX's collectives and lax.ppermute only.
A program may use at most 128 MiB of HBM per device.

v0:
```python
import jax
import jax.numpy as jnp
from jax import lax
from jax.sharding import PartitionSpec as P


def on_device(x_blocks, pair_ids, live_count, green_occ, green_virt):
    local_blocks = x_blocks[0]
    pair_list = pair_ids[0, 0]
    live_slots = live_count[0, 0]
    slot_count = local_blocks.shape[0]
    block_size = local_blocks.shape[1]
    ri_cols = local_blocks.shape[2]
    ri_local = ri_cols // block_size
    orbitals = green_occ.shape[0]
    band_orbs = 2 * block_size
    band_count = lax.axis_size("band")
    group_count = lax.axis_size("grp")
    ri_total = ri_local * group_count
    mu_blocks = pair_list // 2
    half_codes = pair_list % 2
    slot_index = jnp.arange(slot_count, dtype=jnp.int32)
    row_index = (
        mu_blocks[:, None] * block_size + jnp.arange(block_size, dtype=jnp.int32)[None, :]
    ).reshape(-1)
    occ_rows = jnp.take(green_occ, row_index, axis=0).reshape(slot_count, block_size, orbitals)
    virt_rows = jnp.take(green_virt, row_index, axis=0).reshape(slot_count, block_size, orbitals)
    live_mask = slot_index < live_slots
    occ_halves = []
    virt_halves = []
    for half in range(2):
        weight = jnp.logical_and(live_mask, half_codes == half).astype(jnp.bfloat16)[:, None, None]
        occ_sel = occ_rows * weight
        virt_sel = virt_rows * weight
        occ_part = lax.dot_general(
            local_blocks, occ_sel, (((0, 1), (0, 1)), ((), ())), preferred_element_type=jnp.float32
        )
        virt_part = lax.dot_general(
            virt_sel, local_blocks, (((0, 1), (0, 1)), ((), ())), preferred_element_type=jnp.float32
        )
        occ_halves.append(occ_part.astype(jnp.bfloat16).reshape(ri_local, 1, block_size, orbitals))
        virt_halves.append(
            virt_part.astype(jnp.bfloat16).reshape(orbitals, ri_local, 1, block_size)
        )
    occ_three = jnp.concatenate(occ_halves, axis=1).reshape(ri_local, band_orbs, orbitals)
    virt_three = jnp.concatenate(virt_halves, axis=2).reshape(orbitals, ri_local, band_orbs)
    moved = lax.all_to_all(
        occ_three.reshape(ri_local, 1, band_orbs, band_count, band_orbs),
        "band",
        split_axis=3,
        concat_axis=1,
        tiled=True,
    )
    moved = moved.reshape(ri_local, orbitals, band_orbs)
    pair_cols = orbitals // group_count
    occ_pairs = lax.all_to_all(
        moved.reshape(ri_local, group_count, pair_cols, band_orbs),
        "grp",
        split_axis=1,
        concat_axis=0,
        tiled=True,
    )
    occ_pairs = occ_pairs.reshape(ri_total, pair_cols, band_orbs)
    virt_pairs = lax.all_to_all(
        virt_three.reshape(group_count, pair_cols, ri_local, band_orbs),
        "grp",
        split_axis=0,
        concat_axis=2,
        tiled=True,
    )
    virt_pairs = virt_pairs.reshape(pair_cols, ri_total, band_orbs)
    partial_value = lax.dot_general(
        occ_pairs, virt_pairs, (((1, 2), (0, 2)), ((), ())), preferred_element_type=jnp.float32
    )
    group_sum = lax.psum_scatter(partial_value, "grp", scatter_dimension=0, tiled=True)
    response = lax.psum_scatter(group_sum, "band", scatter_dimension=0, tiled=True)
    return response


def solution(mesh):
    placed = (P("band", None, None, "grp"), P("grp", "band", None), P("grp", "band"), P(), P())
    return jax.shard_map(
        on_device, mesh=mesh, in_specs=placed, out_specs=P(("grp", "band"), None), check_vma=False
    )
```

profile of v0, /device:TPU:0, one launch (start us, length us, event | category | flops | bytes accessed | tf_op | source)
XLA Modules:
  0.0 237.8 jit_solution(10687282440000746870)
XLA Ops:
  6.5 0.0 copy-start
  6.5 0.0 copy-start.2
  7.3 0.7 and_convert_fusion.1
  7.9 0.7 fusion.6
  8.6 0.1 iota_add_fusion
  8.7 0.1 add.48
  8.8 2.3 gather_fusion
  11.1 0.0 copy-done.2
  11.1 1.2 gather_fusion.1
  12.3 0.1 mul.62
  12.4 0.1 mul.63
  12.5 0.1 mul.57
  12.5 0.1 mul.58
  12.6 0.2 broadcast_multiply_fusion.3
  12.8 0.0 copy-done
  12.8 0.5 fusion.1
  13.3 0.5 copy.16
  13.8 1.4 fusion
  15.2 1.5 copy.15
  16.7 0.2 pad_maximum_fusion
  16.9 0.2 copy.17
  17.2 2.1 reshape_reshape.9
  19.3 3.4 %copy.18 = bf16[16,1,128,4,128]{4,2,0,1,3:T(8,128)(2,1)} copy(bf16[16,1,128,4,128]{4,3,2,0,1:T(4,128)(2,1)} %reshape_reshape.9) | data formatting | bytes 4194304 | tf_op jit(solution)/shard_map/reshape;reshape | solution.py:48
  22.7 4.5 %all-to-all-start = ((bf16[16,1,128,4,128]{4,2,0,1,3:T(8,128)(2,1)}), bf16[16,1,128,4,128]{4,2,0,1,3:T(8,128)(2,1)}, u32[]{:S(2)}, u32[]{:S(2)}) async-start(bf16[16,1,128,4,128]{4,2,0,1,3:T(8,128)(2,1)} %copy.18), calls=%async_computation | async-start | bytes 4194304 | tf_op jit(solution)/shard_map/all_to_all | solution.py:47
  27.2 0.5 bitcast_convert_fusion.1
  27.6 1.3 copy.22
  29.0 0.5 bitcast_convert_fusion
  29.4 1.3 copy.23
  30.7 1.7 pad_maximum_fusion.1
  32.5 7.7 %copy.27 = bf16[512,16,2,64]{3,2,1,0:T(2,128)(2,1)} copy(bf16[512,16,2,64]{0,3,1,2:T(8,128)(2,1)S(1)} %pad_maximum_fusion.1) | data formatting | bytes 4194304 | tf_op jit(solution)/shard_map/reshape;reshape | solution.py:65
  40.1 7.8 %reshape.143 = bf16[8,64,16,128]{3,2,1,0:T(8,128)(2,1)} reshape(bf16[512,16,2,64]{3,2,1,0:T(2,128)(2,1)} %copy.27) | data formatting | bytes 4194304 | tf_op jit(solution)/shard_map/reshape;reshape | solution.py:65
  47.9 5.6 %all-to-all-done = bf16[16,1,128,4,128]{4,2,0,1,3:T(8,128)(2,1)} async-done(((bf16[16,1,128,4,128]{4,2,0,1,3:T(8,128)(2,1)}), bf16[16,1,128,4,128]{4,2,0,1,3:T(8,128)(2,1)}, u32[]{:S(2)}, u32[]{:S(2)}) %all-to-all-start) | async-done | bytes 2097184 | tf_op jit(solution)/shard_map/all_to_all | solution.py:47
  53.6 6.7 %all-to-all-start.2 = ((bf16[8,64,16,128]{3,2,1,0:T(8,128)(2,1)}), bf16[8,64,16,128]{3,2,1,0:T(8,128)(2,1)S(1)}, u32[]{:S(2)}, u32[]{:S(2)}) async-start(bf16[8,64,16,128]{3,2,1,0:T(8,128)(2,1)} %reshape.143), calls=%async_computation.2 | async-start | bytes 4194304 | tf_op jit(solution)/shard_map/all_to_all | solution.py:64
  60.2 1.7 copy.19
  62.0 1.5 copy.20
  63.5 44.8 %all-to-all-done.2 = bf16[8,64,16,128]{3,2,1,0:T(8,128)(2,1)S(1)} async-done(((bf16[8,64,16,128]{3,2,1,0:T(8,128)(2,1)}), bf16[8,64,16,128]{3,2,1,0:T(8,128)(2,1)S(1)}, u32[]{:S(2)}, u32[]{:S(2)}) %all-to-all-start.2) | async-done | bytes 2097184 | tf_op jit(solution)/shard_map/all_to_all | solution.py:64
  108.3 4.3 %all-to-all-start.1 = ((bf16[16,8,64,128]{3,2,0,1:T(8,128)(2,1)}), bf16[16,8,64,128]{3,2,0,1:T(8,128)(2,1)}, u32[]{:S(2)}, u32[]{:S(2)}) async-start(bf16[16,8,64,128]{3,2,0,1:T(8,128)(2,1)} %copy.20), calls=%async_computation.1 | async-start | bytes 4194304 | tf_op jit(solution)/shard_map/all_to_all | solution.py:56
  112.6 0.0 reduce-scatter.2.cloned.1.call-start
  112.7 1.9 copy.26
  114.6 45.8 %all-to-all-done.1 = bf16[16,8,64,128]{3,2,0,1:T(8,128)(2,1)} async-done(((bf16[16,8,64,128]{3,2,0,1:T(8,128)(2,1)}), bf16[16,8,64,128]{3,2,0,1:T(8,128)(2,1)}, u32[]{:S(2)}, u32[]{:S(2)}) %all-to-all-start.1) | async-done | bytes 2097184 | tf_op jit(solution)/shard_map/all_to_all | solution.py:56
  160.4 0.0 copy-start.1
  160.4 3.1 %copy.21 = bf16[8,16,1,64,128]{4,1,0,3,2:T(8,128)(2,1)S(1)} copy(bf16[8,16,1,64,128]{4,3,1,0,2:T(8,128)(2,1)} %bitcast.15) | data formatting | bytes 4194304 | tf_op jit(solution)/shard_map/all_to_all | solution.py:56
  163.5 0.0 copy-done.1
  163.6 0.0 copy-start.3
  163.6 1.3 convolution_bitcast_fusion
  164.9 0.0 reduce-scatter.2.cloned.1.call-update
  164.9 0.0 copy-done.3
  164.9 0.6 dynamic-slice
  166.2 58.3 %reduce-scatter.2.cloned.1.call-done = f32[16,128]{1,0:T(8,128)} async-done(((f32[128,128]{1,0:T(8,128)}), f32[16,128]{1,0:T(8,128)}) %reduce-scatter.2.cloned.1.call-update) | async-done | bytes 8208 | tf_op jit(solution)/shard_map/reduce_scatter | solution.py:75
  224.5 5.9 %all-reduce = f32[16,128]{1,0:T(8,128)S(1)} all-reduce(f32[16,128]{1,0:T(8,128)} %reduce-scatter.2.cloned.1.call-done), channel_id=3, replica_groups=mesh['grp'=8,'band'=4] {'band'}, use_global_device_ids=true, to_apply=%region_1.3.clone | all-reduce | flops 2048 | bytes 16384
  230.4 0.6 constant_dynamic-slice_fusion
  (4 shorter events, 0.0 us)
Async XLA Ops:
  6.5 6.3 %copy-start = (bf16[1,4,64,1024]{3,2,1,0:T(8,128)(2,1)S(1)}, bf16[1,4,64,1024]{3,2,1,0:T(8,128)(2,1)}, u32[]{:S(2)}) copy-start(bf16[1,4,64,1024]{3,2,1,0:T(8,128)(2,1)} %param.7) | copy-start | bytes 1572868
  6.5 4.6 %copy-start.2 = (bf16[512,512]{1,0:T(8,128)(2,1)S(1)}, bf16[512,512]{1,0:T(8,128)(2,1)}, u32[]{:S(2)}) copy-start(bf16[512,512]{1,0:T(8,128)(2,1)} %param.11) | copy-start | bytes 1572868
  22.7 30.9 %all-to-all-start = ((bf16[16,1,128,4,128]{4,2,0,1,3:T(8,128)(2,1)}), bf16[16,1,128,4,128]{4,2,0,1,3:T(8,128)(2,1)}, u32[]{:S(2)}, u32[]{:S(2)}) async-start(bf16[16,1,128,4,128]{4,2,0,1,3:T(8,128)(2,1)} %copy.18), calls=%async_computation | async-start | bytes 4194304 | tf_op jit(solution)/shard_map/all_to_all | solution.py:47
  53.6 54.7 %all-to-all-start.2 = ((bf16[8,64,16,128]{3,2,1,0:T(8,128)(2,1)}), bf16[8,64,16,128]{3,2,1,0:T(8,128)(2,1)S(1)}, u32[]{:S(2)}, u32[]{:S(2)}) async-start(bf16[8,64,16,128]{3,2,1,0:T(8,128)(2,1)} %reshape.143), calls=%async_computation.2 | async-start | bytes 4194304 | tf_op jit(solution)/shard_map/all_to_all | solution.py:64
  108.3 52.2 %all-to-all-start.1 = ((bf16[16,8,64,128]{3,2,0,1:T(8,128)(2,1)}), bf16[16,8,64,128]{3,2,0,1:T(8,128)(2,1)}, u32[]{:S(2)}, u32[]{:S(2)}) async-start(bf16[16,8,64,128]{3,2,0,1:T(8,128)(2,1)} %copy.20), calls=%async_computation.1 | async-start | bytes 4194304 | tf_op jit(solution)/shard_map/all_to_all | solution.py:56
  112.6 111.9 %reduce-scatter.2.cloned.1.call-start = ((), (), s32[]{:S(2)}) async-start(), calls=%async_computation.4 | async-start | bytes 73728 | tf_op jit(solution)/shard_map/reduce_scatter | solution.py:75
  160.4 3.1 %copy-start.1 = (bf16[1,64,8,16,128]{4,3,2,1,0:T(8,128)(2,1)S(1)}, bf16[1,64,8,16,128]{4,3,2,1,0:T(8,128)(2,1)}, u32[]{:S(2)}) copy-start(bf16[1,64,8,16,128]{4,3,2,1,0:T(8,128)(2,1)} %copy.26) | copy-start | bytes 6291460
  163.6 1.4 copy-start.3
Sparse Core Ops, SparseCore 0:
  165.0 59.4 reduce-scatter.1
where the time goes:
time: 239 us; the launch traced here: 238 us
  waiting for transfers between devices  155 us (65%)
  local copies, waits for them, and re-layouts  39.2 us (16%)
  starting transfers between devices  15.5 us (6%)
  between operations  15 us (6%)
  blocking collectives  5.87 us (2%)
  matrix products  4.12 us (2%)
  other arithmetic  3.53 us (1%)
    reduce_scatter x1, waiting for transfers between devices, on_device(): lax.psum_scatter(partial_value, 'grp', scatter_dimension=0, tiled=True)  58.3 us
    all_to_all x1, waiting for transfers between devices, on_device(): lax.all_to_all(moved.reshape(ri_local, group_count, pair_cols, band_orbs)...  45.8 us
    all_to_all x1, waiting for transfers between devices, on_device(): lax.all_to_all(virt_three.reshape(group_count, pair_cols, ri_local, band_...  44.8 us
    another operation x2, local copies, waits for them, and re-layouts, on_device(): virt_three.reshape(group_count, pair_cols, ri_local, band_orbs)  15.4 us
    all_to_all x1, starting transfers between devices, on_device(): lax.all_to_all(virt_three.reshape(group_count, pair_cols, ri_local, band_...  6.66 us
    unnamed x1, blocking collectives  5.87 us
    all_to_all x1, waiting for transfers between devices, on_device(): lax.all_to_all(occ_three.reshape(ri_local, 1, band_orbs, band_count, band...  5.64 us
    another operation x2, local copies, waits for them, and re-layouts, on_device(): occ_three.reshape(ri_local, 1, band_orbs, band_count, band_orbs)  5.53 us
  transfers between devices with their start and end apart: 4, of which 4 were waited for; matrix products, arithmetic and copies ran while one was open for 11% of the time, Pallas kernels for 0%

commit v1 on v0

v1 whole, which is shorter than its diff:
```python
import jax
import jax.numpy as jnp
from jax import lax
from jax.sharding import PartitionSpec as P


def slot_weights(pair_list, live_slots, slot_count):
    slot_index = jnp.arange(slot_count, dtype=jnp.int32)
    live = slot_index[None, :] < live_slots[:, None]
    halves = pair_list % 2
    rows = [jnp.logical_and(live, halves == h) for h in range(2)]
    return jnp.stack(rows, axis=1).astype(jnp.bfloat16)


def block_rows(green, pair_list, block_size):
    mu_blocks = pair_list // 2
    row_index = mu_blocks[..., None] * block_size + jnp.arange(block_size, dtype=jnp.int32)
    taken = jnp.take(green, row_index.reshape(-1), axis=0)
    return taken.reshape(pair_list.shape + (block_size, green.shape[1]))


def on_device(x_blocks, pair_ids, live_count, green_occ, green_virt):
    local_blocks = x_blocks[0]
    slot_count, block_size, ri_cols = local_blocks.shape
    ri_local = ri_cols // block_size
    orbitals = green_occ.shape[0]
    band_orbs = 2 * block_size
    band_count = lax.axis_size("band")
    group_count = lax.axis_size("grp")
    band = lax.axis_index("band")

    pair_list = pair_ids[0, 0]
    live_slots = live_count[0, 0]

    xg = lax.all_gather(local_blocks, "band")
    pg = lax.all_gather(pair_list, "band")
    lg = lax.all_gather(live_slots, "band")
    xb = lax.all_gather(local_blocks, "grp")
    pb = lax.all_gather(pair_list, "grp")
    lb = lax.all_gather(live_slots, "grp")

    occ_cols = lax.dynamic_slice_in_dim(green_occ, band * band_orbs, band_orbs, 1)
    occ_rows = block_rows(occ_cols, pg, block_size)
    wg = slot_weights(pg, lg, slot_count)
    occ_sel = occ_rows[:, None] * wg[:, :, :, None, None]
    xg_r = xg.reshape(band_count, slot_count, block_size, ri_local, block_size)
    occ_three = jnp.einsum(
        "bsipj,bhsil->pbhjl", xg_r, occ_sel, preferred_element_type=jnp.float32
    ).astype(jnp.bfloat16)
    occ_three = occ_three.reshape(ri_local, orbitals, band_orbs)

    wb = slot_weights(pb, lb, slot_count)
    xb_r = xb.reshape(group_count, slot_count, block_size, ri_local, block_size)

    def one_group(carry, item):
        x_one, p_one, w_one = item
        virt_rows = block_rows(green_virt, p_one, block_size)
        virt_sel = virt_rows[None] * w_one[:, :, None, None]
        virt_three = jnp.einsum(
            "hsin,siqj->qnhj", virt_sel, x_one, preferred_element_type=jnp.float32
        ).astype(jnp.bfloat16)
        virt_three = virt_three.reshape(ri_local, orbitals, band_orbs)
        part = lax.dot_general(
            occ_three, virt_three, (((1, 2), (1, 2)), ((), ())),
            preferred_element_type=jnp.float32,
        )
        return carry, part

    unused, parts = lax.scan(one_group, 0, (xb_r, pb, wb))
    partial_value = jnp.transpose(parts, (1, 0, 2)).reshape(ri_local, group_count * ri_local)
    response = lax.psum_scatter(partial_value, "band", scatter_dimension=0, tiled=True)
    return response


def solution(mesh):
    placed = (P("band", None, None, "grp"), P("grp", "band", None), P("grp", "band"), P(), P())
    return jax.shard_map(
        on_device, mesh=mesh, in_specs=placed, out_specs=P(("grp", "band"), None), check_vma=False
    )
```

time: 239 us -> 233 us (0.975)
  waiting for transfers between devices: 155 us -> 39.9 us
  local copies, waits for them, and re-layouts: 39.2 us -> 85.6 us
  blocking collectives: 5.87 us -> 46.9 us
  matrix products: 4.12 us -> 41.2 us
  starting transfers between devices: 15.5 us -> 0.04 us
    all_to_all x3 -> x0, waiting for transfers between devices: 96.3 us -> none  [the longest x1 45.8 us: on_device(): lax.all_to_all(moved.reshape(ri_local, group_count, pair_cols, band_orbs)...]
    reduce_scatter x1 -> x0, waiting for transfers between devices: 58.3 us -> none  [on_device(): lax.psum_scatter(partial_value, 'grp', scatter_dimension=0, tiled=True)]
    reshape x0 -> x11, local copies, waits for them, and re-layouts: none -> 45.5 us  [the longest x8 27.5 us: one_group(): virt_three = virt_three.reshape(ri_local, orbitals, band_orbs)]
    all_gather x0 -> x2, waiting for transfers between devices: none -> 38.5 us  [the longest x1 38.5 us: on_device(): xb = lax.all_gather(local_blocks, 'grp')]
    dot_general x5 -> x17, matrix products: 4.12 us -> 41.2 us  [the longest x8 20.3 us: one_group(): lax.dot_general(occ_three, virt_three, (((1, 2), (1, 2)), ((), ())), pref...]
    all_gather x0 -> x2, blocking collectives: none -> 23.1 us  [the longest x1 18 us: on_device(): pb = lax.all_gather(pair_list, 'grp')]
    another operation x5 -> x0, local copies, waits for them, and re-layouts: 22.5 us -> none  [the longest x2 15.4 us: on_device(): virt_three.reshape(group_count, pair_cols, ri_local, band_orbs)]
    dynamic_slice x0 -> x17, local copies, waits for them, and re-layouts: none -> 19.2 us  [the longest x16 19.2 us: on_device(): unused, parts = lax.scan(one_group, 0, (xb_r, pb, wb))]
  transfers between devices with their start and end apart: 4 -> 2, of which waited for: 4 -> 1; matrix products, arithmetic and copies ran while one was open for 11% -> 9% of each run, Pallas kernels for 0% -> 0%
where the time goes in v1:
time: 233 us; the launch traced here: 232 us
  local copies, waits for them, and re-layouts  85.6 us (37%)
  blocking collectives  46.9 us (20%)
  matrix products  41.2 us (18%)
  waiting for transfers between devices  39.9 us (17%)
  between operations  14.9 us (6%)
  other arithmetic  2.84 us (1%)
    all_gather x1, waiting for transfers between devices, on_device(): xb = lax.all_gather(local_blocks, 'grp')  38.5 us
    reshape x8, local copies, waits for them, and re-layouts, one_group(): virt_three = virt_three.reshape(ri_local, orbitals, band_orbs)  27.5 us
    unnamed x3, blocking collectives  23.8 us
    dot_general x8, matrix products, one_group(): lax.dot_general(occ_three, virt_three, (((1, 2), (1, 2)), ((), ())), pref...  20.3 us
    dynamic_slice x16, local copies, waits for them, and re-layouts, on_device(): unused, parts = lax.scan(one_group, 0, (xb_r, pb, wb))  19.2 us
    all_gather x1, blocking collectives, on_device(): pb = lax.all_gather(pair_list, 'grp')  18 us
    dot_general x8, matrix products, one_group(): jnp.einsum('hsin,siqj->qnhj', virt_sel, x_one, preferred_element_type=jnp...  17.3 us
    gather x9, local copies, waits for them, and re-layouts, block_rows(): taken = jnp.take(green, row_index.reshape(-1), axis=0)  12.4 us
  transfers between devices with their start and end apart: 2, of which 1 were waited for; matrix products, arithmetic and copies ran while one was open for 9% of the time, Pallas kernels for 0%

profile of v1, /device:TPU:0, one launch (start us, length us, event | category | flops | bytes accessed | tf_op | source)
XLA Modules:
  0.0 231.7 jit_solution(2717733902308480687)
XLA Ops:
  6.5 0.7 all-gather.9.cloned.1.call-update
  7.3 0.7 all-gather.7.cloned.1.call-update
  8.7 1.2 dynamic-slice
  9.9 1.4 fusion.29
  12.6 6.4 %all-reduce.1 = s32[4]{0:T(128)S(1)} all-reduce(s32[4]{0:T(128)S(1)} %bitcast_dynamic-update-slice_fusion), channel_id=5, replica_groups=mesh['grp'=8,'band'=4] {'band'}, use_global_device_ids=true, to_apply=%add.1 | all-reduce | flops 4 | bytes 32
  18.9 11.6 %all-reduce = s32[8]{0:T(128)S(1)} all-reduce(s32[8]{0:T(128)S(1)} %bitcast_dynamic-update-slice_fusion.1), channel_id=3, replica_groups=mesh['grp'=8,'band'=4] {'grp'}, use_global_device_ids=true, to_apply=%add | all-reduce | flops 8 | bytes 64
  30.6 5.2 %all-gather.2 = s32[4,1,4]{2,1,0:T(1,128)S(1)} all-gather(s32[1,1,4]{2,1,0:T(1,128)} %param.8), channel_id=4, replica_groups=mesh['grp'=8,'band'=4] {'band'}, dimensions={0}, use_global_device_ids=true | all-gather | bytes 80 | tf_op jit(solution)/shard_map/all_gather | solution.py:36
  36.0 18.0 %all-gather = s32[8,1,4]{2,1,0:T(1,128)S(1)} all-gather(s32[1,1,4]{2,1,0:T(1,128)} %param.8), channel_id=2, replica_groups=mesh['grp'=8,'band'=4] {'grp'}, dimensions={0}, use_global_device_ids=true | all-gather | bytes 144 | tf_op jit(solution)/shard_map/all_gather | solution.py:39
  54.3 3.2 %gather_fusion.1 = bf16[1024,128]{1,0:T(8,128)(2,1)S(1)} fusion(bf16[512,128]{1,0:T(8,128)(2,1)S(1)} %constant_dynamic-slice_fusion.4, s32[1024]{0:T(1024)S(1)} %broadcast_clamp_fusion), kind=kCustom, calls=%fused_computation.1 | custom fusion | bytes 528384 | tf_op jit(solution)/shard_map/jit(_take)/gather | solution.py:18
  58.5 6.4 %reshape.192 = bf16[4,4,64,16,64]{4,3,2,1,0:T(8,128)(2,1)} reshape(bf16[4,4,64,1024]{3,2,1,0:T(8,128)(2,1)} %all-gather.9.cloned.1.call-done) | data formatting | bytes 4194304 | tf_op jit(solution)/shard_map/reshape | solution.py:46
  64.9 3.6 %fusion.11 = bf16[16,4,2,64,128]{4,3,0,2,1:T(8,128)(2,1)S(1)} fusion(bf16[4,4,64,16,64,1]{4,3,2,1,0,5:T(8,128)(2,1)} %bitcast.103, bf16[4,2,4]{2,1,0:T(2,128)(2,1)S(1)} %copy.24, bf16[4,4,64,128]{3,2,1,0:T(8,128)(2,1)S(1)} %broadcast_select_fusion.1), kind=kOutput, calls=%fused_computation.29 | convolution fusion | flops 538968064 | bytes 4456512 | tf_op jit(solution)/shard_map/bsipj,bhsil->pbhjl/dot_general | solution.py:47
  68.7 2.7 %copy.30 = bf16[16,512,128]{2,0,1:T(8,128)(2,1)} copy(bf16[16,512,128]{2,1,0:T(8,128)(2,1)S(1)} %bitcast.104) | data formatting | bytes 4194304 | tf_op jit(solution)/shard_map/while | solution.py:69
  71.4 38.5 %all-gather.7.cloned.1.call-done = bf16[8,4,64,1024]{3,2,1,0:T(8,128)(2,1)} async-done(((bf16[1,4,64,1024]{3,2,1,0:T(8,128)(2,1)}), bf16[8,4,64,1024]{3,2,1,0:T(8,128)(2,1)}) %all-gather.7.cloned.1.call-update) | async-done | bytes 4194320 | tf_op jit(solution)/shard_map/all_gather | solution.py:38
  109.9 11.6 %reshape.191 = bf16[8,4,64,16,64]{4,3,2,1,0:T(8,128)(2,1)} reshape(bf16[8,4,64,1024]{3,2,1,0:T(8,128)(2,1)} %all-gather.7.cloned.1.call-done) | data formatting | bytes 8388608 | tf_op jit(solution)/shard_map/reshape | solution.py:53
  121.5 97.0 %while.12 = (s32[]{:T(128)}, f32[8,16,16]{1,2,0:T(8,128)S(1)}, bf16[8,4,64,16,64]{4,3,2,1,0:T(8,128)(2,1)}, s32[8,4]{1,0:T(8,128)S(1)}, bf16[512,512]{1,0:T(8,12...) while((s32[]{:T(128)}, f32[8,16,16]{1,2,0:T(8,128)S(1)}, ...), condition=%wide.region_1.2_spmd, body=%wide.region_0.1_spmd.sunk | while | flops 572657472 | bytes 14438101 | solution.py:69
  121.7 1.2 gather_fusion
  123.0 1.4 constant_dynamic-slice_fusion.6
  124.4 1.0 copy.47
  125.4 2.2 bitcast_convert_fusion.3
  127.6 3.4 %copy.48 = bf16[16,512,128]{2,0,1:T(8,128)(2,1)S(1)} copy(bf16[16,512,128]{1,2,0:T(8,128)(2,1)} %bitcast.101) | data formatting | bytes 4194304 | tf_op jit(solution)/shard_map/while/body/eval_jaxpr/reshape | solution.py:62
  131.0 2.5 %fusion.45 = f32[8,16,16]{1,2,0:T(8,128)S(1)} fusion(f32[8,16,16]{1,2,0:T(8,128)S(1)} %get-tuple-element.189, s32[]{:T(128)} %get-tuple-element.188, bf16[16,512,128]{2,0,1:T(8,128)(2,1)S(1)} %copy.48, bf16[16,512,128]{2,0,1:T(8,128)(2,1)} %get-tuple-element.202), kind=kOutput, calls=%fused_computation.4.clone.1 | convolution fusion | flops 33554432 | bytes 4202500 | tf_op jit(solution)/shard_map/while/body/eval_jaxpr/dot_general | solution.py:63
  133.8 1.2 gather_fusion
  135.1 1.4 constant_dynamic-slice_fusion.6
  136.5 1.0 copy.47
  137.6 2.2 bitcast_convert_fusion.3
  139.7 3.4 %copy.48 = bf16[16,512,128]{2,0,1:T(8,128)(2,1)S(1)} copy(bf16[16,512,128]{1,2,0:T(8,128)(2,1)} %bitcast.101) | data formatting | bytes 4194304 | tf_op jit(solution)/shard_map/while/body/eval_jaxpr/reshape | solution.py:62
  143.2 2.5 %fusion.45 = f32[8,16,16]{1,2,0:T(8,128)S(1)} fusion(f32[8,16,16]{1,2,0:T(8,128)S(1)} %get-tuple-element.189, s32[]{:T(128)} %get-tuple-element.188, bf16[16,512,128]{2,0,1:T(8,128)(2,1)S(1)} %copy.48, bf16[16,512,128]{2,0,1:T(8,128)(2,1)} %get-tuple-element.202), kind=kOutput, calls=%fused_computation.4.clone.1 | convolution fusion | flops 33554432 | bytes 4202500 | tf_op jit(solution)/shard_map/while/body/eval_jaxpr/dot_general | solution.py:63
  145.9 1.2 gather_fusion
  147.2 1.4 constant_dynamic-slice_fusion.6
  148.7 1.0 copy.47
  149.7 2.2 bitcast_convert_fusion.3
  151.8 3.4 %copy.48 = bf16[16,512,128]{2,0,1:T(8,128)(2,1)S(1)} copy(bf16[16,512,128]{1,2,0:T(8,128)(2,1)} %bitcast.101) | data formatting | bytes 4194304 | tf_op jit(solution)/shard_map/while/body/eval_jaxpr/reshape | solution.py:62
  155.3 2.5 %fusion.45 = f32[8,16,16]{1,2,0:T(8,128)S(1)} fusion(f32[8,16,16]{1,2,0:T(8,128)S(1)} %get-tuple-element.189, s32[]{:T(128)} %get-tuple-element.188, bf16[16,512,128]{2,0,1:T(8,128)(2,1)S(1)} %copy.48, bf16[16,512,128]{2,0,1:T(8,128)(2,1)} %get-tuple-element.202), kind=kOutput, calls=%fused_computation.4.clone.1 | convolution fusion | flops 33554432 | bytes 4202500 | tf_op jit(solution)/shard_map/while/body/eval_jaxpr/dot_general | solution.py:63
  158.0 1.2 gather_fusion
  159.4 1.4 constant_dynamic-slice_fusion.6
  160.8 1.0 copy.47
  161.8 2.2 bitcast_convert_fusion.3
  164.0 3.4 %copy.48 = bf16[16,512,128]{2,0,1:T(8,128)(2,1)S(1)} copy(bf16[16,512,128]{1,2,0:T(8,128)(2,1)} %bitcast.101) | data formatting | bytes 4194304 | tf_op jit(solution)/shard_map/while/body/eval_jaxpr/reshape | solution.py:62
  167.4 2.5 %fusion.45 = f32[8,16,16]{1,2,0:T(8,128)S(1)} fusion(f32[8,16,16]{1,2,0:T(8,128)S(1)} %get-tuple-element.189, s32[]{:T(128)} %get-tuple-element.188, bf16[16,512,128]{2,0,1:T(8,128)(2,1)S(1)} %copy.48, bf16[16,512,128]{2,0,1:T(8,128)(2,1)} %get-tuple-element.202), kind=kOutput, calls=%fused_computation.4.clone.1 | convolution fusion | flops 33554432 | bytes 4202500 | tf_op jit(solution)/shard_map/while/body/eval_jaxpr/dot_general | solution.py:63
  170.2 1.2 gather_fusion
  171.5 1.4 constant_dynamic-slice_fusion.6
  172.9 1.0 copy.47
  173.9 2.2 bitcast_convert_fusion.3
  176.1 3.4 %copy.48 = bf16[16,512,128]{2,0,1:T(8,128)(2,1)S(1)} copy(bf16[16,512,128]{1,2,0:T(8,128)(2,1)} %bitcast.101) | data formatting | bytes 4194304 | tf_op jit(solution)/shard_map/while/body/eval_jaxpr/reshape | solution.py:62
  179.5 2.5 %fusion.45 = f32[8,16,16]{1,2,0:T(8,128)S(1)} fusion(f32[8,16,16]{1,2,0:T(8,128)S(1)} %get-tuple-element.189, s32[]{:T(128)} %get-tuple-element.188, bf16[16,512,128]{2,0,1:T(8,128)(2,1)S(1)} %copy.48, bf16[16,512,128]{2,0,1:T(8,128)(2,1)} %get-tuple-element.202), kind=kOutput, calls=%fused_computation.4.clone.1 | convolution fusion | flops 33554432 | bytes 4202500 | tf_op jit(solution)/shard_map/while/body/eval_jaxpr/dot_general | solution.py:63
  182.3 1.2 gather_fusion
  183.6 1.4 constant_dynamic-slice_fusion.6
  185.0 1.0 copy.47
  186.1 2.2 bitcast_convert_fusion.3
  188.2 3.4 %copy.48 = bf16[16,512,128]{2,0,1:T(8,128)(2,1)S(1)} copy(bf16[16,512,128]{1,2,0:T(8,128)(2,1)} %bitcast.101) | data formatting | bytes 4194304 | tf_op jit(solution)/shard_map/while/body/eval_jaxpr/reshape | solution.py:62
  191.7 2.5 %fusion.45 = f32[8,16,16]{1,2,0:T(8,128)S(1)} fusion(f32[8,16,16]{1,2,0:T(8,128)S(1)} %get-tuple-element.189, s32[]{:T(128)} %get-tuple-element.188, bf16[16,512,128]{2,0,1:T(8,128)(2,1)S(1)} %copy.48, bf16[16,512,128]{2,0,1:T(8,128)(2,1)} %get-tuple-element.202), kind=kOutput, calls=%fused_computation.4.clone.1 | convolution fusion | flops 33554432 | bytes 4202500 | tf_op jit(solution)/shard_map/while/body/eval_jaxpr/dot_general | solution.py:63
  194.4 1.2 gather_fusion
  195.8 1.4 constant_dynamic-slice_fusion.6
  197.2 1.0 copy.47
  198.2 2.2 bitcast_convert_fusion.3
  200.3 3.4 %copy.48 = bf16[16,512,128]{2,0,1:T(8,128)(2,1)S(1)} copy(bf16[16,512,128]{1,2,0:T(8,128)(2,1)} %bitcast.101) | data formatting | bytes 4194304 | tf_op jit(solution)/shard_map/while/body/eval_jaxpr/reshape | solution.py:62
  203.8 2.5 %fusion.45 = f32[8,16,16]{1,2,0:T(8,128)S(1)} fusion(f32[8,16,16]{1,2,0:T(8,128)S(1)} %get-tuple-element.189, s32[]{:T(128)} %get-tuple-element.188, bf16[16,512,128]{2,0,1:T(8,128)(2,1)S(1)} %copy.48, bf16[16,512,128]{2,0,1:T(8,128)(2,1)} %get-tuple-element.202), kind=kOutput, calls=%fused_computation.4.clone.1 | convolution fusion | flops 33554432 | bytes 4202500 | tf_op jit(solution)/shard_map/while/body/eval_jaxpr/dot_general | solution.py:63
  206.5 1.2 gather_fusion
  207.9 1.4 constant_dynamic-slice_fusion.6
  209.3 1.0 copy.47
  210.3 2.2 bitcast_convert_fusion.3
  212.5 3.4 %copy.48 = bf16[16,512,128]{2,0,1:T(8,128)(2,1)S(1)} copy(bf16[16,512,128]{1,2,0:T(8,128)(2,1)} %bitcast.101) | data formatting | bytes 4194304 | tf_op jit(solution)/shard_map/while/body/eval_jaxpr/reshape | solution.py:62
  215.9 2.5 %fusion.45 = f32[8,16,16]{1,2,0:T(8,128)S(1)} fusion(f32[8,16,16]{1,2,0:T(8,128)S(1)} %get-tuple-element.189, s32[]{:T(128)} %get-tuple-element.188, bf16[16,512,128]{2,0,1:T(8,128)(2,1)S(1)} %copy.48, bf16[16,512,128]{2,0,1:T(8,128)(2,1)} %get-tuple-element.202), kind=kOutput, calls=%fused_computation.4.clone.1 | convolution fusion | flops 33554432 | bytes 4202500 | tf_op jit(solution)/shard_map/while/body/eval_jaxpr/dot_general | solution.py:63
  218.5 5.8 %all-reduce.2 = f32[16,128]{1,0:T(8,128)S(1)} all-reduce(f32[16,128]{1,0:T(8,128)S(1)} %copy.39), channel_id=6, replica_groups=mesh['grp'=8,'band'=4] {'band'}, use_global_device_ids=true, to_apply=%region_2.3.clone | all-reduce | flops 2048 | bytes 16384
  (95 shorter events, 6.1 us)
Async XLA Ops:
  6.5 47.7 %copy-start = (bf16[512,512]{1,0:T(8,128)(2,1)S(1)}, bf16[512,512]{1,0:T(8,128)(2,1)}, u32[]{:S(2)}) copy-start(bf16[512,512]{1,0:T(8,128)(2,1)} %param.10) | copy-start | bytes 1572868
  6.5 52.0 %all-gather.9.cloned.1.call-start = ((), (), s32[]{:S(2)}) async-start(), calls=%async_computation.1 | async-start | bytes 2621440 | tf_op jit(solution)/shard_map/all_gather | solution.py:35
  7.3 102.6 %all-gather.7.cloned.1.call-start = ((), (), s32[]{:S(2)}) async-start(), calls=%async_computation | async-start | bytes 4718592 | tf_op jit(solution)/shard_map/all_gather | solution.py:38
  71.4 50.1 %copy-start.1 = (bf16[512,512]{1,0:T(8,128)(2,1)S(1)}, bf16[512,512]{1,0:T(8,128)(2,1)}, u32[]{:S(2)}) copy-start(bf16[512,512]{1,0:T(8,128)(2,1)} %param.11) | copy-start | bytes 1572868
Sparse Core Ops, SparseCore 0:
  8.9 25.2 all-gather.8
  36.4 73.4 all-gather.6

commit v2 on v1

v2 whole, which is shorter than its diff:
```python
import jax
import jax.numpy as jnp
from jax import lax
from jax.sharding import PartitionSpec as P

META = 128


def on_device(x_blocks, pair_ids, live_count, green_occ, green_virt):
    local_blocks = x_blocks[0]
    slot_count, block_size, ri_cols = local_blocks.shape
    ri_local = ri_cols // block_size
    orbitals = green_occ.shape[0]
    band_orbs = 2 * block_size
    band_count = lax.axis_size("band")
    group_count = lax.axis_size("grp")
    band = lax.axis_index("band")
    flat = slot_count * block_size * block_size
    code_count = 2 * (orbitals // block_size)

    pair_list = pair_ids[0, 0]
    live_slots = live_count[0, 0]

    live = (jnp.arange(slot_count, dtype=jnp.int32) < live_slots).astype(local_blocks.dtype)
    masked = local_blocks * live[:, None, None]
    xt = masked.reshape(slot_count, block_size, ri_local, block_size)
    xt = jnp.transpose(xt, (2, 0, 3, 1)).reshape(ri_local, flat)
    meta = jnp.zeros((ri_local, META), local_blocks.dtype)
    meta = meta.at[0, :slot_count].set(pair_list.astype(local_blocks.dtype))
    packed = jnp.concatenate([xt, meta], axis=1)

    xg = lax.all_gather(packed, "band")
    xb = lax.all_gather(packed, "grp")
    codes_g = xg[:, 0, flat:flat + slot_count].astype(jnp.float32).astype(jnp.int32)
    codes_b = xb[:, 0, flat:flat + slot_count].astype(jnp.float32).astype(jnp.int32)

    occ_cols = lax.dynamic_slice_in_dim(green_occ, band * band_orbs, band_orbs, 1)
    row_index = (codes_g // 2)[..., None] * block_size + jnp.arange(block_size, dtype=jnp.int32)
    occ_rows = jnp.take(occ_cols, row_index.reshape(-1), axis=0)
    occ_rows = occ_rows.reshape(band_count, slot_count, block_size, band_orbs)
    halves = (codes_g % 2)[:, None, :] == jnp.arange(2, dtype=jnp.int32)[None, :, None]
    occ_sel = occ_rows[:, None] * halves.astype(occ_rows.dtype)[..., None, None]
    xg_x = xg[:, :, :flat].reshape(band_count, ri_local, slot_count, block_size, block_size)
    occ_three = jnp.einsum(
        "bpsji,bhsil->plbhj", xg_x, occ_sel, preferred_element_type=jnp.float32
    ).astype(jnp.bfloat16)
    occ_three = occ_three.reshape(ri_local, band_orbs, orbitals)

    folded = lax.dot_general(
        occ_three, green_virt, (((2,), (1,)), ((), ())), preferred_element_type=jnp.float32
    )
    folded = folded.reshape(ri_local, 2, block_size, orbitals // block_size, block_size)
    folded = jnp.transpose(folded, (0, 3, 1, 2, 4)).reshape(ri_local, code_count, block_size * block_size)

    xb_x = xb[:, :, :flat]
    chunk = max(1, min(group_count, (8 << 20) // (ri_local * flat * 4)))
    while group_count % chunk:
        chunk -= 1

    def one_chunk(item):
        x_part, code_part = item
        sel = jnp.take(folded, code_part.reshape(-1), axis=1)
        sel = sel.reshape(ri_local, chunk, flat)
        return jnp.einsum(
            "pgk,gqk->gpq", sel, x_part.astype(jnp.float32),
            precision=lax.Precision.HIGHEST, preferred_element_type=jnp.float32,
        )

    steps = group_count // chunk
    if steps == 1:
        parts = one_chunk((xb_x, codes_b))
    else:
        parts = lax.map(
            one_chunk,
            (xb_x.reshape(steps, chunk, ri_local, flat), codes_b.reshape(steps, chunk, slot_count)),
        ).reshape(group_count, ri_local, ri_local)
    partial_value = jnp.transpose(parts, (1, 0, 2)).reshape(ri_local, group_count * ri_local)
    response = lax.psum_scatter(partial_value, "band", scatter_dimension=0, tiled=True)
    return response


def solution(mesh):
    placed = (P("band", None, None, "grp"), P("grp", "band", None), P("grp", "band"), P(), P())
    return jax.shard_map(
        on_device, mesh=mesh, in_specs=placed, out_specs=P(("grp", "band"), None), check_vma=False
    )
```

time: 233 us -> 172 us (0.74)
  blocking collectives: 46.9 us -> 5.75 us
  matrix products: 41.2 us -> 15.7 us
  waiting for transfers between devices: 39.9 us -> 52.4 us
  local copies, waits for them, and re-layouts: 85.6 us -> 73.9 us
  other arithmetic: 2.84 us -> 8.8 us
    reshape x10 -> x4, local copies, waits for them, and re-layouts: 45.4 us -> 18.3 us  [the longest x2 12 us: on_device(): jnp.transpose(folded, (0, 3, 1, 2, 4))]
    dot_general x17 -> x3, matrix products: 41.2 us -> 15.7 us  [the longest x1 9.83 us: one_chunk(): jnp.einsum('pgk,gqk->gpq', sel, x_part.astype(jnp.float32), precision=lax...]
    all_gather x2 -> x0, blocking collectives: 23.1 us -> none  [the longest x1 18 us: on_device(): pb = lax.all_gather(pair_list, 'grp')]
    gather x9 -> x4, local copies, waits for them, and re-layouts: 12.4 us -> 31.8 us  [the longest x3 28.5 us: one_chunk(): sel = jnp.take(folded, code_part.reshape(-1), axis=1)]
    dynamic_slice x16 -> x0, local copies, waits for them, and re-layouts: 19.2 us -> none  [on_device(): unused, parts = lax.scan(one_group, 0, (xb_r, pb, wb))]
    unnamed x3 -> x1, blocking collectives: 23.8 us -> 5.75 us
    all_gather x2, waiting for transfers between devices: 38.5 us -> 51.7 us  [the longest x1 29.1 us: on_device(): xb = lax.all_gather(packed, 'grp')]
    dot_general x0 -> x1, local copies, waits for them, and re-layouts: none -> 9.35 us  [on_device(): lax.dot_general(occ_three, green_virt, (((2,), (1,)), ((), ())), preferre...]
  transfers between devices with their start and end apart: 2 -> 2, of which waited for: 1 -> 2; matrix products, arithmetic and copies ran while one was open for 9% -> 28% of each run, Pallas kernels for 0% -> 0%
where the time goes in v2:
time: 172 us; the launch traced here: 171 us
  local copies, waits for them, and re-layouts  73.9 us (43%)
  waiting for transfers between devices  52.4 us (30%)
  matrix products  15.7 us (9%)
  between operations  14.9 us (9%)
  other arithmetic  8.8 us (5%)
  blocking collectives  5.75 us (3%)
    all_gather x1, waiting for transfers between devices, on_device(): xb = lax.all_gather(packed, 'grp')  29.1 us
    gather x3, local copies, waits for them, and re-layouts, one_chunk(): sel = jnp.take(folded, code_part.reshape(-1), axis=1)  28.5 us
    all_gather x1, waiting for transfers between devices, on_device(): xg = lax.all_gather(packed, 'band')  22.6 us
    reshape x2, local copies, waits for them, and re-layouts, on_device(): jnp.transpose(folded, (0, 3, 1, 2, 4))  12 us
    dot_general x1, matrix products, one_chunk(): jnp.einsum('pgk,gqk->gpq', sel, x_part.astype(jnp.float32), precision=lax...  9.83 us
    dot_general x1, local copies, waits for them, and re-layouts, on_device(): lax.dot_general(occ_three, green_virt, (((2,), (1,)), ((), ())), preferre...  9.35 us
    convert_element_type x1, local copies, waits for them, and re-layouts, on_device(): occ_three = jnp.einsum('bpsji,bhsil->plbhj', xg_x, occ_sel, preferred_ele...  7.3 us
    unnamed x1, blocking collectives  5.75 us
  transfers between devices with their start and end apart: 2, of which 2 were waited for; matrix products, arithmetic and copies ran while one was open for 28% of the time, Pallas kernels for 0%

profile of v2, /device:TPU:0, one launch (start us, length us, event | category | flops | bytes accessed | tf_op | source)
XLA Modules:
  0.0 171.5 jit_solution(5487119526886648516)
XLA Ops:
  6.5 0.0 copy-start
  6.5 0.0 copy-start.2
  6.5 0.0 all-gather.7.cloned.1.call-start
  6.5 1.8 %squeeze.4 = bf16[4,64,16,64]{3,2,1,0:T(8,128)(2,1)S(1)} reshape(bf16[1,4,64,1024]{3,2,1,0:T(8,128)(2,1)} %param.7) | data formatting | bytes 1048576 | tf_op jit(solution)/shard_map/squeeze | solution.py:10
  8.4 0.0 copy-start.3
  8.4 1.0 copy.17
  10.0 0.1 multiply_bitcast_fusion
  10.2 0.8 reshape.178
  11.0 0.0 copy-done.2
  11.0 0.9 fusion.15
  11.9 0.0 all-gather.7.cloned.1.call-update
  11.9 0.0 all-gather.5.cloned.1.call-start
  12.0 0.7 all-gather.5.cloned.1.call-update
  12.7 0.0 copy-done.3
  12.7 0.6 dynamic-slice.7
  13.9 0.9 constant_dynamic-slice_fusion.1
  14.8 22.6 %all-gather.7.cloned.1.call-done = bf16[64,16512]{1,0:T(8,128)(2,1)} async-done(((bf16[16,16512]{1,0:T(8,128)(2,1)}), bf16[64,16512]{1,0:T(8,128)(2,1)}) %all-gather.7.cloned.1.call-update) | async-done | bytes 2113552 | tf_op jit(solution)/shard_map/all_gather | solution.py:32
  37.4 1.7 %slice.38 = bf16[4,16,16384]{2,1,0:T(8,128)(2,1)S(1)} slice(bf16[4,16,16512]{2,1,0:T(8,128)(2,1)} %bitcast.66), slice={[0:4], [0:16], [0:16384]} | slice | bytes 4194304 | tf_op jit(solution)/shard_map/slice | solution.py:43
  39.2 0.7 fusion.24
  39.9 0.1 iota_add_fusion
  40.0 0.1 add.100
  40.1 5.5 %reshape.201 = bf16[4,16,4,64,64,1]{4,3,2,1,0,5:T(8,128)(2,1)} reshape(bf16[4,16,16384]{2,1,0:T(8,128)(2,1)S(1)} %slice.38) | data formatting | bytes 4194304 | tf_op jit(solution)/shard_map/reshape | solution.py:43
  45.6 3.2 %gather_fusion = bf16[1024,128]{1,0:T(8,128)(2,1)S(1)} fusion(bf16[512,128]{1,0:T(8,128)(2,1)S(1)} %constant_dynamic-slice_fusion.1, s32[1024]{0:T(1024)S(1)} %broadcast_clamp_fusion), kind=kCustom, calls=%fused_computation | custom fusion | bytes 528384 | tf_op jit(solution)/shard_map/jit(_take)/gather | solution.py:39
  48.8 0.1 compare_and_fusion
  48.9 0.7 and_select_fusion
  49.6 0.2 broadcast_select_fusion.1
  49.8 3.5 %fusion.5 = bf16[16,128,4,2,64]{1,4,0,3,2:T(8,128)(2,1)S(1)} fusion(bf16[4,16,4,64,64,1]{4,3,2,1,0,5:T(8,128)(2,1)} %reshape.201, bf16[4,2,4]{2,1,0:T(2,128)(2,1)S(1)} %compare_convert_fusion, bf16[4,4,64,128]{3,2,1,0:T(8,128)(2,1)S(1)} %broadcast_select_fusion.1), kind=kOutput, calls=%fused_computation.10 | convolution fusion | flops 538968064 | bytes 4456512 | tf_op jit(solution)/shard_map/bpsji,bhsil->plbhj/dot_general | solution.py:44
  53.3 7.3 %copy.19 = bf16[16,128,4,2,64]{4,3,2,1,0:T(2,128)(2,1)} copy(bf16[16,128,4,2,64]{1,4,0,3,2:T(8,128)(2,1)S(1)} %fusion.5) | data formatting | bytes 4194304 | tf_op jit(solution)/shard_map/convert_element_type | solution.py:46
  60.6 9.3 %reshape.203 = bf16[16,2,64,512,1]{3,2,1,0,4:T(8,128)(2,1)S(1)} reshape(bf16[16,128,4,2,64]{4,3,2,1,0:T(2,128)(2,1)} %copy.19) | data formatting | bytes 4194304 | tf_op jit(solution)/shard_map/dot_general | solution.py:49
  70.0 0.0 copy-done
  70.0 2.4 %convolution_bitcast_fusion = f32[16,8,2,64,64]{4,3,1,2,0:T(8,128)S(1)} fusion(bf16[8,64,512,1,1]{2,1,0,4,3:T(8,128)(2,1)S(1)} %bitcast.59, bf16[16,2,64,512,1]{3,2,1,0,4:T(8,128)(2,1)S(1)} %reshape.203), kind=kOutput, calls=%fused_computation.9 | convolution fusion | flops 1073741824 | bytes 6815744 | tf_op jit(solution)/shard_map/dot_general | solution.py:49
  72.4 4.1 %copy.30 = f32[16,8,2,64,64]{4,3,0,2,1:T(8,128)} copy(f32[16,8,2,64,64]{4,3,1,2,0:T(8,128)S(1)} %convolution_bitcast_fusion) | data formatting | bytes 8388608 | tf_op jit(solution)/shard_map/reshape | solution.py:53
  76.4 7.9 %reshape.207 = f32[16,16,4096]{2,0,1:T(8,128)} reshape(f32[16,8,2,64,64]{4,3,0,2,1:T(8,128)} %copy.30) | data formatting | bytes 8388608 | tf_op jit(solution)/shard_map/reshape | solution.py:53
  84.4 29.1 %all-gather.5.cloned.1.call-done = bf16[128,16512]{1,0:T(8,128)(2,1)} async-done(((bf16[16,16512]{1,0:T(8,128)(2,1)}), bf16[128,16512]{1,0:T(8,128)(2,1)}) %all-gather.5.cloned.1.call-update) | async-done | bytes 4227088 | tf_op jit(solution)/shard_map/all_gather | solution.py:33
  113.4 0.7 fusion.27
  114.2 0.7 fusion.20
  114.9 0.1 convert_element_type.100
  115.0 6.5 %gather_fusion.1 = f32[32,16,4096]{2,1,0:T(8,128)} fusion(f32[16,16,4096]{2,0,1:T(8,128)} %reshape.207, s32[1024]{0:T(1024)S(1)} %pad_clamp_fusion), kind=kCustom, calls=%fused_computation.1 | custom fusion | bytes 16777344 | tf_op jit(solution)/shard_map/jit(_take)/gather | solution.py:62
  121.5 11.5 %copy.22 = f32[16,32,4096]{2,1,0:T(8,128)} copy(f32[16,32,4096]{2,0,1:T(8,128)} %bitcast.60) | data formatting | bytes 16777216 | tf_op jit(solution)/shard_map/jit(_take)/gather | solution.py:62
  133.0 0.0 slice-start
  133.0 10.6 %gather.15 = f32[16,8,16384]{2,1,0:T(8,128)} reshape(f32[16,32,4096]{2,1,0:T(8,128)} %copy.22) | data formatting | bytes 16777216 | tf_op jit(solution)/shard_map/jit(_take)/gather | solution.py:62
  143.6 0.1 copy.18
  143.7 0.0 slice-start.1
  143.7 0.1 broadcast_in_dim.31
  143.8 0.0 copy-start.1
  143.8 4.5 %broadcast_select_fusion = f32[16,8,16384]{2,1,0:T(8,128)S(1)} fusion(f32[16,8,16384]{2,1,0:T(8,128)} %gather.15, pred[8,16384]{1,0:T(8,128)(4,1)S(1)} %bitcast.70), kind=kLoop, calls=%fused_computation.8 | loop fusion | flops 2097152 | bytes 16908288 | tf_op jit(solution)/shard_map/jit(_take)/select_n | solution.py:62
  148.3 0.0 slice-done
  148.3 0.0 slice-done.1
  148.3 9.8 %fusion.9 = f32[16,8,16]{2,0,1:T(8,128)S(1)} fusion(bf16[8,16,16512]{2,1,0:T(8,128)(2,1)S(1)} %bitcast.65, f32[16,8,16384]{2,1,0:T(8,128)S(1)} %broadcast_select_fusion), kind=kOutput, calls=%fused_computation.12 | convolution fusion | flops 402653184 | bytes 12591104 | tf_op jit(solution)/shard_map/pgk,gqk->gpq/dot_general | solution.py:64
  158.2 0.1 reshape.181
  158.3 5.8 %all-reduce.1 = f32[16,128]{1,0:T(8,128)S(1)} all-reduce(f32[16,128]{1,0:T(8,128)S(1)} %reshape.181), channel_id=4, replica_groups=mesh['grp'=8,'band'=4] {'band'}, use_global_device_ids=true, to_apply=%region_0.0.clone | all-reduce | flops 2048 | bytes 16384
  164.0 0.6 constant_dynamic-slice_fusion
  164.6 0.0 copy-done.1
  (11 shorter events, 0.1 us)
Async XLA Ops:
  6.5 63.4 %copy-start = (bf16[512,512]{1,0:T(8,128)(2,1)S(1)}, bf16[512,512]{1,0:T(8,128)(2,1)}, u32[]{:S(2)}) copy-start(bf16[512,512]{1,0:T(8,128)(2,1)} %param.11) | copy-start | bytes 1572868
  6.5 4.5 %copy-start.2 = (s32[1,1,4]{2,1,0:T(1,128)S(1)}, s32[1,1,4]{2,1,0:T(1,128)}, u32[]{:S(2)}) copy-start(s32[1,1,4]{2,1,0:T(1,128)} %param.8) | copy-start | bytes 52
  6.5 30.9 %all-gather.7.cloned.1.call-start = ((), (), s32[]{:S(2)}) async-start(), calls=%async_computation.1 | async-start | bytes 2641920 | tf_op jit(solution)/shard_map/all_gather | solution.py:32
  8.4 4.3 %copy-start.3 = (u32[32]{0:T(128)S(1)}, u32[32]{0:T(128)}, u32[]{:S(2)}) copy-start(u32[32]{0:T(128)} %constant.100) | copy-start | bytes 388
  11.9 101.5 %all-gather.5.cloned.1.call-start = ((), (), s32[]{:S(2)}) async-start(), calls=%async_computation | async-start | bytes 4755456 | tf_op jit(solution)/shard_map/all_gather | solution.py:33
  133.0 15.3 %slice-start = ((s8[4227072]{0:T(1024)(128)(4,1)}), s8[32768]{0:T(1024)(128)(4,1)S(1)}, s32[]{:S(2)}) async-start(s8[4227072]{0:T(1024)(128)(4,1)} %bitcast.63), calls=%async_computation.2 | async-start | bytes 65536
  143.7 4.6 %slice-start.1 = ((s8[4227072]{0:T(1024)(128)(4,1)}), s8[4194304]{0:T(1024)(128)(4,1)S(1)}, s32[]{:S(2)}) async-start(s8[4227072]{0:T(1024)(128)(4,1)} %bitcast.63), calls=%async_computation.3 | async-start | bytes 8388608
  143.8 20.9 %copy-start.1 = (bf16[512,512]{1,0:T(8,128)(2,1)S(1)}, bf16[512,512]{1,0:T(8,128)(2,1)}, u32[]{:S(2)}) copy-start(bf16[512,512]{1,0:T(8,128)(2,1)} %param.11) | copy-start | bytes 1572868
Sparse Core Ops, SparseCore 0:
  12.0 25.3 all-gather.6
  39.6 73.7 all-gather.4

commit v3 on v2

--- a/solution.py
+++ b/solution.py
@@ -4,6 +4,33 @@
 from jax.sharding import PartitionSpec as P
 
 META = 128
+
+
+def snake(count):
+    half = count // 2
+    return [2 * o for o in range(half)] + [2 * o + 1 for o in reversed(range(half))]
+
+
+def ring_gather(buf, axis, count):
+    order = snake(count)
+    pos_of = [order.index(d) for d in range(count)]
+    fwd = [(order[k], order[(k + 1) % count]) for k in range(count)]
+    bwd = [(order[k], order[(k - 1) % count]) for k in range(count)]
+    me = lax.axis_index(axis)
+    pos = jnp.array(pos_of, jnp.int32)[me]
+    order_arr = jnp.array(order, jnp.int32)
+    got = [(me, buf)]
+    ahead = behind = buf
+    for step in range(1, count // 2):
+        ahead = lax.ppermute(ahead, axis, fwd)
+        behind = lax.ppermute(behind, axis, bwd)
+        got.append((order_arr[(pos - step) % count], ahead))
+        got.append((order_arr[(pos + step) % count], behind))
+    rows = buf.shape[0] // 2
+    first = lax.ppermute(ahead[:rows], axis, fwd)
+    second = lax.ppermute(behind[rows:], axis, bwd)
+    got.append((order_arr[(pos + count // 2) % count], jnp.concatenate([first, second], axis=0)))
+    return got
 
 
 def on_device(x_blocks, pair_ids, live_count, green_occ, green_virt):
@@ -29,10 +56,11 @@
     meta = meta.at[0, :slot_count].set(pair_list.astype(local_blocks.dtype))
     packed = jnp.concatenate([xt, meta], axis=1)
 
-    xg = lax.all_gather(packed, "band")
-    xb = lax.all_gather(packed, "grp")
+    band_got = ring_gather(packed, "band", band_count)
+    band_ids = jnp.stack([src for src, unused in band_got])
+    xg = jnp.stack([buf for unused, buf in band_got])
     codes_g = xg[:, 0, flat:flat + slot_count].astype(jnp.float32).astype(jnp.int32)
-    codes_b = xb[:, 0, flat:flat + slot_count].astype(jnp.float32).astype(jnp.int32)
+    grp_got = ring_gather(packed, "grp", group_count)
 
     occ_cols = lax.dynamic_slice_in_dim(green_occ, band * band_orbs, band_orbs, 1)
     row_index = (codes_g // 2)[..., None] * block_size + jnp.arange(block_size, dtype=jnp.int32)
@@ -46,35 +74,28 @@
     ).astype(jnp.bfloat16)
     occ_three = occ_three.reshape(ri_local, band_orbs, orbitals)
 
+    col_index = (band_ids[:, None] * band_orbs + jnp.arange(band_orbs, dtype=jnp.int32)).reshape(-1)
+    virt_cols = jnp.take(green_virt, col_index, axis=1)
     folded = lax.dot_general(
-        occ_three, green_virt, (((2,), (1,)), ((), ())), preferred_element_type=jnp.float32
+        occ_three, virt_cols, (((2,), (1,)), ((), ())), preferred_element_type=jnp.float32
     )
     folded = folded.reshape(ri_local, 2, block_size, orbitals // block_size, block_size)
     folded = jnp.transpose(folded, (0, 3, 1, 2, 4)).reshape(ri_local, code_count, block_size * block_size)
 
-    xb_x = xb[:, :, :flat]
-    chunk = max(1, min(group_count, (8 << 20) // (ri_local * flat * 4)))
-    while group_count % chunk:
-        chunk -= 1
+    fold_hi = folded.astype(jnp.bfloat16)
+    fold_lo = (folded - fold_hi.astype(jnp.float32)).astype(jnp.bfloat16)
 
-    def one_chunk(item):
-        x_part, code_part = item
-        sel = jnp.take(folded, code_part.reshape(-1), axis=1)
-        sel = sel.reshape(ri_local, chunk, flat)
-        return jnp.einsum(
-            "pgk,gqk->gpq", sel, x_part.astype(jnp.float32),
-            precision=lax.Precision.HIGHEST, preferred_element_type=jnp.float32,
-        )
-
-    steps = group_count // chunk
-    if steps == 1:
-        parts = one_chunk((xb_x, codes_b))
-    else:
-        parts = lax.map(
-            one_chunk,
-            (xb_x.reshape(steps, chunk, ri_local, flat), codes_b.reshape(steps, chunk, slot_count)),
-        ).reshape(group_count, ri_local, ri_local)
-    partial_value = jnp.transpose(parts, (1, 0, 2)).reshape(ri_local, group_count * ri_local)
+    partial_value = jnp.zeros((ri_local, group_count * ri_local), jnp.float32)
+    for src, buf in grp_got:
+        codes = buf[0, flat:flat + slot_count].astype(jnp.float32).astype(jnp.int32)
+        x_part = buf[:, :flat]
+        part = jnp.zeros((ri_local, ri_local), jnp.float32)
+        for table in (fold_hi, fold_lo):
+            sel = jnp.take(table, codes, axis=1).reshape(ri_local, flat)
+            part = part + lax.dot_general(
+                sel, x_part, (((1,), (1,)), ((), ())), preferred_element_type=jnp.float32
+            )
+        partial_value = lax.dynamic_update_slice_in_dim(partial_value, part, src * ri_local, 1)
     response = lax.psum_scatter(partial_value, "band", scatter_dimension=0, tiled=True)
     return response
 

time: 172 us -> 177 us (1.029)
  waiting for transfers between devices: 52.4 us -> 5.29 us
  local copies, waits for them, and re-layouts: 73.9 us -> 89.5 us
  starting transfers between devices: 0.04 us -> 13.3 us
  other arithmetic: 8.8 us -> 21.8 us
  matrix products: 15.7 us -> 25.7 us
  between operations: 14.9 us -> 13 us
    all_gather x2 -> x0, waiting for transfers between devices: 51.7 us -> none  [the longest x1 29.1 us: on_device(): xb = lax.all_gather(packed, 'grp')]
    ppermute x0 -> x12, starting transfers between devices: none -> 13.3 us  [the longest x4 5.6 us: ring_gather(): ahead = lax.ppermute(ahead, axis, fwd)]
    dot_general x2 -> x17, matrix products: 12.2 us -> 22.2 us  [the longest x16 19.9 us: on_device(): lax.dot_general(sel, x_part, (((1,), (1,)), ((), ())), preferred_element_...]
    gather x3 -> x17, local copies, waits for them, and re-layouts: 28.5 us -> 34.3 us  [the longest x16 31.7 us: on_device(): sel = jnp.take(table, codes, axis=1).reshape(ri_local, flat)]
    ppermute x0 -> x12, waiting for transfers between devices: none -> 5.29 us  [the longest x2 1.82 us: ring_gather(): second = lax.ppermute(behind[rows:], axis, bwd)]
    and x1 -> x9, other arithmetic: 0.01 us -> 4.94 us  [the longest x8 4.86 us: on_device(): sel = jnp.take(table, codes, axis=1).reshape(ri_local, flat)]
    unnamed x1 -> x8, other arithmetic: 0.01 us -> 4.88 us
    convert_element_type x3 -> x1, other arithmetic: 2.16 us -> 5.78 us  [on_device(): fold_lo = (folded - fold_hi.astype(jnp.float32)).astype(jnp.bfloat16)]
  transfers between devices with their start and end apart: 2 -> 12, of which waited for: 2 -> 4; matrix products, arithmetic and copies ran while one was open for 28% -> 66% of each run, Pallas kernels for 0% -> 0%
where the time goes in v3:
time: 177 us; the launch traced here: 175 us
  local copies, waits for them, and re-layouts  89.5 us (51%)
  matrix products  25.7 us (15%)
  other arithmetic  21.8 us (12%)
  starting transfers between devices  13.3 us (8%)
  between operations  13 us (7%)
  blocking collectives  6.09 us (3%)
  waiting for transfers between devices  5.29 us (3%)
    gather x16, local copies, waits for them, and re-layouts, on_device(): sel = jnp.take(table, codes, axis=1).reshape(ri_local, flat)  31.7 us
    dot_general x16, matrix products, on_device(): lax.dot_general(sel, x_part, (((1,), (1,)), ((), ())), preferred_element_...  19.9 us
    reshape x2, local copies, waits for them, and re-layouts, on_device(): jnp.transpose(folded, (0, 3, 1, 2, 4))  12.1 us
    dot_general x1, local copies, waits for them, and re-layouts, on_device(): lax.dot_general(occ_three, virt_cols, (((2,), (1,)), ((), ())), preferred...  9.41 us
    convert_element_type x1, local copies, waits for them, and re-layouts, on_device(): occ_three = jnp.einsum('bpsji,bhsil->plbhj', xg_x, occ_sel, preferred_ele...  7.35 us
    unnamed x1, blocking collectives  6.09 us
    convert_element_type x1, other arithmetic, on_device(): fold_lo = (folded - fold_hi.astype(jnp.float32)).astype(jnp.bfloat16)  5.78 us
    reshape x1, local copies, waits for them, and re-layouts, on_device(): xg[:, :, :flat]  5.71 us
  transfers between devices with their start and end apart: 12, of which 4 were waited for; matrix products, arithmetic and copies ran while one was open for 66% of the time, Pallas kernels for 0%

profile of v3, /device:TPU:0, one launch (start us, length us, event | category | flops | bytes accessed | tf_op | source)
XLA Modules:
  0.0 174.8 jit_solution(11820564112839151137)
XLA Ops:
  0.0 1.8 %squeeze.4 = bf16[4,64,16,64]{3,2,1,0:T(8,128)(2,1)S(1)} reshape(bf16[1,4,64,1024]{3,2,1,0:T(8,128)(2,1)} %param.13) | data formatting | bytes 1048576 | tf_op jit(solution)/shard_map/squeeze | solution.py:37
  2.6 1.0 copy.44
  4.5 0.9 fusion.52
  5.4 2.9 %collective-permute-start = (bf16[16,16512]{1,0:T(8,128)(2,1)}, bf16[16,16512]{1,0:T(8,128)(2,1)S(1)}, u32[]{:S(2)}, u32[]{:S(2)}) collective-permute-start(bf16[16,16512]{1,0:T(8,128)(2,1)} %get-tuple-element.37), channel_id=1, source_target_pairs={{0,2},{2,3},{3,1},{1,0},{4,6},{6,7},{7,5},{5,4},{8,10},{10,11},{11... | collective-permute-start | bytes 1585160 | tf_op jit(solution)/shard_map/ppermute | solution.py:25
  8.4 1.6 collective-permute-start.4
  13.6 1.9 %add_multiply_fusion = s32[4]{0:T(128)S(1)} fusion(s32[1]{0:T(128)} %get-tuple-element.62, s32[1]{0:T(128)} %get-tuple-element.63, s32[1]{0:T(128)} %get-tuple-element.61, s32[1]{0:T(128)} %bitcast.19), kind=kLoop, calls=%fused_computation.154 | loop fusion | flops 16 | bytes 32 | tf_op jit(solution)/shard_map/mul | solution.py:77
  26.1 1.3 copy.46
  27.3 2.6 %gather_fusion.1 = bf16[512,512]{1,0:T(8,128)(2,1)} fusion(bf16[512,512]{0,1:T(8,128)(2,1)S(1)} %copy.46, s32[1024]{0:T(1024)S(1)} %pad_clamp_fusion.8), kind=kCustom, calls=%fused_computation.17 | custom fusion | bytes 1050624 | tf_op jit(solution)/shard_map/jit(_take)/gather | solution.py:78
  30.0 1.2 select_bitcast_fusion.16
  31.2 1.0 copy.47
  33.6 2.0 %collective-permute-start.2 = (bf16[8,16512]{1,0:T(8,128)(2,1)S(1)}, bf16[8,16512]{1,0:T(8,128)(2,1)S(1)}, u32[]{:S(2)}, u32[]{:S(2)}) collective-permute-start(bf16[8,16512]{1,0:T(8,128)(2,1)S(1)} %slice.133), channel_id=1, source_target_pairs={{0,2},{2,3},{3,1},{1,0},{4,6},{6,7},{7,5},{5,4},{8,10},{10,11},{11... | collective-permute-start | bytes 792584 | tf_op jit(solution)/shard_map/ppermute | solution.py:30
  35.7 1.6 collective-permute-start.7
  39.3 1.0 collective-permute-done.2
  40.3 1.8 %collective-permute-done.3 = bf16[8,16512]{1,0:T(8,128)(2,1)S(1)} collective-permute-done((bf16[8,16512]{1,0:T(8,128)(2,1)S(1)}, bf16[8,16512]{1,0:T(8,128)(2,1)S(1)}, u32[]{:S(2)}, u32[]{:S(2)}) %collective-permute-start.3) | collective-permute-done | bytes 264224 | tf_op jit(solution)/shard_map/ppermute | solution.py:31
  42.4 1.5 pad_maximum_fusion
  44.0 5.7 %reshape.550 = bf16[4,16,4,64,64,1]{4,3,2,1,0,5:T(8,128)(2,1)} reshape(bf16[4,16,16384]{2,1,0:T(8,128)(2,1)S(1)} %pad_maximum_fusion) | data formatting | bytes 4194304 | tf_op jit(solution)/shard_map/reshape | solution.py:71
  49.7 3.2 %gather_fusion = bf16[1024,128]{1,0:T(8,128)(2,1)S(1)} fusion(bf16[512,128]{1,0:T(8,128)(2,1)S(1)} %constant_dynamic-slice_fusion.1, s32[1024]{0:T(1024)S(1)} %broadcast_clamp_fusion), kind=kCustom, calls=%fused_computation.16 | custom fusion | bytes 528384 | tf_op jit(solution)/shard_map/jit(_take)/gather | solution.py:67
  53.1 3.5 %fusion.2 = bf16[16,128,4,2,64]{1,4,0,3,2:T(8,128)(2,1)S(1)} fusion(bf16[4,16,4,64,64,1]{4,3,2,1,0,5:T(8,128)(2,1)} %reshape.550, bf16[4,2,4]{2,1,0:T(2,128)(2,1)S(1)} %compare_convert_fusion, bf16[4,4,64,128]{3,2,1,0:T(8,128)(2,1)S(1)} %broadcast_select_fusion), kind=kOutput, calls=%fused_computation.23 | convolution fusion | flops 538968064 | bytes 4456512 | tf_op jit(solution)/shard_map/bpsji,bhsil->plbhj/dot_general | solution.py:72
  56.6 7.4 %copy.45 = bf16[16,128,4,2,64]{4,3,2,1,0:T(2,128)(2,1)} copy(bf16[16,128,4,2,64]{1,4,0,3,2:T(8,128)(2,1)S(1)} %fusion.2) | data formatting | bytes 4194304 | tf_op jit(solution)/shard_map/convert_element_type | solution.py:74
  64.0 9.4 %reshape.552 = bf16[16,2,64,512,1]{3,2,1,0,4:T(8,128)(2,1)S(1)} reshape(bf16[16,128,4,2,64]{4,3,2,1,0:T(2,128)(2,1)} %copy.45) | data formatting | bytes 4194304 | tf_op jit(solution)/shard_map/dot_general | solution.py:79
  73.4 2.4 %convolution_bitcast_fusion = f32[16,8,2,64,64]{4,3,1,2,0:T(8,128)S(1)} fusion(bf16[8,64,512,1,1]{2,1,0,4,3:T(8,128)(2,1)S(1)} %bitcast.207, bf16[16,2,64,512,1]{3,2,1,0,4:T(8,128)(2,1)S(1)} %reshape.552), kind=kOutput, calls=%fused_computation.22 | convolution fusion | flops 1073741824 | bytes 6815744 | tf_op jit(solution)/shard_map/dot_general | solution.py:79
  75.8 4.1 %copy.72 = f32[16,8,2,64,64]{4,3,0,2,1:T(8,128)} copy(f32[16,8,2,64,64]{4,3,1,2,0:T(8,128)S(1)} %convolution_bitcast_fusion) | data formatting | bytes 8388608 | tf_op jit(solution)/shard_map/reshape | solution.py:83
  79.9 8.0 %reshape.557 = f32[16,16,4096]{2,0,1:T(8,128)} reshape(f32[16,8,2,64,64]{4,3,0,2,1:T(8,128)} %copy.72) | data formatting | bytes 8388608 | tf_op jit(solution)/shard_map/reshape | solution.py:83
  87.8 5.8 %subtract_convert_fusion = (bf16[16,16,4096]{2,0,1:T(8,128)(2,1)S(1)}, bf16[16,16,4096]{2,0,1:T(8,128)(2,1)}) fusion(f32[16,16,4096]{2,0,1:T(8,128)} %reshape.557), kind=kLoop, calls=%fused_computation.21 | loop fusion | flops 4194304 | bytes 8388608 | tf_op jit(solution)/shard_map/convert_element_type | solution.py:86
  93.6 3.0 %gather_fusion.6 = bf16[4,16,4096]{2,1,0:T(8,128)(2,1)} fusion(bf16[16,16,4096]{2,0,1:T(8,128)(2,1)} %get-tuple-element.33, s32[1024]{0:T(1024)S(1)} %pad_clamp_fusion.5), kind=kCustom, calls=%fused_computation.4.clone | custom fusion | bytes 1048592 | tf_op jit(solution)/shard_map/jit(_take)/gather | solution.py:94
  96.6 1.4 gather_fusion.7
  98.0 1.4 gather_fusion.5
  99.4 3.0 %gather_fusion.4 = bf16[4,16,4096]{2,1,0:T(8,128)(2,1)} fusion(bf16[16,16,4096]{2,0,1:T(8,128)(2,1)} %get-tuple-element.33, s32[1024]{0:T(1024)S(1)} %pad_clamp_fusion.6), kind=kCustom, calls=%fused_computation.2.clone | custom fusion | bytes 1048592 | tf_op jit(solution)/shard_map/jit(_take)/gather | solution.py:94
  102.3 3.0 %gather_fusion.2 = bf16[4,16,4096]{2,1,0:T(8,128)(2,1)} fusion(bf16[16,16,4096]{2,0,1:T(8,128)(2,1)} %get-tuple-element.33, s32[1024]{0:T(1024)S(1)} %pad_clamp_fusion.7), kind=kCustom, calls=%fused_computation.clone | custom fusion | bytes 1048592 | tf_op jit(solution)/shard_map/jit(_take)/gather | solution.py:94
  105.3 1.4 gather_fusion.3
  106.7 1.4 select_bitcast_fusion.13
  109.8 1.4 fusion.25
  111.2 1.3 convolution_add_fusion.6
  112.6 0.8 copy.78
  114.0 1.4 fusion.22
  115.4 1.5 convolution_add_fusion.5
  117.9 2.2 %gather_fusion.10 = bf16[4,16,4096]{2,1,0:T(8,128)(2,1)S(1)} fusion(bf16[16,16,4096]{2,0,1:T(8,128)(2,1)} %get-tuple-element.33, s32[1024]{0:T(1024)S(1)} %pad_clamp_fusion.3), kind=kCustom, calls=%fused_computation.8.clone | custom fusion | bytes 1048592 | tf_op jit(solution)/shard_map/jit(_take)/gather | solution.py:94
  120.0 1.4 gather_fusion.11
  122.1 3.0 %gather_fusion.8 = bf16[4,16,4096]{2,1,0:T(8,128)(2,1)} fusion(bf16[16,16,4096]{2,0,1:T(8,128)(2,1)} %get-tuple-element.33, s32[1024]{0:T(1024)S(1)} %pad_clamp_fusion.4), kind=kCustom, calls=%fused_computation.6.clone | custom fusion | bytes 1048592 | tf_op jit(solution)/shard_map/jit(_take)/gather | solution.py:94
  125.1 1.4 gather_fusion.9
  126.5 1.4 select_bitcast_fusion.9
  128.2 1.6 collective-permute-start.9
  129.8 1.4 fusion.19
  131.1 1.3 convolution_add_fusion.4
  134.0 1.4 fusion.16
  135.4 1.5 convolution_add_fusion.3
  137.2 1.6 collective-permute-done.9
  139.4 2.2 %gather_fusion.14 = bf16[4,16,4096]{2,1,0:T(8,128)(2,1)S(1)} fusion(bf16[16,16,4096]{2,0,1:T(8,128)(2,1)} %get-tuple-element.33, s32[1024]{0:T(1024)S(1)} %pad_clamp_fusion.1), kind=kCustom, calls=%fused_computation.12.clone | custom fusion | bytes 1048592 | tf_op jit(solution)/shard_map/jit(_take)/gather | solution.py:94
  141.6 1.4 gather_fusion.15
  143.0 0.9 collective-permute-done.8
  144.6 3.0 %gather_fusion.12 = bf16[4,16,4096]{2,1,0:T(8,128)(2,1)} fusion(bf16[16,16,4096]{2,0,1:T(8,128)(2,1)} %get-tuple-element.33, s32[1024]{0:T(1024)S(1)} %pad_clamp_fusion.2), kind=kCustom, calls=%fused_computation.10.clone | custom fusion | bytes 1048592 | tf_op jit(solution)/shard_map/jit(_take)/gather | solution.py:94
  147.6 1.4 gather_fusion.13
  149.0 1.8 %slice.147 = bf16[8,16512]{1,0:T(8,128)(2,1)} slice(bf16[16,16512]{1,0:T(8,128)(2,1)} %collective-permute-done.8), slice={[0:8], [0:16512]} | slice | bytes 528384 | tf_op jit(solution)/shard_map/slice | solution.py:30
  151.5 1.0 slice.149
  152.5 1.3 collective-permute-start.11
  153.8 1.2 select_bitcast_fusion.3
  155.3 1.4 fusion.13
  156.6 1.3 convolution_add_fusion.2
  158.0 1.4 fusion.10
  159.7 1.3 convolution_add_fusion.1
  162.0 2.2 %gather_fusion.16 = bf16[4,16,4096]{2,1,0:T(8,128)(2,1)S(1)} fusion(bf16[16,16,4096]{2,0,1:T(8,128)(2,1)} %get-tuple-element.33, s32[1024]{0:T(1024)S(1)} %pad_clamp_fusion), kind=kCustom, calls=%fused_computation.14.clone | custom fusion | bytes 1048592 | tf_op jit(solution)/shard_map/jit(_take)/gather | solution.py:94
  165.1 1.4 fusion.28
  166.5 1.3 convolution_add_fusion
  168.1 6.1 %all-reduce.1 = f32[16,128]{1,0:T(8,128)S(1)} all-reduce(f32[16,128]{1,0:T(8,128)S(1)} %dynamic_update_slice.31), channel_id=2, replica_groups=mesh['grp'=8,'band'=4] {'band'}, use_global_device_ids=true, to_apply=%region_0.2.clone | all-reduce | flops 2048 | bytes 16384
  (128 shorter events, 18.9 us)
Async XLA Ops:
  0.0 32.2 %copy-start = (bf16[512,512]{1,0:T(8,128)(2,1)S(1)}, bf16[512,512]{1,0:T(8,128)(2,1)}, u32[]{:S(2)}) copy-start(bf16[512,512]{1,0:T(8,128)(2,1)} %param.16) | copy-start | bytes 1572868
  2.6 1.9 %copy-start.15 = (s32[1,1,4]{2,1,0:T(1,128)S(1)}, s32[1,1,4]{2,1,0:T(1,128)}, u32[]{:S(2)}) copy-start(s32[1,1,4]{2,1,0:T(1,128)} %param.14) | copy-start | bytes 52
  3.6 6.8 %copy-start.18 = (s32[4]{0:T(128)S(1)}, s32[4]{0:T(128)}, u32[]{:S(2)}) copy-start(s32[4]{0:T(128)} %constant.203.clone) | copy-start | bytes 52
  3.6 9.3 %copy-start.14 = (s32[4]{0:T(128)S(1)}, s32[4]{0:T(128)}, u32[]{:S(2)}) copy-start(s32[4]{0:T(128)} %constant.204.clone) | copy-start | bytes 52
  3.7 12.0 %copy-start.17 = (s32[8]{0:T(128)S(1)}, s32[8]{0:T(128)}, u32[]{:S(2)}) copy-start(s32[8]{0:T(128)} %constant.205.clone) | copy-start | bytes 100
  3.7 17.3 %copy-start.13 = (s32[8]{0:T(128)S(1)}, s32[8]{0:T(128)}, u32[]{:S(2)}) copy-start(s32[8]{0:T(128)} %constant.206.clone) | copy-start | bytes 100
  5.4 36.7 %copy-start.2 = (bf16[1,16,16512]{2,1,0:T(8,128)(2,1)}, bf16[1,16,16512]{2,1,0:T(8,128)(2,1)S(1)}, u32[]{:S(2)}) copy-start(bf16[1,16,16512]{2,1,0:T(8,128)(2,1)S(1)} %get-tuple-element.36) | copy-start | bytes 1585156
  5.4 28.1 %collective-permute-start = (bf16[16,16512]{1,0:T(8,128)(2,1)}, bf16[16,16512]{1,0:T(8,128)(2,1)S(1)}, u32[]{:S(2)}, u32[]{:S(2)}) collective-permute-start(bf16[16,16512]{1,0:T(8,128)(2,1)} %get-tuple-element.37), channel_id=1, source_target_pairs={{0,2},{2,3},{3,1},{1,0},{4,6},{6,7},{7,5},{5,4},{8,10},{10,11},{11... | collective-permute-start | bytes 1585160 | tf_op jit(solution)/shard_map/ppermute | solution.py:25
  8.4 27.3 %collective-permute-start.1 = (bf16[16,16512]{1,0:T(8,128)(2,1)}, bf16[16,16512]{1,0:T(8,128)(2,1)S(1)}, u32[]{:S(2)}, u32[]{:S(2)}) collective-permute-start(bf16[16,16512]{1,0:T(8,128)(2,1)} %get-tuple-element.37), channel_id=1, source_target_pairs={{0,1},{2,0},{3,2},{1,3},{4,5},{6,4},{7,6},{5,7},{8,9},{10,8},{11,1... | collective-permute-start | bytes 1585160 | tf_op jit(solution)/shard_map/ppermute | solution.py:26
  8.4 29.6 %collective-permute-start.4 = (bf16[16,16512]{1,0:T(8,128)(2,1)}, bf16[16,16512]{1,0:T(8,128)(2,1)}, u32[]{:S(2)}, u32[]{:S(2)}) collective-permute-start(bf16[16,16512]{1,0:T(8,128)(2,1)} %get-tuple-element.37), channel_id=1, source_target_pairs={{0,8},{8,16},{16,24},{24,28},{28,20},{20,12},{12,4},{4,0},{1,9},{9... | collective-permute-start | bytes 1585160 | tf_op jit(solution)/shard_map/ppermute | solution.py:25
  9.9 25.8 %collective-permute-start.5 = (bf16[16,16512]{1,0:T(8,128)(2,1)}, bf16[16,16512]{1,0:T(8,128)(2,1)}, u32[]{:S(2)}, u32[]{:S(2)}) collective-permute-start(bf16[16,16512]{1,0:T(8,128)(2,1)} %get-tuple-element.37), channel_id=1, source_target_pairs={{0,4},{8,0},{16,8},{24,16},{28,24},{20,28},{12,20},{4,12},{1,5},{9... | collective-permute-start | bytes 1585160 | tf_op jit(solution)/shard_map/ppermute | solution.py:26
  30.0 2.3 %copy-start.16 = (u32[32]{0:T(128)S(1)}, u32[32]{0:T(128)}, u32[]{:S(2)}) copy-start(u32[32]{0:T(128)} %constant.214) | copy-start | bytes 388
  33.6 8.6 %copy-start.3 = (bf16[16,16512]{1,0:T(8,128)(2,1)}, bf16[16,16512]{1,0:T(8,128)(2,1)S(1)}, u32[]{:S(2)}) copy-start(bf16[16,16512]{1,0:T(8,128)(2,1)S(1)} %collective-permute-done) | copy-start | bytes 1585156
  33.6 6.7 %collective-permute-start.2 = (bf16[8,16512]{1,0:T(8,128)(2,1)S(1)}, bf16[8,16512]{1,0:T(8,128)(2,1)S(1)}, u32[]{:S(2)}, u32[]{:S(2)}) collective-permute-start(bf16[8,16512]{1,0:T(8,128)(2,1)S(1)} %slice.133), channel_id=1, source_target_pairs={{0,2},{2,3},{3,1},{1,0},{4,6},{6,7},{7,5},{5,4},{8,10},{10,11},{11... | collective-permute-start | bytes 792584 | tf_op jit(solution)/shard_map/ppermute | solution.py:30
  35.6 6.6 %copy-start.4 = (bf16[16,16512]{1,0:T(8,128)(2,1)}, bf16[16,16512]{1,0:T(8,128)(2,1)S(1)}, u32[]{:S(2)}) copy-start(bf16[16,16512]{1,0:T(8,128)(2,1)S(1)} %collective-permute-done.1) | copy-start | bytes 1585156
  35.7 6.4 %collective-permute-start.3 = (bf16[8,16512]{1,0:T(8,128)(2,1)S(1)}, bf16[8,16512]{1,0:T(8,128)(2,1)S(1)}, u32[]{:S(2)}, u32[]{:S(2)}) collective-permute-start(bf16[8,16512]{1,0:T(8,128)(2,1)S(1)} %slice.134), channel_id=1, source_target_pairs={{0,1},{2,0},{3,2},{1,3},{4,5},{6,4},{7,6},{5,7},{8,9},{10,8},{11,1... | collective-permute-start | bytes 792584 | tf_op jit(solution)/shard_map/ppermute | solution.py:31
  35.7 81.5 %collective-permute-start.7 = (bf16[16,16512]{1,0:T(8,128)(2,1)}, bf16[16,16512]{1,0:T(8,128)(2,1)}, u32[]{:S(2)}, u32[]{:S(2)}) collective-permute-start(bf16[16,16512]{1,0:T(8,128)(2,1)} %collective-permute-done.5), channel_id=1, source_target_pairs={{0,4},{8,0},{16,8},{24,16},{28,24},{20,28},{12,20},{4,12},{1,5},{9... | collective-permute-start | bytes 1585160 | tf_op jit(solution)/shard_map/ppermute | solution.py:26
  38.0 83.5 %collective-permute-start.6 = (bf16[16,16512]{1,0:T(8,128)(2,1)}, bf16[16,16512]{1,0:T(8,128)(2,1)}, u32[]{:S(2)}, u32[]{:S(2)}) collective-permute-start(bf16[16,16512]{1,0:T(8,128)(2,1)} %collective-permute-done.4), channel_id=1, source_target_pairs={{0,8},{8,16},{16,24},{24,28},{28,20},{20,12},{12,4},{4,0},{1,9},{9... | collective-permute-start | bytes 1585160 | tf_op jit(solution)/shard_map/ppermute | solution.py:25
  64.0 9.4 %copy-start.12 = (bf16[512,512]{1,0:T(8,128)(2,1)S(1)}, bf16[512,512]{1,0:T(8,128)(2,1)}, u32[]{:S(2)}) copy-start(bf16[512,512]{1,0:T(8,128)(2,1)} %copy.47) | copy-start | bytes 1572868
  106.7 1.5 copy-start.10
  106.7 1.6 copy-start.11
  108.4 1.0 copy-start.5
  108.5 1.2 copy-start.6
  126.5 1.5 copy-start.7
  128.2 10.6 %collective-permute-start.9 = (bf16[16,16512]{1,0:T(8,128)(2,1)}, bf16[16,16512]{1,0:T(8,128)(2,1)}, u32[]{:S(2)}, u32[]{:S(2)}) collective-permute-start(bf16[16,16512]{1,0:T(8,128)(2,1)} %collective-permute-done.7), channel_id=1, source_target_pairs={{0,4},{8,0},{16,8},{24,16},{28,24},{20,28},{12,20},{4,12},{1,5},{9... | collective-permute-start | bytes 1585160 | tf_op jit(solution)/shard_map/ppermute | solution.py:26
  133.5 10.4 %collective-permute-start.8 = (bf16[16,16512]{1,0:T(8,128)(2,1)}, bf16[16,16512]{1,0:T(8,128)(2,1)}, u32[]{:S(2)}, u32[]{:S(2)}) collective-permute-start(bf16[16,16512]{1,0:T(8,128)(2,1)} %collective-permute-done.6), channel_id=1, source_target_pairs={{0,8},{8,16},{16,24},{24,28},{28,20},{20,12},{12,4},{4,0},{1,9},{9... | collective-permute-start | bytes 1585160 | tf_op jit(solution)/shard_map/ppermute | solution.py:25
  148.9 6.1 %copy-start.8 = (bf16[4,16,4096]{2,1,0:T(8,128)(2,1)S(1)}, bf16[4,16,4096]{2,1,0:T(8,128)(2,1)}, u32[]{:S(2)}) copy-start(bf16[4,16,4096]{2,1,0:T(8,128)(2,1)} %gather_fusion.12) | copy-start | bytes 1572868
  148.9 6.1 %copy-start.9 = (bf16[4,16,4096]{2,1,0:T(8,128)(2,1)S(1)}, bf16[4,16,4096]{2,1,0:T(8,128)(2,1)}, u32[]{:S(2)}) copy-start(bf16[4,16,4096]{2,1,0:T(8,128)(2,1)} %gather_fusion.13) | copy-start | bytes 1572868
  150.7 10.6 %collective-permute-start.10 = (bf16[8,16512]{1,0:T(8,128)(2,1)}, bf16[8,16512]{1,0:T(8,128)(2,1)}, u32[]{:S(2)}, u32[]{:S(2)}) collective-permute-start(bf16[8,16512]{1,0:T(8,128)(2,1)} %slice.147), channel_id=1, source_target_pairs={{0,8},{8,16},{16,24},{24,28},{28,20},{20,12},{12,4},{4,0},{1,9},{9... | collective-permute-start | bytes 792584 | tf_op jit(solution)/shard_map/ppermute | solution.py:30
  152.5 12.5 %collective-permute-start.11 = (bf16[8,16512]{1,0:T(8,128)(2,1)S(1)}, bf16[8,16512]{1,0:T(8,128)(2,1)}, u32[]{:S(2)}, u32[]{:S(2)}) collective-permute-start(bf16[8,16512]{1,0:T(8,128)(2,1)S(1)} %slice.149), channel_id=1, source_target_pairs={{0,4},{8,0},{16,8},{24,16},{28,24},{20,28},{12,20},{4,12},{1,5},{9... | collective-permute-start | bytes 792584 | tf_op jit(solution)/shard_map/ppermute | solution.py:31
  164.9 9.8 %copy-start.1 = (bf16[512,512]{1,0:T(8,128)(2,1)S(1)}, bf16[512,512]{1,0:T(8,128)(2,1)}, u32[]{:S(2)}) copy-start(bf16[512,512]{1,0:T(8,128)(2,1)} %param.16) | copy-start | bytes 1572868

commit v4 on v3

--- a/solution.py
+++ b/solution.py
@@ -1,6 +1,8 @@
 import jax
 import jax.numpy as jnp
 from jax import lax
+from jax.experimental import pallas as pl
+from jax.experimental.pallas import tpu as pltpu
 from jax.sharding import PartitionSpec as P
 
 META = 128
@@ -33,6 +35,35 @@
     return got
 
 
+def contract_kernel(codes_ref, hi_ref, lo_ref, x_ref, out_ref, *, slots, width):
+    g = pl.program_id(0)
+    acc = jnp.zeros(out_ref.shape[1:], jnp.float32)
+    for s in range(slots):
+        code = codes_ref[g, s]
+        xs = x_ref[0, :, s * width:(s + 1) * width]
+        for table in (hi_ref, lo_ref):
+            acc = acc + lax.dot_general(
+                table[code], xs, (((1,), (1,)), ((), ())), preferred_element_type=jnp.float32
+            )
+    out_ref[0] = acc
+
+
+def contract(codes, table_hi, table_lo, xstack, slots, width):
+    groups, rows, unused = xstack.shape
+    codes_total, ri, unused = table_hi.shape
+    table_spec = pl.BlockSpec((codes_total, ri, width), lambda g, c: (0, 0, 0))
+    grid_spec = pltpu.PrefetchScalarGridSpec(
+        num_scalar_prefetch=1,
+        grid=(groups,),
+        in_specs=[table_spec, table_spec, pl.BlockSpec((1, rows, slots * width), lambda g, c: (g, 0, 0))],
+        out_specs=pl.BlockSpec((1, ri, rows), lambda g, c: (g, 0, 0)),
+    )
+    body = lambda *refs: contract_kernel(*refs, slots=slots, width=width)
+    return pl.pallas_call(
+        body, out_shape=jax.ShapeDtypeStruct((groups, ri, rows), jnp.float32), grid_spec=grid_spec
+    )(codes, table_hi, table_lo, xstack)
+
+
 def on_device(x_blocks, pair_ids, live_count, green_occ, green_virt):
     local_blocks = x_blocks[0]
     slot_count, block_size, ri_cols = local_blocks.shape
@@ -56,10 +87,15 @@
     meta = meta.at[0, :slot_count].set(pair_list.astype(local_blocks.dtype))
     packed = jnp.concatenate([xt, meta], axis=1)
 
-    band_got = ring_gather(packed, "band", band_count)
+    rows2d = masked.reshape(slot_count * block_size, ri_cols)
+    meta_rows = jnp.zeros((16, ri_cols), local_blocks.dtype)
+    meta_rows = meta_rows.at[0, :slot_count].set(pair_list.astype(local_blocks.dtype))
+    band_packed = jnp.concatenate([rows2d, meta_rows], axis=0)
+    band_got = ring_gather(band_packed, "band", band_count)
     band_ids = jnp.stack([src for src, unused in band_got])
     xg = jnp.stack([buf for unused, buf in band_got])
-    codes_g = xg[:, 0, flat:flat + slot_count].astype(jnp.float32).astype(jnp.int32)
+    kdim = slot_count * block_size
+    codes_g = xg[:, kdim, :slot_count].astype(jnp.float32).astype(jnp.int32)
     grp_got = ring_gather(packed, "grp", group_count)
 
     occ_cols = lax.dynamic_slice_in_dim(green_occ, band * band_orbs, band_orbs, 1)
@@ -68,11 +104,12 @@
     occ_rows = occ_rows.reshape(band_count, slot_count, block_size, band_orbs)
     halves = (codes_g % 2)[:, None, :] == jnp.arange(2, dtype=jnp.int32)[None, :, None]
     occ_sel = occ_rows[:, None] * halves.astype(occ_rows.dtype)[..., None, None]
-    xg_x = xg[:, :, :flat].reshape(band_count, ri_local, slot_count, block_size, block_size)
-    occ_three = jnp.einsum(
-        "bpsji,bhsil->plbhj", xg_x, occ_sel, preferred_element_type=jnp.float32
+    occ_sel = occ_sel.reshape(band_count, 2, kdim, band_orbs)
+    occ_raw = jnp.einsum(
+        "bkr,bhkl->bhrl", xg[:, :kdim, :], occ_sel, preferred_element_type=jnp.float32
     ).astype(jnp.bfloat16)
-    occ_three = occ_three.reshape(ri_local, band_orbs, orbitals)
+    occ_raw = occ_raw.reshape(band_count, 2, ri_local, block_size, band_orbs)
+    occ_three = jnp.transpose(occ_raw, (2, 4, 0, 1, 3)).reshape(ri_local, band_orbs, orbitals)
 
     col_index = (band_ids[:, None] * band_orbs + jnp.arange(band_orbs, dtype=jnp.int32)).reshape(-1)
     virt_cols = jnp.take(green_virt, col_index, axis=1)
@@ -82,20 +119,19 @@
     folded = folded.reshape(ri_local, 2, block_size, orbitals // block_size, block_size)
     folded = jnp.transpose(folded, (0, 3, 1, 2, 4)).reshape(ri_local, code_count, block_size * block_size)
 
-    fold_hi = folded.astype(jnp.bfloat16)
-    fold_lo = (folded - fold_hi.astype(jnp.float32)).astype(jnp.bfloat16)
+    fold_hi = lax.reduce_precision(folded, exponent_bits=8, mantissa_bits=7)
+    fold_lo = (folded - fold_hi).astype(jnp.bfloat16)
+    fold_hi = fold_hi.astype(jnp.bfloat16)
+    fold_hi = jnp.transpose(fold_hi, (1, 0, 2))
+    fold_lo = jnp.transpose(fold_lo, (1, 0, 2))
 
-    partial_value = jnp.zeros((ri_local, group_count * ri_local), jnp.float32)
-    for src, buf in grp_got:
-        codes = buf[0, flat:flat + slot_count].astype(jnp.float32).astype(jnp.int32)
-        x_part = buf[:, :flat]
-        part = jnp.zeros((ri_local, ri_local), jnp.float32)
-        for table in (fold_hi, fold_lo):
-            sel = jnp.take(table, codes, axis=1).reshape(ri_local, flat)
-            part = part + lax.dot_general(
-                sel, x_part, (((1,), (1,)), ((), ())), preferred_element_type=jnp.float32
-            )
-        partial_value = lax.dynamic_update_slice_in_dim(partial_value, part, src * ri_local, 1)
+    grp_ids = jnp.stack([src for src, unused in grp_got])
+    xstack = jnp.stack([buf for unused, buf in grp_got])
+    codes_b = xstack[:, 0, flat:flat + slot_count].astype(jnp.float32).astype(jnp.int32)
+    parts = contract(codes_b, fold_hi, fold_lo, xstack, slot_count, block_size * block_size)
+    order = jnp.zeros((group_count,), jnp.int32).at[grp_ids].set(jnp.arange(group_count, dtype=jnp.int32))
+    parts = jnp.take(parts, order, axis=0)
+    partial_value = jnp.transpose(parts, (1, 0, 2)).reshape(ri_local, group_count * ri_local)
     response = lax.psum_scatter(partial_value, "band", scatter_dimension=0, tiled=True)
     return response
 

time: 177 us -> 144 us (0.81)
  local copies, waits for them, and re-layouts: 89.5 us -> 65.7 us
  matrix products: 25.7 us -> 6.66 us
  waiting for transfers between devices: 5.29 us -> 17.2 us
  Pallas kernels: 0 us -> 9.83 us
  other arithmetic: 21.8 us -> 15.6 us
  between operations: 13 us -> 8.09 us
    gather x16 -> x1, local copies, waits for them, and re-layouts: 31.7 us -> 1.39 us  [on_device(): parts = jnp.take(parts, order, axis=0)]
    dot_general x17 -> x1, matrix products: 23.4 us -> 3.26 us  [on_device(): jnp.einsum('bkr,bhkl->bhrl', xg[:, :kdim, :], occ_sel, preferred_element_...]
    transpose x1 -> x2, local copies, waits for them, and re-layouts: 0.99 us -> 11.4 us  [the longest x1 7.3 us: on_device(): jnp.transpose(occ_raw, (2, 4, 0, 1, 3))]
    pallas_call x0 -> x1, Pallas kernels: none -> 9.83 us  [contract(): pl.pallas_call(body, out_shape=jax.ShapeDtypeStruct((groups, ri, rows), j...]
    unnamed x41 -> x23, local copies, waits for them, and re-layouts: 2.95 us -> 11.8 us
    reshape x17 -> x1, local copies, waits for them, and re-layouts: 7.92 us -> 0.08 us  [on_device(): jnp.transpose(parts, (1, 0, 2)).reshape(ri_local, group_count * ri_local)]
    ppermute x4, waiting for transfers between devices: 0.93 us -> 6.45 us  [ring_gather(): ahead = lax.ppermute(ahead, axis, fwd)]
    transpose x0 -> x1, other arithmetic: none -> 4.93 us  [on_device(): fold_lo = jnp.transpose(fold_lo, (1, 0, 2))]
  transfers between devices with their start and end apart: 12 -> 12, of which waited for: 4 -> 6; matrix products, arithmetic and copies ran while one was open for 66% -> 57% of each run, Pallas kernels for 0% -> 0%
where the time goes in v4:
time: 144 us; the launch traced here: 142 us
  local copies, waits for them, and re-layouts  65.7 us (46%)
  waiting for transfers between devices  17.2 us (12%)
  other arithmetic  15.6 us (11%)
  starting transfers between devices  13.3 us (9%)
  Pallas kernels  9.83 us (7%)
  between operations  8.09 us (6%)
  matrix products  6.66 us (5%)
  blocking collectives  5.75 us (4%)
    unnamed x23, local copies, waits for them, and re-layouts  11.8 us
    pallas_call x1, Pallas kernels, contract(): pl.pallas_call(body, out_shape=jax.ShapeDtypeStruct((groups, ri, rows), j...  9.83 us
    dot_general x1, local copies, waits for them, and re-layouts, on_device(): lax.dot_general(occ_three, virt_cols, (((2,), (1,)), ((), ())), preferred...  9.35 us
    reshape x1, local copies, waits for them, and re-layouts, on_device(): jnp.transpose(folded, (0, 3, 1, 2, 4))  7.88 us
    ppermute x4, starting transfers between devices, ring_gather(): ahead = lax.ppermute(ahead, axis, fwd)  7.75 us
    transpose x1, local copies, waits for them, and re-layouts, on_device(): jnp.transpose(occ_raw, (2, 4, 0, 1, 3))  7.3 us
    ppermute x4, waiting for transfers between devices, ring_gather(): ahead = lax.ppermute(ahead, axis, fwd)  6.45 us
    unnamed x1, blocking collectives  5.75 us
  transfers between devices with their start and end apart: 12, of which 6 were waited for; matrix products, arithmetic and copies ran while one was open for 57% of the time, Pallas kernels for 0%

profile of v4, /device:TPU:0, one launch (start us, length us, event | category | flops | bytes accessed | tf_op | source)
XLA Modules:
  0.0 142.2 jit_solution(15684864520947387811)
XLA Ops:
  0.0 0.7 convert_bitcast_fusion.1
  1.5 1.1 bitcast_multiply_fusion
  2.7 1.1 fusion.28
  3.8 2.9 %collective-permute-start.8 = (bf16[272,1024]{1,0:T(8,128)(2,1)}, bf16[272,1024]{1,0:T(8,128)(2,1)}, u32[]{:S(2)}, u32[]{:S(2)}) collective-permute-start(bf16[272,1024]{1,0:T(8,128)(2,1)} %get-tuple-element.34), channel_id=1, source_target_pairs={{0,2},{2,3},{3,1},{1,0},{4,6},{6,7},{7,5},{5,4},{8,10},{10,11},{11... | collective-permute-start | bytes 1671176 | tf_op jit(solution)/shard_map/ppermute | solution.py:27
  6.8 1.8 %squeeze.6 = bf16[4,64,16,64]{3,2,1,0:T(8,128)(2,1)S(1)} reshape(bf16[1,4,64,1024]{3,2,1,0:T(8,128)(2,1)} %param.13) | data formatting | bytes 1048576 | tf_op jit(solution)/shard_map/squeeze | solution.py:68
  8.6 1.0 copy.38
  9.6 0.1 multiply_bitcast_fusion
  9.7 0.8 reshape.604
  10.6 1.6 %collective-permute-start = (bf16[16,16512]{1,0:T(8,128)(2,1)S(1)}, bf16[16,16512]{1,0:T(8,128)(2,1)}, u32[]{:S(2)}, u32[]{:S(2)}) collective-permute-start(bf16[16,16512]{1,0:T(8,128)(2,1)S(1)} %fusion.13), channel_id=1, source_target_pairs={{0,8},{8,16},{16,24},{24,28},{28,20},{20,12},{12,4},{4,0},{1,9},{9... | collective-permute-start | bytes 1585160 | tf_op jit(solution)/shard_map/ppermute | solution.py:27
  12.2 0.4 collective-permute-start.1
  12.7 0.6 dynamic_slice.48
  15.3 0.9 bitcast_dynamic-update-slice_fusion.6
  16.2 0.6 dynamic_slice.39
  21.3 0.7 fusion.30
  21.9 4.3 %stack.76 = s32[8,1]{0,1:T(1,128)S(1)} concatenate(s32[1,1]{0,1:T(1,128)} %bitcast, s32[1,1]{0,1:T(1,128)} %bitcast.2, s32[1,1]{0,1:T(1,128)} %bitcast.4, s32[1,1]{0,1:T(1,128)} %bitcast.6, s32[1,1]{0,1:T(1,128)} %bitcast.8, s32[1,1]{0,1:T(1,128)} %bitcast.10, s32[1,1]{0,1:T(1,128)} %bitcast.12, s32[1,1]{0,1:T(1,128)} %bitcast.14), dimensions={0} | concatenate | bytes 64 | tf_op jit(solution)/shard_map/stack | solution.py:128
  26.3 0.6 scatter_custom_fusion
  27.0 1.3 copy.43
  28.3 0.7 fusion.31
  28.9 1.9 %add_multiply_fusion = s32[4]{0:T(128)S(1)} fusion(s32[1]{0:T(128)} %get-tuple-element.43, s32[1]{0:T(128)} %get-tuple-element.44, s32[1]{0:T(128)} %get-tuple-element.42, s32[1]{0:T(128)} %bitcast.43), kind=kLoop, calls=%fused_computation.75 | loop fusion | flops 16 | bytes 32 | tf_op jit(solution)/shard_map/mul | solution.py:114
  31.0 0.6 dynamic-slice.13
  32.4 1.6 %collective-permute-start.2 = (bf16[16,16512]{1,0:T(8,128)(2,1)}, bf16[16,16512]{1,0:T(8,128)(2,1)}, u32[]{:S(2)}, u32[]{:S(2)}) collective-permute-start(bf16[16,16512]{1,0:T(8,128)(2,1)} %collective-permute-done), channel_id=1, source_target_pairs={{0,8},{8,16},{16,24},{24,28},{28,20},{20,12},{12,4},{4,0},{1,9},{9... | collective-permute-start | bytes 1585160 | tf_op jit(solution)/shard_map/ppermute | solution.py:27
  34.0 1.9 %bitcast_dynamic-update-slice_fusion.5 = bf16[8,16,16512]{2,1,0:T(8,128)(2,1)} fusion(bf16[8,16,16512]{2,1,0:T(8,128)(2,1)} %bitcast_dynamic-update-slice_fusion.6, bf16[16,16512]{1,0:T(8,128)(2,1)} %collective-permute-done), kind=kLoop, calls=%fused_computation.33 | loop fusion | bytes 1056768
  35.9 0.5 collective-permute-start.3
  36.3 1.0 slice.69
  37.3 2.0 %collective-permute-start.10 = (bf16[136,1024]{1,0:T(8,128)(2,1)S(1)}, bf16[136,1024]{1,0:T(8,128)(2,1)S(1)}, u32[]{:S(2)}, u32[]{:S(2)}) collective-permute-start(bf16[136,1024]{1,0:T(8,128)(2,1)S(1)} %slice.69), channel_id=1, source_target_pairs={{0,2},{2,3},{3,1},{1,0},{4,6},{6,7},{7,5},{5,4},{8,10},{10,11},{11... | collective-permute-start | bytes 835592 | tf_op jit(solution)/shard_map/ppermute | solution.py:32
  39.4 1.0 slice.70
  40.4 1.9 %bitcast_dynamic-update-slice_fusion.4 = bf16[8,16,16512]{2,1,0:T(8,128)(2,1)} fusion(bf16[8,16,16512]{2,1,0:T(8,128)(2,1)} %bitcast_dynamic-update-slice_fusion.5, bf16[16,16512]{1,0:T(8,128)(2,1)} %collective-permute-done.1), kind=kLoop, calls=%fused_computation.32 | loop fusion | bytes 1056768
  42.2 3.0 %collective-permute-done.10 = bf16[136,1024]{1,0:T(8,128)(2,1)S(1)} collective-permute-done((bf16[136,1024]{1,0:T(8,128)(2,1)S(1)}, bf16[136,1024]{1,0:T(8,128)(2,1)S(1)}, u32[]{:S(2)}, u32[]{:S(2)}) %collective-permute-start.10) | collective-permute-done | bytes 278560 | tf_op jit(solution)/shard_map/ppermute | solution.py:32
  45.2 1.7 %collective-permute-done.11 = bf16[136,1024]{1,0:T(8,128)(2,1)S(1)} collective-permute-done((bf16[136,1024]{1,0:T(8,128)(2,1)S(1)}, bf16[136,1024]{1,0:T(8,128)(2,1)S(1)}, u32[]{:S(2)}, u32[]{:S(2)}) %collective-permute-start.11) | collective-permute-done | bytes 278560 | tf_op jit(solution)/shard_map/ppermute | solution.py:33
  47.0 0.7 and_select_fusion
  47.7 0.1 add.297
  48.0 3.2 %gather_fusion = bf16[1024,128]{1,0:T(8,128)(2,1)S(1)} fusion(bf16[512,128]{1,0:T(8,128)(2,1)S(1)} %constant_dynamic-slice_fusion.1, s32[1024]{0:T(1024)S(1)} %get-tuple-element.46), kind=kCustom, calls=%fused_computation | custom fusion | bytes 528384 | tf_op jit(solution)/shard_map/jit(_take)/gather | solution.py:103
  51.2 0.2 broadcast_select_fusion
  51.4 0.1 copy.40
  51.7 0.1 mul.65
  51.8 3.3 %convert_bitcast_fusion = bf16[4,2,1024,128]{2,3,1,0:T(8,128)(2,1)} fusion(bf16[1,272,1024]{2,1,0:T(8,128)(2,1)S(1)} %maximum_bitcast_fusion, bf16[1,272,1024]{2,1,0:T(8,128)(2,1)} %bitcast.31, bf16[1,272,1024]{2,1,0:T(8,128)(2,1)} %bitcast.30, bf16[1,272,1024]{2,1,0:T(8,128)(2,1)S(1)} %copy-done.1, bf16[4,2,256]{2,1,0:T(2,128)(2,1)S(1)} %mul.65, ...), kind=kOutput, calls=%fused_computation.17 | convolution fusion | flops 546570240 | bytes 4591616 | tf_op jit(solution)/shard_map/bkr,bhkl->bhrl/dot_general | solution.py:108
  55.0 3.0 %copy.41 = bf16[4,2,1024,128]{3,2,1,0:T(8,128)(2,1)S(1)} copy(bf16[4,2,1024,128]{2,3,1,0:T(8,128)(2,1)} %convert_bitcast_fusion) | data formatting | bytes 4194304 | tf_op jit(solution)/shard_map/convert_element_type | solution.py:110
  58.1 7.3 %copy.42 = bf16[16,128,4,2,64]{4,3,2,1,0:T(2,128)(2,1)} copy(bf16[16,128,4,2,64]{1,4,0,3,2:T(8,128)(2,1)S(1)} %bitcast.104) | data formatting | bytes 4194304 | tf_op jit(solution)/shard_map/transpose | solution.py:112
  65.4 9.3 %reshape.642 = bf16[16,2,64,512,1]{3,2,1,0,4:T(8,128)(2,1)S(1)} reshape(bf16[16,128,4,2,64]{4,3,2,1,0:T(2,128)(2,1)} %copy.42) | data formatting | bytes 4194304 | tf_op jit(solution)/shard_map/dot_general | solution.py:116
  74.7 2.6 %gather_fusion.1 = bf16[512,512]{1,0:T(8,128)(2,1)} fusion(bf16[512,512]{0,1:T(8,128)(2,1)S(1)} %copy.43, s32[1024]{0:T(1024)S(1)} %get-tuple-element.45), kind=kCustom, calls=%fused_computation.1 | custom fusion | bytes 1050624 | tf_op jit(solution)/shard_map/jit(_take)/gather | solution.py:115
  77.4 1.2 select_bitcast_fusion
  78.5 1.1 copy.44
  79.6 3.4 %convolution_bitcast_fusion = f32[16,8,2,64,64]{4,3,1,2,0:T(8,128)S(1)} fusion(bf16[8,64,512,1,1]{2,1,0,4,3:T(8,128)(2,1)} %bitcast.106, bf16[16,2,64,512,1]{3,2,1,0,4:T(8,128)(2,1)S(1)} %reshape.642), kind=kOutput, calls=%fused_computation.7 | convolution fusion | flops 1073741824 | bytes 6815744 | tf_op jit(solution)/shard_map/dot_general | solution.py:116
  83.0 4.1 %copy.45 = f32[16,8,2,64,64]{4,3,0,2,1:T(8,128)} copy(f32[16,8,2,64,64]{4,3,1,2,0:T(8,128)S(1)} %convolution_bitcast_fusion) | data formatting | bytes 8388608 | tf_op jit(solution)/shard_map/transpose | solution.py:120
  87.1 7.9 %reshape.606 = f32[16,16,4096]{2,0,1:T(8,128)} reshape(f32[16,8,2,64,64]{4,3,0,2,1:T(8,128)} %copy.45) | data formatting | bytes 8388608 | tf_op jit(solution)/shard_map/reshape | solution.py:120
  95.0 4.9 %fusion.1 = (bf16[16,16,4096]{2,1,0:T(8,128)(2,1)}, bf16[16,16,4096]{2,1,0:T(8,128)(2,1)}) fusion(f32[16,16,4096]{2,0,1:T(8,128)} %reshape.606), kind=kLoop, calls=%fused_computation.8 | loop fusion | flops 4194304 | bytes 8388608 | tf_op jit(solution)/shard_map/transpose | solution.py:126
  99.9 1.6 %collective-permute-start.4 = (bf16[16,16512]{1,0:T(8,128)(2,1)}, bf16[16,16512]{1,0:T(8,128)(2,1)S(1)}, u32[]{:S(2)}, u32[]{:S(2)}) collective-permute-start(bf16[16,16512]{1,0:T(8,128)(2,1)} %collective-permute-done.2), channel_id=1, source_target_pairs={{0,8},{8,16},{16,24},{24,28},{28,20},{20,12},{12,4},{4,0},{1,9},{9... | collective-permute-start | bytes 1585160 | tf_op jit(solution)/shard_map/ppermute | solution.py:27
  101.5 1.9 %bitcast_dynamic-update-slice_fusion.3 = bf16[8,16,16512]{2,1,0:T(8,128)(2,1)} fusion(bf16[8,16,16512]{2,1,0:T(8,128)(2,1)} %bitcast_dynamic-update-slice_fusion.4, bf16[16,16512]{1,0:T(8,128)(2,1)} %collective-permute-done.2), kind=kLoop, calls=%fused_computation.31 | loop fusion | bytes 1056768
  103.4 0.5 collective-permute-start.5
  103.9 1.9 %bitcast_dynamic-update-slice_fusion.2 = bf16[8,16,16512]{2,1,0:T(8,128)(2,1)} fusion(bf16[8,16,16512]{2,1,0:T(8,128)(2,1)} %bitcast_dynamic-update-slice_fusion.3, bf16[16,16512]{1,0:T(8,128)(2,1)} %collective-permute-done.3), kind=kLoop, calls=%fused_computation.30 | loop fusion | bytes 1056768
  105.8 6.4 %collective-permute-done.4 = bf16[16,16512]{1,0:T(8,128)(2,1)S(1)} collective-permute-done((bf16[16,16512]{1,0:T(8,128)(2,1)}, bf16[16,16512]{1,0:T(8,128)(2,1)S(1)}, u32[]{:S(2)}, u32[]{:S(2)}) %collective-permute-start.4) | collective-permute-done | bytes 528416 | tf_op jit(solution)/shard_map/ppermute | solution.py:27
  112.2 1.6 %collective-permute-start.6 = (bf16[8,16512]{1,0:T(8,128)(2,1)S(1)}, bf16[8,16512]{1,0:T(8,128)(2,1)S(1)}, u32[]{:S(2)}, u32[]{:S(2)}) collective-permute-start(bf16[8,16512]{1,0:T(8,128)(2,1)S(1)} %slice.66), channel_id=1, source_target_pairs={{0,8},{8,16},{16,24},{24,28},{28,20},{20,12},{12,4},{4,0},{1,9},{9... | collective-permute-start | bytes 792584 | tf_op jit(solution)/shard_map/ppermute | solution.py:32
  113.9 1.9 %collective-permute-done.5 = bf16[16,16512]{1,0:T(8,128)(2,1)S(1)} collective-permute-done((bf16[16,16512]{1,0:T(8,128)(2,1)}, bf16[16,16512]{1,0:T(8,128)(2,1)S(1)}, u32[]{:S(2)}, u32[]{:S(2)}) %collective-permute-start.5) | collective-permute-done | bytes 528416 | tf_op jit(solution)/shard_map/ppermute | solution.py:28
  115.8 0.5 collective-permute-start.7
  116.3 0.8 bitcast_dynamic-update-slice_fusion.1
  117.1 0.8 bitcast_dynamic-update-slice_fusion
  117.9 0.8 collective-permute-done.6
  118.7 3.5 %collective-permute-done.7 = bf16[8,16512]{1,0:T(8,128)(2,1)S(1)} collective-permute-done((bf16[8,16512]{1,0:T(8,128)(2,1)S(1)}, bf16[8,16512]{1,0:T(8,128)(2,1)S(1)}, u32[]{:S(2)}, u32[]{:S(2)}) %collective-permute-start.7) | collective-permute-done | bytes 264224 | tf_op jit(solution)/shard_map/ppermute | solution.py:33
  122.2 0.9 fusion.14.refs_3_
  123.1 1.3 fusion.18
  124.4 9.8 %shard_map.91 = f32[8,16,16]{2,1,0:T(8,128)} custom-call(s32[8,4]{1,0:T(8,128)} %bitcast.107, bf16[16,16,4096]{2,1,0:T(8,128)(2,1)} %get-tuple-element.32.refs_1_, bf16[16,16,4096]{2,1,0:T(8,128)(2,1)} %get-tuple-element.31.refs_2_, bf16[8,16,16512]{2,1,0:T(8,128)(2,1)} %fusion.14.refs_3_), custom_call_target="tpu_custom_call" | custom-call | tf_op jit(solution)/shard_map/pallas_call | solution.py:62
  134.2 1.4 gather_fusion.2
  135.8 5.8 %all-reduce.2 = f32[16,128]{1,0:T(8,128)S(1)} all-reduce(f32[16,128]{1,0:T(8,128)S(1)} %reshape.607), channel_id=2, replica_groups=mesh['grp'=8,'band'=4] {'band'}, use_global_device_ids=true, to_apply=%region_1.0.clone | all-reduce | flops 2048 | bytes 16384
  141.6 0.6 constant_dynamic-slice_fusion
  (52 shorter events, 1.2 us)
Async XLA Ops:
  0.0 31.0 %copy-start = (bf16[512,512]{1,0:T(8,128)(2,1)S(1)}, bf16[512,512]{1,0:T(8,128)(2,1)}, u32[]{:S(2)}) copy-start(bf16[512,512]{1,0:T(8,128)(2,1)} %param.16) | copy-start | bytes 1572868
  3.8 8.9 %copy-start.6 = (s32[4]{0:T(128)S(1)}, s32[4]{0:T(128)}, u32[]{:S(2)}) copy-start(s32[4]{0:T(128)} %constant.218.clone) | copy-start | bytes 52
  3.8 32.5 %collective-permute-start.8 = (bf16[272,1024]{1,0:T(8,128)(2,1)}, bf16[272,1024]{1,0:T(8,128)(2,1)}, u32[]{:S(2)}, u32[]{:S(2)}) collective-permute-start(bf16[272,1024]{1,0:T(8,128)(2,1)} %get-tuple-element.34), channel_id=1, source_target_pairs={{0,2},{2,3},{3,1},{1,0},{4,6},{6,7},{7,5},{5,4},{8,10},{10,11},{11... | collective-permute-start | bytes 1671176 | tf_op jit(solution)/shard_map/ppermute | solution.py:27
  6.8 32.6 %collective-permute-start.9 = (bf16[272,1024]{1,0:T(8,128)(2,1)}, bf16[272,1024]{1,0:T(8,128)(2,1)}, u32[]{:S(2)}, u32[]{:S(2)}) collective-permute-start(bf16[272,1024]{1,0:T(8,128)(2,1)} %get-tuple-element.34), channel_id=1, source_target_pairs={{0,1},{2,0},{3,2},{1,3},{4,5},{6,4},{7,6},{5,7},{8,9},{10,8},{11,1... | collective-permute-start | bytes 1671176 | tf_op jit(solution)/shard_map/ppermute | solution.py:28
  8.5 7.7 %copy-start.5 = (s32[8]{0:T(128)S(1)}, s32[8]{0:T(128)}, u32[]{:S(2)}) copy-start(s32[8]{0:T(128)} %constant.220.clone) | copy-start | bytes 100
  8.5 12.7 %copy-start.2 = (s32[8]{0:T(128)S(1)}, s32[8]{0:T(128)}, u32[]{:S(2)}) copy-start(s32[8]{0:T(128)} %constant.221.clone) | copy-start | bytes 100
  8.6 19.7 %copy-start.3 = (s32[4]{0:T(128)S(1)}, s32[4]{0:T(128)}, u32[]{:S(2)}) copy-start(s32[4]{0:T(128)} %constant.219.clone) | copy-start | bytes 52
  9.6 21.4 %copy-start.4 = (u32[32]{0:T(128)S(1)}, u32[32]{0:T(128)}, u32[]{:S(2)}) copy-start(u32[32]{0:T(128)} %constant.231) | copy-start | bytes 388
  10.5 36.4 %copy-start.1 = (bf16[1,272,1024]{2,1,0:T(8,128)(2,1)S(1)}, bf16[1,272,1024]{2,1,0:T(8,128)(2,1)}, u32[]{:S(2)}) copy-start(bf16[1,272,1024]{2,1,0:T(8,128)(2,1)} %get-tuple-element.33) | copy-start | bytes 1671172
  10.6 21.7 %collective-permute-start = (bf16[16,16512]{1,0:T(8,128)(2,1)S(1)}, bf16[16,16512]{1,0:T(8,128)(2,1)}, u32[]{:S(2)}, u32[]{:S(2)}) collective-permute-start(bf16[16,16512]{1,0:T(8,128)(2,1)S(1)} %fusion.13), channel_id=1, source_target_pairs={{0,8},{8,16},{16,24},{24,28},{28,20},{20,12},{12,4},{4,0},{1,9},{9... | collective-permute-start | bytes 1585160 | tf_op jit(solution)/shard_map/ppermute | solution.py:27
  12.2 23.7 %collective-permute-start.1 = (bf16[16,16512]{1,0:T(8,128)(2,1)S(1)}, bf16[16,16512]{1,0:T(8,128)(2,1)}, u32[]{:S(2)}, u32[]{:S(2)}) collective-permute-start(bf16[16,16512]{1,0:T(8,128)(2,1)S(1)} %fusion.13), channel_id=1, source_target_pairs={{0,4},{8,0},{16,8},{24,16},{28,24},{20,28},{12,20},{4,12},{1,5},{9... | collective-permute-start | bytes 1585160 | tf_op jit(solution)/shard_map/ppermute | solution.py:28
  32.4 67.6 %collective-permute-start.2 = (bf16[16,16512]{1,0:T(8,128)(2,1)}, bf16[16,16512]{1,0:T(8,128)(2,1)}, u32[]{:S(2)}, u32[]{:S(2)}) collective-permute-start(bf16[16,16512]{1,0:T(8,128)(2,1)} %collective-permute-done), channel_id=1, source_target_pairs={{0,8},{8,16},{16,24},{24,28},{28,20},{20,12},{12,4},{4,0},{1,9},{9... | collective-permute-start | bytes 1585160 | tf_op jit(solution)/shard_map/ppermute | solution.py:27
  35.9 67.5 %collective-permute-start.3 = (bf16[16,16512]{1,0:T(8,128)(2,1)}, bf16[16,16512]{1,0:T(8,128)(2,1)}, u32[]{:S(2)}, u32[]{:S(2)}) collective-permute-start(bf16[16,16512]{1,0:T(8,128)(2,1)} %collective-permute-done.1), channel_id=1, source_target_pairs={{0,4},{8,0},{16,8},{24,16},{28,24},{20,28},{12,20},{4,12},{1,5},{9... | collective-permute-start | bytes 1585160 | tf_op jit(solution)/shard_map/ppermute | solution.py:28
  37.3 7.9 %collective-permute-start.10 = (bf16[136,1024]{1,0:T(8,128)(2,1)S(1)}, bf16[136,1024]{1,0:T(8,128)(2,1)S(1)}, u32[]{:S(2)}, u32[]{:S(2)}) collective-permute-start(bf16[136,1024]{1,0:T(8,128)(2,1)S(1)} %slice.69), channel_id=1, source_target_pairs={{0,2},{2,3},{3,1},{1,0},{4,6},{6,7},{7,5},{5,4},{8,10},{10,11},{11... | collective-permute-start | bytes 835592 | tf_op jit(solution)/shard_map/ppermute | solution.py:32
  40.3 6.6 %collective-permute-start.11 = (bf16[136,1024]{1,0:T(8,128)(2,1)S(1)}, bf16[136,1024]{1,0:T(8,128)(2,1)S(1)}, u32[]{:S(2)}, u32[]{:S(2)}) collective-permute-start(bf16[136,1024]{1,0:T(8,128)(2,1)S(1)} %slice.70), channel_id=1, source_target_pairs={{0,1},{2,0},{3,2},{1,3},{4,5},{6,4},{7,6},{5,7},{8,9},{10,8},{11,1... | collective-permute-start | bytes 835592 | tf_op jit(solution)/shard_map/ppermute | solution.py:33
  99.9 12.3 %collective-permute-start.4 = (bf16[16,16512]{1,0:T(8,128)(2,1)}, bf16[16,16512]{1,0:T(8,128)(2,1)S(1)}, u32[]{:S(2)}, u32[]{:S(2)}) collective-permute-start(bf16[16,16512]{1,0:T(8,128)(2,1)} %collective-permute-done.2), channel_id=1, source_target_pairs={{0,8},{8,16},{16,24},{24,28},{28,20},{20,12},{12,4},{4,0},{1,9},{9... | collective-permute-start | bytes 1585160 | tf_op jit(solution)/shard_map/ppermute | solution.py:27
  103.4 12.3 %collective-permute-start.5 = (bf16[16,16512]{1,0:T(8,128)(2,1)}, bf16[16,16512]{1,0:T(8,128)(2,1)S(1)}, u32[]{:S(2)}, u32[]{:S(2)}) collective-permute-start(bf16[16,16512]{1,0:T(8,128)(2,1)} %collective-permute-done.3), channel_id=1, source_target_pairs={{0,4},{8,0},{16,8},{24,16},{28,24},{20,28},{12,20},{4,12},{1,5},{9... | collective-permute-start | bytes 1585160 | tf_op jit(solution)/shard_map/ppermute | solution.py:28
  112.2 6.4 %collective-permute-start.6 = (bf16[8,16512]{1,0:T(8,128)(2,1)S(1)}, bf16[8,16512]{1,0:T(8,128)(2,1)S(1)}, u32[]{:S(2)}, u32[]{:S(2)}) collective-permute-start(bf16[8,16512]{1,0:T(8,128)(2,1)S(1)} %slice.66), channel_id=1, source_target_pairs={{0,8},{8,16},{16,24},{24,28},{28,20},{20,12},{12,4},{4,0},{1,9},{9... | collective-permute-start | bytes 792584 | tf_op jit(solution)/shard_map/ppermute | solution.py:32
  115.8 6.4 %collective-permute-start.7 = (bf16[8,16512]{1,0:T(8,128)(2,1)S(1)}, bf16[8,16512]{1,0:T(8,128)(2,1)S(1)}, u32[]{:S(2)}, u32[]{:S(2)}) collective-permute-start(bf16[8,16512]{1,0:T(8,128)(2,1)S(1)} %slice.67), channel_id=1, source_target_pairs={{0,4},{8,0},{16,8},{24,16},{28,24},{20,28},{12,20},{4,12},{1,5},{9... | collective-permute-start | bytes 792584 | tf_op jit(solution)/shard_map/ppermute | solution.py:33

commit v5 on v4

--- a/solution.py
+++ b/solution.py
@@ -87,7 +87,8 @@
     meta = meta.at[0, :slot_count].set(pair_list.astype(local_blocks.dtype))
     packed = jnp.concatenate([xt, meta], axis=1)
 
-    rows2d = masked.reshape(slot_count * block_size, ri_cols)
+    rows2d = masked.reshape(slot_count, block_size, ri_local, block_size)
+    rows2d = jnp.transpose(rows2d, (0, 1, 3, 2)).reshape(slot_count * block_size, ri_cols)
     meta_rows = jnp.zeros((16, ri_cols), local_blocks.dtype)
     meta_rows = meta_rows.at[0, :slot_count].set(pair_list.astype(local_blocks.dtype))
     band_packed = jnp.concatenate([rows2d, meta_rows], axis=0)
@@ -108,22 +109,26 @@
     occ_raw = jnp.einsum(
         "bkr,bhkl->bhrl", xg[:, :kdim, :], occ_sel, preferred_element_type=jnp.float32
     ).astype(jnp.bfloat16)
-    occ_raw = occ_raw.reshape(band_count, 2, ri_local, block_size, band_orbs)
-    occ_three = jnp.transpose(occ_raw, (2, 4, 0, 1, 3)).reshape(ri_local, band_orbs, orbitals)
+    occ_raw = occ_raw.reshape(band_count, 2, block_size, ri_local, band_orbs)
 
-    col_index = (band_ids[:, None] * band_orbs + jnp.arange(band_orbs, dtype=jnp.int32)).reshape(-1)
-    virt_cols = jnp.take(green_virt, col_index, axis=1)
+    virt_cols = jnp.concatenate(
+        [lax.dynamic_slice_in_dim(green_virt, band_ids[k] * band_orbs, band_orbs, 1) for k in range(band_count)],
+        axis=1,
+    ).reshape(orbitals, band_count, 2, block_size)
     folded = lax.dot_general(
-        occ_three, virt_cols, (((2,), (1,)), ((), ())), preferred_element_type=jnp.float32
+        occ_raw, virt_cols, (((0, 1, 2), (1, 2, 3)), ((), ())), preferred_element_type=jnp.float32
     )
-    folded = folded.reshape(ri_local, 2, block_size, orbitals // block_size, block_size)
-    folded = jnp.transpose(folded, (0, 3, 1, 2, 4)).reshape(ri_local, code_count, block_size * block_size)
-
     fold_hi = lax.reduce_precision(folded, exponent_bits=8, mantissa_bits=7)
     fold_lo = (folded - fold_hi).astype(jnp.bfloat16)
     fold_hi = fold_hi.astype(jnp.bfloat16)
-    fold_hi = jnp.transpose(fold_hi, (1, 0, 2))
-    fold_lo = jnp.transpose(fold_lo, (1, 0, 2))
+
+    def table(part):
+        part = part.reshape(ri_local, 2, block_size, orbitals // block_size, block_size)
+        part = jnp.transpose(part, (3, 1, 0, 2, 4))
+        return part.reshape(code_count, ri_local, block_size * block_size)
+
+    fold_hi = table(fold_hi)
+    fold_lo = table(fold_lo)
 
     grp_ids = jnp.stack([src for src, unused in grp_got])
     xstack = jnp.stack([buf for unused, buf in grp_got])

time: 144 us -> 143 us (level)
  other arithmetic: 15.6 us -> 6.46 us
  local copies, waits for them, and re-layouts: 65.7 us -> 70.7 us
  between operations: 8.09 us -> 10.1 us
    reshape x1 -> x8, local copies, waits for them, and re-layouts: 7.88 us -> 34.6 us  [the longest x4 20.5 us: table(): part.reshape(ri_local, 2, block_size, orbitals // block_size, block_size)]
    transpose x2 -> x1, local copies, waits for them, and re-layouts: 11.4 us -> 0.68 us  [on_device(): xt = jnp.transpose(xt, (2, 0, 3, 1)).reshape(ri_local, flat)]
    dot_general x1 -> x0, local copies, waits for them, and re-layouts: 9.35 us -> none  [on_device(): lax.dot_general(occ_three, virt_cols, (((2,), (1,)), ((), ())), preferred...]
    transpose x2 -> x1, other arithmetic: 5.07 us -> 0.61 us  [on_device(): jnp.transpose(rows2d, (0, 1, 3, 2))]
    mul x2 -> x0, other arithmetic: 3.09 us -> none  [the longest x1 1.95 us: on_device(): band_ids[:, None] * band_orbs + jnp.arange(band_orbs, dtype=jnp.int32)]
    gather x1 -> x0, local copies, waits for them, and re-layouts: 2.65 us -> none  [on_device(): virt_cols = jnp.take(green_virt, col_index, axis=1)]
    unnamed x23 -> x20, local copies, waits for them, and re-layouts: 11.8 us -> 10.5 us
  transfers between devices with their start and end apart: 12 -> 12, of which waited for: 6 -> 6; matrix products, arithmetic and copies ran while one was open for 57% -> 52% of each run, Pallas kernels for 0% -> 0%
where the time goes in v5:
time: 143 us; the launch traced here: 141 us
  local copies, waits for them, and re-layouts  70.7 us (49%)
  waiting for transfers between devices  17.3 us (12%)
  starting transfers between devices  13.3 us (9%)
  between operations  10.1 us (7%)
  Pallas kernels  9.84 us (7%)
  matrix products  7.79 us (5%)
  other arithmetic  6.46 us (5%)
  blocking collectives  5.75 us (4%)
    reshape x4, local copies, waits for them, and re-layouts, table(): part.reshape(ri_local, 2, block_size, orbitals // block_size, block_size)  20.5 us
    reshape x2, local copies, waits for them, and re-layouts, table(): return part.reshape(code_count, ri_local, block_size * block_size)  13.2 us
    unnamed x20, local copies, waits for them, and re-layouts  10.5 us
    pallas_call x1, Pallas kernels, contract(): pl.pallas_call(body, out_shape=jax.ShapeDtypeStruct((groups, ri, rows), j...  9.84 us
    ppermute x4, starting transfers between devices, ring_gather(): ahead = lax.ppermute(ahead, axis, fwd)  7.78 us
    ppermute x4, waiting for transfers between devices, ring_gather(): ahead = lax.ppermute(ahead, axis, fwd)  6.46 us
    unnamed x1, blocking collectives  5.75 us
    ppermute x2, waiting for transfers between devices, ring_gather(): second = lax.ppermute(behind[rows:], axis, bwd)  5.22 us
  transfers between devices with their start and end apart: 12, of which 6 were waited for; matrix products, arithmetic and copies ran while one was open for 52% of the time, Pallas kernels for 0%

profile of v5, /device:TPU:0, one launch (start us, length us, event | category | flops | bytes accessed | tf_op | source)
XLA Modules:
  0.0 141.3 jit_solution(9272992043274920602)
XLA Ops:
  0.0 0.7 convert_bitcast_fusion.1
  0.7 1.8 %squeeze.4 = bf16[4,64,16,64]{3,2,1,0:T(8,128)(2,1)S(1)} reshape(bf16[1,4,64,1024]{3,2,1,0:T(8,128)(2,1)} %param.13) | data formatting | bytes 1048576 | tf_op jit(solution)/shard_map/squeeze | solution.py:68
  2.4 2.2 %copy.43 = bf16[4,64,16,64]{1,0,2,3:T(4,128)(2,1)S(1)} copy(bf16[4,64,16,64]{3,2,1,0:T(8,128)(2,1)S(1)} %squeeze.4) | data formatting | bytes 1048576 | tf_op jit(solution)/shard_map/squeeze | solution.py:68
  5.3 0.6 multiply_bitcast_fusion
  5.9 0.7 reshape.521
  6.6 0.2 copy.46
  6.8 0.9 fusion.27
  7.7 2.9 %collective-permute-start.8 = (bf16[272,1024]{1,0:T(8,128)(2,1)}, bf16[272,1024]{1,0:T(8,128)(2,1)}, u32[]{:S(2)}, u32[]{:S(2)}) collective-permute-start(bf16[272,1024]{1,0:T(8,128)(2,1)} %get-tuple-element.36), channel_id=1, source_target_pairs={{0,2},{2,3},{3,1},{1,0},{4,6},{6,7},{7,5},{5,4},{8,10},{10,11},{11... | collective-permute-start | bytes 1671176 | tf_op jit(solution)/shard_map/ppermute | solution.py:27
  10.7 0.7 copy.44
  11.4 0.8 reshape.520
  12.3 1.6 %collective-permute-start = (bf16[16,16512]{1,0:T(8,128)(2,1)S(1)}, bf16[16,16512]{1,0:T(8,128)(2,1)}, u32[]{:S(2)}, u32[]{:S(2)}) collective-permute-start(bf16[16,16512]{1,0:T(8,128)(2,1)S(1)} %fusion.12), channel_id=1, source_target_pairs={{0,8},{8,16},{16,24},{24,28},{28,20},{20,12},{12,4},{4,0},{1,9},{9... | collective-permute-start | bytes 1585160 | tf_op jit(solution)/shard_map/ppermute | solution.py:27
  13.9 0.4 collective-permute-start.1
  14.3 0.6 dynamic_slice.61
  16.9 0.7 fusion.30
  19.5 0.8 bitcast_dynamic-update-slice_fusion.6
  20.3 0.6 dynamic_slice.51
  25.6 1.0 constant_dynamic-slice_fusion.3
  26.7 0.2 copy.49
  27.0 0.7 fusion.29
  27.7 4.6 %stack.70 = s32[8,1]{0,1:T(1,128)S(1)} concatenate(s32[1,1]{0,1:T(1,128)} %bitcast, s32[1,1]{0,1:T(1,128)} %bitcast.2, s32[1,1]{0,1:T(1,128)} %bitcast.4, s32[1,1]{0,1:T(1,128)} %bitcast.6, s32[1,1]{0,1:T(1,128)} %bitcast.8, s32[1,1]{0,1:T(1,128)} %bitcast.10, s32[1,1]{0,1:T(1,128)} %bitcast.12, s32[1,1]{0,1:T(1,128)} %bitcast.14), dimensions={0} | concatenate | bytes 64 | tf_op jit(solution)/shard_map/stack | solution.py:133
  32.2 0.6 scatter_custom_fusion
  32.8 0.6 dynamic-slice.13
  34.1 1.6 %collective-permute-start.2 = (bf16[16,16512]{1,0:T(8,128)(2,1)}, bf16[16,16512]{1,0:T(8,128)(2,1)}, u32[]{:S(2)}, u32[]{:S(2)}) collective-permute-start(bf16[16,16512]{1,0:T(8,128)(2,1)} %collective-permute-done), channel_id=1, source_target_pairs={{0,8},{8,16},{16,24},{24,28},{28,20},{20,12},{12,4},{4,0},{1,9},{9... | collective-permute-start | bytes 1585160 | tf_op jit(solution)/shard_map/ppermute | solution.py:27
  35.8 1.9 %bitcast_dynamic-update-slice_fusion.5 = bf16[8,16,16512]{2,1,0:T(8,128)(2,1)} fusion(bf16[8,16,16512]{2,1,0:T(8,128)(2,1)} %bitcast_dynamic-update-slice_fusion.6, bf16[16,16512]{1,0:T(8,128)(2,1)} %collective-permute-done), kind=kLoop, calls=%fused_computation.33 | loop fusion | bytes 1056768
  37.7 0.5 collective-permute-start.3
  38.1 1.0 slice.67
  39.1 2.0 %collective-permute-start.10 = (bf16[136,1024]{1,0:T(8,128)(2,1)S(1)}, bf16[136,1024]{1,0:T(8,128)(2,1)S(1)}, u32[]{:S(2)}, u32[]{:S(2)}) collective-permute-start(bf16[136,1024]{1,0:T(8,128)(2,1)S(1)} %slice.67), channel_id=1, source_target_pairs={{0,2},{2,3},{3,1},{1,0},{4,6},{6,7},{7,5},{5,4},{8,10},{10,11},{11... | collective-permute-start | bytes 835592 | tf_op jit(solution)/shard_map/ppermute | solution.py:32
  41.1 1.0 slice.68
  42.1 1.9 %bitcast_dynamic-update-slice_fusion.4 = bf16[8,16,16512]{2,1,0:T(8,128)(2,1)} fusion(bf16[8,16,16512]{2,1,0:T(8,128)(2,1)} %bitcast_dynamic-update-slice_fusion.5, bf16[16,16512]{1,0:T(8,128)(2,1)} %collective-permute-done.1), kind=kLoop, calls=%fused_computation.32 | loop fusion | bytes 1056768
  44.0 2.9 %collective-permute-done.10 = bf16[136,1024]{1,0:T(8,128)(2,1)S(1)} collective-permute-done((bf16[136,1024]{1,0:T(8,128)(2,1)S(1)}, bf16[136,1024]{1,0:T(8,128)(2,1)S(1)}, u32[]{:S(2)}, u32[]{:S(2)}) %collective-permute-start.10) | collective-permute-done | bytes 278560 | tf_op jit(solution)/shard_map/ppermute | solution.py:32
  47.0 1.7 %collective-permute-done.11 = bf16[136,1024]{1,0:T(8,128)(2,1)S(1)} collective-permute-done((bf16[136,1024]{1,0:T(8,128)(2,1)S(1)}, bf16[136,1024]{1,0:T(8,128)(2,1)S(1)}, u32[]{:S(2)}, u32[]{:S(2)}) %collective-permute-start.11) | collective-permute-done | bytes 278560 | tf_op jit(solution)/shard_map/ppermute | solution.py:33
  48.7 0.7 and_select_fusion
  49.5 0.1 add.257
  49.8 3.2 %gather_fusion = bf16[1024,128]{1,0:T(8,128)(2,1)S(1)} fusion(bf16[512,128]{1,0:T(8,128)(2,1)S(1)} %get-tuple-element.51, s32[1024]{0:T(1024)S(1)} %broadcast_clamp_fusion), kind=kCustom, calls=%fused_computation | custom fusion | bytes 528384 | tf_op jit(solution)/shard_map/jit(_take)/gather | solution.py:104
  53.0 0.2 broadcast_select_fusion
  53.2 0.1 copy.47
  53.4 0.1 mul.63
  53.5 3.3 %convert_bitcast_fusion = bf16[4,2,1024,128]{2,3,1,0:T(8,128)(2,1)} fusion(bf16[1,272,1024]{2,1,0:T(8,128)(2,1)S(1)} %maximum_bitcast_fusion, bf16[1,272,1024]{2,1,0:T(8,128)(2,1)} %bitcast.31, bf16[1,272,1024]{2,1,0:T(8,128)(2,1)} %bitcast.30, bf16[1,272,1024]{2,1,0:T(8,128)(2,1)S(1)} %get-tuple-element.35, bf16[4,2,256]{2,1,0:T(2,128)(2,1)S(1)} %mul.63, ...), kind=kOutput, calls=%fused_computation.16 | convolution fusion | flops 546570240 | bytes 4591616 | tf_op jit(solution)/shard_map/bkr,bhkl->bhrl/dot_general | solution.py:109
  56.8 4.0 %copy.48 = bf16[4,2,1024,128]{3,2,1,0:T(8,128)(2,1)} copy(bf16[4,2,1024,128]{2,3,1,0:T(8,128)(2,1)} %convert_bitcast_fusion) | data formatting | bytes 4194304 | tf_op jit(solution)/shard_map/convert_element_type | solution.py:111
  60.8 4.5 %fusion = (bf16[16,128,512]{2,1,0:T(8,128)(2,1)S(1)}, bf16[16,128,512]{2,1,0:T(8,128)(2,1)}) fusion(bf16[512,4,2,64,1]{0,3,2,1,4:T(8,128)(2,1)S(1)} %bitcast.101, bf16[4,2,64,16,128]{4,3,2,1,0:T(8,128)(2,1)} %bitcast.100), kind=kOutput, calls=%fused_computation.5 | convolution fusion | flops 1077936128 | bytes 6815744 | tf_op jit(solution)/shard_map/dot_general | solution.py:118
  65.3 6.2 %reshape.524 = bf16[16,2,64,8,64]{4,3,2,1,0:T(8,128)(2,1)} reshape(bf16[16,128,512]{2,1,0:T(8,128)(2,1)} %get-tuple-element.32) | data formatting | bytes 4194304 | tf_op jit(solution)/shard_map/reshape | solution.py:126
  71.5 5.3 %copy.65 = bf16[16,2,64,8,64]{4,2,0,1,3:T(8,128)(2,1)} copy(bf16[16,2,64,8,64]{4,3,2,1,0:T(8,128)(2,1)} %reshape.524) | data formatting | bytes 4194304 | tf_op jit(solution)/shard_map/reshape | solution.py:126
  76.8 6.6 %reshape.525.refs_1_ = bf16[16,16,4096]{2,1,0:T(8,128)(2,1)} reshape(bf16[8,2,16,64,64]{4,3,2,1,0:T(8,128)(2,1)} %bitcast.98) | data formatting | bytes 4194304 | tf_op jit(solution)/shard_map/reshape | solution.py:128
  83.4 3.7 %reshape.526 = bf16[16,2,64,8,64]{4,3,2,1,0:T(8,128)(2,1)} reshape(bf16[16,128,512]{2,1,0:T(8,128)(2,1)S(1)} %get-tuple-element.31) | data formatting | bytes 4194304 | tf_op jit(solution)/shard_map/reshape | solution.py:126
  87.1 5.3 %copy.64 = bf16[16,2,64,8,64]{4,2,0,1,3:T(8,128)(2,1)} copy(bf16[16,2,64,8,64]{4,3,2,1,0:T(8,128)(2,1)} %reshape.526) | data formatting | bytes 4194304 | tf_op jit(solution)/shard_map/reshape | solution.py:126
  92.4 6.6 %reshape.527.refs_2_ = bf16[16,16,4096]{2,1,0:T(8,128)(2,1)} reshape(bf16[8,2,16,64,64]{4,3,2,1,0:T(8,128)(2,1)} %bitcast.99) | data formatting | bytes 4194304 | tf_op jit(solution)/shard_map/reshape | solution.py:128
  99.0 1.6 %collective-permute-start.4 = (bf16[16,16512]{1,0:T(8,128)(2,1)}, bf16[16,16512]{1,0:T(8,128)(2,1)S(1)}, u32[]{:S(2)}, u32[]{:S(2)}) collective-permute-start(bf16[16,16512]{1,0:T(8,128)(2,1)} %collective-permute-done.2), channel_id=1, source_target_pairs={{0,8},{8,16},{16,24},{24,28},{28,20},{20,12},{12,4},{4,0},{1,9},{9... | collective-permute-start | bytes 1585160 | tf_op jit(solution)/shard_map/ppermute | solution.py:27
  100.6 1.9 %bitcast_dynamic-update-slice_fusion.3 = bf16[8,16,16512]{2,1,0:T(8,128)(2,1)} fusion(bf16[8,16,16512]{2,1,0:T(8,128)(2,1)} %bitcast_dynamic-update-slice_fusion.4, bf16[16,16512]{1,0:T(8,128)(2,1)} %collective-permute-done.2), kind=kLoop, calls=%fused_computation.31 | loop fusion | bytes 1056768
  102.6 0.4 collective-permute-start.5
  103.0 1.9 %bitcast_dynamic-update-slice_fusion.2 = bf16[8,16,16512]{2,1,0:T(8,128)(2,1)} fusion(bf16[8,16,16512]{2,1,0:T(8,128)(2,1)} %bitcast_dynamic-update-slice_fusion.3, bf16[16,16512]{1,0:T(8,128)(2,1)} %collective-permute-done.3), kind=kLoop, calls=%fused_computation.30 | loop fusion | bytes 1056768
  104.9 6.5 %collective-permute-done.4 = bf16[16,16512]{1,0:T(8,128)(2,1)S(1)} collective-permute-done((bf16[16,16512]{1,0:T(8,128)(2,1)}, bf16[16,16512]{1,0:T(8,128)(2,1)S(1)}, u32[]{:S(2)}, u32[]{:S(2)}) %collective-permute-start.4) | collective-permute-done | bytes 528416 | tf_op jit(solution)/shard_map/ppermute | solution.py:27
  111.4 1.6 %collective-permute-start.6 = (bf16[8,16512]{1,0:T(8,128)(2,1)S(1)}, bf16[8,16512]{1,0:T(8,128)(2,1)S(1)}, u32[]{:S(2)}, u32[]{:S(2)}) collective-permute-start(bf16[8,16512]{1,0:T(8,128)(2,1)S(1)} %slice.64), channel_id=1, source_target_pairs={{0,8},{8,16},{16,24},{24,28},{28,20},{20,12},{12,4},{4,0},{1,9},{9... | collective-permute-start | bytes 792584 | tf_op jit(solution)/shard_map/ppermute | solution.py:32
  113.0 1.9 %collective-permute-done.5 = bf16[16,16512]{1,0:T(8,128)(2,1)S(1)} collective-permute-done((bf16[16,16512]{1,0:T(8,128)(2,1)}, bf16[16,16512]{1,0:T(8,128)(2,1)S(1)}, u32[]{:S(2)}, u32[]{:S(2)}) %collective-permute-start.5) | collective-permute-done | bytes 528416 | tf_op jit(solution)/shard_map/ppermute | solution.py:28
  114.9 0.5 collective-permute-start.7
  115.4 0.8 bitcast_dynamic-update-slice_fusion.1
  116.2 0.8 bitcast_dynamic-update-slice_fusion
  117.0 0.8 collective-permute-done.6
  117.8 3.5 %collective-permute-done.7 = bf16[8,16512]{1,0:T(8,128)(2,1)S(1)} collective-permute-done((bf16[8,16512]{1,0:T(8,128)(2,1)S(1)}, bf16[8,16512]{1,0:T(8,128)(2,1)S(1)}, u32[]{:S(2)}, u32[]{:S(2)}) %collective-permute-start.7) | collective-permute-done | bytes 264224 | tf_op jit(solution)/shard_map/ppermute | solution.py:33
  121.3 0.9 fusion.13.refs_3_
  122.2 1.3 fusion.17
  123.5 9.8 %shard_map.91 = f32[8,16,16]{2,1,0:T(8,128)} custom-call(s32[8,4]{1,0:T(8,128)} %bitcast.103, bf16[16,16,4096]{2,1,0:T(8,128)(2,1)} %reshape.525.refs_1_, bf16[16,16,4096]{2,1,0:T(8,128)(2,1)} %reshape.527.refs_2_, bf16[8,16,16512]{2,1,0:T(8,128)(2,1)} %fusion.13.refs_3_), custom_call_target="tpu_custom_call" | custom-call | tf_op jit(solution)/shard_map/pallas_call | solution.py:62
  133.4 1.4 gather_fusion.1
  134.9 5.8 %all-reduce.2 = f32[16,128]{1,0:T(8,128)S(1)} all-reduce(f32[16,128]{1,0:T(8,128)S(1)} %reshape.528), channel_id=2, replica_groups=mesh['grp'=8,'band'=4] {'band'}, use_global_device_ids=true, to_apply=%region_1.0.clone | all-reduce | flops 2048 | bytes 16384
  140.7 0.6 constant_dynamic-slice_fusion.5
  (45 shorter events, 0.9 us)
Async XLA Ops:
  5.9 8.5 %copy-start.5 = (s32[4]{0:T(128)S(1)}, s32[4]{0:T(128)}, u32[]{:S(2)}) copy-start(s32[4]{0:T(128)} %constant.209.clone) | copy-start | bytes 52
  5.9 11.0 %copy-start.2 = (s32[4]{0:T(128)S(1)}, s32[4]{0:T(128)}, u32[]{:S(2)}) copy-start(s32[4]{0:T(128)} %constant.210.clone) | copy-start | bytes 52
  6.6 13.8 %copy-start.4 = (s32[8]{0:T(128)S(1)}, s32[8]{0:T(128)}, u32[]{:S(2)}) copy-start(s32[8]{0:T(128)} %constant.211.clone) | copy-start | bytes 100
  6.6 19.0 %copy-start = (bf16[512,512]{1,0:T(8,128)(2,1)S(1)}, bf16[512,512]{1,0:T(8,128)(2,1)}, u32[]{:S(2)}) copy-start(bf16[512,512]{1,0:T(8,128)(2,1)} %param.17) | copy-start | bytes 1572868
  7.7 30.4 %collective-permute-start.8 = (bf16[272,1024]{1,0:T(8,128)(2,1)}, bf16[272,1024]{1,0:T(8,128)(2,1)}, u32[]{:S(2)}, u32[]{:S(2)}) collective-permute-start(bf16[272,1024]{1,0:T(8,128)(2,1)} %get-tuple-element.36), channel_id=1, source_target_pairs={{0,2},{2,3},{3,1},{1,0},{4,6},{6,7},{7,5},{5,4},{8,10},{10,11},{11... | collective-permute-start | bytes 1671176 | tf_op jit(solution)/shard_map/ppermute | solution.py:27
  10.7 30.4 %collective-permute-start.9 = (bf16[272,1024]{1,0:T(8,128)(2,1)}, bf16[272,1024]{1,0:T(8,128)(2,1)}, u32[]{:S(2)}, u32[]{:S(2)}) collective-permute-start(bf16[272,1024]{1,0:T(8,128)(2,1)} %get-tuple-element.36), channel_id=1, source_target_pairs={{0,1},{2,0},{3,2},{1,3},{4,5},{6,4},{7,6},{5,7},{8,9},{10,8},{11,1... | collective-permute-start | bytes 1671176 | tf_op jit(solution)/shard_map/ppermute | solution.py:28
  11.4 15.6 %copy-start.1 = (s32[8]{0:T(128)S(1)}, s32[8]{0:T(128)}, u32[]{:S(2)}) copy-start(s32[8]{0:T(128)} %constant.212.clone) | copy-start | bytes 100
  11.4 21.4 %copy-start.3 = (u32[32]{0:T(128)S(1)}, u32[32]{0:T(128)}, u32[]{:S(2)}) copy-start(u32[32]{0:T(128)} %constant.222) | copy-start | bytes 388
  12.3 21.9 %collective-permute-start = (bf16[16,16512]{1,0:T(8,128)(2,1)S(1)}, bf16[16,16512]{1,0:T(8,128)(2,1)}, u32[]{:S(2)}, u32[]{:S(2)}) collective-permute-start(bf16[16,16512]{1,0:T(8,128)(2,1)S(1)} %fusion.12), channel_id=1, source_target_pairs={{0,8},{8,16},{16,24},{24,28},{28,20},{20,12},{12,4},{4,0},{1,9},{9... | collective-permute-start | bytes 1585160 | tf_op jit(solution)/shard_map/ppermute | solution.py:27
  13.9 23.8 %collective-permute-start.1 = (bf16[16,16512]{1,0:T(8,128)(2,1)S(1)}, bf16[16,16512]{1,0:T(8,128)(2,1)}, u32[]{:S(2)}, u32[]{:S(2)}) collective-permute-start(bf16[16,16512]{1,0:T(8,128)(2,1)S(1)} %fusion.12), channel_id=1, source_target_pairs={{0,4},{8,0},{16,8},{24,16},{28,24},{20,28},{12,20},{4,12},{1,5},{9... | collective-permute-start | bytes 1585160 | tf_op jit(solution)/shard_map/ppermute | solution.py:28
  34.1 64.9 %collective-permute-start.2 = (bf16[16,16512]{1,0:T(8,128)(2,1)}, bf16[16,16512]{1,0:T(8,128)(2,1)}, u32[]{:S(2)}, u32[]{:S(2)}) collective-permute-start(bf16[16,16512]{1,0:T(8,128)(2,1)} %collective-permute-done), channel_id=1, source_target_pairs={{0,8},{8,16},{16,24},{24,28},{28,20},{20,12},{12,4},{4,0},{1,9},{9... | collective-permute-start | bytes 1585160 | tf_op jit(solution)/shard_map/ppermute | solution.py:27
  37.7 64.9 %collective-permute-start.3 = (bf16[16,16512]{1,0:T(8,128)(2,1)}, bf16[16,16512]{1,0:T(8,128)(2,1)}, u32[]{:S(2)}, u32[]{:S(2)}) collective-permute-start(bf16[16,16512]{1,0:T(8,128)(2,1)} %collective-permute-done.1), channel_id=1, source_target_pairs={{0,4},{8,0},{16,8},{24,16},{28,24},{20,28},{12,20},{4,12},{1,5},{9... | collective-permute-start | bytes 1585160 | tf_op jit(solution)/shard_map/ppermute | solution.py:28
  39.1 7.9 %collective-permute-start.10 = (bf16[136,1024]{1,0:T(8,128)(2,1)S(1)}, bf16[136,1024]{1,0:T(8,128)(2,1)S(1)}, u32[]{:S(2)}, u32[]{:S(2)}) collective-permute-start(bf16[136,1024]{1,0:T(8,128)(2,1)S(1)} %slice.67), channel_id=1, source_target_pairs={{0,2},{2,3},{3,1},{1,0},{4,6},{6,7},{7,5},{5,4},{8,10},{10,11},{11... | collective-permute-start | bytes 835592 | tf_op jit(solution)/shard_map/ppermute | solution.py:32
  42.1 6.6 %collective-permute-start.11 = (bf16[136,1024]{1,0:T(8,128)(2,1)S(1)}, bf16[136,1024]{1,0:T(8,128)(2,1)S(1)}, u32[]{:S(2)}, u32[]{:S(2)}) collective-permute-start(bf16[136,1024]{1,0:T(8,128)(2,1)S(1)} %slice.68), channel_id=1, source_target_pairs={{0,1},{2,0},{3,2},{1,3},{4,5},{6,4},{7,6},{5,7},{8,9},{10,8},{11,1... | collective-permute-start | bytes 835592 | tf_op jit(solution)/shard_map/ppermute | solution.py:33
  99.0 12.3 %collective-permute-start.4 = (bf16[16,16512]{1,0:T(8,128)(2,1)}, bf16[16,16512]{1,0:T(8,128)(2,1)S(1)}, u32[]{:S(2)}, u32[]{:S(2)}) collective-permute-start(bf16[16,16512]{1,0:T(8,128)(2,1)} %collective-permute-done.2), channel_id=1, source_target_pairs={{0,8},{8,16},{16,24},{24,28},{28,20},{20,12},{12,4},{4,0},{1,9},{9... | collective-permute-start | bytes 1585160 | tf_op jit(solution)/shard_map/ppermute | solution.py:27
  102.6 12.3 %collective-permute-start.5 = (bf16[16,16512]{1,0:T(8,128)(2,1)}, bf16[16,16512]{1,0:T(8,128)(2,1)S(1)}, u32[]{:S(2)}, u32[]{:S(2)}) collective-permute-start(bf16[16,16512]{1,0:T(8,128)(2,1)} %collective-permute-done.3), channel_id=1, source_target_pairs={{0,4},{8,0},{16,8},{24,16},{28,24},{20,28},{12,20},{4,12},{1,5},{9... | collective-permute-start | bytes 1585160 | tf_op jit(solution)/shard_map/ppermute | solution.py:28
  111.4 6.4 %collective-permute-start.6 = (bf16[8,16512]{1,0:T(8,128)(2,1)S(1)}, bf16[8,16512]{1,0:T(8,128)(2,1)S(1)}, u32[]{:S(2)}, u32[]{:S(2)}) collective-permute-start(bf16[8,16512]{1,0:T(8,128)(2,1)S(1)} %slice.64), channel_id=1, source_target_pairs={{0,8},{8,16},{16,24},{24,28},{28,20},{20,12},{12,4},{4,0},{1,9},{9... | collective-permute-start | bytes 792584 | tf_op jit(solution)/shard_map/ppermute | solution.py:32
  114.9 6.4 %collective-permute-start.7 = (bf16[8,16512]{1,0:T(8,128)(2,1)S(1)}, bf16[8,16512]{1,0:T(8,128)(2,1)S(1)}, u32[]{:S(2)}, u32[]{:S(2)}) collective-permute-start(bf16[8,16512]{1,0:T(8,128)(2,1)S(1)} %slice.65), channel_id=1, source_target_pairs={{0,4},{8,0},{16,8},{24,16},{28,24},{20,28},{12,20},{4,12},{1,5},{9... | collective-permute-start | bytes 792584 | tf_op jit(solution)/shard_map/ppermute | solution.py:33

commit v6 on v5

--- a/solution.py
+++ b/solution.py
@@ -98,6 +98,9 @@
     kdim = slot_count * block_size
     codes_g = xg[:, kdim, :slot_count].astype(jnp.float32).astype(jnp.int32)
     grp_got = ring_gather(packed, "grp", group_count)
+    early = [buf for unused, buf in grp_got[3:5]]
+    xg, *early = lax.optimization_barrier([xg] + early)
+    grp_got[3:5] = [(src, buf) for (src, unused), buf in zip(grp_got[3:5], early)]
 
     occ_cols = lax.dynamic_slice_in_dim(green_occ, band * band_orbs, band_orbs, 1)
     row_index = (codes_g // 2)[..., None] * block_size + jnp.arange(block_size, dtype=jnp.int32)
@@ -110,6 +113,9 @@
         "bkr,bhkl->bhrl", xg[:, :kdim, :], occ_sel, preferred_element_type=jnp.float32
     ).astype(jnp.bfloat16)
     occ_raw = occ_raw.reshape(band_count, 2, block_size, ri_local, band_orbs)
+    later = [buf for unused, buf in grp_got[5:7]]
+    occ_raw, *later = lax.optimization_barrier([occ_raw] + later)
+    grp_got[5:7] = [(src, buf) for (src, unused), buf in zip(grp_got[5:7], later)]
 
     virt_cols = jnp.concatenate(
         [lax.dynamic_slice_in_dim(green_virt, band_ids[k] * band_orbs, band_orbs, 1) for k in range(band_count)],
@@ -118,17 +124,11 @@
     folded = lax.dot_general(
         occ_raw, virt_cols, (((0, 1, 2), (1, 2, 3)), ((), ())), preferred_element_type=jnp.float32
     )
+    folded = folded.reshape(ri_local, 2, block_size, orbitals // block_size, block_size)
+    folded = jnp.transpose(folded, (3, 1, 0, 2, 4)).reshape(code_count, ri_local, block_size * block_size)
     fold_hi = lax.reduce_precision(folded, exponent_bits=8, mantissa_bits=7)
     fold_lo = (folded - fold_hi).astype(jnp.bfloat16)
     fold_hi = fold_hi.astype(jnp.bfloat16)
-
-    def table(part):
-        part = part.reshape(ri_local, 2, block_size, orbitals // block_size, block_size)
-        part = jnp.transpose(part, (3, 1, 0, 2, 4))
-        return part.reshape(code_count, ri_local, block_size * block_size)
-
-    fold_hi = table(fold_hi)
-    fold_lo = table(fold_lo)
 
     grp_ids = jnp.stack([src for src, unused in grp_got])
     xstack = jnp.stack([buf for unused, buf in grp_got])

time: 143 us -> 128 us (0.90)
  local copies, waits for them, and re-layouts: 70.7 us -> 58.2 us
  waiting for transfers between devices: 17.3 us -> 8.54 us
  other arithmetic: 6.46 us -> 12.2 us
    reshape x6 -> x1, local copies, waits for them, and re-layouts: 33.7 us -> 7.88 us  [on_device(): jnp.transpose(folded, (3, 1, 0, 2, 4))]
    dot_general x0 -> x2, local copies, waits for them, and re-layouts: none -> 9.82 us  [on_device(): lax.dot_general(occ_raw, virt_cols, (((0, 1, 2), (1, 2, 3)), ((), ())), p...]
    convert_element_type x0 -> x2, other arithmetic: none -> 4.93 us  [the longest x1 4.92 us: on_device(): fold_lo = (folded - fold_hi).astype(jnp.bfloat16)]
    transpose x0 -> x1, local copies, waits for them, and re-layouts: none -> 4.09 us  [on_device(): jnp.transpose(folded, (3, 1, 0, 2, 4))]
    ppermute x4, waiting for transfers between devices: 6.46 us -> 2.48 us  [ring_gather(): ahead = lax.ppermute(ahead, axis, fwd)]
    ppermute x2, waiting for transfers between devices: 5.22 us -> 1.69 us  [ring_gather(): second = lax.ppermute(behind[rows:], axis, bwd)]
    dot_general x1, matrix products: 4.52 us -> 6.4 us  [on_device(): lax.dot_general(occ_raw, virt_cols, (((0, 1, 2), (1, 2, 3)), ((), ())), p...]
    unnamed x20 -> x24, local copies, waits for them, and re-layouts: 10.5 us -> 11.5 us
  transfers between devices with their start and end apart: 12 -> 12, of which waited for: 6 -> 4; matrix products, arithmetic and copies ran while one was open for 52% -> 31% of each run, Pallas kernels for 0% -> 0%
where the time goes in v6:
time: 128 us; the launch traced here: 127 us
  local copies, waits for them, and re-layouts  58.2 us (45%)
  starting transfers between devices  13.3 us (10%)
  other arithmetic  12.2 us (10%)
  between operations  10.1 us (8%)
  Pallas kernels  9.83 us (8%)
  matrix products  8.71 us (7%)
  waiting for transfers between devices  8.54 us (7%)
  blocking collectives  6.19 us (5%)
    unnamed x24, local copies, waits for them, and re-layouts  11.5 us
    pallas_call x1, Pallas kernels, contract(): pl.pallas_call(body, out_shape=jax.ShapeDtypeStruct((groups, ri, rows), j...  9.83 us
    dot_general x2, local copies, waits for them, and re-layouts, on_device(): lax.dot_general(occ_raw, virt_cols, (((0, 1, 2), (1, 2, 3)), ((), ())), p...  9.82 us
    reshape x1, local copies, waits for them, and re-layouts, on_device(): jnp.transpose(folded, (3, 1, 0, 2, 4))  7.88 us
    ppermute x4, starting transfers between devices, ring_gather(): ahead = lax.ppermute(ahead, axis, fwd)  7.77 us
    dot_general x1, matrix products, on_device(): lax.dot_general(occ_raw, virt_cols, (((0, 1, 2), (1, 2, 3)), ((), ())), p...  6.4 us
    unnamed x1, blocking collectives  6.19 us
    convert_element_type x1, other arithmetic, on_device(): fold_lo = (folded - fold_hi).astype(jnp.bfloat16)  4.92 us
  transfers between devices with their start and end apart: 12, of which 4 were waited for; matrix products, arithmetic and copies ran while one was open for 31% of the time, Pallas kernels for 0%

profile of v6, /device:TPU:0, one launch (start us, length us, event | category | flops | bytes accessed | tf_op | source)
XLA Modules:
  0.0 127.0 jit_solution(18162121946339388187)
XLA Ops:
  0.0 0.7 convert_bitcast_fusion.1
  0.7 1.8 %squeeze.4 = bf16[4,64,16,64]{3,2,1,0:T(8,128)(2,1)S(1)} reshape(bf16[1,4,64,1024]{3,2,1,0:T(8,128)(2,1)} %param.13) | data formatting | bytes 1048576 | tf_op jit(solution)/shard_map/squeeze | solution.py:68
  2.4 2.2 %copy.42 = bf16[4,64,16,64]{1,0,2,3:T(4,128)(2,1)S(1)} copy(bf16[4,64,16,64]{3,2,1,0:T(8,128)(2,1)S(1)} %squeeze.4) | data formatting | bytes 1048576 | tf_op jit(solution)/shard_map/squeeze | solution.py:68
  5.3 0.6 multiply_bitcast_fusion
  5.9 0.7 reshape.514
  6.5 0.2 copy.44
  6.8 0.9 fusion.29
  7.7 2.9 %collective-permute-start.2 = (bf16[272,1024]{1,0:T(8,128)(2,1)}, bf16[272,1024]{1,0:T(8,128)(2,1)S(1)}, u32[]{:S(2)}, u32[]{:S(2)}) collective-permute-start(bf16[272,1024]{1,0:T(8,128)(2,1)} %get-tuple-element.46), channel_id=1, source_target_pairs={{0,2},{2,3},{3,1},{1,0},{4,6},{6,7},{7,5},{5,4},{8,10},{10,11},{11... | collective-permute-start | bytes 1671176 | tf_op jit(solution)/shard_map/ppermute | solution.py:27
  10.6 0.7 copy.43
  11.3 0.8 reshape.513
  12.2 1.6 %collective-permute-start = (bf16[16,16512]{1,0:T(8,128)(2,1)S(1)}, bf16[16,16512]{1,0:T(8,128)(2,1)}, u32[]{:S(2)}, u32[]{:S(2)}) collective-permute-start(bf16[16,16512]{1,0:T(8,128)(2,1)S(1)} %fusion.15), channel_id=1, source_target_pairs={{0,8},{8,16},{16,24},{24,28},{28,20},{20,12},{12,4},{4,0},{1,9},{9... | collective-permute-start | bytes 1585160 | tf_op jit(solution)/shard_map/ppermute | solution.py:27
  13.9 0.4 collective-permute-start.1
  14.3 0.6 dynamic_slice.61
  16.9 0.6 fusion.31
  19.4 0.9 bitcast_dynamic-update-slice_fusion.6
  20.3 0.6 dynamic_slice.51
  25.5 1.0 constant_dynamic-slice_fusion.3
  26.6 1.5 %reshape.548 = bf16[8,64,4,2,64]{4,3,2,1,0:T(2,128)(2,1)} reshape(bf16[512,512]{1,0:T(8,128)(2,1)S(1)} %pad_maximum_fusion.1) | data formatting | bytes 1048576 | tf_op jit(solution)/shard_map/dot_general | solution.py:124
  28.1 0.1 add.249
  28.2 0.7 fusion.30
  28.9 4.6 %stack.70 = s32[8,1]{0,1:T(1,128)S(1)} concatenate(s32[1,1]{0,1:T(1,128)} %bitcast, s32[1,1]{0,1:T(1,128)} %bitcast.2, s32[1,1]{0,1:T(1,128)} %bitcast.4, s32[1,1]{0,1:T(1,128)} %bitcast.6, s32[1,1]{0,1:T(1,128)} %bitcast.8, s32[1,1]{0,1:T(1,128)} %bitcast.10, s32[1,1]{0,1:T(1,128)} %bitcast.12, s32[1,1]{0,1:T(1,128)} %bitcast.14), dimensions={0} | concatenate | bytes 64 | tf_op jit(solution)/shard_map/stack | solution.py:133
  33.4 0.6 scatter_custom_fusion
  34.1 0.6 dynamic-slice.13
  35.4 1.6 %collective-permute-start.6 = (bf16[16,16512]{1,0:T(8,128)(2,1)}, bf16[16,16512]{1,0:T(8,128)(2,1)}, u32[]{:S(2)}, u32[]{:S(2)}) collective-permute-start(bf16[16,16512]{1,0:T(8,128)(2,1)} %collective-permute-done), channel_id=1, source_target_pairs={{0,8},{8,16},{16,24},{24,28},{28,20},{20,12},{12,4},{4,0},{1,9},{9... | collective-permute-start | bytes 1585160 | tf_op jit(solution)/shard_map/ppermute | solution.py:27
  37.0 0.5 collective-permute-start.7
  37.4 1.9 %bitcast_dynamic-update-slice_fusion.5 = bf16[8,16,16512]{2,1,0:T(8,128)(2,1)} fusion(bf16[8,16,16512]{2,1,0:T(8,128)(2,1)} %bitcast_dynamic-update-slice_fusion.6, bf16[16,16512]{1,0:T(8,128)(2,1)} %collective-permute-done), kind=kLoop, calls=%fused_computation.31 | loop fusion | bytes 1056768
  39.4 2.0 %collective-permute-start.4 = (bf16[136,1024]{1,0:T(8,128)(2,1)S(1)}, bf16[136,1024]{1,0:T(8,128)(2,1)S(1)}, u32[]{:S(2)}, u32[]{:S(2)}) collective-permute-start(bf16[136,1024]{1,0:T(8,128)(2,1)S(1)} %slice.64), channel_id=1, source_target_pairs={{0,2},{2,3},{3,1},{1,0},{4,6},{6,7},{7,5},{5,4},{8,10},{10,11},{11... | collective-permute-start | bytes 835592 | tf_op jit(solution)/shard_map/ppermute | solution.py:32
  41.4 1.0 slice.65
  42.4 1.9 %bitcast_dynamic-update-slice_fusion.4 = bf16[8,16,16512]{2,1,0:T(8,128)(2,1)} fusion(bf16[8,16,16512]{2,1,0:T(8,128)(2,1)} %bitcast_dynamic-update-slice_fusion.5, bf16[16,16512]{1,0:T(8,128)(2,1)} %collective-permute-done.1), kind=kLoop, calls=%fused_computation.30 | loop fusion | bytes 1056768
  44.3 3.0 %collective-permute-done.4 = bf16[136,1024]{1,0:T(8,128)(2,1)S(1)} collective-permute-done((bf16[136,1024]{1,0:T(8,128)(2,1)S(1)}, bf16[136,1024]{1,0:T(8,128)(2,1)S(1)}, u32[]{:S(2)}, u32[]{:S(2)}) %collective-permute-start.4) | collective-permute-done | bytes 278560 | tf_op jit(solution)/shard_map/ppermute | solution.py:32
  47.2 1.7 %collective-permute-done.5 = bf16[136,1024]{1,0:T(8,128)(2,1)S(1)} collective-permute-done((bf16[136,1024]{1,0:T(8,128)(2,1)S(1)}, bf16[136,1024]{1,0:T(8,128)(2,1)S(1)}, u32[]{:S(2)}, u32[]{:S(2)}) %collective-permute-start.5) | collective-permute-done | bytes 278560 | tf_op jit(solution)/shard_map/ppermute | solution.py:33
  49.0 1.3 %pad_maximum_fusion = bf16[4,272,1024]{2,1,0:T(8,128)(2,1)S(1)} fusion(bf16[1,272,1024]{2,1,0:T(8,128)(2,1)S(1)} %maximum_bitcast_fusion, bf16[1,272,1024]{2,1,0:T(8,128)(2,1)} %bitcast.25, bf16[1,272,1024]{2,1,0:T(8,128)(2,1)S(1)} %bitcast.96, bf16[1,272,1024]{2,1,0:T(8,128)(2,1)S(1)} %get-tuple-element.45), kind=kLoop, calls=%fused_computation.9 | loop fusion | flops 3342336 | bytes 4456448 | tf_op jit(solution)/shard_map/stack | solution.py:97
  50.4 0.1 add.257
  50.6 0.1 add.247
  50.7 3.2 %gather_fusion = bf16[1024,128]{1,0:T(8,128)(2,1)S(1)} fusion(bf16[512,128]{1,0:T(8,128)(2,1)S(1)} %get-tuple-element.61, s32[1024]{0:T(1024)S(1)} %broadcast_clamp_fusion), kind=kCustom, calls=%fused_computation | custom fusion | bytes 528384 | tf_op jit(solution)/shard_map/jit(_take)/gather | solution.py:107
  53.9 0.2 broadcast_select_fusion
  54.1 0.1 copy.45
  54.4 0.1 mul.63
  54.5 1.9 %bitcast_dynamic-update-slice_fusion.3 = bf16[8,16,16512]{2,1,0:T(8,128)(2,1)} fusion(bf16[8,16,16512]{2,1,0:T(8,128)(2,1)} %bitcast_dynamic-update-slice_fusion.4, bf16[16,16512]{1,0:T(8,128)(2,1)} %collective-permute-done.6), kind=kLoop, calls=%fused_computation.29 | loop fusion | bytes 1056768
  56.4 1.6 %collective-permute-start.8 = (bf16[16,16512]{1,0:T(8,128)(2,1)}, bf16[16,16512]{1,0:T(8,128)(2,1)S(1)}, u32[]{:S(2)}, u32[]{:S(2)}) collective-permute-start(bf16[16,16512]{1,0:T(8,128)(2,1)} %collective-permute-done.6), channel_id=1, source_target_pairs={{0,8},{8,16},{16,24},{24,28},{28,20},{20,12},{12,4},{4,0},{1,9},{9... | collective-permute-start | bytes 1585160 | tf_op jit(solution)/shard_map/ppermute | solution.py:27
  58.0 0.5 collective-permute-start.9
  58.4 1.9 %bitcast_dynamic-update-slice_fusion.2 = bf16[8,16,16512]{2,1,0:T(8,128)(2,1)} fusion(bf16[8,16,16512]{2,1,0:T(8,128)(2,1)} %bitcast_dynamic-update-slice_fusion.3, bf16[16,16512]{1,0:T(8,128)(2,1)} %collective-permute-done.7), kind=kLoop, calls=%fused_computation.28 | loop fusion | bytes 1056768
  60.4 2.3 %convert_bitcast_fusion = bf16[4,2,1024,128]{2,3,1,0:T(8,128)(2,1)S(1)} fusion(bf16[4,272,1024]{2,1,0:T(8,128)(2,1)} %copy-done, bf16[4,2,256]{2,1,0:T(2,128)(2,1)S(1)} %mul.63, bf16[4,256,128]{1,2,0:T(8,128)(2,1)S(1)} %copy.45), kind=kOutput, calls=%fused_computation.12 | convolution fusion | flops 538181632 | bytes 4460544 | tf_op jit(solution)/shard_map/bkr,bhkl->bhrl/dot_general | solution.py:112
  62.7 2.6 %copy.46 = bf16[4,2,1024,128]{3,2,1,0:T(8,128)(2,1)} copy(bf16[4,2,1024,128]{2,3,1,0:T(8,128)(2,1)S(1)} %convert_bitcast_fusion) | data formatting | bytes 4194304 | tf_op jit(solution)/shard_map/convert_element_type | solution.py:114
  65.3 2.5 %collective-permute-done.8 = bf16[16,16512]{1,0:T(8,128)(2,1)S(1)} collective-permute-done((bf16[16,16512]{1,0:T(8,128)(2,1)}, bf16[16,16512]{1,0:T(8,128)(2,1)S(1)}, u32[]{:S(2)}, u32[]{:S(2)}) %collective-permute-start.8) | collective-permute-done | bytes 528416 | tf_op jit(solution)/shard_map/ppermute | solution.py:27
  67.7 1.4 %collective-permute-done.9 = bf16[16,16512]{1,0:T(8,128)(2,1)} collective-permute-done((bf16[16,16512]{1,0:T(8,128)(2,1)}, bf16[16,16512]{1,0:T(8,128)(2,1)}, u32[]{:S(2)}, u32[]{:S(2)}) %collective-permute-start.9) | collective-permute-done | bytes 528416 | tf_op jit(solution)/shard_map/ppermute | solution.py:28
  69.1 8.3 %reshape.547 = bf16[16,2,64,4,2,64]{2,1,0,5,4,3:T(2,128)(2,1)} reshape(bf16[16,128,4,2,64]{1,0,4,3,2:T(8,128)(2,1)} %bitcast.94) | data formatting | bytes 4194304 | tf_op jit(solution)/shard_map/dot_general | solution.py:124
  77.4 6.4 %fusion.3 = f32[8,2,16,64,64]{4,3,0,1,2:T(8,128)S(1)} fusion(bf16[16,2,64,4,2,64,1]{2,1,0,5,4,3,6:T(2,128)(2,1)} %bitcast.95, bf16[8,64,4,2,64,1,1]{4,3,2,1,0,6,5:T(2,128)(2,1)S(1)} %bitcast.98), kind=kOutput, calls=%fused_computation.8 | convolution fusion | flops 1073741824 | bytes 6815744 | tf_op jit(solution)/shard_map/dot_general | solution.py:124
  83.9 4.1 %copy.52 = f32[8,2,16,64,64]{4,3,2,1,0:T(8,128)} copy(f32[8,2,16,64,64]{4,3,0,1,2:T(8,128)S(1)} %fusion.3) | data formatting | bytes 8388608 | tf_op jit(solution)/shard_map/transpose | solution.py:128
  87.9 7.9 %reshape.516 = f32[16,16,4096]{2,1,0:T(8,128)} reshape(f32[8,2,16,64,64]{4,3,2,1,0:T(8,128)} %copy.52) | data formatting | bytes 8388608 | tf_op jit(solution)/shard_map/reshape | solution.py:128
  95.8 1.6 %collective-permute-start.10 = (bf16[8,16512]{1,0:T(8,128)(2,1)S(1)}, bf16[8,16512]{1,0:T(8,128)(2,1)S(1)}, u32[]{:S(2)}, u32[]{:S(2)}) collective-permute-start(bf16[8,16512]{1,0:T(8,128)(2,1)S(1)} %slice.67), channel_id=1, source_target_pairs={{0,8},{8,16},{16,24},{24,28},{28,20},{20,12},{12,4},{4,0},{1,9},{9... | collective-permute-start | bytes 792584 | tf_op jit(solution)/shard_map/ppermute | solution.py:32
  97.5 1.0 slice.68
  98.4 0.5 collective-permute-start.11
  98.9 0.8 bitcast_dynamic-update-slice_fusion.1
  99.8 1.9 %bitcast_dynamic-update-slice_fusion = bf16[8,16,16512]{2,1,0:T(8,128)(2,1)} fusion(bf16[8,16,16512]{2,1,0:T(8,128)(2,1)} %bitcast_dynamic-update-slice_fusion.1, bf16[16,16512]{1,0:T(8,128)(2,1)} %collective-permute-done.9), kind=kLoop, calls=%fused_computation.26 | loop fusion | bytes 1056768
  101.6 4.9 %fusion = (bf16[16,16,4096]{2,1,0:T(8,128)(2,1)}, bf16[16,16,4096]{2,1,0:T(8,128)(2,1)}) fusion(f32[16,16,4096]{2,1,0:T(8,128)} %reshape.516), kind=kLoop, calls=%fused_computation.5 | loop fusion | flops 4194304 | bytes 8388608 | tf_op jit(solution)/shard_map/convert_element_type | solution.py:130
  106.6 0.9 fusion.16.refs_3_
  107.5 1.3 %fusion.20 = s32[8,1,4]{2,1,0:T(1,128)} fusion(bf16[8,16,16512]{2,1,0:T(8,128)(2,1)} %fusion.16.refs_3_), kind=kLoop, calls=%fused_computation.47 | loop fusion | flops 64 | bytes 192 | tf_op jit(solution)/shard_map/convert_element_type | solution.py:135
  108.8 9.8 %shard_map.91 = f32[8,16,16]{2,1,0:T(8,128)} custom-call(s32[8,4]{1,0:T(8,128)} %bitcast.99, bf16[16,16,4096]{2,1,0:T(8,128)(2,1)} %get-tuple-element.42.refs_1_, bf16[16,16,4096]{2,1,0:T(8,128)(2,1)} %get-tuple-element.41.refs_2_, bf16[8,16,16512]{2,1,0:T(8,128)(2,1)} %fusion.16.refs_3_), custom_call_target="tpu_custom_call" | custom-call | tf_op jit(solution)/shard_map/pallas_call | solution.py:62
  118.6 1.4 %gather_fusion.1 = f32[8,16,16]{2,1,0:T(8,128)S(1)} fusion(f32[8,16,16]{2,1,0:T(8,128)} %shard_map.91, s32[1024]{0:T(1024)S(1)} %pad_clamp_fusion), kind=kCustom, calls=%fused_computation.1 | custom fusion | bytes 16416 | tf_op jit(solution)/shard_map/jit(_take)/gather | solution.py:138
  120.0 0.1 select_bitcast_fusion
  120.1 0.1 reshape.517
  120.2 6.2 %all-reduce.2 = f32[16,128]{1,0:T(8,128)S(1)} all-reduce(f32[16,128]{1,0:T(8,128)S(1)} %reshape.517), channel_id=2, replica_groups=mesh['grp'=8,'band'=4] {'band'}, use_global_device_ids=true, to_apply=%region_1.0.clone | all-reduce | flops 2048 | bytes 16384
  126.4 0.6 constant_dynamic-slice_fusion.5
  (49 shorter events, 0.6 us)
Async XLA Ops:
  7.7 31.6 %collective-permute-start.2 = (bf16[272,1024]{1,0:T(8,128)(2,1)}, bf16[272,1024]{1,0:T(8,128)(2,1)S(1)}, u32[]{:S(2)}, u32[]{:S(2)}) collective-permute-start(bf16[272,1024]{1,0:T(8,128)(2,1)} %get-tuple-element.46), channel_id=1, source_target_pairs={{0,2},{2,3},{3,1},{1,0},{4,6},{6,7},{7,5},{5,4},{8,10},{10,11},{11... | collective-permute-start | bytes 1671176 | tf_op jit(solution)/shard_map/ppermute | solution.py:27
  10.6 30.8 %collective-permute-start.3 = (bf16[272,1024]{1,0:T(8,128)(2,1)}, bf16[272,1024]{1,0:T(8,128)(2,1)}, u32[]{:S(2)}, u32[]{:S(2)}) collective-permute-start(bf16[272,1024]{1,0:T(8,128)(2,1)} %get-tuple-element.46), channel_id=1, source_target_pairs={{0,1},{2,0},{3,2},{1,3},{4,5},{6,4},{7,6},{5,7},{8,9},{10,8},{11,1... | collective-permute-start | bytes 1671176 | tf_op jit(solution)/shard_map/ppermute | solution.py:28
  10.6 3.7 %copy-start.7 = (s32[4]{0:T(128)S(1)}, s32[4]{0:T(128)}, u32[]{:S(2)}) copy-start(s32[4]{0:T(128)} %constant.209.clone) | copy-start | bytes 52
  10.6 6.2 %copy-start.4 = (s32[4]{0:T(128)S(1)}, s32[4]{0:T(128)}, u32[]{:S(2)}) copy-start(s32[4]{0:T(128)} %constant.210.clone) | copy-start | bytes 52
  11.3 8.9 %copy-start.6 = (s32[8]{0:T(128)S(1)}, s32[8]{0:T(128)}, u32[]{:S(2)}) copy-start(s32[8]{0:T(128)} %constant.211.clone) | copy-start | bytes 100
  12.2 13.3 %copy-start.2 = (bf16[512,512]{1,0:T(8,128)(2,1)S(1)}, bf16[512,512]{1,0:T(8,128)(2,1)}, u32[]{:S(2)}) copy-start(bf16[512,512]{1,0:T(8,128)(2,1)} %param.17) | copy-start | bytes 1572868
  12.2 23.1 %collective-permute-start = (bf16[16,16512]{1,0:T(8,128)(2,1)S(1)}, bf16[16,16512]{1,0:T(8,128)(2,1)}, u32[]{:S(2)}, u32[]{:S(2)}) collective-permute-start(bf16[16,16512]{1,0:T(8,128)(2,1)S(1)} %fusion.15), channel_id=1, source_target_pairs={{0,8},{8,16},{16,24},{24,28},{28,20},{20,12},{12,4},{4,0},{1,9},{9... | collective-permute-start | bytes 1585160 | tf_op jit(solution)/shard_map/ppermute | solution.py:27
  13.9 23.1 %collective-permute-start.1 = (bf16[16,16512]{1,0:T(8,128)(2,1)S(1)}, bf16[16,16512]{1,0:T(8,128)(2,1)}, u32[]{:S(2)}, u32[]{:S(2)}) collective-permute-start(bf16[16,16512]{1,0:T(8,128)(2,1)S(1)} %fusion.15), channel_id=1, source_target_pairs={{0,4},{8,0},{16,8},{24,16},{28,24},{20,28},{12,20},{4,12},{1,5},{9... | collective-permute-start | bytes 1585160 | tf_op jit(solution)/shard_map/ppermute | solution.py:28
  20.3 7.9 %copy-start.3 = (s32[8]{0:T(128)S(1)}, s32[8]{0:T(128)}, u32[]{:S(2)}) copy-start(s32[8]{0:T(128)} %constant.212.clone) | copy-start | bytes 100
  20.3 13.8 %copy-start.5 = (u32[32]{0:T(128)S(1)}, u32[32]{0:T(128)}, u32[]{:S(2)}) copy-start(u32[32]{0:T(128)} %constant.222) | copy-start | bytes 388
  35.4 19.1 %collective-permute-start.6 = (bf16[16,16512]{1,0:T(8,128)(2,1)}, bf16[16,16512]{1,0:T(8,128)(2,1)}, u32[]{:S(2)}, u32[]{:S(2)}) collective-permute-start(bf16[16,16512]{1,0:T(8,128)(2,1)} %collective-permute-done), channel_id=1, source_target_pairs={{0,8},{8,16},{16,24},{24,28},{28,20},{20,12},{12,4},{4,0},{1,9},{9... | collective-permute-start | bytes 1585160 | tf_op jit(solution)/shard_map/ppermute | solution.py:27
  37.0 17.5 %collective-permute-start.7 = (bf16[16,16512]{1,0:T(8,128)(2,1)}, bf16[16,16512]{1,0:T(8,128)(2,1)}, u32[]{:S(2)}, u32[]{:S(2)}) collective-permute-start(bf16[16,16512]{1,0:T(8,128)(2,1)} %collective-permute-done.1), channel_id=1, source_target_pairs={{0,4},{8,0},{16,8},{24,16},{28,24},{20,28},{12,20},{4,12},{1,5},{9... | collective-permute-start | bytes 1585160 | tf_op jit(solution)/shard_map/ppermute | solution.py:28
  39.4 7.9 %collective-permute-start.4 = (bf16[136,1024]{1,0:T(8,128)(2,1)S(1)}, bf16[136,1024]{1,0:T(8,128)(2,1)S(1)}, u32[]{:S(2)}, u32[]{:S(2)}) collective-permute-start(bf16[136,1024]{1,0:T(8,128)(2,1)S(1)} %slice.64), channel_id=1, source_target_pairs={{0,2},{2,3},{3,1},{1,0},{4,6},{6,7},{7,5},{5,4},{8,10},{10,11},{11... | collective-permute-start | bytes 835592 | tf_op jit(solution)/shard_map/ppermute | solution.py:32
  42.4 6.6 %collective-permute-start.5 = (bf16[136,1024]{1,0:T(8,128)(2,1)S(1)}, bf16[136,1024]{1,0:T(8,128)(2,1)S(1)}, u32[]{:S(2)}, u32[]{:S(2)}) collective-permute-start(bf16[136,1024]{1,0:T(8,128)(2,1)S(1)} %slice.65), channel_id=1, source_target_pairs={{0,1},{2,0},{3,2},{1,3},{4,5},{6,4},{7,6},{5,7},{8,9},{10,8},{11,1... | collective-permute-start | bytes 835592 | tf_op jit(solution)/shard_map/ppermute | solution.py:33
  50.3 6.1 %copy-start = (bf16[4,272,1024]{2,1,0:T(8,128)(2,1)}, bf16[4,272,1024]{2,1,0:T(8,128)(2,1)S(1)}, u32[]{:S(2)}) copy-start(bf16[4,272,1024]{2,1,0:T(8,128)(2,1)S(1)} %pad_maximum_fusion) | copy-start | bytes 6684676
  56.4 11.3 %collective-permute-start.8 = (bf16[16,16512]{1,0:T(8,128)(2,1)}, bf16[16,16512]{1,0:T(8,128)(2,1)S(1)}, u32[]{:S(2)}, u32[]{:S(2)}) collective-permute-start(bf16[16,16512]{1,0:T(8,128)(2,1)} %collective-permute-done.6), channel_id=1, source_target_pairs={{0,8},{8,16},{16,24},{24,28},{28,20},{20,12},{12,4},{4,0},{1,9},{9... | collective-permute-start | bytes 1585160 | tf_op jit(solution)/shard_map/ppermute | solution.py:27
  58.0 11.1 %collective-permute-start.9 = (bf16[16,16512]{1,0:T(8,128)(2,1)}, bf16[16,16512]{1,0:T(8,128)(2,1)}, u32[]{:S(2)}, u32[]{:S(2)}) collective-permute-start(bf16[16,16512]{1,0:T(8,128)(2,1)} %collective-permute-done.7), channel_id=1, source_target_pairs={{0,4},{8,0},{16,8},{24,16},{28,24},{20,28},{12,20},{4,12},{1,5},{9... | collective-permute-start | bytes 1585160 | tf_op jit(solution)/shard_map/ppermute | solution.py:28
  69.1 8.3 %copy-start.1 = (bf16[8,64,4,2,64]{4,3,2,1,0:T(2,128)(2,1)S(1)}, bf16[8,64,4,2,64]{4,3,2,1,0:T(2,128)(2,1)}, u32[]{:S(2)}) copy-start(bf16[8,64,4,2,64]{4,3,2,1,0:T(2,128)(2,1)} %reshape.548) | copy-start | bytes 1572868
  95.8 10.7 %collective-permute-start.10 = (bf16[8,16512]{1,0:T(8,128)(2,1)S(1)}, bf16[8,16512]{1,0:T(8,128)(2,1)S(1)}, u32[]{:S(2)}, u32[]{:S(2)}) collective-permute-start(bf16[8,16512]{1,0:T(8,128)(2,1)S(1)} %slice.67), channel_id=1, source_target_pairs={{0,8},{8,16},{16,24},{24,28},{28,20},{20,12},{12,4},{4,0},{1,9},{9... | collective-permute-start | bytes 792584 | tf_op jit(solution)/shard_map/ppermute | solution.py:32
  98.4 8.1 %collective-permute-start.11 = (bf16[8,16512]{1,0:T(8,128)(2,1)S(1)}, bf16[8,16512]{1,0:T(8,128)(2,1)S(1)}, u32[]{:S(2)}, u32[]{:S(2)}) collective-permute-start(bf16[8,16512]{1,0:T(8,128)(2,1)S(1)} %slice.68), channel_id=1, source_target_pairs={{0,4},{8,0},{16,8},{24,16},{28,24},{20,28},{12,20},{4,12},{1,5},{9... | collective-permute-start | bytes 792584 | tf_op jit(solution)/shard_map/ppermute | solution.py:33

commit v7 on v6

--- a/solution.py
+++ b/solution.py
@@ -21,18 +21,21 @@
     me = lax.axis_index(axis)
     pos = jnp.array(pos_of, jnp.int32)[me]
     order_arr = jnp.array(order, jnp.int32)
-    got = [(me, buf)]
+    shifts = [0]
+    got = [buf]
     ahead = behind = buf
     for step in range(1, count // 2):
         ahead = lax.ppermute(ahead, axis, fwd)
         behind = lax.ppermute(behind, axis, bwd)
-        got.append((order_arr[(pos - step) % count], ahead))
-        got.append((order_arr[(pos + step) % count], behind))
+        got += [ahead, behind]
+        shifts += [-step, step]
     rows = buf.shape[0] // 2
     first = lax.ppermute(ahead[:rows], axis, fwd)
     second = lax.ppermute(behind[rows:], axis, bwd)
-    got.append((order_arr[(pos + count // 2) % count], jnp.concatenate([first, second], axis=0)))
-    return got
+    got.append(jnp.concatenate([first, second], axis=0))
+    shifts.append(count // 2)
+    sources = order_arr[(pos + jnp.array(shifts, jnp.int32)) % count]
+    return sources, got
 
 
 def contract_kernel(codes_ref, hi_ref, lo_ref, x_ref, out_ref, *, slots, width):
@@ -92,15 +95,13 @@
     meta_rows = jnp.zeros((16, ri_cols), local_blocks.dtype)
     meta_rows = meta_rows.at[0, :slot_count].set(pair_list.astype(local_blocks.dtype))
     band_packed = jnp.concatenate([rows2d, meta_rows], axis=0)
-    band_got = ring_gather(band_packed, "band", band_count)
-    band_ids = jnp.stack([src for src, unused in band_got])
-    xg = jnp.stack([buf for unused, buf in band_got])
+    band_ids, band_got = ring_gather(band_packed, "band", band_count)
+    xg = jnp.stack(band_got)
     kdim = slot_count * block_size
     codes_g = xg[:, kdim, :slot_count].astype(jnp.float32).astype(jnp.int32)
-    grp_got = ring_gather(packed, "grp", group_count)
-    early = [buf for unused, buf in grp_got[3:5]]
-    xg, *early = lax.optimization_barrier([xg] + early)
-    grp_got[3:5] = [(src, buf) for (src, unused), buf in zip(grp_got[3:5], early)]
+    grp_ids, grp_got = ring_gather(packed, "grp", group_count)
+    xg, *early = lax.optimization_barrier([xg] + grp_got[3:5])
+    grp_got[3:5] = early
 
     occ_cols = lax.dynamic_slice_in_dim(green_occ, band * band_orbs, band_orbs, 1)
     row_index = (codes_g // 2)[..., None] * block_size + jnp.arange(block_size, dtype=jnp.int32)
@@ -113,9 +114,8 @@
         "bkr,bhkl->bhrl", xg[:, :kdim, :], occ_sel, preferred_element_type=jnp.float32
     ).astype(jnp.bfloat16)
     occ_raw = occ_raw.reshape(band_count, 2, block_size, ri_local, band_orbs)
-    later = [buf for unused, buf in grp_got[5:7]]
-    occ_raw, *later = lax.optimization_barrier([occ_raw] + later)
-    grp_got[5:7] = [(src, buf) for (src, unused), buf in zip(grp_got[5:7], later)]
+    occ_raw, *later = lax.optimization_barrier([occ_raw] + grp_got[5:7])
+    grp_got[5:7] = later
 
     virt_cols = jnp.concatenate(
         [lax.dynamic_slice_in_dim(green_virt, band_ids[k] * band_orbs, band_orbs, 1) for k in range(band_count)],
@@ -124,14 +124,14 @@
     folded = lax.dot_general(
         occ_raw, virt_cols, (((0, 1, 2), (1, 2, 3)), ((), ())), preferred_element_type=jnp.float32
     )
+    folded = lax.optimization_barrier(folded)
     folded = folded.reshape(ri_local, 2, block_size, orbitals // block_size, block_size)
     folded = jnp.transpose(folded, (3, 1, 0, 2, 4)).reshape(code_count, ri_local, block_size * block_size)
     fold_hi = lax.reduce_precision(folded, exponent_bits=8, mantissa_bits=7)
     fold_lo = (folded - fold_hi).astype(jnp.bfloat16)
     fold_hi = fold_hi.astype(jnp.bfloat16)
 
-    grp_ids = jnp.stack([src for src, unused in grp_got])
-    xstack = jnp.stack([buf for unused, buf in grp_got])
+    xstack = jnp.stack(grp_got)
     codes_b = xstack[:, 0, flat:flat + slot_count].astype(jnp.float32).astype(jnp.int32)
     parts = contract(codes_b, fold_hi, fold_lo, xstack, slot_count, block_size * block_size)
     order = jnp.zeros((group_count,), jnp.int32).at[grp_ids].set(jnp.arange(group_count, dtype=jnp.int32))

time: 128 us -> 127 us (level)
  between operations: 10.1 us -> 4.22 us
  other arithmetic: 12.2 us -> 14.7 us
  local copies, waits for them, and re-layouts: 58.2 us -> 60.2 us
  waiting for transfers between devices: 8.54 us -> 10.3 us
  matrix products: 8.71 us -> 7.2 us
    reshape x0 -> x2, local copies, waits for them, and re-layouts: none -> 15.3 us  [on_device(): folded.reshape(ri_local, 2, block_size, orbitals // block_size, block_size)]
    dot_general x2 -> x0, local copies, waits for them, and re-layouts: 9.82 us -> none  [on_device(): lax.dot_general(occ_raw, virt_cols, (((0, 1, 2), (1, 2, 3)), ((), ())), p...]
    another operation x1 -> x0, local copies, waits for them, and re-layouts: 4.57 us -> none  [on_device(): grp_ids = jnp.stack([src for src, unused in grp_got])]
    transpose x1 -> x0, local copies, waits for them, and re-layouts: 4.09 us -> none  [on_device(): jnp.transpose(folded, (3, 1, 0, 2, 4))]
    slice x2, local copies, waits for them, and re-layouts: 0.04 us -> 1.94 us  [ring_gather(): first = lax.ppermute(ahead[:rows], axis, fwd)]
    ppermute x4, waiting for transfers between devices: 2.48 us -> 4.17 us  [ring_gather(): ahead = lax.ppermute(ahead, axis, fwd)]
    dot_general x1, matrix products: 6.4 us -> 4.9 us  [on_device(): lax.dot_general(occ_raw, virt_cols, (((0, 1, 2), (1, 2, 3)), ((), ())), p...]
    reshape x2, local copies, waits for them, and re-layouts: 0.87 us -> 2.29 us  [on_device(): jnp.transpose(rows2d, (0, 1, 3, 2))]
  transfers between devices with their start and end apart: 12 -> 12, of which waited for: 4 -> 5; matrix products, arithmetic and copies ran while one was open for 31% -> 30% of each run, Pallas kernels for 0% -> 0%
where the time goes in v7:
time: 127 us; the launch traced here: 125 us
  local copies, waits for them, and re-layouts  60.2 us (47%)
  other arithmetic  14.7 us (12%)
  starting transfers between devices  12.8 us (10%)
  waiting for transfers between devices  10.3 us (8%)
  Pallas kernels  9.84 us (8%)
  matrix products  7.2 us (6%)
  blocking collectives  6.15 us (5%)
  between operations  4.22 us (3%)
    reshape x2, local copies, waits for them, and re-layouts, on_device(): folded.reshape(ri_local, 2, block_size, orbitals // block_size, block_size)  15.3 us
    unnamed x30, local copies, waits for them, and re-layouts  12.5 us
    pallas_call x1, Pallas kernels, contract(): pl.pallas_call(body, out_shape=jax.ShapeDtypeStruct((groups, ri, rows), j...  9.84 us
    ppermute x4, starting transfers between devices, ring_gather(): ahead = lax.ppermute(ahead, axis, fwd)  7.94 us
    reshape x1, local copies, waits for them, and re-layouts, on_device(): jnp.transpose(folded, (3, 1, 0, 2, 4))  7.89 us
    unnamed x1, blocking collectives  6.15 us
    convert_element_type x1, other arithmetic, on_device(): fold_lo = (folded - fold_hi).astype(jnp.bfloat16)  4.97 us
    dot_general x1, matrix products, on_device(): lax.dot_general(occ_raw, virt_cols, (((0, 1, 2), (1, 2, 3)), ((), ())), p...  4.9 us
  transfers between devices with their start and end apart: 12, of which 5 were waited for; matrix products, arithmetic and copies ran while one was open for 30% of the time, Pallas kernels for 0%

profile of v7, /device:TPU:0, one launch (start us, length us, event | category | flops | bytes accessed | tf_op | source)
XLA Modules:
  0.0 125.4 jit_solution(8364698674146222628)
XLA Ops:
  0.0 0.7 convert_bitcast_fusion.1
  0.7 1.8 %squeeze.9 = bf16[4,64,16,64]{3,2,1,0:T(8,128)(2,1)S(1)} reshape(bf16[1,4,64,1024]{3,2,1,0:T(8,128)(2,1)} %param.15) | data formatting | bytes 1048576 | tf_op jit(solution)/shard_map/squeeze | solution.py:71
  2.5 2.2 %copy.42 = bf16[4,64,16,64]{1,0,2,3:T(4,128)(2,1)S(1)} copy(bf16[4,64,16,64]{3,2,1,0:T(8,128)(2,1)S(1)} %squeeze.9) | data formatting | bytes 1048576 | tf_op jit(solution)/shard_map/squeeze | solution.py:71
  5.3 1.6 %multiply_bitcast_fusion = (bf16[4,64,64,16]{1,0,3,2:T(4,128)(2,1)}, bf16[16,4,64,64]{3,1,0,2:T(4,128)(2,1)S(1)}) fusion(bf16[4,64,16,64]{1,0,2,3:T(4,128)(2,1)S(1)} %copy.42, bf16[4]{0:T(256)(128)(2,1)S(1)} %compare_convert_fusion.1), kind=kLoop, calls=%fused_computation.20 | loop fusion | flops 262144 | bytes 1572872 | tf_op jit(solution)/shard_map/transpose | solution.py:94
  6.9 2.1 %reshape.204 = bf16[256,1024]{0,1:T(8,128)(2,1)S(1)} reshape(bf16[4,64,64,16]{1,0,3,2:T(4,128)(2,1)} %get-tuple-element.43) | data formatting | bytes 1048576 | tf_op jit(solution)/shard_map/reshape | solution.py:94
  9.0 0.2 copy.44
  9.2 1.0 fusion.26
  10.2 2.9 %collective-permute-start.2 = (bf16[272,1024]{1,0:T(8,128)(2,1)}, bf16[272,1024]{1,0:T(8,128)(2,1)}, u32[]{:S(2)}, u32[]{:S(2)}) collective-permute-start(bf16[272,1024]{1,0:T(8,128)(2,1)} %get-tuple-element.46), channel_id=1, source_target_pairs={{0,2},{2,3},{3,1},{1,0},{4,6},{6,7},{7,5},{5,4},{8,10},{10,11},{11... | collective-permute-start | bytes 1671176 | tf_op jit(solution)/shard_map/ppermute | solution.py:28
  13.2 0.7 copy.43
  13.9 0.8 reshape.203
  14.8 1.6 %collective-permute-start = (bf16[16,16512]{1,0:T(8,128)(2,1)S(1)}, bf16[16,16512]{1,0:T(8,128)(2,1)}, u32[]{:S(2)}, u32[]{:S(2)}) collective-permute-start(bf16[16,16512]{1,0:T(8,128)(2,1)S(1)} %fusion.10), channel_id=1, source_target_pairs={{0,8},{8,16},{16,24},{24,28},{28,20},{20,12},{12,4},{4,0},{1,9},{9... | collective-permute-start | bytes 1585160 | tf_op jit(solution)/shard_map/ppermute | solution.py:28
  16.4 0.4 collective-permute-start.1
  16.8 0.6 dynamic_slice.23
  17.4 0.7 compare_select_fusion.4
  18.1 0.6 dynamic_slice.21
  18.7 0.7 compare_select_fusion.7
  19.4 0.6 gather_fusion.2
  20.0 0.6 fusion.27
  23.2 0.9 bitcast_dynamic-update-slice_fusion.6
  24.0 0.6 gather_fusion
  24.7 0.6 scatter_custom_fusion
  25.3 0.1 constant_dynamic-slice_fusion.3
  25.5 1.0 copy.48
  26.6 0.6 dynamic-slice.13
  27.9 0.5 collective-permute-done
  28.4 1.8 %collective-permute-start.6 = (bf16[16,16512]{1,0:T(8,128)(2,1)}, bf16[16,16512]{1,0:T(8,128)(2,1)}, u32[]{:S(2)}, u32[]{:S(2)}) collective-permute-start(bf16[16,16512]{1,0:T(8,128)(2,1)} %collective-permute-done), channel_id=1, source_target_pairs={{0,8},{8,16},{16,24},{24,28},{28,20},{20,12},{12,4},{4,0},{1,9},{9... | collective-permute-start | bytes 1585160 | tf_op jit(solution)/shard_map/ppermute | solution.py:28
  30.2 0.2 collective-permute-start.7
  30.4 1.9 %bitcast_dynamic-update-slice_fusion.5 = bf16[8,16,16512]{2,1,0:T(8,128)(2,1)} fusion(bf16[8,16,16512]{2,1,0:T(8,128)(2,1)} %bitcast_dynamic-update-slice_fusion.6, bf16[16,16512]{1,0:T(8,128)(2,1)} %collective-permute-done), kind=kLoop, calls=%fused_computation.32 | loop fusion | bytes 1056768
  32.3 1.0 slice.84
  33.3 1.6 %collective-permute-start.4 = (bf16[136,1024]{1,0:T(8,128)(2,1)S(1)}, bf16[136,1024]{1,0:T(8,128)(2,1)S(1)}, u32[]{:S(2)}, u32[]{:S(2)}) collective-permute-start(bf16[136,1024]{1,0:T(8,128)(2,1)S(1)} %slice.84), channel_id=1, source_target_pairs={{0,2},{2,3},{3,1},{1,0},{4,6},{6,7},{7,5},{5,4},{8,10},{10,11},{11... | collective-permute-start | bytes 835592 | tf_op jit(solution)/shard_map/ppermute | solution.py:33
  34.9 1.0 slice.85
  35.9 1.9 %bitcast_dynamic-update-slice_fusion.4 = bf16[8,16,16512]{2,1,0:T(8,128)(2,1)} fusion(bf16[8,16,16512]{2,1,0:T(8,128)(2,1)} %bitcast_dynamic-update-slice_fusion.5, bf16[16,16512]{1,0:T(8,128)(2,1)} %collective-permute-done.1), kind=kLoop, calls=%fused_computation.31 | loop fusion | bytes 1056768
  37.8 3.4 %collective-permute-done.4 = bf16[136,1024]{1,0:T(8,128)(2,1)S(1)} collective-permute-done((bf16[136,1024]{1,0:T(8,128)(2,1)S(1)}, bf16[136,1024]{1,0:T(8,128)(2,1)S(1)}, u32[]{:S(2)}, u32[]{:S(2)}) %collective-permute-start.4) | collective-permute-done | bytes 278560 | tf_op jit(solution)/shard_map/ppermute | solution.py:33
  41.2 1.3 %collective-permute-done.5 = bf16[136,1024]{1,0:T(8,128)(2,1)S(1)} collective-permute-done((bf16[136,1024]{1,0:T(8,128)(2,1)S(1)}, bf16[136,1024]{1,0:T(8,128)(2,1)S(1)}, u32[]{:S(2)}, u32[]{:S(2)}) %collective-permute-start.5) | collective-permute-done | bytes 278560 | tf_op jit(solution)/shard_map/ppermute | solution.py:34
  42.5 1.5 %pad_maximum_fusion = bf16[4,272,1024]{2,1,0:T(8,128)(2,1)S(1)} fusion(bf16[1,272,1024]{2,1,0:T(8,128)(2,1)S(1)} %maximum_bitcast_fusion, bf16[1,272,1024]{2,1,0:T(8,128)(2,1)} %bitcast.12, bf16[1,272,1024]{2,1,0:T(8,128)(2,1)} %bitcast.11, bf16[1,272,1024]{2,1,0:T(8,128)(2,1)S(1)} %get-tuple-element.45), kind=kLoop, calls=%fused_computation.9 | loop fusion | flops 3342336 | bytes 4456448 | tf_op jit(solution)/shard_map/stack | solution.py:99
  44.4 3.2 %gather_fusion.1 = bf16[1024,128]{1,0:T(8,128)(2,1)S(1)} fusion(bf16[512,128]{1,0:T(8,128)(2,1)S(1)} %constant_dynamic-slice_fusion.4, s32[1024]{0:T(1024)S(1)} %broadcast_clamp_fusion), kind=kCustom, calls=%fused_computation.1 | custom fusion | bytes 528384 | tf_op jit(solution)/shard_map/jit(_take)/gather | solution.py:108
  47.6 0.2 broadcast_select_fusion
  47.8 0.1 copy.45
  48.1 0.1 mul.68
  48.2 1.9 %bitcast_dynamic-update-slice_fusion.3 = bf16[8,16,16512]{2,1,0:T(8,128)(2,1)} fusion(bf16[8,16,16512]{2,1,0:T(8,128)(2,1)} %bitcast_dynamic-update-slice_fusion.4, bf16[16,16512]{1,0:T(8,128)(2,1)} %collective-permute-done.6), kind=kLoop, calls=%fused_computation.30 | loop fusion | bytes 1056768
  50.1 1.6 %collective-permute-start.8 = (bf16[16,16512]{1,0:T(8,128)(2,1)}, bf16[16,16512]{1,0:T(8,128)(2,1)}, u32[]{:S(2)}, u32[]{:S(2)}) collective-permute-start(bf16[16,16512]{1,0:T(8,128)(2,1)} %collective-permute-done.6), channel_id=1, source_target_pairs={{0,8},{8,16},{16,24},{24,28},{28,20},{20,12},{12,4},{4,0},{1,9},{9... | collective-permute-start | bytes 1585160 | tf_op jit(solution)/shard_map/ppermute | solution.py:28
  51.6 0.5 collective-permute-start.9
  52.1 1.9 %bitcast_dynamic-update-slice_fusion.2 = bf16[8,16,16512]{2,1,0:T(8,128)(2,1)} fusion(bf16[8,16,16512]{2,1,0:T(8,128)(2,1)} %bitcast_dynamic-update-slice_fusion.3, bf16[16,16512]{1,0:T(8,128)(2,1)} %collective-permute-done.7), kind=kLoop, calls=%fused_computation.29 | loop fusion | bytes 1056768
  54.0 2.3 %convert_bitcast_fusion = bf16[4,2,1024,128]{2,3,1,0:T(8,128)(2,1)S(1)} fusion(bf16[4,272,1024]{2,1,0:T(8,128)(2,1)} %copy-done.3, bf16[4,2,256]{2,1,0:T(2,128)(2,1)S(1)} %mul.68, bf16[4,256,128]{1,2,0:T(8,128)(2,1)S(1)} %copy.45), kind=kOutput, calls=%fused_computation.14 | convolution fusion | flops 538181632 | bytes 4460544 | tf_op jit(solution)/shard_map/bkr,bhkl->bhrl/dot_general | solution.py:113
  56.3 2.6 %copy.46 = bf16[4,2,1024,128]{3,2,1,0:T(8,128)(2,1)} copy(bf16[4,2,1024,128]{2,3,1,0:T(8,128)(2,1)S(1)} %convert_bitcast_fusion) | data formatting | bytes 4194304 | tf_op jit(solution)/shard_map/convert_element_type | solution.py:115
  59.0 3.7 %collective-permute-done.8 = bf16[16,16512]{1,0:T(8,128)(2,1)} collective-permute-done((bf16[16,16512]{1,0:T(8,128)(2,1)}, bf16[16,16512]{1,0:T(8,128)(2,1)}, u32[]{:S(2)}, u32[]{:S(2)}) %collective-permute-start.8) | collective-permute-done | bytes 528416 | tf_op jit(solution)/shard_map/ppermute | solution.py:28
  62.7 1.5 %collective-permute-done.9 = bf16[16,16512]{1,0:T(8,128)(2,1)} collective-permute-done((bf16[16,16512]{1,0:T(8,128)(2,1)}, bf16[16,16512]{1,0:T(8,128)(2,1)}, u32[]{:S(2)}, u32[]{:S(2)}) %collective-permute-start.9) | collective-permute-done | bytes 528416 | tf_op jit(solution)/shard_map/ppermute | solution.py:29
  64.2 4.9 %convolution_bitcast_fusion = f32[16,128,512]{2,1,0:T(8,128)} fusion(bf16[512,4,2,64,1]{0,3,2,1,4:T(8,128)(2,1)S(1)} %bitcast.81, bf16[4,2,64,16,128]{4,3,2,1,0:T(8,128)(2,1)} %bitcast.80), kind=kOutput, calls=%fused_computation.10 | convolution fusion | flops 1073741824 | bytes 6815744 | tf_op jit(solution)/shard_map/dot_general | solution.py:124
  69.1 7.1 %reshape.207 = f32[16,2,64,8,64]{4,3,2,1,0:T(8,128)} reshape(f32[16,128,512]{2,1,0:T(8,128)} %convolution_bitcast_fusion) | data formatting | bytes 8388608 | tf_op jit(solution)/shard_map/reshape | solution.py:128
  76.2 8.2 %copy.59 = f32[16,2,64,8,64]{4,2,0,1,3:T(8,128)} copy(f32[16,2,64,8,64]{4,3,2,1,0:T(8,128)} %reshape.207) | data formatting | bytes 8388608 | tf_op jit(solution)/shard_map/reshape | solution.py:128
  84.4 7.9 %reshape.208 = f32[16,16,4096]{2,1,0:T(8,128)} reshape(f32[8,2,16,64,64]{4,3,2,1,0:T(8,128)} %bitcast.79) | data formatting | bytes 8388608 | tf_op jit(solution)/shard_map/reshape | solution.py:129
  92.3 1.0 slice.87
  93.2 1.6 %collective-permute-start.10 = (bf16[8,16512]{1,0:T(8,128)(2,1)S(1)}, bf16[8,16512]{1,0:T(8,128)(2,1)S(1)}, u32[]{:S(2)}, u32[]{:S(2)}) collective-permute-start(bf16[8,16512]{1,0:T(8,128)(2,1)S(1)} %slice.87), channel_id=1, source_target_pairs={{0,8},{8,16},{16,24},{24,28},{28,20},{20,12},{12,4},{4,0},{1,9},{9... | collective-permute-start | bytes 792584 | tf_op jit(solution)/shard_map/ppermute | solution.py:33
  94.9 1.0 slice.88
  95.9 0.5 collective-permute-start.11
  96.3 1.9 %bitcast_dynamic-update-slice_fusion.1 = bf16[8,16,16512]{2,1,0:T(8,128)(2,1)} fusion(bf16[8,16,16512]{2,1,0:T(8,128)(2,1)} %bitcast_dynamic-update-slice_fusion.2, bf16[16,16512]{1,0:T(8,128)(2,1)} %collective-permute-done.8), kind=kLoop, calls=%fused_computation.28 | loop fusion | bytes 1056768
  98.2 1.9 %bitcast_dynamic-update-slice_fusion = bf16[8,16,16512]{2,1,0:T(8,128)(2,1)} fusion(bf16[8,16,16512]{2,1,0:T(8,128)(2,1)} %bitcast_dynamic-update-slice_fusion.1, bf16[16,16512]{1,0:T(8,128)(2,1)} %collective-permute-done.9), kind=kLoop, calls=%fused_computation.27 | loop fusion | bytes 1056768
  100.1 5.0 %fusion = (bf16[16,16,4096]{2,1,0:T(8,128)(2,1)}, bf16[16,16,4096]{2,1,0:T(8,128)(2,1)}) fusion(f32[16,16,4096]{2,1,0:T(8,128)} %reshape.208), kind=kLoop, calls=%fused_computation.8 | loop fusion | flops 4194304 | bytes 8388608 | tf_op jit(solution)/shard_map/convert_element_type | solution.py:131
  105.1 0.8 fusion.11.refs_3_
  105.9 1.3 %fusion.15 = s32[8,1,4]{2,1,0:T(1,128)} fusion(bf16[8,16,16512]{2,1,0:T(8,128)(2,1)} %fusion.11.refs_3_), kind=kLoop, calls=%fused_computation.48 | loop fusion | flops 64 | bytes 192 | tf_op jit(solution)/shard_map/convert_element_type | solution.py:135
  107.2 9.8 %shard_map.109 = f32[8,16,16]{2,1,0:T(8,128)} custom-call(s32[8,4]{1,0:T(8,128)} %bitcast.83, bf16[16,16,4096]{2,1,0:T(8,128)(2,1)} %get-tuple-element.42.refs_1_, bf16[16,16,4096]{2,1,0:T(8,128)(2,1)} %get-tuple-element.41.refs_2_, bf16[8,16,16512]{2,1,0:T(8,128)(2,1)} %fusion.11.refs_3_), custom_call_target="tpu_custom_call" | custom-call | tf_op jit(solution)/shard_map/pallas_call | solution.py:65
  117.1 1.4 %gather_fusion.3 = f32[8,16,16]{2,1,0:T(8,128)S(1)} fusion(f32[8,16,16]{2,1,0:T(8,128)} %shard_map.109, s32[1024]{0:T(1024)S(1)} %pad_clamp_fusion), kind=kCustom, calls=%fused_computation.3 | custom fusion | bytes 16416 | tf_op jit(solution)/shard_map/jit(_take)/gather | solution.py:138
  118.7 6.2 %all-reduce.2 = f32[16,128]{1,0:T(8,128)S(1)} all-reduce(f32[16,128]{1,0:T(8,128)S(1)} %reshape.209), channel_id=2, replica_groups=mesh['grp'=8,'band'=4] {'band'}, use_global_device_ids=true, to_apply=%region_1.0.clone | all-reduce | flops 2048 | bytes 16384
  124.8 0.6 constant_dynamic-slice_fusion.5
  (59 shorter events, 1.0 us)
Async XLA Ops:
  0.0 27.9 %copy-start = (bf16[512,512]{1,0:T(8,128)(2,1)S(1)}, bf16[512,512]{1,0:T(8,128)(2,1)}, u32[]{:S(2)}) copy-start(bf16[512,512]{1,0:T(8,128)(2,1)} %param.18) | copy-start | bytes 1572868
  10.2 22.1 %collective-permute-start.2 = (bf16[272,1024]{1,0:T(8,128)(2,1)}, bf16[272,1024]{1,0:T(8,128)(2,1)}, u32[]{:S(2)}, u32[]{:S(2)}) collective-permute-start(bf16[272,1024]{1,0:T(8,128)(2,1)} %get-tuple-element.46), channel_id=1, source_target_pairs={{0,2},{2,3},{3,1},{1,0},{4,6},{6,7},{7,5},{5,4},{8,10},{10,11},{11... | collective-permute-start | bytes 1671176 | tf_op jit(solution)/shard_map/ppermute | solution.py:28
  13.1 21.8 %collective-permute-start.3 = (bf16[272,1024]{1,0:T(8,128)(2,1)}, bf16[272,1024]{1,0:T(8,128)(2,1)}, u32[]{:S(2)}, u32[]{:S(2)}) collective-permute-start(bf16[272,1024]{1,0:T(8,128)(2,1)} %get-tuple-element.46), channel_id=1, source_target_pairs={{0,1},{2,0},{3,2},{1,3},{4,5},{6,4},{7,6},{5,7},{8,9},{10,8},{11,1... | collective-permute-start | bytes 1671176 | tf_op jit(solution)/shard_map/ppermute | solution.py:29
  13.1 3.7 %copy-start.10 = (s32[4]{0:T(128)S(1)}, s32[4]{0:T(128)}, u32[]{:S(2)}) copy-start(s32[4]{0:T(128)} %constant.167.clone) | copy-start | bytes 52
  13.1 4.3 %copy-start.9 = (s32[4]{0:T(128)S(1)}, s32[4]{0:T(128)}, u32[]{:S(2)}) copy-start(s32[4]{0:T(128)} %constant.169.clone) | copy-start | bytes 52
  13.1 5.0 %copy-start.8 = (s32[8]{0:T(128)S(1)}, s32[8]{0:T(128)}, u32[]{:S(2)}) copy-start(s32[8]{0:T(128)} %constant.170.clone) | copy-start | bytes 100
  13.1 5.6 %copy-start.7 = (s32[8]{0:T(128)S(1)}, s32[8]{0:T(128)}, u32[]{:S(2)}) copy-start(s32[8]{0:T(128)} %constant.172.clone) | copy-start | bytes 100
  13.2 6.2 %copy-start.2 = (s32[4]{0:T(128)S(1)}, s32[4]{0:T(128)}, u32[]{:S(2)}) copy-start(s32[4]{0:T(128)} %constant.168.clone) | copy-start | bytes 52
  13.9 10.2 %copy-start.1 = (s32[8]{0:T(128)S(1)}, s32[8]{0:T(128)}, u32[]{:S(2)}) copy-start(s32[8]{0:T(128)} %constant.171.clone) | copy-start | bytes 100
  14.7 10.6 %copy-start.5 = (bf16[512,512]{1,0:T(8,128)(2,1)S(1)}, bf16[512,512]{1,0:T(8,128)(2,1)}, u32[]{:S(2)}) copy-start(bf16[512,512]{1,0:T(8,128)(2,1)} %param.19) | copy-start | bytes 1572868
  14.8 13.6 %collective-permute-start = (bf16[16,16512]{1,0:T(8,128)(2,1)S(1)}, bf16[16,16512]{1,0:T(8,128)(2,1)}, u32[]{:S(2)}, u32[]{:S(2)}) collective-permute-start(bf16[16,16512]{1,0:T(8,128)(2,1)S(1)} %fusion.10), channel_id=1, source_target_pairs={{0,8},{8,16},{16,24},{24,28},{28,20},{20,12},{12,4},{4,0},{1,9},{9... | collective-permute-start | bytes 1585160 | tf_op jit(solution)/shard_map/ppermute | solution.py:28
  16.4 13.8 %collective-permute-start.1 = (bf16[16,16512]{1,0:T(8,128)(2,1)S(1)}, bf16[16,16512]{1,0:T(8,128)(2,1)}, u32[]{:S(2)}, u32[]{:S(2)}) collective-permute-start(bf16[16,16512]{1,0:T(8,128)(2,1)S(1)} %fusion.10), channel_id=1, source_target_pairs={{0,4},{8,0},{16,8},{24,16},{28,24},{20,28},{12,20},{4,12},{1,5},{9... | collective-permute-start | bytes 1585160 | tf_op jit(solution)/shard_map/ppermute | solution.py:29
  23.2 3.5 %copy-start.6 = (u32[32]{0:T(128)S(1)}, u32[32]{0:T(128)}, u32[]{:S(2)}) copy-start(u32[32]{0:T(128)} %constant.182) | copy-start | bytes 388
  28.4 19.8 %collective-permute-start.6 = (bf16[16,16512]{1,0:T(8,128)(2,1)}, bf16[16,16512]{1,0:T(8,128)(2,1)}, u32[]{:S(2)}, u32[]{:S(2)}) collective-permute-start(bf16[16,16512]{1,0:T(8,128)(2,1)} %collective-permute-done), channel_id=1, source_target_pairs={{0,8},{8,16},{16,24},{24,28},{28,20},{20,12},{12,4},{4,0},{1,9},{9... | collective-permute-start | bytes 1585160 | tf_op jit(solution)/shard_map/ppermute | solution.py:28
  30.2 18.0 %collective-permute-start.7 = (bf16[16,16512]{1,0:T(8,128)(2,1)}, bf16[16,16512]{1,0:T(8,128)(2,1)}, u32[]{:S(2)}, u32[]{:S(2)}) collective-permute-start(bf16[16,16512]{1,0:T(8,128)(2,1)} %collective-permute-done.1), channel_id=1, source_target_pairs={{0,4},{8,0},{16,8},{24,16},{28,24},{20,28},{12,20},{4,12},{1,5},{9... | collective-permute-start | bytes 1585160 | tf_op jit(solution)/shard_map/ppermute | solution.py:29
  33.3 7.9 %collective-permute-start.4 = (bf16[136,1024]{1,0:T(8,128)(2,1)S(1)}, bf16[136,1024]{1,0:T(8,128)(2,1)S(1)}, u32[]{:S(2)}, u32[]{:S(2)}) collective-permute-start(bf16[136,1024]{1,0:T(8,128)(2,1)S(1)} %slice.84), channel_id=1, source_target_pairs={{0,2},{2,3},{3,1},{1,0},{4,6},{6,7},{7,5},{5,4},{8,10},{10,11},{11... | collective-permute-start | bytes 835592 | tf_op jit(solution)/shard_map/ppermute | solution.py:33
  35.9 6.6 %collective-permute-start.5 = (bf16[136,1024]{1,0:T(8,128)(2,1)S(1)}, bf16[136,1024]{1,0:T(8,128)(2,1)S(1)}, u32[]{:S(2)}, u32[]{:S(2)}) collective-permute-start(bf16[136,1024]{1,0:T(8,128)(2,1)S(1)} %slice.85), channel_id=1, source_target_pairs={{0,1},{2,0},{3,2},{1,3},{4,5},{6,4},{7,6},{5,7},{8,9},{10,8},{11,1... | collective-permute-start | bytes 835592 | tf_op jit(solution)/shard_map/ppermute | solution.py:34
  44.0 6.1 %copy-start.3 = (bf16[4,272,1024]{2,1,0:T(8,128)(2,1)}, bf16[4,272,1024]{2,1,0:T(8,128)(2,1)S(1)}, u32[]{:S(2)}) copy-start(bf16[4,272,1024]{2,1,0:T(8,128)(2,1)S(1)} %pad_maximum_fusion) | copy-start | bytes 6684676
  50.1 12.6 %collective-permute-start.8 = (bf16[16,16512]{1,0:T(8,128)(2,1)}, bf16[16,16512]{1,0:T(8,128)(2,1)}, u32[]{:S(2)}, u32[]{:S(2)}) collective-permute-start(bf16[16,16512]{1,0:T(8,128)(2,1)} %collective-permute-done.6), channel_id=1, source_target_pairs={{0,8},{8,16},{16,24},{24,28},{28,20},{20,12},{12,4},{4,0},{1,9},{9... | collective-permute-start | bytes 1585160 | tf_op jit(solution)/shard_map/ppermute | solution.py:28
  51.6 12.5 %collective-permute-start.9 = (bf16[16,16512]{1,0:T(8,128)(2,1)}, bf16[16,16512]{1,0:T(8,128)(2,1)}, u32[]{:S(2)}, u32[]{:S(2)}) collective-permute-start(bf16[16,16512]{1,0:T(8,128)(2,1)} %collective-permute-done.7), channel_id=1, source_target_pairs={{0,4},{8,0},{16,8},{24,16},{28,24},{20,28},{12,20},{4,12},{1,5},{9... | collective-permute-start | bytes 1585160 | tf_op jit(solution)/shard_map/ppermute | solution.py:29
  56.3 7.9 %copy-start.4 = (bf16[512,512]{0,1:T(8,128)(2,1)S(1)}, bf16[512,512]{0,1:T(8,128)(2,1)}, u32[]{:S(2)}) copy-start(bf16[512,512]{0,1:T(8,128)(2,1)} %copy.48) | copy-start | bytes 1572868
  93.2 11.8 %collective-permute-start.10 = (bf16[8,16512]{1,0:T(8,128)(2,1)S(1)}, bf16[8,16512]{1,0:T(8,128)(2,1)S(1)}, u32[]{:S(2)}, u32[]{:S(2)}) collective-permute-start(bf16[8,16512]{1,0:T(8,128)(2,1)S(1)} %slice.87), channel_id=1, source_target_pairs={{0,8},{8,16},{16,24},{24,28},{28,20},{20,12},{12,4},{4,0},{1,9},{9... | collective-permute-start | bytes 792584 | tf_op jit(solution)/shard_map/ppermute | solution.py:33
  95.9 9.2 %collective-permute-start.11 = (bf16[8,16512]{1,0:T(8,128)(2,1)S(1)}, bf16[8,16512]{1,0:T(8,128)(2,1)S(1)}, u32[]{:S(2)}, u32[]{:S(2)}) collective-permute-start(bf16[8,16512]{1,0:T(8,128)(2,1)S(1)} %slice.88), channel_id=1, source_target_pairs={{0,4},{8,0},{16,8},{24,16},{28,24},{20,28},{12,20},{4,12},{1,5},{9... | collective-permute-start | bytes 792584 | tf_op jit(solution)/shard_map/ppermute | solution.py:34

commit v8 on v7

--- a/solution.py
+++ b/solution.py
@@ -38,33 +38,59 @@
     return sources, got
 
 
-def contract_kernel(codes_ref, hi_ref, lo_ref, x_ref, out_ref, *, slots, width):
-    g = pl.program_id(0)
-    acc = jnp.zeros(out_ref.shape[1:], jnp.float32)
+def contract_kernel(codes_ref, table_ref, x_ref, out_ref, hi_ref, lo_ref, dense_ref, *, slots, width, ri, chunk):
+    step = pl.program_id(0)
+
+    @pl.when(step == 0)
+    def split():
+        full = table_ref[...]
+        hi = full.astype(jnp.bfloat16)
+        hi_ref[...] = hi
+        lo_ref[...] = (full - hi.astype(jnp.float32)).astype(jnp.bfloat16)
+
+    out_ref[...] = jnp.zeros(out_ref.shape, jnp.float32)
     for s in range(slots):
-        code = codes_ref[g, s]
-        xs = x_ref[0, :, s * width:(s + 1) * width]
-        for table in (hi_ref, lo_ref):
-            acc = acc + lax.dot_general(
-                table[code], xs, (((1,), (1,)), ((), ())), preferred_element_type=jnp.float32
-            )
-    out_ref[0] = acc
+        xs = x_ref[:, s * width:(s + 1) * width]
+        dense = lax.dot_general(
+            hi_ref[...], xs, (((1,), (1,)), ((), ())), preferred_element_type=jnp.float32
+        )
+        dense = dense + lax.dot_general(
+            lo_ref[...], xs, (((1,), (1,)), ((), ())), preferred_element_type=jnp.float32
+        )
+        dense_ref[...] = dense
+        for c in range(chunk):
+            code = codes_ref[step * chunk + c, s]
+            start = pl.multiple_of(code * ri, ri)
+            out_ref[0, :, c * ri:(c + 1) * ri] += dense_ref[pl.ds(start, ri), c * ri:(c + 1) * ri]
 
 
-def contract(codes, table_hi, table_lo, xstack, slots, width):
-    groups, rows, unused = xstack.shape
-    codes_total, ri, unused = table_hi.shape
-    table_spec = pl.BlockSpec((codes_total, ri, width), lambda g, c: (0, 0, 0))
+def contract(codes, table, xrows, groups, slots, width):
+    codes_total, ri, unused = table.shape
+    flat = slots * width
+    chunk = groups
+    while chunk > 1 and (chunk * ri * flat * 2 > (4 << 20) or groups % chunk):
+        chunk -= 1
+    steps = groups // chunk
+    table2 = table.reshape(codes_total * ri, width)
     grid_spec = pltpu.PrefetchScalarGridSpec(
         num_scalar_prefetch=1,
-        grid=(groups,),
-        in_specs=[table_spec, table_spec, pl.BlockSpec((1, rows, slots * width), lambda g, c: (g, 0, 0))],
-        out_specs=pl.BlockSpec((1, ri, rows), lambda g, c: (g, 0, 0)),
+        grid=(steps,),
+        in_specs=[
+            pl.BlockSpec((codes_total * ri, width), lambda g, c: (0, 0)),
+            pl.BlockSpec((chunk * ri, flat), lambda g, c: (g, 0)),
+        ],
+        out_specs=pl.BlockSpec((1, ri, chunk * ri), lambda g, c: (g, 0, 0)),
+        scratch_shapes=[
+            pltpu.VMEM((codes_total * ri, width), jnp.bfloat16),
+            pltpu.VMEM((codes_total * ri, width), jnp.bfloat16),
+            pltpu.VMEM((codes_total * ri, chunk * ri), jnp.float32),
+        ],
     )
-    body = lambda *refs: contract_kernel(*refs, slots=slots, width=width)
-    return pl.pallas_call(
-        body, out_shape=jax.ShapeDtypeStruct((groups, ri, rows), jnp.float32), grid_spec=grid_spec
-    )(codes, table_hi, table_lo, xstack)
+    body = lambda *refs: contract_kernel(*refs, slots=slots, width=width, ri=ri, chunk=chunk)
+    out = pl.pallas_call(
+        body, out_shape=jax.ShapeDtypeStruct((steps, ri, chunk * ri), jnp.float32), grid_spec=grid_spec
+    )(codes, table2, xrows)
+    return jnp.transpose(out, (1, 0, 2)).reshape(ri, groups * ri)
 
 
 def on_device(x_blocks, pair_ids, live_count, green_occ, green_virt):
@@ -127,16 +153,13 @@
     folded = lax.optimization_barrier(folded)
     folded = folded.reshape(ri_local, 2, block_size, orbitals // block_size, block_size)
     folded = jnp.transpose(folded, (3, 1, 0, 2, 4)).reshape(code_count, ri_local, block_size * block_size)
-    fold_hi = lax.reduce_precision(folded, exponent_bits=8, mantissa_bits=7)
-    fold_lo = (folded - fold_hi).astype(jnp.bfloat16)
-    fold_hi = fold_hi.astype(jnp.bfloat16)
-
     xstack = jnp.stack(grp_got)
     codes_b = xstack[:, 0, flat:flat + slot_count].astype(jnp.float32).astype(jnp.int32)
-    parts = contract(codes_b, fold_hi, fold_lo, xstack, slot_count, block_size * block_size)
+    xrows = xstack.reshape(group_count * ri_local, flat + META)
+    arrived = contract(codes_b, folded, xrows, group_count, slot_count, block_size * block_size)
     order = jnp.zeros((group_count,), jnp.int32).at[grp_ids].set(jnp.arange(group_count, dtype=jnp.int32))
-    parts = jnp.take(parts, order, axis=0)
-    partial_value = jnp.transpose(parts, (1, 0, 2)).reshape(ri_local, group_count * ri_local)
+    arrived = arrived.reshape(ri_local, group_count, ri_local)
+    partial_value = jnp.take(arrived, order, axis=1).reshape(ri_local, group_count * ri_local)
     response = lax.psum_scatter(partial_value, "band", scatter_dimension=0, tiled=True)
     return response
 

time: 127 us -> 120 us (0.945)
  other arithmetic: 14.7 us -> 8.32 us
  local copies, waits for them, and re-layouts: 60.2 us -> 61.8 us
  matrix products: 7.2 us -> 5.61 us
    another operation x0 -> x3, local copies, waits for them, and re-layouts: none -> 8.68 us  [the longest x1 7.89 us: contract(): table2 = table.reshape(codes_total * ri, width)]
    reshape x2 -> x0, local copies, waits for them, and re-layouts: 7.97 us -> none  [the longest x1 7.89 us: on_device(): jnp.transpose(folded, (3, 1, 0, 2, 4))]
    convert_element_type x1 -> x0, other arithmetic: 4.97 us -> none  [on_device(): fold_lo = (folded - fold_hi).astype(jnp.bfloat16)]
    dot_general x1, matrix products: 4.9 us -> 3.31 us  [on_device(): lax.dot_general(occ_raw, virt_cols, (((0, 1, 2), (1, 2, 3)), ((), ())), p...]
    convert_element_type x1, other arithmetic: 1.31 us -> 0.01 us  [on_device(): xstack[:, 0, flat:flat + slot_count].astype(jnp.float32).astype(jnp.int32)]
    unnamed x30 -> x33, local copies, waits for them, and re-layouts: 12.5 us -> 12.6 us
  transfers between devices with their start and end apart: 12 -> 12, of which waited for: 5 -> 5; matrix products, arithmetic and copies ran while one was open for 30% -> 50% of each run, Pallas kernels for 0% -> 0%
where the time goes in v8:
time: 120 us; the launch traced here: 119 us
  local copies, waits for them, and re-layouts  61.8 us (52%)
  starting transfers between devices  13.1 us (11%)
  waiting for transfers between devices  9.95 us (8%)
  Pallas kernels  9.41 us (8%)
  other arithmetic  8.32 us (7%)
  blocking collectives  6.21 us (5%)
  matrix products  5.61 us (5%)
  between operations  4.2 us (4%)
    reshape x2, local copies, waits for them, and re-layouts, on_device(): folded.reshape(ri_local, 2, block_size, orbitals // block_size, block_size)  15.3 us
    unnamed x33, local copies, waits for them, and re-layouts  12.6 us
    pallas_call x1, Pallas kernels, contract(): pl.pallas_call(body, out_shape=jax.ShapeDtypeStruct((steps, ri, chunk * r...  9.41 us
    ppermute x4, starting transfers between devices, ring_gather(): ahead = lax.ppermute(ahead, axis, fwd)  7.94 us
    another operation x1, local copies, waits for them, and re-layouts, contract(): table2 = table.reshape(codes_total * ri, width)  7.89 us
    unnamed x1, blocking collectives  6.21 us
    squeeze x2, local copies, waits for them, and re-layouts, on_device(): local_blocks = x_blocks[0]  3.93 us
    ppermute x4, waiting for transfers between devices, ring_gather(): ahead = lax.ppermute(ahead, axis, fwd)  3.77 us
  transfers between devices with their start and end apart: 12, of which 5 were waited for; matrix products, arithmetic and copies ran while one was open for 50% of the time, Pallas kernels for 0%

profile of v8, /device:TPU:0, one launch (start us, length us, event | category | flops | bytes accessed | tf_op | source)
XLA Modules:
  0.0 118.6 jit_solution(11583784004162316485)
XLA Ops:
  0.0 0.7 convert_bitcast_fusion.2
  0.7 1.8 %squeeze.9 = bf16[4,64,16,64]{3,2,1,0:T(8,128)(2,1)S(1)} reshape(bf16[1,4,64,1024]{3,2,1,0:T(8,128)(2,1)} %param.15) | data formatting | bytes 1048576 | tf_op jit(solution)/shard_map/squeeze | solution.py:97
  2.5 2.2 %copy.215 = bf16[4,64,16,64]{1,0,2,3:T(4,128)(2,1)S(1)} copy(bf16[4,64,16,64]{3,2,1,0:T(8,128)(2,1)S(1)} %squeeze.9) | data formatting | bytes 1048576 | tf_op jit(solution)/shard_map/squeeze | solution.py:97
  5.3 1.6 %multiply_bitcast_fusion = (bf16[4,64,64,16]{1,0,3,2:T(4,128)(2,1)}, bf16[16,4,64,64]{3,1,0,2:T(4,128)(2,1)S(1)}) fusion(bf16[4,64,16,64]{1,0,2,3:T(4,128)(2,1)S(1)} %copy.215, bf16[4]{0:T(256)(128)(2,1)S(1)} %compare_convert_fusion.1), kind=kLoop, calls=%fused_computation.17 | loop fusion | flops 262144 | bytes 1572872 | tf_op jit(solution)/shard_map/transpose | solution.py:120
  6.9 2.1 %reshape.204 = bf16[256,1024]{0,1:T(8,128)(2,1)S(1)} reshape(bf16[4,64,64,16]{1,0,3,2:T(4,128)(2,1)} %get-tuple-element.41) | data formatting | bytes 1048576 | tf_op jit(solution)/shard_map/reshape | solution.py:120
  9.0 0.2 copy.217
  9.2 1.0 fusion.24
  10.2 2.9 %collective-permute-start.2 = (bf16[272,1024]{1,0:T(8,128)(2,1)}, bf16[272,1024]{1,0:T(8,128)(2,1)}, u32[]{:S(2)}, u32[]{:S(2)}) collective-permute-start(bf16[272,1024]{1,0:T(8,128)(2,1)} %get-tuple-element.44), channel_id=1, source_target_pairs={{0,2},{2,3},{3,1},{1,0},{4,6},{6,7},{7,5},{5,4},{8,10},{10,11},{11... | collective-permute-start | bytes 1671176 | tf_op jit(solution)/shard_map/ppermute | solution.py:28
  13.2 0.7 copy.216
  13.9 0.8 reshape.203
  14.8 1.6 %collective-permute-start = (bf16[16,16512]{1,0:T(8,128)(2,1)S(1)}, bf16[16,16512]{1,0:T(8,128)(2,1)}, u32[]{:S(2)}, u32[]{:S(2)}) collective-permute-start(bf16[16,16512]{1,0:T(8,128)(2,1)S(1)} %fusion.9), channel_id=1, source_target_pairs={{0,8},{8,16},{16,24},{24,28},{28,20},{20,12},{12,4},{4,0},{1,9},{9... | collective-permute-start | bytes 1585160 | tf_op jit(solution)/shard_map/ppermute | solution.py:28
  16.4 0.4 collective-permute-start.1
  16.8 0.6 dynamic_slice.21
  17.4 0.7 compare_select_fusion.7
  18.1 0.6 gather_fusion
  18.8 0.6 scatter_custom_fusion
  19.4 0.6 dynamic_slice.23
  20.0 0.7 compare_select_fusion.4
  20.7 0.6 gather_fusion.2
  21.3 0.6 fusion.25
  24.5 0.9 bitcast_dynamic-update-slice_fusion.6
  25.5 1.0 copy.221
  26.8 0.6 dynamic-slice.13
  28.1 0.4 collective-permute-done
  28.4 1.8 %collective-permute-start.6 = (bf16[16,16512]{1,0:T(8,128)(2,1)}, bf16[16,16512]{1,0:T(8,128)(2,1)}, u32[]{:S(2)}, u32[]{:S(2)}) collective-permute-start(bf16[16,16512]{1,0:T(8,128)(2,1)} %collective-permute-done), channel_id=1, source_target_pairs={{0,8},{8,16},{16,24},{24,28},{28,20},{20,12},{12,4},{4,0},{1,9},{9... | collective-permute-start | bytes 1585160 | tf_op jit(solution)/shard_map/ppermute | solution.py:28
  30.2 0.2 collective-permute-start.7
  30.4 1.9 %bitcast_dynamic-update-slice_fusion.5 = bf16[8,16,16512]{2,1,0:T(8,128)(2,1)} fusion(bf16[8,16,16512]{2,1,0:T(8,128)(2,1)} %bitcast_dynamic-update-slice_fusion.6, bf16[16,16512]{1,0:T(8,128)(2,1)} %collective-permute-done), kind=kLoop, calls=%fused_computation.29 | loop fusion | bytes 1056768
  32.3 1.0 slice.84
  33.3 1.7 %collective-permute-start.4 = (bf16[136,1024]{1,0:T(8,128)(2,1)S(1)}, bf16[136,1024]{1,0:T(8,128)(2,1)S(1)}, u32[]{:S(2)}, u32[]{:S(2)}) collective-permute-start(bf16[136,1024]{1,0:T(8,128)(2,1)S(1)} %slice.84), channel_id=1, source_target_pairs={{0,2},{2,3},{3,1},{1,0},{4,6},{6,7},{7,5},{5,4},{8,10},{10,11},{11... | collective-permute-start | bytes 835592 | tf_op jit(solution)/shard_map/ppermute | solution.py:33
  35.0 1.0 slice.85
  36.0 1.9 %bitcast_dynamic-update-slice_fusion.4 = bf16[8,16,16512]{2,1,0:T(8,128)(2,1)} fusion(bf16[8,16,16512]{2,1,0:T(8,128)(2,1)} %bitcast_dynamic-update-slice_fusion.5, bf16[16,16512]{1,0:T(8,128)(2,1)} %collective-permute-done.1), kind=kLoop, calls=%fused_computation.28 | loop fusion | bytes 1056768
  37.9 3.3 %collective-permute-done.4 = bf16[136,1024]{1,0:T(8,128)(2,1)S(1)} collective-permute-done((bf16[136,1024]{1,0:T(8,128)(2,1)S(1)}, bf16[136,1024]{1,0:T(8,128)(2,1)S(1)}, u32[]{:S(2)}, u32[]{:S(2)}) %collective-permute-start.4) | collective-permute-done | bytes 278560 | tf_op jit(solution)/shard_map/ppermute | solution.py:33
  41.2 1.4 %collective-permute-done.5 = bf16[136,1024]{1,0:T(8,128)(2,1)S(1)} collective-permute-done((bf16[136,1024]{1,0:T(8,128)(2,1)S(1)}, bf16[136,1024]{1,0:T(8,128)(2,1)S(1)}, u32[]{:S(2)}, u32[]{:S(2)}) %collective-permute-start.5) | collective-permute-done | bytes 278560 | tf_op jit(solution)/shard_map/ppermute | solution.py:34
  42.6 1.5 %pad_maximum_fusion = bf16[4,272,1024]{2,1,0:T(8,128)(2,1)S(1)} fusion(bf16[1,272,1024]{2,1,0:T(8,128)(2,1)S(1)} %maximum_bitcast_fusion, bf16[1,272,1024]{2,1,0:T(8,128)(2,1)} %bitcast.12, bf16[1,272,1024]{2,1,0:T(8,128)(2,1)} %bitcast.11, bf16[1,272,1024]{2,1,0:T(8,128)(2,1)S(1)} %get-tuple-element.43), kind=kLoop, calls=%fused_computation.6 | loop fusion | flops 3342336 | bytes 4456448 | tf_op jit(solution)/shard_map/stack | solution.py:125
  44.5 3.2 %gather_fusion.1 = bf16[1024,128]{1,0:T(8,128)(2,1)S(1)} fusion(bf16[512,128]{1,0:T(8,128)(2,1)S(1)} %constant_dynamic-slice_fusion.4, s32[1024]{0:T(1024)S(1)} %broadcast_clamp_fusion), kind=kCustom, calls=%fused_computation.1 | custom fusion | bytes 528384 | tf_op jit(solution)/shard_map/jit(_take)/gather | solution.py:134
  47.7 0.2 broadcast_select_fusion
  47.9 0.1 copy.218
  48.3 1.9 %bitcast_dynamic-update-slice_fusion.3 = bf16[8,16,16512]{2,1,0:T(8,128)(2,1)} fusion(bf16[8,16,16512]{2,1,0:T(8,128)(2,1)} %bitcast_dynamic-update-slice_fusion.4, bf16[16,16512]{1,0:T(8,128)(2,1)} %collective-permute-done.6), kind=kLoop, calls=%fused_computation.27 | loop fusion | bytes 1056768
  50.2 1.6 %collective-permute-start.8 = (bf16[16,16512]{1,0:T(8,128)(2,1)}, bf16[16,16512]{1,0:T(8,128)(2,1)}, u32[]{:S(2)}, u32[]{:S(2)}) collective-permute-start(bf16[16,16512]{1,0:T(8,128)(2,1)} %collective-permute-done.6), channel_id=1, source_target_pairs={{0,8},{8,16},{16,24},{24,28},{28,20},{20,12},{12,4},{4,0},{1,9},{9... | collective-permute-start | bytes 1585160 | tf_op jit(solution)/shard_map/ppermute | solution.py:28
  51.8 0.4 collective-permute-start.9
  52.2 1.9 %bitcast_dynamic-update-slice_fusion.2 = bf16[8,16,16512]{2,1,0:T(8,128)(2,1)} fusion(bf16[8,16,16512]{2,1,0:T(8,128)(2,1)} %bitcast_dynamic-update-slice_fusion.3, bf16[16,16512]{1,0:T(8,128)(2,1)} %collective-permute-done.7), kind=kLoop, calls=%fused_computation.26 | loop fusion | bytes 1056768
  54.1 2.3 %convert_bitcast_fusion = bf16[4,2,1024,128]{2,3,1,0:T(8,128)(2,1)S(1)} fusion(bf16[4,272,1024]{2,1,0:T(8,128)(2,1)} %copy-done.3, bf16[4,2,256]{2,1,0:T(2,128)(2,1)S(1)} %mul.68, bf16[4,256,128]{1,2,0:T(8,128)(2,1)S(1)} %copy.218), kind=kOutput, calls=%fused_computation.11 | convolution fusion | flops 538181632 | bytes 4460544 | tf_op jit(solution)/shard_map/bkr,bhkl->bhrl/dot_general | solution.py:139
  56.4 2.7 %copy.219 = bf16[4,2,1024,128]{3,2,1,0:T(8,128)(2,1)} copy(bf16[4,2,1024,128]{2,3,1,0:T(8,128)(2,1)S(1)} %convert_bitcast_fusion) | data formatting | bytes 4194304 | tf_op jit(solution)/shard_map/convert_element_type | solution.py:141
  59.1 3.4 %collective-permute-done.8 = bf16[16,16512]{1,0:T(8,128)(2,1)} collective-permute-done((bf16[16,16512]{1,0:T(8,128)(2,1)}, bf16[16,16512]{1,0:T(8,128)(2,1)}, u32[]{:S(2)}, u32[]{:S(2)}) %collective-permute-start.8) | collective-permute-done | bytes 528416 | tf_op jit(solution)/shard_map/ppermute | solution.py:28
  62.5 1.5 %collective-permute-done.9 = bf16[16,16512]{1,0:T(8,128)(2,1)} collective-permute-done((bf16[16,16512]{1,0:T(8,128)(2,1)}, bf16[16,16512]{1,0:T(8,128)(2,1)}, u32[]{:S(2)}, u32[]{:S(2)}) %collective-permute-start.9) | collective-permute-done | bytes 528416 | tf_op jit(solution)/shard_map/ppermute | solution.py:29
  64.0 1.0 slice.87
  65.0 1.6 %collective-permute-start.10 = (bf16[8,16512]{1,0:T(8,128)(2,1)S(1)}, bf16[8,16512]{1,0:T(8,128)(2,1)S(1)}, u32[]{:S(2)}, u32[]{:S(2)}) collective-permute-start(bf16[8,16512]{1,0:T(8,128)(2,1)S(1)} %slice.87), channel_id=1, source_target_pairs={{0,8},{8,16},{16,24},{24,28},{28,20},{20,12},{12,4},{4,0},{1,9},{9... | collective-permute-start | bytes 792584 | tf_op jit(solution)/shard_map/ppermute | solution.py:33
  66.6 1.0 slice.88
  67.6 0.7 collective-permute-start.11
  68.3 1.9 %bitcast_dynamic-update-slice_fusion.1 = bf16[8,16,16512]{2,1,0:T(8,128)(2,1)} fusion(bf16[8,16,16512]{2,1,0:T(8,128)(2,1)} %bitcast_dynamic-update-slice_fusion.2, bf16[16,16512]{1,0:T(8,128)(2,1)} %collective-permute-done.8), kind=kLoop, calls=%fused_computation.25 | loop fusion | bytes 1056768
  70.2 1.9 %bitcast_dynamic-update-slice_fusion = bf16[8,16,16512]{2,1,0:T(8,128)(2,1)} fusion(bf16[8,16,16512]{2,1,0:T(8,128)(2,1)} %bitcast_dynamic-update-slice_fusion.1, bf16[16,16512]{1,0:T(8,128)(2,1)} %collective-permute-done.9), kind=kLoop, calls=%fused_computation.24 | loop fusion | bytes 1056768
  72.0 3.3 %convolution_bitcast_fusion = f32[16,128,512]{2,1,0:T(8,128)} fusion(bf16[512,4,2,64,1]{0,3,2,1,4:T(8,128)(2,1)S(1)} %bitcast.83, bf16[4,2,64,16,128]{4,3,2,1,0:T(8,128)(2,1)S(1)} %bitcast.81), kind=kOutput, calls=%fused_computation.7 | convolution fusion | flops 1073741824 | bytes 6815744 | tf_op jit(solution)/shard_map/dot_general | solution.py:150
  75.3 7.1 %reshape.207 = f32[16,2,64,8,64]{4,3,2,1,0:T(8,128)} reshape(f32[16,128,512]{2,1,0:T(8,128)} %convolution_bitcast_fusion) | data formatting | bytes 8388608 | tf_op jit(solution)/shard_map/reshape | solution.py:154
  82.4 8.2 %copy.233 = f32[16,2,64,8,64]{4,2,0,1,3:T(8,128)} copy(f32[16,2,64,8,64]{4,3,2,1,0:T(8,128)} %reshape.207) | data formatting | bytes 8388608 | tf_op jit(solution)/shard_map/reshape | solution.py:154
  90.7 7.9 %reshape_reshape.3.refs_1_ = f32[256,4096]{1,0:T(8,128)} reshape(f32[8,2,16,64,64]{4,3,2,1,0:T(8,128)} %bitcast.80) | data formatting | bytes 8388608 | tf_op jit(solution)/shard_map/reshape;reshape | solution.py:74
  98.5 0.9 fusion.10
  99.4 0.7 slice.89
  100.1 0.1 copy.229
  100.2 0.7 copy.224.refs_0_
  100.9 9.4 %shard_map.109 = f32[1,16,128]{2,1,0:T(8,128)} custom-call(s32[8,4]{1,0:T(8,128)} %copy.224.refs_0_, f32[256,4096]{1,0:T(8,128)} %reshape_reshape.3.refs_1_, bf16[128,16512]{1,0:T(8,128)(2,1)} %bitcast.82), custom_call_target="tpu_custom_call" | custom-call | tf_op jit(solution)/shard_map/pallas_call | solution.py:90
  110.3 0.8 reshape_reshape_transpose.3
  111.1 0.6 gather_fusion.3
  111.8 6.2 %all-reduce.2 = f32[16,128]{1,0:T(8,128)S(1)} all-reduce(f32[16,128]{1,0:T(8,128)S(1)} %broadcast_select_fusion.1), channel_id=2, replica_groups=mesh['grp'=8,'band'=4] {'band'}, use_global_device_ids=true, to_apply=%region_1.0.clone | all-reduce | flops 2048 | bytes 16384
  118.0 0.6 constant_dynamic-slice_fusion.5
  (67 shorter events, 1.3 us)
Async XLA Ops:
  0.0 28.0 %copy-start = (bf16[512,512]{1,0:T(8,128)(2,1)S(1)}, bf16[512,512]{1,0:T(8,128)(2,1)}, u32[]{:S(2)}) copy-start(bf16[512,512]{1,0:T(8,128)(2,1)} %param.18) | copy-start | bytes 1572868
  10.2 22.1 %collective-permute-start.2 = (bf16[272,1024]{1,0:T(8,128)(2,1)}, bf16[272,1024]{1,0:T(8,128)(2,1)}, u32[]{:S(2)}, u32[]{:S(2)}) collective-permute-start(bf16[272,1024]{1,0:T(8,128)(2,1)} %get-tuple-element.44), channel_id=1, source_target_pairs={{0,2},{2,3},{3,1},{1,0},{4,6},{6,7},{7,5},{5,4},{8,10},{10,11},{11... | collective-permute-start | bytes 1671176 | tf_op jit(solution)/shard_map/ppermute | solution.py:28
  13.1 21.9 %collective-permute-start.3 = (bf16[272,1024]{1,0:T(8,128)(2,1)}, bf16[272,1024]{1,0:T(8,128)(2,1)}, u32[]{:S(2)}, u32[]{:S(2)}) collective-permute-start(bf16[272,1024]{1,0:T(8,128)(2,1)} %get-tuple-element.44), channel_id=1, source_target_pairs={{0,1},{2,0},{3,2},{1,3},{4,5},{6,4},{7,6},{5,7},{8,9},{10,8},{11,1... | collective-permute-start | bytes 1671176 | tf_op jit(solution)/shard_map/ppermute | solution.py:29
  13.1 3.7 %copy-start.11 = (s32[8]{0:T(128)S(1)}, s32[8]{0:T(128)}, u32[]{:S(2)}) copy-start(s32[8]{0:T(128)} %constant.170.clone) | copy-start | bytes 100
  13.1 4.3 %copy-start.10 = (s32[8]{0:T(128)S(1)}, s32[8]{0:T(128)}, u32[]{:S(2)}) copy-start(s32[8]{0:T(128)} %constant.172.clone) | copy-start | bytes 100
  13.1 5.0 %copy-start.2 = (s32[8]{0:T(128)S(1)}, s32[8]{0:T(128)}, u32[]{:S(2)}) copy-start(s32[8]{0:T(128)} %constant.171.clone) | copy-start | bytes 100
  13.1 6.3 %copy-start.9 = (s32[4]{0:T(128)S(1)}, s32[4]{0:T(128)}, u32[]{:S(2)}) copy-start(s32[4]{0:T(128)} %constant.167.clone) | copy-start | bytes 52
  13.2 6.8 %copy-start.8 = (s32[4]{0:T(128)S(1)}, s32[4]{0:T(128)}, u32[]{:S(2)}) copy-start(s32[4]{0:T(128)} %constant.169.clone) | copy-start | bytes 52
  13.2 7.5 %copy-start.1 = (s32[4]{0:T(128)S(1)}, s32[4]{0:T(128)}, u32[]{:S(2)}) copy-start(s32[4]{0:T(128)} %constant.168.clone) | copy-start | bytes 52
  14.7 10.6 %copy-start.6 = (bf16[512,512]{1,0:T(8,128)(2,1)S(1)}, bf16[512,512]{1,0:T(8,128)(2,1)}, u32[]{:S(2)}) copy-start(bf16[512,512]{1,0:T(8,128)(2,1)} %param.19) | copy-start | bytes 1572868
  14.8 13.6 %collective-permute-start = (bf16[16,16512]{1,0:T(8,128)(2,1)S(1)}, bf16[16,16512]{1,0:T(8,128)(2,1)}, u32[]{:S(2)}, u32[]{:S(2)}) collective-permute-start(bf16[16,16512]{1,0:T(8,128)(2,1)S(1)} %fusion.9), channel_id=1, source_target_pairs={{0,8},{8,16},{16,24},{24,28},{28,20},{20,12},{12,4},{4,0},{1,9},{9... | collective-permute-start | bytes 1585160 | tf_op jit(solution)/shard_map/ppermute | solution.py:28
  16.4 13.8 %collective-permute-start.1 = (bf16[16,16512]{1,0:T(8,128)(2,1)S(1)}, bf16[16,16512]{1,0:T(8,128)(2,1)}, u32[]{:S(2)}, u32[]{:S(2)}) collective-permute-start(bf16[16,16512]{1,0:T(8,128)(2,1)S(1)} %fusion.9), channel_id=1, source_target_pairs={{0,4},{8,0},{16,8},{24,16},{28,24},{20,28},{12,20},{4,12},{1,5},{9... | collective-permute-start | bytes 1585160 | tf_op jit(solution)/shard_map/ppermute | solution.py:29
  21.3 5.4 %copy-start.7 = (u32[32]{0:T(128)S(1)}, u32[32]{0:T(128)}, u32[]{:S(2)}) copy-start(u32[32]{0:T(128)} %constant.182) | copy-start | bytes 388
  28.4 19.9 %collective-permute-start.6 = (bf16[16,16512]{1,0:T(8,128)(2,1)}, bf16[16,16512]{1,0:T(8,128)(2,1)}, u32[]{:S(2)}, u32[]{:S(2)}) collective-permute-start(bf16[16,16512]{1,0:T(8,128)(2,1)} %collective-permute-done), channel_id=1, source_target_pairs={{0,8},{8,16},{16,24},{24,28},{28,20},{20,12},{12,4},{4,0},{1,9},{9... | collective-permute-start | bytes 1585160 | tf_op jit(solution)/shard_map/ppermute | solution.py:28
  30.2 18.1 %collective-permute-start.7 = (bf16[16,16512]{1,0:T(8,128)(2,1)}, bf16[16,16512]{1,0:T(8,128)(2,1)}, u32[]{:S(2)}, u32[]{:S(2)}) collective-permute-start(bf16[16,16512]{1,0:T(8,128)(2,1)} %collective-permute-done.1), channel_id=1, source_target_pairs={{0,4},{8,0},{16,8},{24,16},{28,24},{20,28},{12,20},{4,12},{1,5},{9... | collective-permute-start | bytes 1585160 | tf_op jit(solution)/shard_map/ppermute | solution.py:29
  33.3 7.9 %collective-permute-start.4 = (bf16[136,1024]{1,0:T(8,128)(2,1)S(1)}, bf16[136,1024]{1,0:T(8,128)(2,1)S(1)}, u32[]{:S(2)}, u32[]{:S(2)}) collective-permute-start(bf16[136,1024]{1,0:T(8,128)(2,1)S(1)} %slice.84), channel_id=1, source_target_pairs={{0,2},{2,3},{3,1},{1,0},{4,6},{6,7},{7,5},{5,4},{8,10},{10,11},{11... | collective-permute-start | bytes 835592 | tf_op jit(solution)/shard_map/ppermute | solution.py:33
  36.0 6.6 %collective-permute-start.5 = (bf16[136,1024]{1,0:T(8,128)(2,1)S(1)}, bf16[136,1024]{1,0:T(8,128)(2,1)S(1)}, u32[]{:S(2)}, u32[]{:S(2)}) collective-permute-start(bf16[136,1024]{1,0:T(8,128)(2,1)S(1)} %slice.85), channel_id=1, source_target_pairs={{0,1},{2,0},{3,2},{1,3},{4,5},{6,4},{7,6},{5,7},{8,9},{10,8},{11,1... | collective-permute-start | bytes 835592 | tf_op jit(solution)/shard_map/ppermute | solution.py:34
  44.1 6.1 %copy-start.3 = (bf16[4,272,1024]{2,1,0:T(8,128)(2,1)}, bf16[4,272,1024]{2,1,0:T(8,128)(2,1)S(1)}, u32[]{:S(2)}) copy-start(bf16[4,272,1024]{2,1,0:T(8,128)(2,1)S(1)} %pad_maximum_fusion) | copy-start | bytes 6684676
  50.2 12.3 %collective-permute-start.8 = (bf16[16,16512]{1,0:T(8,128)(2,1)}, bf16[16,16512]{1,0:T(8,128)(2,1)}, u32[]{:S(2)}, u32[]{:S(2)}) collective-permute-start(bf16[16,16512]{1,0:T(8,128)(2,1)} %collective-permute-done.6), channel_id=1, source_target_pairs={{0,8},{8,16},{16,24},{24,28},{28,20},{20,12},{12,4},{4,0},{1,9},{9... | collective-permute-start | bytes 1585160 | tf_op jit(solution)/shard_map/ppermute | solution.py:28
  51.8 12.3 %collective-permute-start.9 = (bf16[16,16512]{1,0:T(8,128)(2,1)}, bf16[16,16512]{1,0:T(8,128)(2,1)}, u32[]{:S(2)}, u32[]{:S(2)}) collective-permute-start(bf16[16,16512]{1,0:T(8,128)(2,1)} %collective-permute-done.7), channel_id=1, source_target_pairs={{0,4},{8,0},{16,8},{24,16},{28,24},{20,28},{12,20},{4,12},{1,5},{9... | collective-permute-start | bytes 1585160 | tf_op jit(solution)/shard_map/ppermute | solution.py:29
  59.1 12.9 %copy-start.4 = (bf16[4,2,1024,128]{3,2,1,0:T(8,128)(2,1)S(1)}, bf16[4,2,1024,128]{3,2,1,0:T(8,128)(2,1)}, u32[]{:S(2)}) copy-start(bf16[4,2,1024,128]{3,2,1,0:T(8,128)(2,1)} %copy.219) | copy-start | bytes 6291460
  59.1 12.9 %copy-start.5 = (bf16[512,512]{0,1:T(8,128)(2,1)S(1)}, bf16[512,512]{0,1:T(8,128)(2,1)}, u32[]{:S(2)}) copy-start(bf16[512,512]{0,1:T(8,128)(2,1)} %copy.221) | copy-start | bytes 1572868
  65.0 33.5 %collective-permute-start.10 = (bf16[8,16512]{1,0:T(8,128)(2,1)S(1)}, bf16[8,16512]{1,0:T(8,128)(2,1)S(1)}, u32[]{:S(2)}, u32[]{:S(2)}) collective-permute-start(bf16[8,16512]{1,0:T(8,128)(2,1)S(1)} %slice.87), channel_id=1, source_target_pairs={{0,8},{8,16},{16,24},{24,28},{28,20},{20,12},{12,4},{4,0},{1,9},{9... | collective-permute-start | bytes 792584 | tf_op jit(solution)/shard_map/ppermute | solution.py:33
  67.6 30.9 %collective-permute-start.11 = (bf16[8,16512]{1,0:T(8,128)(2,1)S(1)}, bf16[8,16512]{1,0:T(8,128)(2,1)S(1)}, u32[]{:S(2)}, u32[]{:S(2)}) collective-permute-start(bf16[8,16512]{1,0:T(8,128)(2,1)S(1)} %slice.88), channel_id=1, source_target_pairs={{0,4},{8,0},{16,8},{24,16},{28,24},{20,28},{12,20},{4,12},{1,5},{9... | collective-permute-start | bytes 792584 | tf_op jit(solution)/shard_map/ppermute | solution.py:34

commit v9 on v8

--- a/solution.py
+++ b/solution.py
@@ -38,15 +38,25 @@
     return sources, got
 
 
-def contract_kernel(codes_ref, table_ref, x_ref, out_ref, hi_ref, lo_ref, dense_ref, *, slots, width, ri, chunk):
+def contract_kernel(codes_ref, table_ref, x_ref, out_ref, hi_ref, lo_ref, dense_ref, *, slots, width, ri, chunk, blk):
     step = pl.program_id(0)
 
     @pl.when(step == 0)
     def split():
-        full = table_ref[...]
-        hi = full.astype(jnp.bfloat16)
-        hi_ref[...] = hi
-        lo_ref[...] = (full - hi.astype(jnp.float32)).astype(jnp.bfloat16)
+        lam_count = 2 * blk
+        tiles = table_ref.shape[0] // (ri * lam_count)
+        per_tile = 128 // blk
+        for h in range(2):
+            for j in range(blk):
+                for t in range(tiles):
+                    start = (h * blk + j) * tiles + t
+                    rows = table_ref[pl.ds(start, ri, stride=lam_count * tiles), :]
+                    hi = rows.astype(jnp.bfloat16)
+                    lo = (rows - hi.astype(jnp.float32)).astype(jnp.bfloat16)
+                    for u in range(per_tile):
+                        code = 2 * (t * per_tile + u) + h
+                        hi_ref[code * ri:(code + 1) * ri, j * blk:(j + 1) * blk] = hi[:, u * blk:(u + 1) * blk]
+                        lo_ref[code * ri:(code + 1) * ri, j * blk:(j + 1) * blk] = lo[:, u * blk:(u + 1) * blk]
 
     out_ref[...] = jnp.zeros(out_ref.shape, jnp.float32)
     for s in range(slots):
@@ -64,19 +74,21 @@
             out_ref[0, :, c * ri:(c + 1) * ri] += dense_ref[pl.ds(start, ri), c * ri:(c + 1) * ri]
 
 
-def contract(codes, table, xrows, groups, slots, width):
-    codes_total, ri, unused = table.shape
+def contract(codes, folded, xrows, groups, slots, blk):
+    ri, lam_count, orbitals = folded.shape
+    width = blk * blk
+    codes_total = 2 * (orbitals // blk)
     flat = slots * width
     chunk = groups
     while chunk > 1 and (chunk * ri * flat * 2 > (4 << 20) or groups % chunk):
         chunk -= 1
     steps = groups // chunk
-    table2 = table.reshape(codes_total * ri, width)
+    table2 = folded.reshape(ri * lam_count * (orbitals // 128), 128)
     grid_spec = pltpu.PrefetchScalarGridSpec(
         num_scalar_prefetch=1,
         grid=(steps,),
         in_specs=[
-            pl.BlockSpec((codes_total * ri, width), lambda g, c: (0, 0)),
+            pl.BlockSpec(table2.shape, lambda g, c: (0, 0)),
             pl.BlockSpec((chunk * ri, flat), lambda g, c: (g, 0)),
         ],
         out_specs=pl.BlockSpec((1, ri, chunk * ri), lambda g, c: (g, 0, 0)),
@@ -86,7 +98,7 @@
             pltpu.VMEM((codes_total * ri, chunk * ri), jnp.float32),
         ],
     )
-    body = lambda *refs: contract_kernel(*refs, slots=slots, width=width, ri=ri, chunk=chunk)
+    body = lambda *refs: contract_kernel(*refs, slots=slots, width=width, ri=ri, chunk=chunk, blk=blk)
     out = pl.pallas_call(
         body, out_shape=jax.ShapeDtypeStruct((steps, ri, chunk * ri), jnp.float32), grid_spec=grid_spec
     )(codes, table2, xrows)
@@ -150,13 +162,10 @@
     folded = lax.dot_general(
         occ_raw, virt_cols, (((0, 1, 2), (1, 2, 3)), ((), ())), preferred_element_type=jnp.float32
     )
-    folded = lax.optimization_barrier(folded)
-    folded = folded.reshape(ri_local, 2, block_size, orbitals // block_size, block_size)
-    folded = jnp.transpose(folded, (3, 1, 0, 2, 4)).reshape(code_count, ri_local, block_size * block_size)
     xstack = jnp.stack(grp_got)
     codes_b = xstack[:, 0, flat:flat + slot_count].astype(jnp.float32).astype(jnp.int32)
     xrows = xstack.reshape(group_count * ri_local, flat + META)
-    arrived = contract(codes_b, folded, xrows, group_count, slot_count, block_size * block_size)
+    arrived = contract(codes_b, folded, xrows, group_count, slot_count, block_size)
     order = jnp.zeros((group_count,), jnp.int32).at[grp_ids].set(jnp.arange(group_count, dtype=jnp.int32))
     arrived = arrived.reshape(ri_local, group_count, ri_local)
     partial_value = jnp.take(arrived, order, axis=1).reshape(ri_local, group_count * ri_local)

time: 120 us -> 103 us (0.86)
  local copies, waits for them, and re-layouts: 61.8 us -> 42.6 us
  Pallas kernels: 9.41 us -> 11.9 us
    reshape x2 -> x1, local copies, waits for them, and re-layouts: 15.3 us -> 4.78 us  [contract(): table2 = folded.reshape(ri * lam_count * (orbitals // 128), 128)]
    another operation x1 -> x0, local copies, waits for them, and re-layouts: 7.89 us -> none  [contract(): table2 = table.reshape(codes_total * ri, width)]
    ppermute x2, waiting for transfers between devices: 3.26 us -> 0.01 us  [ring_gather(): first = lax.ppermute(ahead[:rows], axis, fwd)]
    ppermute x2, waiting for transfers between devices: 1.38 us -> 4.47 us  [ring_gather(): second = lax.ppermute(behind[rows:], axis, bwd)]
    pallas_call x1, Pallas kernels: 9.41 us -> 11.9 us  [contract(): pl.pallas_call(body, out_shape=jax.ShapeDtypeStruct((steps, ri, chunk * r...]
    ppermute x4, waiting for transfers between devices: 3.77 us -> 5.39 us  [ring_gather(): ahead = lax.ppermute(ahead, axis, fwd)]
    reshape x2, local copies, waits for them, and re-layouts: 2.29 us -> 0.88 us  [on_device(): jnp.transpose(rows2d, (0, 1, 3, 2))]
    unnamed x33 -> x29, local copies, waits for them, and re-layouts: 12.6 us -> 14 us
  transfers between devices with their start and end apart: 12 -> 12, of which waited for: 5 -> 3; matrix products, arithmetic and copies ran while one was open for 50% -> 39% of each run, Pallas kernels for 0% -> 0%
where the time goes in v9:
time: 103 us; the launch traced here: 102 us
  local copies, waits for them, and re-layouts  42.6 us (41%)
  starting transfers between devices  13.5 us (13%)
  Pallas kernels  11.9 us (12%)
  waiting for transfers between devices  10.8 us (10%)
  other arithmetic  7.88 us (8%)
  blocking collectives  5.86 us (6%)
  matrix products  5.61 us (5%)
  between operations  4.24 us (4%)
    unnamed x29, local copies, waits for them, and re-layouts  14 us
    pallas_call x1, Pallas kernels, contract(): pl.pallas_call(body, out_shape=jax.ShapeDtypeStruct((steps, ri, chunk * r...  11.9 us
    ppermute x4, starting transfers between devices, ring_gather(): ahead = lax.ppermute(ahead, axis, fwd)  8.7 us
    unnamed x1, blocking collectives  5.86 us
    ppermute x4, waiting for transfers between devices, ring_gather(): ahead = lax.ppermute(ahead, axis, fwd)  5.39 us
    reshape x1, local copies, waits for them, and re-layouts, contract(): table2 = folded.reshape(ri * lam_count * (orbitals // 128), 128)  4.78 us
    ppermute x2, waiting for transfers between devices, ring_gather(): second = lax.ppermute(behind[rows:], axis, bwd)  4.47 us
    squeeze x2, local copies, waits for them, and re-layouts, on_device(): local_blocks = x_blocks[0]  3.93 us
  transfers between devices with their start and end apart: 12, of which 3 were waited for; matrix products, arithmetic and copies ran while one was open for 39% of the time, Pallas kernels for 0%

profile of v9, /device:TPU:0, one launch (start us, length us, event | category | flops | bytes accessed | tf_op | source)
XLA Modules:
  0.0 102.3 jit_solution(13758603288967270255)
XLA Ops:
  0.0 0.7 convert_bitcast_fusion.2
  0.7 1.8 %squeeze.9 = bf16[4,64,16,64]{3,2,1,0:T(8,128)(2,1)S(1)} reshape(bf16[1,4,64,1024]{3,2,1,0:T(8,128)(2,1)} %param.15) | data formatting | bytes 1048576 | tf_op jit(solution)/shard_map/squeeze | solution.py:109
  2.5 2.2 %copy.203 = bf16[4,64,16,64]{1,0,2,3:T(4,128)(2,1)S(1)} copy(bf16[4,64,16,64]{3,2,1,0:T(8,128)(2,1)S(1)} %squeeze.9) | data formatting | bytes 1048576 | tf_op jit(solution)/shard_map/squeeze | solution.py:109
  5.3 0.6 multiply_bitcast_fusion
  5.9 0.7 copy.204
  6.6 0.8 reshape.203
  7.5 0.9 fusion.9
  8.3 3.0 %collective-permute-start = (bf16[16,16512]{1,0:T(8,128)(2,1)}, bf16[16,16512]{1,0:T(8,128)(2,1)}, u32[]{:S(2)}, u32[]{:S(2)}) collective-permute-start(bf16[16,16512]{1,0:T(8,128)(2,1)} %fusion.9), channel_id=1, source_target_pairs={{0,8},{8,16},{16,24},{24,28},{28,20},{20,12},{12,4},{4,0},{1,9},{9... | collective-permute-start | bytes 1585160 | tf_op jit(solution)/shard_map/ppermute | solution.py:28
  11.4 0.7 reshape.204
  12.1 0.2 copy.205
  12.3 0.9 fusion.24
  13.2 2.0 %collective-permute-start.2 = (bf16[272,1024]{1,0:T(8,128)(2,1)}, bf16[272,1024]{1,0:T(8,128)(2,1)}, u32[]{:S(2)}, u32[]{:S(2)}) collective-permute-start(bf16[272,1024]{1,0:T(8,128)(2,1)} %get-tuple-element.44), channel_id=1, source_target_pairs={{0,2},{2,3},{3,1},{1,0},{4,6},{6,7},{7,5},{5,4},{8,10},{10,11},{11... | collective-permute-start | bytes 1671176 | tf_op jit(solution)/shard_map/ppermute | solution.py:28
  15.2 0.8 bitcast_dynamic-update-slice_fusion.6
  16.1 0.6 dynamic_slice.21
  16.7 0.7 compare_select_fusion.7
  17.4 0.6 gather_fusion
  18.0 0.6 scatter_custom_fusion
  18.6 0.6 dynamic_slice.23
  19.2 0.7 compare_select_fusion.4
  19.9 0.6 gather_fusion.2
  20.6 0.6 fusion.25
  23.8 1.1 %constant_dynamic-slice_fusion.3 = (bf16[512,128]{1,0:T(8,128)(2,1)S(1)}, bf16[512,128]{1,0:T(8,128)(2,1)S(1)}, bf16[512,128]{1,0:T(8,128)(2,1)S(1)}, bf16[512,128]{1,0:T(8,128)(2,1)S(1)}) fusion(bf16[512,512]{1,0:T(8,128)(2,1)} %param.19, s32[]{:T(128)S(6)} %select_n.116, s32[]{:T(128)S(6)} %select_n.117, s32[]{:T(128)S(6)} %select_n.119, s32[]{:T(128)S(6)} %select_n.118), kind=kLoop, calls=%fused_computation.75 | loop fusion | bytes 1048592 | tf_op jit(solution)/shard_map/dynamic_slice | solution.py:159
  25.0 0.2 copy.209
  25.3 0.1 broadcast_in_dim.43
  25.4 0.6 dynamic-slice.13
  26.7 2.1 %collective-permute-start.6 = (bf16[16,16512]{1,0:T(8,128)(2,1)}, bf16[16,16512]{1,0:T(8,128)(2,1)}, u32[]{:S(2)}, u32[]{:S(2)}) collective-permute-start(bf16[16,16512]{1,0:T(8,128)(2,1)} %collective-permute-done), channel_id=1, source_target_pairs={{0,8},{8,16},{16,24},{24,28},{28,20},{20,12},{12,4},{4,0},{1,9},{9... | collective-permute-start | bytes 1585160 | tf_op jit(solution)/shard_map/ppermute | solution.py:28
  28.8 1.9 %bitcast_dynamic-update-slice_fusion.5 = bf16[8,16,16512]{2,1,0:T(8,128)(2,1)} fusion(bf16[8,16,16512]{2,1,0:T(8,128)(2,1)} %bitcast_dynamic-update-slice_fusion.6, bf16[16,16512]{1,0:T(8,128)(2,1)} %collective-permute-done), kind=kLoop, calls=%fused_computation.28 | loop fusion | bytes 1056768
  30.8 1.0 slice.84
  31.7 2.0 %collective-permute-start.4 = (bf16[136,1024]{1,0:T(8,128)(2,1)S(1)}, bf16[136,1024]{1,0:T(8,128)(2,1)S(1)}, u32[]{:S(2)}, u32[]{:S(2)}) collective-permute-start(bf16[136,1024]{1,0:T(8,128)(2,1)S(1)} %slice.84), channel_id=1, source_target_pairs={{0,2},{2,3},{3,1},{1,0},{4,6},{6,7},{7,5},{5,4},{8,10},{10,11},{11... | collective-permute-start | bytes 835592 | tf_op jit(solution)/shard_map/ppermute | solution.py:33
  33.8 1.9 %bitcast_dynamic-update-slice_fusion.4 = bf16[8,16,16512]{2,1,0:T(8,128)(2,1)} fusion(bf16[8,16,16512]{2,1,0:T(8,128)(2,1)} %bitcast_dynamic-update-slice_fusion.5, bf16[16,16512]{1,0:T(8,128)(2,1)} %collective-permute-done.1), kind=kLoop, calls=%fused_computation.27 | loop fusion | bytes 1056768
  35.6 4.5 %collective-permute-done.5 = bf16[136,1024]{1,0:T(8,128)(2,1)S(1)} collective-permute-done((bf16[136,1024]{1,0:T(8,128)(2,1)S(1)}, bf16[136,1024]{1,0:T(8,128)(2,1)S(1)}, u32[]{:S(2)}, u32[]{:S(2)}) %collective-permute-start.5) | collective-permute-done | bytes 278560 | tf_op jit(solution)/shard_map/ppermute | solution.py:34
  40.1 1.3 %pad_maximum_fusion = bf16[4,272,1024]{2,1,0:T(8,128)(2,1)S(1)} fusion(bf16[1,272,1024]{2,1,0:T(8,128)(2,1)S(1)} %maximum_bitcast_fusion, bf16[1,272,1024]{2,1,0:T(8,128)(2,1)S(1)} %bitcast.78, bf16[1,272,1024]{2,1,0:T(8,128)(2,1)} %bitcast.11, bf16[1,272,1024]{2,1,0:T(8,128)(2,1)S(1)} %get-tuple-element.43), kind=kLoop, calls=%fused_computation.5 | loop fusion | flops 3342336 | bytes 4456448 | tf_op jit(solution)/shard_map/stack | solution.py:137
  41.5 1.4 %copy-done.3 = bf16[4,272,1024]{2,1,0:T(8,128)(2,1)} copy-done((bf16[4,272,1024]{2,1,0:T(8,128)(2,1)}, bf16[4,272,1024]{2,1,0:T(8,128)(2,1)S(1)}, u32[]{:S(2)}) %copy-start.3) | copy-done | bytes 2228248
  43.0 0.1 add.166
  43.2 0.1 mul.68
  43.3 0.1 add.156
  43.4 3.2 %gather_fusion.1 = bf16[1024,128]{1,0:T(8,128)(2,1)S(1)} fusion(bf16[512,128]{1,0:T(8,128)(2,1)S(1)} %constant_dynamic-slice_fusion.4, s32[1024]{0:T(1024)S(1)} %broadcast_clamp_fusion), kind=kCustom, calls=%fused_computation.1 | custom fusion | bytes 528384 | tf_op jit(solution)/shard_map/jit(_take)/gather | solution.py:146
  46.7 0.2 broadcast_select_fusion
  46.9 0.1 copy.206
  47.0 1.9 %bitcast_dynamic-update-slice_fusion.3 = bf16[8,16,16512]{2,1,0:T(8,128)(2,1)} fusion(bf16[8,16,16512]{2,1,0:T(8,128)(2,1)} %bitcast_dynamic-update-slice_fusion.4, bf16[16,16512]{1,0:T(8,128)(2,1)} %collective-permute-done.6), kind=kLoop, calls=%fused_computation.26 | loop fusion | bytes 1056768
  48.9 1.6 %collective-permute-start.8 = (bf16[16,16512]{1,0:T(8,128)(2,1)}, bf16[16,16512]{1,0:T(8,128)(2,1)}, u32[]{:S(2)}, u32[]{:S(2)}) collective-permute-start(bf16[16,16512]{1,0:T(8,128)(2,1)} %collective-permute-done.6), channel_id=1, source_target_pairs={{0,8},{8,16},{16,24},{24,28},{28,20},{20,12},{12,4},{4,0},{1,9},{9... | collective-permute-start | bytes 1585160 | tf_op jit(solution)/shard_map/ppermute | solution.py:28
  50.5 0.4 collective-permute-start.9
  51.0 1.9 %bitcast_dynamic-update-slice_fusion.2 = bf16[8,16,16512]{2,1,0:T(8,128)(2,1)} fusion(bf16[8,16,16512]{2,1,0:T(8,128)(2,1)} %bitcast_dynamic-update-slice_fusion.3, bf16[16,16512]{1,0:T(8,128)(2,1)} %collective-permute-done.7), kind=kLoop, calls=%fused_computation.25 | loop fusion | bytes 1056768
  52.9 2.3 %convert_bitcast_fusion = bf16[4,2,1024,128]{2,3,1,0:T(8,128)(2,1)S(1)} fusion(bf16[4,272,1024]{2,1,0:T(8,128)(2,1)} %copy-done.3, bf16[4,2,256]{2,1,0:T(2,128)(2,1)S(1)} %mul.68, bf16[4,256,128]{1,2,0:T(8,128)(2,1)S(1)} %copy.206), kind=kOutput, calls=%fused_computation.10 | convolution fusion | flops 538181632 | bytes 4460544 | tf_op jit(solution)/shard_map/bkr,bhkl->bhrl/dot_general | solution.py:151
  55.2 2.7 %copy.207 = bf16[4,2,1024,128]{3,2,1,0:T(8,128)(2,1)} copy(bf16[4,2,1024,128]{2,3,1,0:T(8,128)(2,1)S(1)} %convert_bitcast_fusion) | data formatting | bytes 4194304 | tf_op jit(solution)/shard_map/convert_element_type | solution.py:153
  57.8 5.4 %collective-permute-done.8 = bf16[16,16512]{1,0:T(8,128)(2,1)} collective-permute-done((bf16[16,16512]{1,0:T(8,128)(2,1)}, bf16[16,16512]{1,0:T(8,128)(2,1)}, u32[]{:S(2)}, u32[]{:S(2)}) %collective-permute-start.8) | collective-permute-done | bytes 528416 | tf_op jit(solution)/shard_map/ppermute | solution.py:28
  63.2 0.9 collective-permute-done.9
  64.1 1.0 slice.88
  65.1 0.9 collective-permute-start.11
  66.0 1.0 slice.87
  67.0 1.4 %collective-permute-start.10 = (bf16[8,16512]{1,0:T(8,128)(2,1)S(1)}, bf16[8,16512]{1,0:T(8,128)(2,1)S(1)}, u32[]{:S(2)}, u32[]{:S(2)}) collective-permute-start(bf16[8,16512]{1,0:T(8,128)(2,1)S(1)} %slice.87), channel_id=1, source_target_pairs={{0,8},{8,16},{16,24},{24,28},{28,20},{20,12},{12,4},{4,0},{1,9},{9... | collective-permute-start | bytes 792584 | tf_op jit(solution)/shard_map/ppermute | solution.py:33
  68.4 1.9 %bitcast_dynamic-update-slice_fusion.1 = bf16[8,16,16512]{2,1,0:T(8,128)(2,1)} fusion(bf16[8,16,16512]{2,1,0:T(8,128)(2,1)} %bitcast_dynamic-update-slice_fusion.2, bf16[16,16512]{1,0:T(8,128)(2,1)} %collective-permute-done.8), kind=kLoop, calls=%fused_computation.24 | loop fusion | bytes 1056768
  70.2 1.9 %bitcast_dynamic-update-slice_fusion = bf16[8,16,16512]{2,1,0:T(8,128)(2,1)} fusion(bf16[8,16,16512]{2,1,0:T(8,128)(2,1)} %bitcast_dynamic-update-slice_fusion.1, bf16[16,16512]{1,0:T(8,128)(2,1)} %collective-permute-done.9), kind=kLoop, calls=%fused_computation.23 | loop fusion | bytes 1056768
  72.1 3.3 %convolution_bitcast_fusion = f32[16,128,512]{2,1,0:T(8,128)} fusion(bf16[512,4,2,64,1]{0,3,2,1,4:T(8,128)(2,1)S(1)} %bitcast.77, bf16[4,2,64,16,128]{4,3,2,1,0:T(8,128)(2,1)S(1)} %bitcast.75), kind=kOutput, calls=%fused_computation.6 | convolution fusion | flops 1073741824 | bytes 6815744 | tf_op jit(solution)/shard_map/dot_general | solution.py:162
  75.4 4.8 %reshape.207.refs_1_ = f32[8192,128]{1,0:T(8,128)} reshape(f32[16,128,512]{2,1,0:T(8,128)} %convolution_bitcast_fusion) | data formatting | bytes 8388608 | tf_op jit(solution)/shard_map/reshape | solution.py:86
  80.2 0.8 fusion.10
  81.0 0.7 slice.89
  81.8 0.1 copy.216
  81.9 0.7 copy.211.refs_0_
  82.5 11.9 %shard_map.109 = f32[1,16,128]{2,1,0:T(8,128)} custom-call(s32[8,4]{1,0:T(8,128)} %copy.211.refs_0_, f32[8192,128]{1,0:T(8,128)} %reshape.207.refs_1_, bf16[128,16512]{1,0:T(8,128)(2,1)} %bitcast.76), custom_call_target="tpu_custom_call" | custom-call | tf_op jit(solution)/shard_map/pallas_call | solution.py:102
  94.4 0.8 reshape_reshape_transpose.3
  95.2 0.6 gather_fusion.3
  95.9 5.9 %all-reduce.2 = f32[16,128]{1,0:T(8,128)S(1)} all-reduce(f32[16,128]{1,0:T(8,128)S(1)} %broadcast_select_fusion.1), channel_id=2, replica_groups=mesh['grp'=8,'band'=4] {'band'}, use_global_device_ids=true, to_apply=%region_1.0.clone | all-reduce | flops 2048 | bytes 16384
  101.7 0.6 constant_dynamic-slice_fusion.5
  (61 shorter events, 0.9 us)
Async XLA Ops:
  0.0 26.6 %copy-start = (bf16[512,512]{1,0:T(8,128)(2,1)S(1)}, bf16[512,512]{1,0:T(8,128)(2,1)}, u32[]{:S(2)}) copy-start(bf16[512,512]{1,0:T(8,128)(2,1)} %param.18) | copy-start | bytes 1572868
  8.3 18.4 %collective-permute-start = (bf16[16,16512]{1,0:T(8,128)(2,1)}, bf16[16,16512]{1,0:T(8,128)(2,1)}, u32[]{:S(2)}, u32[]{:S(2)}) collective-permute-start(bf16[16,16512]{1,0:T(8,128)(2,1)} %fusion.9), channel_id=1, source_target_pairs={{0,8},{8,16},{16,24},{24,28},{28,20},{20,12},{12,4},{4,0},{1,9},{9... | collective-permute-start | bytes 1585160 | tf_op jit(solution)/shard_map/ppermute | solution.py:28
  11.4 19.3 %collective-permute-start.1 = (bf16[16,16512]{1,0:T(8,128)(2,1)}, bf16[16,16512]{1,0:T(8,128)(2,1)}, u32[]{:S(2)}, u32[]{:S(2)}) collective-permute-start(bf16[16,16512]{1,0:T(8,128)(2,1)} %fusion.9), channel_id=1, source_target_pairs={{0,4},{8,0},{16,8},{24,16},{28,24},{20,28},{12,20},{4,12},{1,5},{9... | collective-permute-start | bytes 1585160 | tf_op jit(solution)/shard_map/ppermute | solution.py:29
  12.0 4.0 %copy-start.9 = (s32[8]{0:T(128)S(1)}, s32[8]{0:T(128)}, u32[]{:S(2)}) copy-start(s32[8]{0:T(128)} %constant.170.clone) | copy-start | bytes 100
  12.0 4.6 %copy-start.8 = (s32[8]{0:T(128)S(1)}, s32[8]{0:T(128)}, u32[]{:S(2)}) copy-start(s32[8]{0:T(128)} %constant.172.clone) | copy-start | bytes 100
  12.1 5.3 %copy-start.2 = (s32[8]{0:T(128)S(1)}, s32[8]{0:T(128)}, u32[]{:S(2)}) copy-start(s32[8]{0:T(128)} %constant.171.clone) | copy-start | bytes 100
  12.1 6.6 %copy-start.7 = (s32[4]{0:T(128)S(1)}, s32[4]{0:T(128)}, u32[]{:S(2)}) copy-start(s32[4]{0:T(128)} %constant.167.clone) | copy-start | bytes 52
  12.1 7.1 %copy-start.6 = (s32[4]{0:T(128)S(1)}, s32[4]{0:T(128)}, u32[]{:S(2)}) copy-start(s32[4]{0:T(128)} %constant.169.clone) | copy-start | bytes 52
  12.1 7.8 %copy-start.1 = (s32[4]{0:T(128)S(1)}, s32[4]{0:T(128)}, u32[]{:S(2)}) copy-start(s32[4]{0:T(128)} %constant.168.clone) | copy-start | bytes 52
  13.2 17.5 %collective-permute-start.3 = (bf16[272,1024]{1,0:T(8,128)(2,1)}, bf16[272,1024]{1,0:T(8,128)(2,1)S(1)}, u32[]{:S(2)}, u32[]{:S(2)}) collective-permute-start(bf16[272,1024]{1,0:T(8,128)(2,1)} %get-tuple-element.44), channel_id=1, source_target_pairs={{0,1},{2,0},{3,2},{1,3},{4,5},{6,4},{7,6},{5,7},{8,9},{10,8},{11,1... | collective-permute-start | bytes 1671176 | tf_op jit(solution)/shard_map/ppermute | solution.py:29
  13.2 17.5 %collective-permute-start.2 = (bf16[272,1024]{1,0:T(8,128)(2,1)}, bf16[272,1024]{1,0:T(8,128)(2,1)}, u32[]{:S(2)}, u32[]{:S(2)}) collective-permute-start(bf16[272,1024]{1,0:T(8,128)(2,1)} %get-tuple-element.44), channel_id=1, source_target_pairs={{0,2},{2,3},{3,1},{1,0},{4,6},{6,7},{7,5},{5,4},{8,10},{10,11},{11... | collective-permute-start | bytes 1671176 | tf_op jit(solution)/shard_map/ppermute | solution.py:28
  16.1 9.3 %copy-start.5 = (u32[32]{0:T(128)S(1)}, u32[32]{0:T(128)}, u32[]{:S(2)}) copy-start(u32[32]{0:T(128)} %constant.182) | copy-start | bytes 388
  26.7 20.3 %collective-permute-start.6 = (bf16[16,16512]{1,0:T(8,128)(2,1)}, bf16[16,16512]{1,0:T(8,128)(2,1)}, u32[]{:S(2)}, u32[]{:S(2)}) collective-permute-start(bf16[16,16512]{1,0:T(8,128)(2,1)} %collective-permute-done), channel_id=1, source_target_pairs={{0,8},{8,16},{16,24},{24,28},{28,20},{20,12},{12,4},{4,0},{1,9},{9... | collective-permute-start | bytes 1585160 | tf_op jit(solution)/shard_map/ppermute | solution.py:28
  30.7 16.4 %collective-permute-start.7 = (bf16[16,16512]{1,0:T(8,128)(2,1)}, bf16[16,16512]{1,0:T(8,128)(2,1)}, u32[]{:S(2)}, u32[]{:S(2)}) collective-permute-start(bf16[16,16512]{1,0:T(8,128)(2,1)} %collective-permute-done.1), channel_id=1, source_target_pairs={{0,4},{8,0},{16,8},{24,16},{28,24},{20,28},{12,20},{4,12},{1,5},{9... | collective-permute-start | bytes 1585160 | tf_op jit(solution)/shard_map/ppermute | solution.py:29
  30.7 9.4 %collective-permute-start.5 = (bf16[136,1024]{1,0:T(8,128)(2,1)S(1)}, bf16[136,1024]{1,0:T(8,128)(2,1)S(1)}, u32[]{:S(2)}, u32[]{:S(2)}) collective-permute-start(bf16[136,1024]{1,0:T(8,128)(2,1)S(1)} %slice.85), channel_id=1, source_target_pairs={{0,1},{2,0},{3,2},{1,3},{4,5},{6,4},{7,6},{5,7},{8,9},{10,8},{11,1... | collective-permute-start | bytes 835592 | tf_op jit(solution)/shard_map/ppermute | solution.py:34
  31.7 8.4 %collective-permute-start.4 = (bf16[136,1024]{1,0:T(8,128)(2,1)S(1)}, bf16[136,1024]{1,0:T(8,128)(2,1)S(1)}, u32[]{:S(2)}, u32[]{:S(2)}) collective-permute-start(bf16[136,1024]{1,0:T(8,128)(2,1)S(1)} %slice.84), channel_id=1, source_target_pairs={{0,2},{2,3},{3,1},{1,0},{4,6},{6,7},{7,5},{5,4},{8,10},{10,11},{11... | collective-permute-start | bytes 835592 | tf_op jit(solution)/shard_map/ppermute | solution.py:33
  41.5 1.4 %copy-start.3 = (bf16[4,272,1024]{2,1,0:T(8,128)(2,1)}, bf16[4,272,1024]{2,1,0:T(8,128)(2,1)S(1)}, u32[]{:S(2)}) copy-start(bf16[4,272,1024]{2,1,0:T(8,128)(2,1)S(1)} %pad_maximum_fusion) | copy-start | bytes 6684676
  48.9 14.3 %collective-permute-start.8 = (bf16[16,16512]{1,0:T(8,128)(2,1)}, bf16[16,16512]{1,0:T(8,128)(2,1)}, u32[]{:S(2)}, u32[]{:S(2)}) collective-permute-start(bf16[16,16512]{1,0:T(8,128)(2,1)} %collective-permute-done.6), channel_id=1, source_target_pairs={{0,8},{8,16},{16,24},{24,28},{28,20},{20,12},{12,4},{4,0},{1,9},{9... | collective-permute-start | bytes 1585160 | tf_op jit(solution)/shard_map/ppermute | solution.py:28
  50.5 13.6 %collective-permute-start.9 = (bf16[16,16512]{1,0:T(8,128)(2,1)}, bf16[16,16512]{1,0:T(8,128)(2,1)}, u32[]{:S(2)}, u32[]{:S(2)}) collective-permute-start(bf16[16,16512]{1,0:T(8,128)(2,1)} %collective-permute-done.7), channel_id=1, source_target_pairs={{0,4},{8,0},{16,8},{24,16},{28,24},{20,28},{12,20},{4,12},{1,5},{9... | collective-permute-start | bytes 1585160 | tf_op jit(solution)/shard_map/ppermute | solution.py:29
  57.8 14.3 %copy-start.4 = (bf16[4,2,1024,128]{3,2,1,0:T(8,128)(2,1)S(1)}, bf16[4,2,1024,128]{3,2,1,0:T(8,128)(2,1)}, u32[]{:S(2)}) copy-start(bf16[4,2,1024,128]{3,2,1,0:T(8,128)(2,1)} %copy.207) | copy-start | bytes 6291460
  65.1 15.1 %collective-permute-start.11 = (bf16[8,16512]{1,0:T(8,128)(2,1)S(1)}, bf16[8,16512]{1,0:T(8,128)(2,1)S(1)}, u32[]{:S(2)}, u32[]{:S(2)}) collective-permute-start(bf16[8,16512]{1,0:T(8,128)(2,1)S(1)} %slice.88), channel_id=1, source_target_pairs={{0,4},{8,0},{16,8},{24,16},{28,24},{20,28},{12,20},{4,12},{1,5},{9... | collective-permute-start | bytes 792584 | tf_op jit(solution)/shard_map/ppermute | solution.py:34
  67.0 13.3 %collective-permute-start.10 = (bf16[8,16512]{1,0:T(8,128)(2,1)S(1)}, bf16[8,16512]{1,0:T(8,128)(2,1)S(1)}, u32[]{:S(2)}, u32[]{:S(2)}) collective-permute-start(bf16[8,16512]{1,0:T(8,128)(2,1)S(1)} %slice.87), channel_id=1, source_target_pairs={{0,8},{8,16},{16,24},{24,28},{28,20},{20,12},{12,4},{4,0},{1,9},{9... | collective-permute-start | bytes 792584 | tf_op jit(solution)/shard_map/ppermute | solution.py:33

commit v10 on v9

--- a/solution.py
+++ b/solution.py
@@ -49,7 +49,8 @@
         for h in range(2):
             for j in range(blk):
                 for t in range(tiles):
-                    start = (h * blk + j) * tiles + t
+                    lam = h * blk + j
+                    start = ((lam // 8) * tiles + t) * 8 + lam % 8
                     rows = table_ref[pl.ds(start, ri, stride=lam_count * tiles), :]
                     hi = rows.astype(jnp.bfloat16)
                     lo = (rows - hi.astype(jnp.float32)).astype(jnp.bfloat16)
@@ -83,7 +84,9 @@
     while chunk > 1 and (chunk * ri * flat * 2 > (4 << 20) or groups % chunk):
         chunk -= 1
     steps = groups // chunk
-    table2 = folded.reshape(ri * lam_count * (orbitals // 128), 128)
+    tiles = orbitals // 128
+    table2 = folded.reshape(ri, lam_count // 8, 8, tiles, 128)
+    table2 = jnp.transpose(table2, (0, 1, 3, 2, 4)).reshape(ri * lam_count * tiles, 128)
     grid_spec = pltpu.PrefetchScalarGridSpec(
         num_scalar_prefetch=1,
         grid=(steps,),

time: 103 us -> 102 us (level)
  matrix products: 5.61 us -> 8.45 us
  local copies, waits for them, and re-layouts: 42.6 us -> 41 us
  other arithmetic: 7.88 us -> 6.8 us
  waiting for transfers between devices: 10.8 us -> 9.75 us
    dot_general x0 -> x2, local copies, waits for them, and re-layouts: none -> 6.62 us  [on_device(): lax.dot_general(occ_raw, virt_cols, (((0, 1, 2), (1, 2, 3)), ((), ())), p...]
    reshape x1 -> x0, local copies, waits for them, and re-layouts: 4.78 us -> none  [contract(): table2 = folded.reshape(ri * lam_count * (orbitals // 128), 128)]
    dot_general x1, matrix products: 3.31 us -> 6.14 us  [on_device(): lax.dot_general(occ_raw, virt_cols, (((0, 1, 2), (1, 2, 3)), ((), ())), p...]
    slice x2, local copies, waits for them, and re-layouts: 1.94 us -> 0.04 us  [ring_gather(): first = lax.ppermute(ahead[:rows], axis, fwd)]
    unnamed x29 -> x31, local copies, waits for them, and re-layouts: 14 us -> 12.7 us
    another operation x3, other arithmetic: 2.26 us -> 1.2 us  [on_device(): xg = jnp.stack(band_got)]
    ppermute x4, waiting for transfers between devices: 5.39 us -> 4.35 us  [ring_gather(): ahead = lax.ppermute(ahead, axis, fwd)]
  transfers between devices with their start and end apart: 12 -> 12, of which waited for: 3 -> 3; matrix products, arithmetic and copies ran while one was open for 39% -> 40% of each run, Pallas kernels for 0% -> 0%
where the time goes in v10:
time: 102 us
  local copies, waits for them, and re-layouts  41 us (40%)
  starting transfers between devices  13.5 us (13%)
  Pallas kernels  11.9 us (12%)
  waiting for transfers between devices  9.75 us (10%)
  matrix products  8.45 us (8%)
  other arithmetic  6.8 us (7%)
  blocking collectives  5.86 us (6%)
  between operations  4.38 us (4%)
    unnamed x31, local copies, waits for them, and re-layouts  12.7 us
    pallas_call x1, Pallas kernels, contract(): pl.pallas_call(body, out_shape=jax.ShapeDtypeStruct((steps, ri, chunk * r...  11.9 us
    ppermute x4, starting transfers between devices, ring_gather(): ahead = lax.ppermute(ahead, axis, fwd)  8.7 us
    dot_general x2, local copies, waits for them, and re-layouts, on_device(): lax.dot_general(occ_raw, virt_cols, (((0, 1, 2), (1, 2, 3)), ((), ())), p...  6.62 us
    dot_general x1, matrix products, on_device(): lax.dot_general(occ_raw, virt_cols, (((0, 1, 2), (1, 2, 3)), ((), ())), p...  6.14 us
    unnamed x1, blocking collectives  5.86 us
    ppermute x2, waiting for transfers between devices, ring_gather(): second = lax.ppermute(behind[rows:], axis, bwd)  4.47 us
    ppermute x4, waiting for transfers between devices, ring_gather(): ahead = lax.ppermute(ahead, axis, fwd)  4.35 us
  transfers between devices with their start and end apart: 12, of which 3 were waited for; matrix products, arithmetic and copies ran while one was open for 40% of the time, Pallas kernels for 0%

profile of v10, /device:TPU:0, one launch (start us, length us, event | category | flops | bytes accessed | tf_op | source)
XLA Modules:
  0.0 101.6 jit_solution(17965624757354031889)
XLA Ops:
  0.0 0.7 convert_bitcast_fusion.2
  0.7 1.8 %squeeze.9 = bf16[4,64,16,64]{3,2,1,0:T(8,128)(2,1)S(1)} reshape(bf16[1,4,64,1024]{3,2,1,0:T(8,128)(2,1)} %param.15) | data formatting | bytes 1048576 | tf_op jit(solution)/shard_map/squeeze | solution.py:112
  2.5 2.2 %copy.223 = bf16[4,64,16,64]{1,0,2,3:T(4,128)(2,1)S(1)} copy(bf16[4,64,16,64]{3,2,1,0:T(8,128)(2,1)S(1)} %squeeze.9) | data formatting | bytes 1048576 | tf_op jit(solution)/shard_map/squeeze | solution.py:112
  5.3 0.6 multiply_bitcast_fusion
  5.9 0.7 copy.224
  6.6 0.8 reshape.205
  7.5 0.8 fusion.11
  8.3 3.0 %collective-permute-start = (bf16[16,16512]{1,0:T(8,128)(2,1)}, bf16[16,16512]{1,0:T(8,128)(2,1)}, u32[]{:S(2)}, u32[]{:S(2)}) collective-permute-start(bf16[16,16512]{1,0:T(8,128)(2,1)} %fusion.11), channel_id=1, source_target_pairs={{0,8},{8,16},{16,24},{24,28},{28,20},{20,12},{12,4},{4,0},{1,9},{9... | collective-permute-start | bytes 1585160 | tf_op jit(solution)/shard_map/ppermute | solution.py:28
  11.3 0.7 reshape.206
  12.1 0.2 copy.225
  12.3 0.9 fusion.26
  13.2 2.0 %collective-permute-start.2 = (bf16[272,1024]{1,0:T(8,128)(2,1)}, bf16[272,1024]{1,0:T(8,128)(2,1)S(1)}, u32[]{:S(2)}, u32[]{:S(2)}) collective-permute-start(bf16[272,1024]{1,0:T(8,128)(2,1)} %get-tuple-element.44), channel_id=1, source_target_pairs={{0,2},{2,3},{3,1},{1,0},{4,6},{6,7},{7,5},{5,4},{8,10},{10,11},{11... | collective-permute-start | bytes 1671176 | tf_op jit(solution)/shard_map/ppermute | solution.py:28
  15.2 0.8 bitcast_dynamic-update-slice_fusion.6
  16.1 0.6 dynamic_slice.21
  16.7 0.7 compare_select_fusion.7
  17.3 0.6 gather_fusion
  18.0 0.6 scatter_custom_fusion
  18.6 0.6 dynamic_slice.23
  19.2 0.7 compare_select_fusion.4
  19.9 0.6 gather_fusion.2
  20.6 0.7 fusion.27
  23.9 0.1 add.158
  24.0 1.1 %constant_dynamic-slice_fusion.3 = (bf16[512,128]{1,0:T(8,128)(2,1)S(1)}, bf16[512,128]{1,0:T(8,128)(2,1)S(1)}, bf16[512,128]{1,0:T(8,128)(2,1)S(1)}, bf16[512,128]{1,0:T(8,128)(2,1)S(1)}) fusion(bf16[512,512]{1,0:T(8,128)(2,1)} %param.19, s32[]{:T(128)S(6)} %select_n.116, s32[]{:T(128)S(6)} %select_n.117, s32[]{:T(128)S(6)} %select_n.119, s32[]{:T(128)S(6)} %select_n.118), kind=kLoop, calls=%fused_computation.76 | loop fusion | bytes 1048592 | tf_op jit(solution)/shard_map/dynamic_slice | solution.py:162
  25.2 1.5 %reshape.257 = bf16[4,128,4,2,64]{4,3,2,1,0:T(2,128)(2,1)} reshape(bf16[512,512]{1,0:T(8,128)(2,1)S(1)} %pad_maximum_fusion.1) | data formatting | bytes 1048576 | tf_op jit(solution)/shard_map/dot_general | solution.py:165
  26.8 0.1 broadcast_in_dim.43
  26.9 0.6 dynamic-slice.13
  28.2 2.1 %collective-permute-start.6 = (bf16[16,16512]{1,0:T(8,128)(2,1)}, bf16[16,16512]{1,0:T(8,128)(2,1)S(1)}, u32[]{:S(2)}, u32[]{:S(2)}) collective-permute-start(bf16[16,16512]{1,0:T(8,128)(2,1)} %collective-permute-done), channel_id=1, source_target_pairs={{0,8},{8,16},{16,24},{24,28},{28,20},{20,12},{12,4},{4,0},{1,9},{9... | collective-permute-start | bytes 1585160 | tf_op jit(solution)/shard_map/ppermute | solution.py:28
  30.3 1.9 %bitcast_dynamic-update-slice_fusion.5 = bf16[8,16,16512]{2,1,0:T(8,128)(2,1)} fusion(bf16[8,16,16512]{2,1,0:T(8,128)(2,1)} %bitcast_dynamic-update-slice_fusion.6, bf16[16,16512]{1,0:T(8,128)(2,1)} %collective-permute-done), kind=kLoop, calls=%fused_computation.29 | loop fusion | bytes 1056768
  32.3 2.0 %collective-permute-start.4 = (bf16[136,1024]{1,0:T(8,128)(2,1)S(1)}, bf16[136,1024]{1,0:T(8,128)(2,1)S(1)}, u32[]{:S(2)}, u32[]{:S(2)}) collective-permute-start(bf16[136,1024]{1,0:T(8,128)(2,1)S(1)} %slice.84), channel_id=1, source_target_pairs={{0,2},{2,3},{3,1},{1,0},{4,6},{6,7},{7,5},{5,4},{8,10},{10,11},{11... | collective-permute-start | bytes 835592 | tf_op jit(solution)/shard_map/ppermute | solution.py:33
  34.3 1.9 %bitcast_dynamic-update-slice_fusion.4 = bf16[8,16,16512]{2,1,0:T(8,128)(2,1)} fusion(bf16[8,16,16512]{2,1,0:T(8,128)(2,1)} %bitcast_dynamic-update-slice_fusion.5, bf16[16,16512]{1,0:T(8,128)(2,1)} %collective-permute-done.1), kind=kLoop, calls=%fused_computation.28 | loop fusion | bytes 1056768
  36.2 4.5 %collective-permute-done.5 = bf16[136,1024]{1,0:T(8,128)(2,1)S(1)} collective-permute-done((bf16[136,1024]{1,0:T(8,128)(2,1)S(1)}, bf16[136,1024]{1,0:T(8,128)(2,1)S(1)}, u32[]{:S(2)}, u32[]{:S(2)}) %collective-permute-start.5) | collective-permute-done | bytes 278560 | tf_op jit(solution)/shard_map/ppermute | solution.py:34
  40.7 0.3 pad_maximum_fusion
  41.0 1.4 %copy-done.3 = bf16[4,272,1024]{2,1,0:T(8,128)(2,1)} copy-done((bf16[4,272,1024]{2,1,0:T(8,128)(2,1)}, bf16[4,272,1024]{2,1,0:T(8,128)(2,1)S(1)}, u32[]{:S(2)}) %copy-start.3) | copy-done | bytes 2228248
  42.5 0.1 add.166
  42.7 0.1 mul.68
  42.8 0.1 add.156
  42.9 3.2 %gather_fusion.1 = bf16[1024,128]{1,0:T(8,128)(2,1)S(1)} fusion(bf16[512,128]{1,0:T(8,128)(2,1)S(1)} %constant_dynamic-slice_fusion.4, s32[1024]{0:T(1024)S(1)} %broadcast_clamp_fusion), kind=kCustom, calls=%fused_computation.1 | custom fusion | bytes 528384 | tf_op jit(solution)/shard_map/jit(_take)/gather | solution.py:149
  46.1 0.2 broadcast_select_fusion
  46.4 0.1 copy.226
  46.5 0.8 copy-done.5
  47.3 0.8 bitcast_dynamic-update-slice_fusion.3
  48.1 1.6 %collective-permute-start.8 = (bf16[16,16512]{1,0:T(8,128)(2,1)}, bf16[16,16512]{1,0:T(8,128)(2,1)S(1)}, u32[]{:S(2)}, u32[]{:S(2)}) collective-permute-start(bf16[16,16512]{1,0:T(8,128)(2,1)} %copy-done.5), channel_id=1, source_target_pairs={{0,8},{8,16},{16,24},{24,28},{28,20},{20,12},{12,4},{4,0},{1,9},{9... | collective-permute-start | bytes 1585160 | tf_op jit(solution)/shard_map/ppermute | solution.py:28
  49.7 0.4 collective-permute-start.9
  50.2 1.9 %bitcast_dynamic-update-slice_fusion.2 = bf16[8,16,16512]{2,1,0:T(8,128)(2,1)} fusion(bf16[8,16,16512]{2,1,0:T(8,128)(2,1)} %bitcast_dynamic-update-slice_fusion.3, bf16[16,16512]{1,0:T(8,128)(2,1)} %collective-permute-done.7), kind=kLoop, calls=%fused_computation.26 | loop fusion | bytes 1056768
  52.1 2.3 %convert_bitcast_fusion = bf16[4,2,1024,128]{2,3,1,0:T(8,128)(2,1)S(1)} fusion(bf16[4,272,1024]{2,1,0:T(8,128)(2,1)} %copy-done.3, bf16[4,2,256]{2,1,0:T(2,128)(2,1)S(1)} %mul.68, bf16[4,256,128]{1,2,0:T(8,128)(2,1)S(1)} %copy.226), kind=kOutput, calls=%fused_computation.10 | convolution fusion | flops 538181632 | bytes 4460544 | tf_op jit(solution)/shard_map/bkr,bhkl->bhrl/dot_general | solution.py:154
  54.4 2.6 %copy.227 = bf16[4,2,1024,128]{3,2,1,0:T(8,128)(2,1)} copy(bf16[4,2,1024,128]{2,3,1,0:T(8,128)(2,1)S(1)} %convert_bitcast_fusion) | data formatting | bytes 4194304 | tf_op jit(solution)/shard_map/convert_element_type | solution.py:156
  57.0 4.3 %collective-permute-done.8 = bf16[16,16512]{1,0:T(8,128)(2,1)S(1)} collective-permute-done((bf16[16,16512]{1,0:T(8,128)(2,1)}, bf16[16,16512]{1,0:T(8,128)(2,1)S(1)}, u32[]{:S(2)}, u32[]{:S(2)}) %collective-permute-start.8) | collective-permute-done | bytes 528416 | tf_op jit(solution)/shard_map/ppermute | solution.py:28
  61.4 0.9 collective-permute-done.9
  62.3 1.0 slice.88
  63.2 1.0 collective-permute-start.11
  64.2 1.3 %collective-permute-start.10 = (bf16[8,16512]{1,0:T(8,128)(2,1)S(1)}, bf16[8,16512]{1,0:T(8,128)(2,1)S(1)}, u32[]{:S(2)}, u32[]{:S(2)}) collective-permute-start(bf16[8,16512]{1,0:T(8,128)(2,1)S(1)} %slice.87), channel_id=1, source_target_pairs={{0,8},{8,16},{16,24},{24,28},{28,20},{20,12},{12,4},{4,0},{1,9},{9... | collective-permute-start | bytes 792584 | tf_op jit(solution)/shard_map/ppermute | solution.py:33
  65.6 5.1 %copy.229 = bf16[16,128,4,2,64]{4,1,3,2,0:T(8,128)(2,1)} copy(bf16[16,128,4,2,64]{1,0,4,3,2:T(8,128)(2,1)} %bitcast.82) | data formatting | bytes 4194304 | tf_op jit(solution)/shard_map/dot_general | solution.py:165
  70.7 0.8 bitcast_dynamic-update-slice_fusion.1
  71.5 1.9 %bitcast_dynamic-update-slice_fusion = bf16[8,16,16512]{2,1,0:T(8,128)(2,1)} fusion(bf16[8,16,16512]{2,1,0:T(8,128)(2,1)} %bitcast_dynamic-update-slice_fusion.1, bf16[16,16512]{1,0:T(8,128)(2,1)} %collective-permute-done.9), kind=kLoop, calls=%fused_computation.24 | loop fusion | bytes 1056768
  73.4 6.1 %fusion = f32[16,16,8,4,128,1,1]{4,2,6,5,3,1,0:T(8,128)} fusion(bf16[4,128,4,2,64,1,1]{4,3,2,1,0,6,5:T(2,128)(2,1)S(1)} %bitcast.88, bf16[16,128,4,2,64]{4,1,3,2,0:T(8,128)(2,1)} %copy.229), kind=kOutput, calls=%fused_computation.5 | convolution fusion | flops 1073741824 | bytes 6815744 | tf_op jit(solution)/shard_map/dot_general | solution.py:165
  79.5 0.8 fusion.12
  80.3 0.7 slice.89
  81.1 0.1 copy.246
  81.2 0.7 copy.233.refs_0_
  81.8 11.9 %shard_map.109 = f32[1,16,128]{2,1,0:T(8,128)} custom-call(s32[8,4]{1,0:T(8,128)} %copy.233.refs_0_, f32[8192,128]{1,0:T(8,128)} %bitcast.84, bf16[128,16512]{1,0:T(8,128)(2,1)} %bitcast.83), custom_call_target="tpu_custom_call" | custom-call | tf_op jit(solution)/shard_map/pallas_call | solution.py:105
  93.7 0.8 reshape_reshape_transpose.3
  94.5 0.6 gather_fusion.3
  95.2 5.9 %all-reduce.2 = f32[16,128]{1,0:T(8,128)S(1)} all-reduce(f32[16,128]{1,0:T(8,128)S(1)} %broadcast_select_fusion.1), channel_id=2, replica_groups=mesh['grp'=8,'band'=4] {'band'}, use_global_device_ids=true, to_apply=%region_1.0.clone | all-reduce | flops 2048 | bytes 16384
  101.1 0.6 constant_dynamic-slice_fusion.5
  (63 shorter events, 0.8 us)
Async XLA Ops:
  0.0 28.1 %copy-start = (bf16[512,512]{1,0:T(8,128)(2,1)S(1)}, bf16[512,512]{1,0:T(8,128)(2,1)}, u32[]{:S(2)}) copy-start(bf16[512,512]{1,0:T(8,128)(2,1)} %param.18) | copy-start | bytes 1572868
  8.3 19.9 %collective-permute-start = (bf16[16,16512]{1,0:T(8,128)(2,1)}, bf16[16,16512]{1,0:T(8,128)(2,1)}, u32[]{:S(2)}, u32[]{:S(2)}) collective-permute-start(bf16[16,16512]{1,0:T(8,128)(2,1)} %fusion.11), channel_id=1, source_target_pairs={{0,8},{8,16},{16,24},{24,28},{28,20},{20,12},{12,4},{4,0},{1,9},{9... | collective-permute-start | bytes 1585160 | tf_op jit(solution)/shard_map/ppermute | solution.py:28
  11.3 20.8 %collective-permute-start.1 = (bf16[16,16512]{1,0:T(8,128)(2,1)}, bf16[16,16512]{1,0:T(8,128)(2,1)}, u32[]{:S(2)}, u32[]{:S(2)}) collective-permute-start(bf16[16,16512]{1,0:T(8,128)(2,1)} %fusion.11), channel_id=1, source_target_pairs={{0,4},{8,0},{16,8},{24,16},{28,24},{20,28},{12,20},{4,12},{1,5},{9... | collective-permute-start | bytes 1585160 | tf_op jit(solution)/shard_map/ppermute | solution.py:29
  12.0 4.0 %copy-start.10 = (s32[8]{0:T(128)S(1)}, s32[8]{0:T(128)}, u32[]{:S(2)}) copy-start(s32[8]{0:T(128)} %constant.170.clone) | copy-start | bytes 100
  12.0 4.6 %copy-start.9 = (s32[8]{0:T(128)S(1)}, s32[8]{0:T(128)}, u32[]{:S(2)}) copy-start(s32[8]{0:T(128)} %constant.172.clone) | copy-start | bytes 100
  12.0 5.3 %copy-start.2 = (s32[8]{0:T(128)S(1)}, s32[8]{0:T(128)}, u32[]{:S(2)}) copy-start(s32[8]{0:T(128)} %constant.171.clone) | copy-start | bytes 100
  12.1 6.6 %copy-start.8 = (s32[4]{0:T(128)S(1)}, s32[4]{0:T(128)}, u32[]{:S(2)}) copy-start(s32[4]{0:T(128)} %constant.167.clone) | copy-start | bytes 52
  12.1 7.2 %copy-start.7 = (s32[4]{0:T(128)S(1)}, s32[4]{0:T(128)}, u32[]{:S(2)}) copy-start(s32[4]{0:T(128)} %constant.169.clone) | copy-start | bytes 52
  12.1 7.8 %copy-start.1 = (s32[4]{0:T(128)S(1)}, s32[4]{0:T(128)}, u32[]{:S(2)}) copy-start(s32[4]{0:T(128)} %constant.168.clone) | copy-start | bytes 52
  13.2 19.0 %collective-permute-start.3 = (bf16[272,1024]{1,0:T(8,128)(2,1)}, bf16[272,1024]{1,0:T(8,128)(2,1)S(1)}, u32[]{:S(2)}, u32[]{:S(2)}) collective-permute-start(bf16[272,1024]{1,0:T(8,128)(2,1)} %get-tuple-element.44), channel_id=1, source_target_pairs={{0,1},{2,0},{3,2},{1,3},{4,5},{6,4},{7,6},{5,7},{8,9},{10,8},{11,1... | collective-permute-start | bytes 1671176 | tf_op jit(solution)/shard_map/ppermute | solution.py:29
  13.2 19.0 %collective-permute-start.2 = (bf16[272,1024]{1,0:T(8,128)(2,1)}, bf16[272,1024]{1,0:T(8,128)(2,1)S(1)}, u32[]{:S(2)}, u32[]{:S(2)}) collective-permute-start(bf16[272,1024]{1,0:T(8,128)(2,1)} %get-tuple-element.44), channel_id=1, source_target_pairs={{0,2},{2,3},{3,1},{1,0},{4,6},{6,7},{7,5},{5,4},{8,10},{10,11},{11... | collective-permute-start | bytes 1671176 | tf_op jit(solution)/shard_map/ppermute | solution.py:28
  18.0 8.9 %copy-start.6 = (u32[32]{0:T(128)S(1)}, u32[32]{0:T(128)}, u32[]{:S(2)}) copy-start(u32[32]{0:T(128)} %constant.182) | copy-start | bytes 388
  28.2 18.3 %collective-permute-start.6 = (bf16[16,16512]{1,0:T(8,128)(2,1)}, bf16[16,16512]{1,0:T(8,128)(2,1)S(1)}, u32[]{:S(2)}, u32[]{:S(2)}) collective-permute-start(bf16[16,16512]{1,0:T(8,128)(2,1)} %collective-permute-done), channel_id=1, source_target_pairs={{0,8},{8,16},{16,24},{24,28},{28,20},{20,12},{12,4},{4,0},{1,9},{9... | collective-permute-start | bytes 1585160 | tf_op jit(solution)/shard_map/ppermute | solution.py:28
  32.2 14.4 %collective-permute-start.7 = (bf16[16,16512]{1,0:T(8,128)(2,1)}, bf16[16,16512]{1,0:T(8,128)(2,1)}, u32[]{:S(2)}, u32[]{:S(2)}) collective-permute-start(bf16[16,16512]{1,0:T(8,128)(2,1)} %collective-permute-done.1), channel_id=1, source_target_pairs={{0,4},{8,0},{16,8},{24,16},{28,24},{20,28},{12,20},{4,12},{1,5},{9... | collective-permute-start | bytes 1585160 | tf_op jit(solution)/shard_map/ppermute | solution.py:29
  32.2 8.4 %collective-permute-start.5 = (bf16[136,1024]{1,0:T(8,128)(2,1)S(1)}, bf16[136,1024]{1,0:T(8,128)(2,1)S(1)}, u32[]{:S(2)}, u32[]{:S(2)}) collective-permute-start(bf16[136,1024]{1,0:T(8,128)(2,1)S(1)} %slice.85), channel_id=1, source_target_pairs={{0,1},{2,0},{3,2},{1,3},{4,5},{6,4},{7,6},{5,7},{8,9},{10,8},{11,1... | collective-permute-start | bytes 835592 | tf_op jit(solution)/shard_map/ppermute | solution.py:34
  32.3 8.4 %collective-permute-start.4 = (bf16[136,1024]{1,0:T(8,128)(2,1)S(1)}, bf16[136,1024]{1,0:T(8,128)(2,1)S(1)}, u32[]{:S(2)}, u32[]{:S(2)}) collective-permute-start(bf16[136,1024]{1,0:T(8,128)(2,1)S(1)} %slice.84), channel_id=1, source_target_pairs={{0,2},{2,3},{3,1},{1,0},{4,6},{6,7},{7,5},{5,4},{8,10},{10,11},{11... | collective-permute-start | bytes 835592 | tf_op jit(solution)/shard_map/ppermute | solution.py:33
  41.0 1.4 %copy-start.3 = (bf16[4,272,1024]{2,1,0:T(8,128)(2,1)}, bf16[4,272,1024]{2,1,0:T(8,128)(2,1)S(1)}, u32[]{:S(2)}) copy-start(bf16[4,272,1024]{2,1,0:T(8,128)(2,1)S(1)} %pad_maximum_fusion) | copy-start | bytes 6684676
  46.5 0.8 copy-start.5
  48.1 13.2 %collective-permute-start.8 = (bf16[16,16512]{1,0:T(8,128)(2,1)}, bf16[16,16512]{1,0:T(8,128)(2,1)S(1)}, u32[]{:S(2)}, u32[]{:S(2)}) collective-permute-start(bf16[16,16512]{1,0:T(8,128)(2,1)} %copy-done.5), channel_id=1, source_target_pairs={{0,8},{8,16},{16,24},{24,28},{28,20},{20,12},{12,4},{4,0},{1,9},{9... | collective-permute-start | bytes 1585160 | tf_op jit(solution)/shard_map/ppermute | solution.py:28
  49.7 12.5 %collective-permute-start.9 = (bf16[16,16512]{1,0:T(8,128)(2,1)}, bf16[16,16512]{1,0:T(8,128)(2,1)}, u32[]{:S(2)}, u32[]{:S(2)}) collective-permute-start(bf16[16,16512]{1,0:T(8,128)(2,1)} %collective-permute-done.7), channel_id=1, source_target_pairs={{0,4},{8,0},{16,8},{24,16},{28,24},{20,28},{12,20},{4,12},{1,5},{9... | collective-permute-start | bytes 1585160 | tf_op jit(solution)/shard_map/ppermute | solution.py:29
  63.2 16.3 %collective-permute-start.11 = (bf16[8,16512]{1,0:T(8,128)(2,1)S(1)}, bf16[8,16512]{1,0:T(8,128)(2,1)S(1)}, u32[]{:S(2)}, u32[]{:S(2)}) collective-permute-start(bf16[8,16512]{1,0:T(8,128)(2,1)S(1)} %slice.88), channel_id=1, source_target_pairs={{0,4},{8,0},{16,8},{24,16},{28,24},{20,28},{12,20},{4,12},{1,5},{9... | collective-permute-start | bytes 792584 | tf_op jit(solution)/shard_map/ppermute | solution.py:34
  64.2 15.3 %collective-permute-start.10 = (bf16[8,16512]{1,0:T(8,128)(2,1)S(1)}, bf16[8,16512]{1,0:T(8,128)(2,1)S(1)}, u32[]{:S(2)}, u32[]{:S(2)}) collective-permute-start(bf16[8,16512]{1,0:T(8,128)(2,1)S(1)} %slice.87), channel_id=1, source_target_pairs={{0,8},{8,16},{16,24},{24,28},{28,20},{20,12},{12,4},{4,0},{1,9},{9... | collective-permute-start | bytes 792584 | tf_op jit(solution)/shard_map/ppermute | solution.py:33
  65.6 7.8 %copy-start.4 = (bf16[4,128,4,2,64]{4,3,2,1,0:T(2,128)(2,1)S(1)}, bf16[4,128,4,2,64]{4,3,2,1,0:T(2,128)(2,1)}, u32[]{:S(2)}) copy-start(bf16[4,128,4,2,64]{4,3,2,1,0:T(2,128)(2,1)} %reshape.257) | copy-start | bytes 1572868

commit v11 on v10

--- a/solution.py
+++ b/solution.py
@@ -172,7 +172,13 @@
     order = jnp.zeros((group_count,), jnp.int32).at[grp_ids].set(jnp.arange(group_count, dtype=jnp.int32))
     arrived = arrived.reshape(ri_local, group_count, ri_local)
     partial_value = jnp.take(arrived, order, axis=1).reshape(ri_local, group_count * ri_local)
-    response = lax.psum_scatter(partial_value, "band", scatter_dimension=0, tiled=True)
+    rows_out = ri_local // band_count
+    blocks = partial_value.reshape(band_count, rows_out, group_count * ri_local)
+    response = lax.dynamic_index_in_dim(blocks, band, 0, keepdims=False)
+    for shift in range(1, band_count):
+        sent = lax.dynamic_index_in_dim(blocks, (band + shift) % band_count, 0, keepdims=False)
+        pairs = [(i, (i + shift) % band_count) for i in range(band_count)]
+        response = response + lax.ppermute(sent, "band", pairs)
     return response
 
 

time: 102 us -> 97.9 us (0.960)
  blocking collectives: 5.86 us -> 0 us
  waiting for transfers between devices: 9.75 us -> 12.8 us
  local copies, waits for them, and re-layouts: 41 us -> 38.9 us
    unnamed x1 -> x0, blocking collectives: 5.86 us -> none
    ppermute x0 -> x3, waiting for transfers between devices: none -> 3.15 us  [on_device(): response = response + lax.ppermute(sent, 'band', pairs)]
    unnamed x31 -> x29, local copies, waits for them, and re-layouts: 12.7 us -> 11.6 us
    dynamic_slice x1, local copies, waits for them, and re-layouts: 1.14 us -> 0.09 us  [on_device(): lax.dynamic_slice_in_dim(green_virt, band_ids[k] * band_orbs, band_orbs, 1)]
  transfers between devices with their start and end apart: 12 -> 15, of which waited for: 3 -> 5; matrix products, arithmetic and copies ran while one was open for 40% -> 40% of each run, Pallas kernels for 0% -> 0%
where the time goes in v11:
time: 97.9 us; the launch traced here: 97.2 us
  local copies, waits for them, and re-layouts  38.9 us (40%)
  starting transfers between devices  14.1 us (14%)
  waiting for transfers between devices  12.8 us (13%)
  Pallas kernels  11.9 us (12%)
  matrix products  8.43 us (9%)
  other arithmetic  7.45 us (8%)
  between operations  3.69 us (4%)
    pallas_call x1, Pallas kernels, contract(): pl.pallas_call(body, out_shape=jax.ShapeDtypeStruct((steps, ri, chunk * r...  11.9 us
    unnamed x29, local copies, waits for them, and re-layouts  11.6 us
    ppermute x4, starting transfers between devices, ring_gather(): ahead = lax.ppermute(ahead, axis, fwd)  8.7 us
    dot_general x2, local copies, waits for them, and re-layouts, on_device(): lax.dot_general(occ_raw, virt_cols, (((0, 1, 2), (1, 2, 3)), ((), ())), p...  6.61 us
    dot_general x1, matrix products, on_device(): lax.dot_general(occ_raw, virt_cols, (((0, 1, 2), (1, 2, 3)), ((), ())), p...  6.13 us
    ppermute x2, waiting for transfers between devices, ring_gather(): second = lax.ppermute(behind[rows:], axis, bwd)  4.45 us
    ppermute x4, waiting for transfers between devices, ring_gather(): ahead = lax.ppermute(ahead, axis, fwd)  4.32 us
    squeeze x2, local copies, waits for them, and re-layouts, on_device(): local_blocks = x_blocks[0]  3.93 us
  transfers between devices with their start and end apart: 15, of which 5 were waited for; matrix products, arithmetic and copies ran while one was open for 40% of the time, Pallas kernels for 0%

profile of v11, /device:TPU:0, one launch (start us, length us, event | category | flops | bytes accessed | tf_op | source)
XLA Modules:
  0.0 97.2 jit_solution(14122693680314381150)
XLA Ops:
  0.0 0.7 convert_bitcast_fusion.2
  0.7 1.8 %squeeze.33 = bf16[4,64,16,64]{3,2,1,0:T(8,128)(2,1)S(1)} reshape(bf16[1,4,64,1024]{3,2,1,0:T(8,128)(2,1)} %param.15) | data formatting | bytes 1048576 | tf_op jit(solution)/shard_map/squeeze | solution.py:112
  2.5 2.2 %copy.210 = bf16[4,64,16,64]{1,0,2,3:T(4,128)(2,1)S(1)} copy(bf16[4,64,16,64]{3,2,1,0:T(8,128)(2,1)S(1)} %squeeze.33) | data formatting | bytes 1048576 | tf_op jit(solution)/shard_map/squeeze | solution.py:112
  5.3 0.6 multiply_bitcast_fusion
  5.9 0.7 copy.211
  6.6 0.8 reshape.204
  7.5 0.9 fusion.11
  8.3 3.0 %collective-permute-start = (bf16[16,16512]{1,0:T(8,128)(2,1)}, bf16[16,16512]{1,0:T(8,128)(2,1)}, u32[]{:S(2)}, u32[]{:S(2)}) collective-permute-start(bf16[16,16512]{1,0:T(8,128)(2,1)} %fusion.11), channel_id=1, source_target_pairs={{0,8},{8,16},{16,24},{24,28},{28,20},{20,12},{12,4},{4,0},{1,9},{9... | collective-permute-start | bytes 1585160 | tf_op jit(solution)/shard_map/ppermute | solution.py:28
  11.4 0.7 reshape.205
  12.1 0.2 copy.212
  12.3 0.9 fusion.33
  13.2 2.0 %collective-permute-start.2 = (bf16[272,1024]{1,0:T(8,128)(2,1)}, bf16[272,1024]{1,0:T(8,128)(2,1)S(1)}, u32[]{:S(2)}, u32[]{:S(2)}) collective-permute-start(bf16[272,1024]{1,0:T(8,128)(2,1)} %get-tuple-element.44), channel_id=1, source_target_pairs={{0,2},{2,3},{3,1},{1,0},{4,6},{6,7},{7,5},{5,4},{8,10},{10,11},{11... | collective-permute-start | bytes 1671176 | tf_op jit(solution)/shard_map/ppermute | solution.py:28
  15.3 0.9 bitcast_dynamic-update-slice_fusion.6
  16.1 0.6 dynamic_slice.34
  16.7 0.7 compare_select_fusion.7
  17.4 0.6 gather_fusion
  18.1 0.6 scatter_custom_fusion
  18.7 0.6 dynamic_slice.36
  19.3 0.7 compare_select_fusion.4
  20.0 0.6 gather_fusion.2
  20.6 0.7 fusion.34
  24.0 0.1 constant_dynamic-slice_fusion.7
  24.1 1.5 %reshape.256 = bf16[4,128,4,2,64]{4,3,2,1,0:T(2,128)(2,1)} reshape(bf16[512,512]{1,0:T(8,128)(2,1)S(1)} %pad_maximum_fusion.1) | data formatting | bytes 1048576 | tf_op jit(solution)/shard_map/dot_general | solution.py:165
  25.7 0.1 broadcast_in_dim.43
  25.9 2.1 %collective-permute-start.6 = (bf16[16,16512]{1,0:T(8,128)(2,1)}, bf16[16,16512]{1,0:T(8,128)(2,1)S(1)}, u32[]{:S(2)}, u32[]{:S(2)}) collective-permute-start(bf16[16,16512]{1,0:T(8,128)(2,1)} %collective-permute-done), channel_id=1, source_target_pairs={{0,8},{8,16},{16,24},{24,28},{28,20},{20,12},{12,4},{4,0},{1,9},{9... | collective-permute-start | bytes 1585160 | tf_op jit(solution)/shard_map/ppermute | solution.py:28
  28.0 1.9 %bitcast_dynamic-update-slice_fusion.5 = bf16[8,16,16512]{2,1,0:T(8,128)(2,1)} fusion(bf16[8,16,16512]{2,1,0:T(8,128)(2,1)} %bitcast_dynamic-update-slice_fusion.6, bf16[16,16512]{1,0:T(8,128)(2,1)} %collective-permute-done), kind=kLoop, calls=%fused_computation.29 | loop fusion | bytes 1056768
  30.0 2.0 %collective-permute-start.4 = (bf16[136,1024]{1,0:T(8,128)(2,1)S(1)}, bf16[136,1024]{1,0:T(8,128)(2,1)S(1)}, u32[]{:S(2)}, u32[]{:S(2)}) collective-permute-start(bf16[136,1024]{1,0:T(8,128)(2,1)S(1)} %slice.84), channel_id=1, source_target_pairs={{0,2},{2,3},{3,1},{1,0},{4,6},{6,7},{7,5},{5,4},{8,10},{10,11},{11... | collective-permute-start | bytes 835592 | tf_op jit(solution)/shard_map/ppermute | solution.py:33
  32.0 1.9 %bitcast_dynamic-update-slice_fusion.4 = bf16[8,16,16512]{2,1,0:T(8,128)(2,1)} fusion(bf16[8,16,16512]{2,1,0:T(8,128)(2,1)} %bitcast_dynamic-update-slice_fusion.5, bf16[16,16512]{1,0:T(8,128)(2,1)} %collective-permute-done.1), kind=kLoop, calls=%fused_computation.28 | loop fusion | bytes 1056768
  33.9 4.4 %collective-permute-done.5 = bf16[136,1024]{1,0:T(8,128)(2,1)S(1)} collective-permute-done((bf16[136,1024]{1,0:T(8,128)(2,1)S(1)}, bf16[136,1024]{1,0:T(8,128)(2,1)S(1)}, u32[]{:S(2)}, u32[]{:S(2)}) %collective-permute-start.5) | collective-permute-done | bytes 278560 | tf_op jit(solution)/shard_map/ppermute | solution.py:34
  38.4 0.3 pad_maximum_fusion
  38.7 1.4 %copy-done.3 = bf16[4,272,1024]{2,1,0:T(8,128)(2,1)} copy-done((bf16[4,272,1024]{2,1,0:T(8,128)(2,1)}, bf16[4,272,1024]{2,1,0:T(8,128)(2,1)S(1)}, u32[]{:S(2)}) %copy-start.3) | copy-done | bytes 2228248
  40.2 0.1 add.203
  40.4 0.1 mul.68
  40.6 3.2 %gather_fusion.1 = bf16[1024,128]{1,0:T(8,128)(2,1)S(1)} fusion(bf16[512,128]{1,0:T(8,128)(2,1)S(1)} %constant_dynamic-slice_fusion.8, s32[1024]{0:T(1024)S(1)} %broadcast_clamp_fusion), kind=kCustom, calls=%fused_computation.1 | custom fusion | bytes 528384 | tf_op jit(solution)/shard_map/jit(_take)/gather | solution.py:149
  43.9 0.2 broadcast_select_fusion
  44.1 0.1 copy.213
  44.3 0.8 copy-done.5
  45.0 0.8 bitcast_dynamic-update-slice_fusion.3
  45.9 1.6 %collective-permute-start.8 = (bf16[16,16512]{1,0:T(8,128)(2,1)}, bf16[16,16512]{1,0:T(8,128)(2,1)S(1)}, u32[]{:S(2)}, u32[]{:S(2)}) collective-permute-start(bf16[16,16512]{1,0:T(8,128)(2,1)} %copy-done.5), channel_id=1, source_target_pairs={{0,8},{8,16},{16,24},{24,28},{28,20},{20,12},{12,4},{4,0},{1,9},{9... | collective-permute-start | bytes 1585160 | tf_op jit(solution)/shard_map/ppermute | solution.py:28
  47.4 0.4 collective-permute-start.9
  47.9 1.9 %bitcast_dynamic-update-slice_fusion.2 = bf16[8,16,16512]{2,1,0:T(8,128)(2,1)} fusion(bf16[8,16,16512]{2,1,0:T(8,128)(2,1)} %bitcast_dynamic-update-slice_fusion.3, bf16[16,16512]{1,0:T(8,128)(2,1)} %collective-permute-done.7), kind=kLoop, calls=%fused_computation.26 | loop fusion | bytes 1056768
  49.8 2.3 %convert_bitcast_fusion = bf16[4,2,1024,128]{2,3,1,0:T(8,128)(2,1)S(1)} fusion(bf16[4,272,1024]{2,1,0:T(8,128)(2,1)} %copy-done.3, bf16[4,2,256]{2,1,0:T(2,128)(2,1)S(1)} %mul.68, bf16[4,256,128]{1,2,0:T(8,128)(2,1)S(1)} %copy.213), kind=kOutput, calls=%fused_computation.10 | convolution fusion | flops 538181632 | bytes 4460544 | tf_op jit(solution)/shard_map/bkr,bhkl->bhrl/dot_general | solution.py:154
  52.1 2.6 %copy.214 = bf16[4,2,1024,128]{3,2,1,0:T(8,128)(2,1)} copy(bf16[4,2,1024,128]{2,3,1,0:T(8,128)(2,1)S(1)} %convert_bitcast_fusion) | data formatting | bytes 4194304 | tf_op jit(solution)/shard_map/convert_element_type | solution.py:156
  54.8 4.3 %collective-permute-done.8 = bf16[16,16512]{1,0:T(8,128)(2,1)S(1)} collective-permute-done((bf16[16,16512]{1,0:T(8,128)(2,1)}, bf16[16,16512]{1,0:T(8,128)(2,1)S(1)}, u32[]{:S(2)}, u32[]{:S(2)}) %collective-permute-start.8) | collective-permute-done | bytes 528416 | tf_op jit(solution)/shard_map/ppermute | solution.py:28
  59.1 0.9 collective-permute-done.9
  60.0 1.0 slice.88
  61.0 1.0 %collective-permute-start.11 = (bf16[8,16512]{1,0:T(8,128)(2,1)S(1)}, bf16[8,16512]{1,0:T(8,128)(2,1)S(1)}, u32[]{:S(2)}, u32[]{:S(2)}) collective-permute-start(bf16[8,16512]{1,0:T(8,128)(2,1)S(1)} %slice.88), channel_id=1, source_target_pairs={{0,4},{8,0},{16,8},{24,16},{28,24},{20,28},{12,20},{4,12},{1,5},{9... | collective-permute-start | bytes 792584 | tf_op jit(solution)/shard_map/ppermute | solution.py:34
  62.0 1.3 %collective-permute-start.10 = (bf16[8,16512]{1,0:T(8,128)(2,1)S(1)}, bf16[8,16512]{1,0:T(8,128)(2,1)S(1)}, u32[]{:S(2)}, u32[]{:S(2)}) collective-permute-start(bf16[8,16512]{1,0:T(8,128)(2,1)S(1)} %slice.87), channel_id=1, source_target_pairs={{0,8},{8,16},{16,24},{24,28},{28,20},{20,12},{12,4},{4,0},{1,9},{9... | collective-permute-start | bytes 792584 | tf_op jit(solution)/shard_map/ppermute | solution.py:33
  63.3 5.1 %copy.216 = bf16[16,128,4,2,64]{4,1,3,2,0:T(8,128)(2,1)} copy(bf16[16,128,4,2,64]{1,0,4,3,2:T(8,128)(2,1)} %bitcast.95) | data formatting | bytes 4194304 | tf_op jit(solution)/shard_map/dot_general | solution.py:165
  68.4 0.8 bitcast_dynamic-update-slice_fusion.1
  69.2 1.9 %bitcast_dynamic-update-slice_fusion = bf16[8,16,16512]{2,1,0:T(8,128)(2,1)} fusion(bf16[8,16,16512]{2,1,0:T(8,128)(2,1)} %bitcast_dynamic-update-slice_fusion.1, bf16[16,16512]{1,0:T(8,128)(2,1)} %collective-permute-done.9), kind=kLoop, calls=%fused_computation.24 | loop fusion | bytes 1056768
  71.1 6.1 %fusion = f32[16,16,8,4,128,1,1]{4,2,6,5,3,1,0:T(8,128)} fusion(bf16[4,128,4,2,64,1,1]{4,3,2,1,0,6,5:T(2,128)(2,1)S(1)} %bitcast.101, bf16[16,128,4,2,64]{4,1,3,2,0:T(8,128)(2,1)} %copy.216), kind=kOutput, calls=%fused_computation.5 | convolution fusion | flops 1073741824 | bytes 6815744 | tf_op jit(solution)/shard_map/dot_general | solution.py:165
  77.2 0.8 fusion.12
  78.0 0.7 slice.89
  78.8 0.1 copy.233
  78.9 0.7 copy.220.refs_0_
  79.5 11.9 %shard_map.109 = f32[1,16,128]{2,1,0:T(8,128)} custom-call(s32[8,4]{1,0:T(8,128)} %copy.220.refs_0_, f32[8192,128]{1,0:T(8,128)} %bitcast.97, bf16[128,16512]{1,0:T(8,128)(2,1)} %bitcast.96), custom_call_target="tpu_custom_call" | custom-call | tf_op jit(solution)/shard_map/pallas_call | solution.py:105
  91.4 0.8 reshape_reshape_transpose.3
  92.2 0.6 gather_fusion.3
  92.8 0.1 gather.26
  93.1 0.4 collective-permute-start.12
  93.5 0.8 collective-permute-done.14
  94.3 2.3 %collective-permute-done.13 = f32[4,128]{1,0:T(4,128)S(1)} collective-permute-done((f32[4,128]{1,0:T(4,128)S(1)}, f32[4,128]{1,0:T(4,128)S(1)}, u32[]{:S(2)}, u32[]{:S(2)}) %collective-permute-start.13) | collective-permute-done | bytes 2080 | tf_op jit(solution)/shard_map/ppermute | solution.py:181
  96.7 0.6 fusion.19
  (68 shorter events, 1.1 us)
Async XLA Ops:
  0.0 25.8 %copy-start = (bf16[512,512]{1,0:T(8,128)(2,1)S(1)}, bf16[512,512]{1,0:T(8,128)(2,1)}, u32[]{:S(2)}) copy-start(bf16[512,512]{1,0:T(8,128)(2,1)} %param.18) | copy-start | bytes 1572868
  8.3 17.5 %collective-permute-start = (bf16[16,16512]{1,0:T(8,128)(2,1)}, bf16[16,16512]{1,0:T(8,128)(2,1)}, u32[]{:S(2)}, u32[]{:S(2)}) collective-permute-start(bf16[16,16512]{1,0:T(8,128)(2,1)} %fusion.11), channel_id=1, source_target_pairs={{0,8},{8,16},{16,24},{24,28},{28,20},{20,12},{12,4},{4,0},{1,9},{9... | collective-permute-start | bytes 1585160 | tf_op jit(solution)/shard_map/ppermute | solution.py:28
  11.4 18.5 %collective-permute-start.1 = (bf16[16,16512]{1,0:T(8,128)(2,1)}, bf16[16,16512]{1,0:T(8,128)(2,1)}, u32[]{:S(2)}, u32[]{:S(2)}) collective-permute-start(bf16[16,16512]{1,0:T(8,128)(2,1)} %fusion.11), channel_id=1, source_target_pairs={{0,4},{8,0},{16,8},{24,16},{28,24},{20,28},{12,20},{4,12},{1,5},{9... | collective-permute-start | bytes 1585160 | tf_op jit(solution)/shard_map/ppermute | solution.py:29
  12.0 4.1 %copy-start.10 = (s32[8]{0:T(128)S(1)}, s32[8]{0:T(128)}, u32[]{:S(2)}) copy-start(s32[8]{0:T(128)} %constant.196.clone) | copy-start | bytes 100
  12.1 4.7 %copy-start.9 = (s32[8]{0:T(128)S(1)}, s32[8]{0:T(128)}, u32[]{:S(2)}) copy-start(s32[8]{0:T(128)} %constant.198.clone) | copy-start | bytes 100
  12.1 5.3 %copy-start.2 = (s32[8]{0:T(128)S(1)}, s32[8]{0:T(128)}, u32[]{:S(2)}) copy-start(s32[8]{0:T(128)} %constant.197.clone) | copy-start | bytes 100
  12.1 6.6 %copy-start.8 = (s32[4]{0:T(128)S(1)}, s32[4]{0:T(128)}, u32[]{:S(2)}) copy-start(s32[4]{0:T(128)} %constant.193.clone) | copy-start | bytes 52
  12.1 7.2 %copy-start.7 = (s32[4]{0:T(128)S(1)}, s32[4]{0:T(128)}, u32[]{:S(2)}) copy-start(s32[4]{0:T(128)} %constant.195.clone) | copy-start | bytes 52
  12.1 7.8 %copy-start.1 = (s32[4]{0:T(128)S(1)}, s32[4]{0:T(128)}, u32[]{:S(2)}) copy-start(s32[4]{0:T(128)} %constant.194.clone) | copy-start | bytes 52
  13.2 10.7 %copy-start.6 = (bf16[512,512]{1,0:T(8,128)(2,1)S(1)}, bf16[512,512]{1,0:T(8,128)(2,1)}, u32[]{:S(2)}) copy-start(bf16[512,512]{1,0:T(8,128)(2,1)} %param.19) | copy-start | bytes 1572868
  13.2 16.6 %collective-permute-start.3 = (bf16[272,1024]{1,0:T(8,128)(2,1)}, bf16[272,1024]{1,0:T(8,128)(2,1)S(1)}, u32[]{:S(2)}, u32[]{:S(2)}) collective-permute-start(bf16[272,1024]{1,0:T(8,128)(2,1)} %get-tuple-element.44), channel_id=1, source_target_pairs={{0,1},{2,0},{3,2},{1,3},{4,5},{6,4},{7,6},{5,7},{8,9},{10,8},{11,1... | collective-permute-start | bytes 1671176 | tf_op jit(solution)/shard_map/ppermute | solution.py:29
  13.2 16.7 %collective-permute-start.2 = (bf16[272,1024]{1,0:T(8,128)(2,1)}, bf16[272,1024]{1,0:T(8,128)(2,1)S(1)}, u32[]{:S(2)}, u32[]{:S(2)}) collective-permute-start(bf16[272,1024]{1,0:T(8,128)(2,1)} %get-tuple-element.44), channel_id=1, source_target_pairs={{0,2},{2,3},{3,1},{1,0},{4,6},{6,7},{7,5},{5,4},{8,10},{10,11},{11... | collective-permute-start | bytes 1671176 | tf_op jit(solution)/shard_map/ppermute | solution.py:28
  25.9 18.3 %collective-permute-start.6 = (bf16[16,16512]{1,0:T(8,128)(2,1)}, bf16[16,16512]{1,0:T(8,128)(2,1)S(1)}, u32[]{:S(2)}, u32[]{:S(2)}) collective-permute-start(bf16[16,16512]{1,0:T(8,128)(2,1)} %collective-permute-done), channel_id=1, source_target_pairs={{0,8},{8,16},{16,24},{24,28},{28,20},{20,12},{12,4},{4,0},{1,9},{9... | collective-permute-start | bytes 1585160 | tf_op jit(solution)/shard_map/ppermute | solution.py:28
  29.9 14.4 %collective-permute-start.7 = (bf16[16,16512]{1,0:T(8,128)(2,1)}, bf16[16,16512]{1,0:T(8,128)(2,1)}, u32[]{:S(2)}, u32[]{:S(2)}) collective-permute-start(bf16[16,16512]{1,0:T(8,128)(2,1)} %collective-permute-done.1), channel_id=1, source_target_pairs={{0,4},{8,0},{16,8},{24,16},{28,24},{20,28},{12,20},{4,12},{1,5},{9... | collective-permute-start | bytes 1585160 | tf_op jit(solution)/shard_map/ppermute | solution.py:29
  29.9 8.4 %collective-permute-start.5 = (bf16[136,1024]{1,0:T(8,128)(2,1)S(1)}, bf16[136,1024]{1,0:T(8,128)(2,1)S(1)}, u32[]{:S(2)}, u32[]{:S(2)}) collective-permute-start(bf16[136,1024]{1,0:T(8,128)(2,1)S(1)} %slice.85), channel_id=1, source_target_pairs={{0,1},{2,0},{3,2},{1,3},{4,5},{6,4},{7,6},{5,7},{8,9},{10,8},{11,1... | collective-permute-start | bytes 835592 | tf_op jit(solution)/shard_map/ppermute | solution.py:34
  30.0 8.4 %collective-permute-start.4 = (bf16[136,1024]{1,0:T(8,128)(2,1)S(1)}, bf16[136,1024]{1,0:T(8,128)(2,1)S(1)}, u32[]{:S(2)}, u32[]{:S(2)}) collective-permute-start(bf16[136,1024]{1,0:T(8,128)(2,1)S(1)} %slice.84), channel_id=1, source_target_pairs={{0,2},{2,3},{3,1},{1,0},{4,6},{6,7},{7,5},{5,4},{8,10},{10,11},{11... | collective-permute-start | bytes 835592 | tf_op jit(solution)/shard_map/ppermute | solution.py:33
  38.7 1.4 %copy-start.3 = (bf16[4,272,1024]{2,1,0:T(8,128)(2,1)}, bf16[4,272,1024]{2,1,0:T(8,128)(2,1)S(1)}, u32[]{:S(2)}) copy-start(bf16[4,272,1024]{2,1,0:T(8,128)(2,1)S(1)} %pad_maximum_fusion) | copy-start | bytes 6684676
  44.2 0.8 copy-start.5
  45.9 13.2 %collective-permute-start.8 = (bf16[16,16512]{1,0:T(8,128)(2,1)}, bf16[16,16512]{1,0:T(8,128)(2,1)S(1)}, u32[]{:S(2)}, u32[]{:S(2)}) collective-permute-start(bf16[16,16512]{1,0:T(8,128)(2,1)} %copy-done.5), channel_id=1, source_target_pairs={{0,8},{8,16},{16,24},{24,28},{28,20},{20,12},{12,4},{4,0},{1,9},{9... | collective-permute-start | bytes 1585160 | tf_op jit(solution)/shard_map/ppermute | solution.py:28
  47.4 12.5 %collective-permute-start.9 = (bf16[16,16512]{1,0:T(8,128)(2,1)}, bf16[16,16512]{1,0:T(8,128)(2,1)}, u32[]{:S(2)}, u32[]{:S(2)}) collective-permute-start(bf16[16,16512]{1,0:T(8,128)(2,1)} %collective-permute-done.7), channel_id=1, source_target_pairs={{0,4},{8,0},{16,8},{24,16},{28,24},{20,28},{12,20},{4,12},{1,5},{9... | collective-permute-start | bytes 1585160 | tf_op jit(solution)/shard_map/ppermute | solution.py:29
  61.0 16.3 %collective-permute-start.11 = (bf16[8,16512]{1,0:T(8,128)(2,1)S(1)}, bf16[8,16512]{1,0:T(8,128)(2,1)S(1)}, u32[]{:S(2)}, u32[]{:S(2)}) collective-permute-start(bf16[8,16512]{1,0:T(8,128)(2,1)S(1)} %slice.88), channel_id=1, source_target_pairs={{0,4},{8,0},{16,8},{24,16},{28,24},{20,28},{12,20},{4,12},{1,5},{9... | collective-permute-start | bytes 792584 | tf_op jit(solution)/shard_map/ppermute | solution.py:34
  62.0 15.3 %collective-permute-start.10 = (bf16[8,16512]{1,0:T(8,128)(2,1)S(1)}, bf16[8,16512]{1,0:T(8,128)(2,1)S(1)}, u32[]{:S(2)}, u32[]{:S(2)}) collective-permute-start(bf16[8,16512]{1,0:T(8,128)(2,1)S(1)} %slice.87), channel_id=1, source_target_pairs={{0,8},{8,16},{16,24},{24,28},{28,20},{20,12},{12,4},{4,0},{1,9},{9... | collective-permute-start | bytes 792584 | tf_op jit(solution)/shard_map/ppermute | solution.py:33
  63.3 7.8 %copy-start.4 = (bf16[4,128,4,2,64]{4,3,2,1,0:T(2,128)(2,1)S(1)}, bf16[4,128,4,2,64]{4,3,2,1,0:T(2,128)(2,1)}, u32[]{:S(2)}) copy-start(bf16[4,128,4,2,64]{4,3,2,1,0:T(2,128)(2,1)} %reshape.256) | copy-start | bytes 1572868
  92.9 1.4 %collective-permute-start.14 = (f32[4,128]{1,0:T(4,128)S(1)}, f32[4,128]{1,0:T(4,128)S(1)}, u32[]{:S(2)}, u32[]{:S(2)}) collective-permute-start(f32[4,128]{1,0:T(4,128)S(1)} %get-tuple-element.50), channel_id=1, source_target_pairs={{0,3},{1,0},{2,1},{3,2},{4,7},{5,4},{6,5},{7,6},{8,11},{9,8},{10,9... | collective-permute-start | bytes 6152 | tf_op jit(solution)/shard_map/ppermute | solution.py:181
  93.0 3.7 %collective-permute-start.13 = (f32[4,128]{1,0:T(4,128)S(1)}, f32[4,128]{1,0:T(4,128)S(1)}, u32[]{:S(2)}, u32[]{:S(2)}) collective-permute-start(f32[4,128]{1,0:T(4,128)S(1)} %get-tuple-element.51), channel_id=1, source_target_pairs={{0,2},{1,3},{2,0},{3,1},{4,6},{5,7},{6,4},{7,5},{8,10},{9,11},{10,... | collective-permute-start | bytes 6152 | tf_op jit(solution)/shard_map/ppermute | solution.py:181
  93.1 3.6 %collective-permute-start.12 = (f32[4,128]{1,0:T(4,128)S(1)}, f32[4,128]{1,0:T(4,128)S(1)}, u32[]{:S(2)}, u32[]{:S(2)}) collective-permute-start(f32[4,128]{1,0:T(4,128)S(1)} %get-tuple-element.49), channel_id=1, source_target_pairs={{0,1},{1,2},{2,3},{3,0},{4,5},{5,6},{6,7},{7,4},{8,9},{9,10},{10,1... | collective-permute-start | bytes 6152 | tf_op jit(solution)/shard_map/ppermute | solution.py:181

commit v12 on v11

--- a/solution.py
+++ b/solution.py
@@ -38,12 +38,13 @@
     return sources, got
 
 
-def contract_kernel(codes_ref, table_ref, x_ref, out_ref, hi_ref, lo_ref, dense_ref, *, slots, width, ri, chunk, blk):
+def contract_kernel(codes_ref, table_ref, x_ref, out_ref, both_ref, dense_ref, *, slots, width, ri, chunk, blk):
     step = pl.program_id(0)
 
     @pl.when(step == 0)
     def split():
         lam_count = 2 * blk
+        half = both_ref.shape[0] // (2 * ri)
         tiles = table_ref.shape[0] // (ri * lam_count)
         per_tile = 128 // blk
         for h in range(2):
@@ -56,23 +57,24 @@
                     lo = (rows - hi.astype(jnp.float32)).astype(jnp.bfloat16)
                     for u in range(per_tile):
                         code = 2 * (t * per_tile + u) + h
-                        hi_ref[code * ri:(code + 1) * ri, j * blk:(j + 1) * blk] = hi[:, u * blk:(u + 1) * blk]
-                        lo_ref[code * ri:(code + 1) * ri, j * blk:(j + 1) * blk] = lo[:, u * blk:(u + 1) * blk]
+                        both_ref[code * ri:(code + 1) * ri, j * blk:(j + 1) * blk] = hi[:, u * blk:(u + 1) * blk]
+                        low = (half + code) * ri
+                        both_ref[low:low + ri, j * blk:(j + 1) * blk] = lo[:, u * blk:(u + 1) * blk]
 
     out_ref[...] = jnp.zeros(out_ref.shape, jnp.float32)
     for s in range(slots):
         xs = x_ref[:, s * width:(s + 1) * width]
         dense = lax.dot_general(
-            hi_ref[...], xs, (((1,), (1,)), ((), ())), preferred_element_type=jnp.float32
-        )
-        dense = dense + lax.dot_general(
-            lo_ref[...], xs, (((1,), (1,)), ((), ())), preferred_element_type=jnp.float32
+            both_ref[...], xs, (((1,), (1,)), ((), ())), preferred_element_type=jnp.float32
         )
         dense_ref[...] = dense
         for c in range(chunk):
             code = codes_ref[step * chunk + c, s]
             start = pl.multiple_of(code * ri, ri)
-            out_ref[0, :, c * ri:(c + 1) * ri] += dense_ref[pl.ds(start, ri), c * ri:(c + 1) * ri]
+            low = pl.multiple_of((code + dense_ref.shape[0] // (2 * ri)) * ri, ri)
+            out_ref[0, :, c * ri:(c + 1) * ri] += (
+                dense_ref[pl.ds(start, ri), c * ri:(c + 1) * ri] + dense_ref[pl.ds(low, ri), c * ri:(c + 1) * ri]
+            )
 
 
 def contract(codes, folded, xrows, groups, slots, blk):
@@ -96,9 +98,8 @@
         ],
         out_specs=pl.BlockSpec((1, ri, chunk * ri), lambda g, c: (g, 0, 0)),
         scratch_shapes=[
-            pltpu.VMEM((codes_total * ri, width), jnp.bfloat16),
-            pltpu.VMEM((codes_total * ri, width), jnp.bfloat16),
-            pltpu.VMEM((codes_total * ri, chunk * ri), jnp.float32),
+            pltpu.VMEM((2 * codes_total * ri, width), jnp.bfloat16),
+            pltpu.VMEM((2 * codes_total * ri, chunk * ri), jnp.float32),
         ],
     )
     body = lambda *refs: contract_kernel(*refs, slots=slots, width=width, ri=ri, chunk=chunk, blk=blk)

time: 97.9 us -> 97.6 us (level)
  no operation moved by 1% of the time
where the time goes in v12:
time: 97.6 us; the launch traced here: 96.9 us
  local copies, waits for them, and re-layouts  38.9 us (40%)
  starting transfers between devices  14.1 us (14%)
  waiting for transfers between devices  12.8 us (13%)
  Pallas kernels  11.5 us (12%)
  matrix products  8.43 us (9%)
  other arithmetic  7.45 us (8%)
  between operations  3.69 us (4%)
    unnamed x29, local copies, waits for them, and re-layouts  11.6 us
    pallas_call x1, Pallas kernels, contract(): pl.pallas_call(body, out_shape=jax.ShapeDtypeStruct((steps, ri, chunk * r...  11.5 us
    ppermute x4, starting transfers between devices, ring_gather(): ahead = lax.ppermute(ahead, axis, fwd)  8.7 us
    dot_general x2, local copies, waits for them, and re-layouts, on_device(): lax.dot_general(occ_raw, virt_cols, (((0, 1, 2), (1, 2, 3)), ((), ())), p...  6.61 us
    dot_general x1, matrix products, on_device(): lax.dot_general(occ_raw, virt_cols, (((0, 1, 2), (1, 2, 3)), ((), ())), p...  6.13 us
    ppermute x2, waiting for transfers between devices, ring_gather(): second = lax.ppermute(behind[rows:], axis, bwd)  4.45 us
    ppermute x4, waiting for transfers between devices, ring_gather(): ahead = lax.ppermute(ahead, axis, fwd)  4.32 us
    squeeze x2, local copies, waits for them, and re-layouts, on_device(): local_blocks = x_blocks[0]  3.93 us
  transfers between devices with their start and end apart: 15, of which 5 were waited for; matrix products, arithmetic and copies ran while one was open for 40% of the time, Pallas kernels for 0%

profile of v12, /device:TPU:0, one launch (start us, length us, event | category | flops | bytes accessed | tf_op | source)
XLA Modules:
  0.0 96.9 jit_solution(4685274487244540803)
XLA Ops:
  0.0 0.7 convert_bitcast_fusion.2
  0.7 1.8 %squeeze.33 = bf16[4,64,16,64]{3,2,1,0:T(8,128)(2,1)S(1)} reshape(bf16[1,4,64,1024]{3,2,1,0:T(8,128)(2,1)} %param.15) | data formatting | bytes 1048576 | tf_op jit(solution)/shard_map/squeeze | solution.py:113
  2.5 2.2 %copy.210 = bf16[4,64,16,64]{1,0,2,3:T(4,128)(2,1)S(1)} copy(bf16[4,64,16,64]{3,2,1,0:T(8,128)(2,1)S(1)} %squeeze.33) | data formatting | bytes 1048576 | tf_op jit(solution)/shard_map/squeeze | solution.py:113
  5.3 0.6 multiply_bitcast_fusion
  5.9 0.7 copy.211
  6.6 0.8 reshape.204
  7.5 0.9 fusion.11
  8.3 3.0 %collective-permute-start = (bf16[16,16512]{1,0:T(8,128)(2,1)}, bf16[16,16512]{1,0:T(8,128)(2,1)}, u32[]{:S(2)}, u32[]{:S(2)}) collective-permute-start(bf16[16,16512]{1,0:T(8,128)(2,1)} %fusion.11), channel_id=1, source_target_pairs={{0,8},{8,16},{16,24},{24,28},{28,20},{20,12},{12,4},{4,0},{1,9},{9... | collective-permute-start | bytes 1585160 | tf_op jit(solution)/shard_map/ppermute | solution.py:28
  11.4 0.7 reshape.205
  12.1 0.2 copy.212
  12.3 0.9 fusion.33
  13.2 2.0 %collective-permute-start.2 = (bf16[272,1024]{1,0:T(8,128)(2,1)}, bf16[272,1024]{1,0:T(8,128)(2,1)S(1)}, u32[]{:S(2)}, u32[]{:S(2)}) collective-permute-start(bf16[272,1024]{1,0:T(8,128)(2,1)} %get-tuple-element.44), channel_id=1, source_target_pairs={{0,2},{2,3},{3,1},{1,0},{4,6},{6,7},{7,5},{5,4},{8,10},{10,11},{11... | collective-permute-start | bytes 1671176 | tf_op jit(solution)/shard_map/ppermute | solution.py:28
  15.3 0.9 bitcast_dynamic-update-slice_fusion.6
  16.1 0.6 dynamic_slice.34
  16.7 0.7 compare_select_fusion.7
  17.4 0.6 gather_fusion
  18.1 0.6 scatter_custom_fusion
  18.7 0.6 dynamic_slice.36
  19.3 0.7 compare_select_fusion.4
  20.0 0.6 gather_fusion.2
  20.6 0.7 fusion.34
  24.0 0.1 constant_dynamic-slice_fusion.7
  24.1 1.5 %reshape.256 = bf16[4,128,4,2,64]{4,3,2,1,0:T(2,128)(2,1)} reshape(bf16[512,512]{1,0:T(8,128)(2,1)S(1)} %pad_maximum_fusion.1) | data formatting | bytes 1048576 | tf_op jit(solution)/shard_map/dot_general | solution.py:166
  25.7 0.1 broadcast_in_dim.43
  25.9 2.1 %collective-permute-start.6 = (bf16[16,16512]{1,0:T(8,128)(2,1)}, bf16[16,16512]{1,0:T(8,128)(2,1)S(1)}, u32[]{:S(2)}, u32[]{:S(2)}) collective-permute-start(bf16[16,16512]{1,0:T(8,128)(2,1)} %collective-permute-done), channel_id=1, source_target_pairs={{0,8},{8,16},{16,24},{24,28},{28,20},{20,12},{12,4},{4,0},{1,9},{9... | collective-permute-start | bytes 1585160 | tf_op jit(solution)/shard_map/ppermute | solution.py:28
  28.0 1.9 %bitcast_dynamic-update-slice_fusion.5 = bf16[8,16,16512]{2,1,0:T(8,128)(2,1)} fusion(bf16[8,16,16512]{2,1,0:T(8,128)(2,1)} %bitcast_dynamic-update-slice_fusion.6, bf16[16,16512]{1,0:T(8,128)(2,1)} %collective-permute-done), kind=kLoop, calls=%fused_computation.29 | loop fusion | bytes 1056768
  30.0 2.0 %collective-permute-start.4 = (bf16[136,1024]{1,0:T(8,128)(2,1)S(1)}, bf16[136,1024]{1,0:T(8,128)(2,1)S(1)}, u32[]{:S(2)}, u32[]{:S(2)}) collective-permute-start(bf16[136,1024]{1,0:T(8,128)(2,1)S(1)} %slice.84), channel_id=1, source_target_pairs={{0,2},{2,3},{3,1},{1,0},{4,6},{6,7},{7,5},{5,4},{8,10},{10,11},{11... | collective-permute-start | bytes 835592 | tf_op jit(solution)/shard_map/ppermute | solution.py:33
  32.0 1.9 %bitcast_dynamic-update-slice_fusion.4 = bf16[8,16,16512]{2,1,0:T(8,128)(2,1)} fusion(bf16[8,16,16512]{2,1,0:T(8,128)(2,1)} %bitcast_dynamic-update-slice_fusion.5, bf16[16,16512]{1,0:T(8,128)(2,1)} %collective-permute-done.1), kind=kLoop, calls=%fused_computation.28 | loop fusion | bytes 1056768
  33.9 4.4 %collective-permute-done.5 = bf16[136,1024]{1,0:T(8,128)(2,1)S(1)} collective-permute-done((bf16[136,1024]{1,0:T(8,128)(2,1)S(1)}, bf16[136,1024]{1,0:T(8,128)(2,1)S(1)}, u32[]{:S(2)}, u32[]{:S(2)}) %collective-permute-start.5) | collective-permute-done | bytes 278560 | tf_op jit(solution)/shard_map/ppermute | solution.py:34
  38.4 0.3 pad_maximum_fusion
  38.7 1.4 %copy-done.3 = bf16[4,272,1024]{2,1,0:T(8,128)(2,1)} copy-done((bf16[4,272,1024]{2,1,0:T(8,128)(2,1)}, bf16[4,272,1024]{2,1,0:T(8,128)(2,1)S(1)}, u32[]{:S(2)}) %copy-start.3) | copy-done | bytes 2228248
  40.2 0.1 add.203
  40.4 0.1 mul.68
  40.6 3.2 %gather_fusion.1 = bf16[1024,128]{1,0:T(8,128)(2,1)S(1)} fusion(bf16[512,128]{1,0:T(8,128)(2,1)S(1)} %constant_dynamic-slice_fusion.8, s32[1024]{0:T(1024)S(1)} %broadcast_clamp_fusion), kind=kCustom, calls=%fused_computation.1 | custom fusion | bytes 528384 | tf_op jit(solution)/shard_map/jit(_take)/gather | solution.py:150
  43.9 0.2 broadcast_select_fusion
  44.1 0.1 copy.213
  44.3 0.8 copy-done.5
  45.0 0.8 bitcast_dynamic-update-slice_fusion.3
  45.9 1.6 %collective-permute-start.8 = (bf16[16,16512]{1,0:T(8,128)(2,1)}, bf16[16,16512]{1,0:T(8,128)(2,1)S(1)}, u32[]{:S(2)}, u32[]{:S(2)}) collective-permute-start(bf16[16,16512]{1,0:T(8,128)(2,1)} %copy-done.5), channel_id=1, source_target_pairs={{0,8},{8,16},{16,24},{24,28},{28,20},{20,12},{12,4},{4,0},{1,9},{9... | collective-permute-start | bytes 1585160 | tf_op jit(solution)/shard_map/ppermute | solution.py:28
  47.4 0.4 collective-permute-start.9
  47.9 1.9 %bitcast_dynamic-update-slice_fusion.2 = bf16[8,16,16512]{2,1,0:T(8,128)(2,1)} fusion(bf16[8,16,16512]{2,1,0:T(8,128)(2,1)} %bitcast_dynamic-update-slice_fusion.3, bf16[16,16512]{1,0:T(8,128)(2,1)} %collective-permute-done.7), kind=kLoop, calls=%fused_computation.26 | loop fusion | bytes 1056768
  49.8 2.3 %convert_bitcast_fusion = bf16[4,2,1024,128]{2,3,1,0:T(8,128)(2,1)S(1)} fusion(bf16[4,272,1024]{2,1,0:T(8,128)(2,1)} %copy-done.3, bf16[4,2,256]{2,1,0:T(2,128)(2,1)S(1)} %mul.68, bf16[4,256,128]{1,2,0:T(8,128)(2,1)S(1)} %copy.213), kind=kOutput, calls=%fused_computation.10 | convolution fusion | flops 538181632 | bytes 4460544 | tf_op jit(solution)/shard_map/bkr,bhkl->bhrl/dot_general | solution.py:155
  52.1 2.6 %copy.214 = bf16[4,2,1024,128]{3,2,1,0:T(8,128)(2,1)} copy(bf16[4,2,1024,128]{2,3,1,0:T(8,128)(2,1)S(1)} %convert_bitcast_fusion) | data formatting | bytes 4194304 | tf_op jit(solution)/shard_map/convert_element_type | solution.py:157
  54.8 4.3 %collective-permute-done.8 = bf16[16,16512]{1,0:T(8,128)(2,1)S(1)} collective-permute-done((bf16[16,16512]{1,0:T(8,128)(2,1)}, bf16[16,16512]{1,0:T(8,128)(2,1)S(1)}, u32[]{:S(2)}, u32[]{:S(2)}) %collective-permute-start.8) | collective-permute-done | bytes 528416 | tf_op jit(solution)/shard_map/ppermute | solution.py:28
  59.1 0.9 collective-permute-done.9
  60.0 1.0 slice.88
  61.0 1.0 %collective-permute-start.11 = (bf16[8,16512]{1,0:T(8,128)(2,1)S(1)}, bf16[8,16512]{1,0:T(8,128)(2,1)S(1)}, u32[]{:S(2)}, u32[]{:S(2)}) collective-permute-start(bf16[8,16512]{1,0:T(8,128)(2,1)S(1)} %slice.88), channel_id=1, source_target_pairs={{0,4},{8,0},{16,8},{24,16},{28,24},{20,28},{12,20},{4,12},{1,5},{9... | collective-permute-start | bytes 792584 | tf_op jit(solution)/shard_map/ppermute | solution.py:34
  62.0 1.3 %collective-permute-start.10 = (bf16[8,16512]{1,0:T(8,128)(2,1)S(1)}, bf16[8,16512]{1,0:T(8,128)(2,1)S(1)}, u32[]{:S(2)}, u32[]{:S(2)}) collective-permute-start(bf16[8,16512]{1,0:T(8,128)(2,1)S(1)} %slice.87), channel_id=1, source_target_pairs={{0,8},{8,16},{16,24},{24,28},{28,20},{20,12},{12,4},{4,0},{1,9},{9... | collective-permute-start | bytes 792584 | tf_op jit(solution)/shard_map/ppermute | solution.py:33
  63.3 5.1 %copy.216 = bf16[16,128,4,2,64]{4,1,3,2,0:T(8,128)(2,1)} copy(bf16[16,128,4,2,64]{1,0,4,3,2:T(8,128)(2,1)} %bitcast.95) | data formatting | bytes 4194304 | tf_op jit(solution)/shard_map/dot_general | solution.py:166
  68.4 0.8 bitcast_dynamic-update-slice_fusion.1
  69.2 1.9 %bitcast_dynamic-update-slice_fusion = bf16[8,16,16512]{2,1,0:T(8,128)(2,1)} fusion(bf16[8,16,16512]{2,1,0:T(8,128)(2,1)} %bitcast_dynamic-update-slice_fusion.1, bf16[16,16512]{1,0:T(8,128)(2,1)} %collective-permute-done.9), kind=kLoop, calls=%fused_computation.24 | loop fusion | bytes 1056768
  71.1 6.1 %fusion = f32[16,16,8,4,128,1,1]{4,2,6,5,3,1,0:T(8,128)} fusion(bf16[4,128,4,2,64,1,1]{4,3,2,1,0,6,5:T(2,128)(2,1)S(1)} %bitcast.101, bf16[16,128,4,2,64]{4,1,3,2,0:T(8,128)(2,1)} %copy.216), kind=kOutput, calls=%fused_computation.5 | convolution fusion | flops 1073741824 | bytes 6815744 | tf_op jit(solution)/shard_map/dot_general | solution.py:166
  77.2 0.8 fusion.12
  78.0 0.7 slice.89
  78.8 0.1 copy.233
  78.9 0.7 copy.220.refs_0_
  79.5 11.5 %shard_map.109 = f32[1,16,128]{2,1,0:T(8,128)} custom-call(s32[8,4]{1,0:T(8,128)} %copy.220.refs_0_, f32[8192,128]{1,0:T(8,128)} %bitcast.97, bf16[128,16512]{1,0:T(8,128)(2,1)} %bitcast.96), custom_call_target="tpu_custom_call" | custom-call | tf_op jit(solution)/shard_map/pallas_call | solution.py:106
  91.1 0.8 reshape_reshape_transpose.3
  91.9 0.6 gather_fusion.3
  92.5 0.1 gather.26
  92.7 0.4 collective-permute-start.12
  93.1 0.8 collective-permute-done.14
  93.9 2.3 %collective-permute-done.13 = f32[4,128]{1,0:T(4,128)S(1)} collective-permute-done((f32[4,128]{1,0:T(4,128)S(1)}, f32[4,128]{1,0:T(4,128)S(1)}, u32[]{:S(2)}, u32[]{:S(2)}) %collective-permute-start.13) | collective-permute-done | bytes 2080 | tf_op jit(solution)/shard_map/ppermute | solution.py:182
  96.3 0.6 fusion.19
  (68 shorter events, 1.1 us)
Async XLA Ops:
  0.0 25.8 %copy-start = (bf16[512,512]{1,0:T(8,128)(2,1)S(1)}, bf16[512,512]{1,0:T(8,128)(2,1)}, u32[]{:S(2)}) copy-start(bf16[512,512]{1,0:T(8,128)(2,1)} %param.18) | copy-start | bytes 1572868
  8.3 17.5 %collective-permute-start = (bf16[16,16512]{1,0:T(8,128)(2,1)}, bf16[16,16512]{1,0:T(8,128)(2,1)}, u32[]{:S(2)}, u32[]{:S(2)}) collective-permute-start(bf16[16,16512]{1,0:T(8,128)(2,1)} %fusion.11), channel_id=1, source_target_pairs={{0,8},{8,16},{16,24},{24,28},{28,20},{20,12},{12,4},{4,0},{1,9},{9... | collective-permute-start | bytes 1585160 | tf_op jit(solution)/shard_map/ppermute | solution.py:28
  11.4 18.5 %collective-permute-start.1 = (bf16[16,16512]{1,0:T(8,128)(2,1)}, bf16[16,16512]{1,0:T(8,128)(2,1)}, u32[]{:S(2)}, u32[]{:S(2)}) collective-permute-start(bf16[16,16512]{1,0:T(8,128)(2,1)} %fusion.11), channel_id=1, source_target_pairs={{0,4},{8,0},{16,8},{24,16},{28,24},{20,28},{12,20},{4,12},{1,5},{9... | collective-permute-start | bytes 1585160 | tf_op jit(solution)/shard_map/ppermute | solution.py:29
  12.0 4.1 %copy-start.10 = (s32[8]{0:T(128)S(1)}, s32[8]{0:T(128)}, u32[]{:S(2)}) copy-start(s32[8]{0:T(128)} %constant.196.clone) | copy-start | bytes 100
  12.1 4.7 %copy-start.9 = (s32[8]{0:T(128)S(1)}, s32[8]{0:T(128)}, u32[]{:S(2)}) copy-start(s32[8]{0:T(128)} %constant.198.clone) | copy-start | bytes 100
  12.1 5.3 %copy-start.2 = (s32[8]{0:T(128)S(1)}, s32[8]{0:T(128)}, u32[]{:S(2)}) copy-start(s32[8]{0:T(128)} %constant.197.clone) | copy-start | bytes 100
  12.1 6.6 %copy-start.8 = (s32[4]{0:T(128)S(1)}, s32[4]{0:T(128)}, u32[]{:S(2)}) copy-start(s32[4]{0:T(128)} %constant.193.clone) | copy-start | bytes 52
  12.1 7.2 %copy-start.7 = (s32[4]{0:T(128)S(1)}, s32[4]{0:T(128)}, u32[]{:S(2)}) copy-start(s32[4]{0:T(128)} %constant.195.clone) | copy-start | bytes 52
  12.1 7.8 %copy-start.1 = (s32[4]{0:T(128)S(1)}, s32[4]{0:T(128)}, u32[]{:S(2)}) copy-start(s32[4]{0:T(128)} %constant.194.clone) | copy-start | bytes 52
  13.2 10.7 %copy-start.6 = (bf16[512,512]{1,0:T(8,128)(2,1)S(1)}, bf16[512,512]{1,0:T(8,128)(2,1)}, u32[]{:S(2)}) copy-start(bf16[512,512]{1,0:T(8,128)(2,1)} %param.19) | copy-start | bytes 1572868
  13.2 16.6 %collective-permute-start.3 = (bf16[272,1024]{1,0:T(8,128)(2,1)}, bf16[272,1024]{1,0:T(8,128)(2,1)S(1)}, u32[]{:S(2)}, u32[]{:S(2)}) collective-permute-start(bf16[272,1024]{1,0:T(8,128)(2,1)} %get-tuple-element.44), channel_id=1, source_target_pairs={{0,1},{2,0},{3,2},{1,3},{4,5},{6,4},{7,6},{5,7},{8,9},{10,8},{11,1... | collective-permute-start | bytes 1671176 | tf_op jit(solution)/shard_map/ppermute | solution.py:29
  13.2 16.7 %collective-permute-start.2 = (bf16[272,1024]{1,0:T(8,128)(2,1)}, bf16[272,1024]{1,0:T(8,128)(2,1)S(1)}, u32[]{:S(2)}, u32[]{:S(2)}) collective-permute-start(bf16[272,1024]{1,0:T(8,128)(2,1)} %get-tuple-element.44), channel_id=1, source_target_pairs={{0,2},{2,3},{3,1},{1,0},{4,6},{6,7},{7,5},{5,4},{8,10},{10,11},{11... | collective-permute-start | bytes 1671176 | tf_op jit(solution)/shard_map/ppermute | solution.py:28
  25.9 18.3 %collective-permute-start.6 = (bf16[16,16512]{1,0:T(8,128)(2,1)}, bf16[16,16512]{1,0:T(8,128)(2,1)S(1)}, u32[]{:S(2)}, u32[]{:S(2)}) collective-permute-start(bf16[16,16512]{1,0:T(8,128)(2,1)} %collective-permute-done), channel_id=1, source_target_pairs={{0,8},{8,16},{16,24},{24,28},{28,20},{20,12},{12,4},{4,0},{1,9},{9... | collective-permute-start | bytes 1585160 | tf_op jit(solution)/shard_map/ppermute | solution.py:28
  29.9 14.4 %collective-permute-start.7 = (bf16[16,16512]{1,0:T(8,128)(2,1)}, bf16[16,16512]{1,0:T(8,128)(2,1)}, u32[]{:S(2)}, u32[]{:S(2)}) collective-permute-start(bf16[16,16512]{1,0:T(8,128)(2,1)} %collective-permute-done.1), channel_id=1, source_target_pairs={{0,4},{8,0},{16,8},{24,16},{28,24},{20,28},{12,20},{4,12},{1,5},{9... | collective-permute-start | bytes 1585160 | tf_op jit(solution)/shard_map/ppermute | solution.py:29
  29.9 8.4 %collective-permute-start.5 = (bf16[136,1024]{1,0:T(8,128)(2,1)S(1)}, bf16[136,1024]{1,0:T(8,128)(2,1)S(1)}, u32[]{:S(2)}, u32[]{:S(2)}) collective-permute-start(bf16[136,1024]{1,0:T(8,128)(2,1)S(1)} %slice.85), channel_id=1, source_target_pairs={{0,1},{2,0},{3,2},{1,3},{4,5},{6,4},{7,6},{5,7},{8,9},{10,8},{11,1... | collective-permute-start | bytes 835592 | tf_op jit(solution)/shard_map/ppermute | solution.py:34
  30.0 8.4 %collective-permute-start.4 = (bf16[136,1024]{1,0:T(8,128)(2,1)S(1)}, bf16[136,1024]{1,0:T(8,128)(2,1)S(1)}, u32[]{:S(2)}, u32[]{:S(2)}) collective-permute-start(bf16[136,1024]{1,0:T(8,128)(2,1)S(1)} %slice.84), channel_id=1, source_target_pairs={{0,2},{2,3},{3,1},{1,0},{4,6},{6,7},{7,5},{5,4},{8,10},{10,11},{11... | collective-permute-start | bytes 835592 | tf_op jit(solution)/shard_map/ppermute | solution.py:33
  38.7 1.4 %copy-start.3 = (bf16[4,272,1024]{2,1,0:T(8,128)(2,1)}, bf16[4,272,1024]{2,1,0:T(8,128)(2,1)S(1)}, u32[]{:S(2)}) copy-start(bf16[4,272,1024]{2,1,0:T(8,128)(2,1)S(1)} %pad_maximum_fusion) | copy-start | bytes 6684676
  44.2 0.8 copy-start.5
  45.9 13.2 %collective-permute-start.8 = (bf16[16,16512]{1,0:T(8,128)(2,1)}, bf16[16,16512]{1,0:T(8,128)(2,1)S(1)}, u32[]{:S(2)}, u32[]{:S(2)}) collective-permute-start(bf16[16,16512]{1,0:T(8,128)(2,1)} %copy-done.5), channel_id=1, source_target_pairs={{0,8},{8,16},{16,24},{24,28},{28,20},{20,12},{12,4},{4,0},{1,9},{9... | collective-permute-start | bytes 1585160 | tf_op jit(solution)/shard_map/ppermute | solution.py:28
  47.4 12.5 %collective-permute-start.9 = (bf16[16,16512]{1,0:T(8,128)(2,1)}, bf16[16,16512]{1,0:T(8,128)(2,1)}, u32[]{:S(2)}, u32[]{:S(2)}) collective-permute-start(bf16[16,16512]{1,0:T(8,128)(2,1)} %collective-permute-done.7), channel_id=1, source_target_pairs={{0,4},{8,0},{16,8},{24,16},{28,24},{20,28},{12,20},{4,12},{1,5},{9... | collective-permute-start | bytes 1585160 | tf_op jit(solution)/shard_map/ppermute | solution.py:29
  61.0 16.3 %collective-permute-start.11 = (bf16[8,16512]{1,0:T(8,128)(2,1)S(1)}, bf16[8,16512]{1,0:T(8,128)(2,1)S(1)}, u32[]{:S(2)}, u32[]{:S(2)}) collective-permute-start(bf16[8,16512]{1,0:T(8,128)(2,1)S(1)} %slice.88), channel_id=1, source_target_pairs={{0,4},{8,0},{16,8},{24,16},{28,24},{20,28},{12,20},{4,12},{1,5},{9... | collective-permute-start | bytes 792584 | tf_op jit(solution)/shard_map/ppermute | solution.py:34
  62.0 15.3 %collective-permute-start.10 = (bf16[8,16512]{1,0:T(8,128)(2,1)S(1)}, bf16[8,16512]{1,0:T(8,128)(2,1)S(1)}, u32[]{:S(2)}, u32[]{:S(2)}) collective-permute-start(bf16[8,16512]{1,0:T(8,128)(2,1)S(1)} %slice.87), channel_id=1, source_target_pairs={{0,8},{8,16},{16,24},{24,28},{28,20},{20,12},{12,4},{4,0},{1,9},{9... | collective-permute-start | bytes 792584 | tf_op jit(solution)/shard_map/ppermute | solution.py:33
  63.3 7.8 %copy-start.4 = (bf16[4,128,4,2,64]{4,3,2,1,0:T(2,128)(2,1)S(1)}, bf16[4,128,4,2,64]{4,3,2,1,0:T(2,128)(2,1)}, u32[]{:S(2)}) copy-start(bf16[4,128,4,2,64]{4,3,2,1,0:T(2,128)(2,1)} %reshape.256) | copy-start | bytes 1572868
  92.6 1.4 %collective-permute-start.14 = (f32[4,128]{1,0:T(4,128)S(1)}, f32[4,128]{1,0:T(4,128)S(1)}, u32[]{:S(2)}, u32[]{:S(2)}) collective-permute-start(f32[4,128]{1,0:T(4,128)S(1)} %get-tuple-element.50), channel_id=1, source_target_pairs={{0,3},{1,0},{2,1},{3,2},{4,7},{5,4},{6,5},{7,6},{8,11},{9,8},{10,9... | collective-permute-start | bytes 6152 | tf_op jit(solution)/shard_map/ppermute | solution.py:182
  92.6 3.7 %collective-permute-start.13 = (f32[4,128]{1,0:T(4,128)S(1)}, f32[4,128]{1,0:T(4,128)S(1)}, u32[]{:S(2)}, u32[]{:S(2)}) collective-permute-start(f32[4,128]{1,0:T(4,128)S(1)} %get-tuple-element.51), channel_id=1, source_target_pairs={{0,2},{1,3},{2,0},{3,1},{4,6},{5,7},{6,4},{7,5},{8,10},{9,11},{10,... | collective-permute-start | bytes 6152 | tf_op jit(solution)/shard_map/ppermute | solution.py:182
  92.7 3.6 %collective-permute-start.12 = (f32[4,128]{1,0:T(4,128)S(1)}, f32[4,128]{1,0:T(4,128)S(1)}, u32[]{:S(2)}, u32[]{:S(2)}) collective-permute-start(f32[4,128]{1,0:T(4,128)S(1)} %get-tuple-element.49), channel_id=1, source_target_pairs={{0,1},{1,2},{2,3},{3,0},{4,5},{5,6},{6,7},{7,4},{8,9},{9,10},{10,1... | collective-permute-start | bytes 6152 | tf_op jit(solution)/shard_map/ppermute | solution.py:182

commit v13 on v12

--- a/solution.py
+++ b/solution.py
@@ -146,9 +146,12 @@
     grp_got[3:5] = early
 
     occ_cols = lax.dynamic_slice_in_dim(green_occ, band * band_orbs, band_orbs, 1)
-    row_index = (codes_g // 2)[..., None] * block_size + jnp.arange(block_size, dtype=jnp.int32)
-    occ_rows = jnp.take(occ_cols, row_index.reshape(-1), axis=0)
-    occ_rows = occ_rows.reshape(band_count, slot_count, block_size, band_orbs)
+    occ_rows = []
+    for buf in band_got:
+        codes_k = buf[kdim, :slot_count].astype(jnp.float32).astype(jnp.int32)
+        row_index = (codes_k // 2)[:, None] * block_size + jnp.arange(block_size, dtype=jnp.int32)
+        occ_rows.append(jnp.take(occ_cols, row_index.reshape(-1), axis=0))
+    occ_rows = jnp.stack(occ_rows).reshape(band_count, slot_count, block_size, band_orbs)
     halves = (codes_g % 2)[:, None, :] == jnp.arange(2, dtype=jnp.int32)[None, :, None]
     occ_sel = occ_rows[:, None] * halves.astype(occ_rows.dtype)[..., None, None]
     occ_sel = occ_sel.reshape(band_count, 2, kdim, band_orbs)

time: 97.6 us -> 101 us (1.035)
  local copies, waits for them, and re-layouts: 38.9 us -> 40.5 us
  other arithmetic: 7.45 us -> 8.88 us
    gather x1 -> x4, local copies, waits for them, and re-layouts: 3.21 us -> 3.42 us  [on_device(): occ_rows.append(jnp.take(occ_cols, row_index.reshape(-1), axis=0))]
    unnamed x29 -> x31, local copies, waits for them, and re-layouts: 11.6 us -> 11.6 us
  transfers between devices with their start and end apart: 15 -> 15, of which waited for: 5 -> 5; matrix products, arithmetic and copies ran while one was open for 40% -> 42% of each run, Pallas kernels for 0% -> 0%
where the time goes in v13:
time: 101 us
  local copies, waits for them, and re-layouts  40.5 us (40%)
  starting transfers between devices  14 us (14%)
  waiting for transfers between devices  13.5 us (13%)
  Pallas kernels  11.5 us (11%)
  other arithmetic  8.88 us (9%)
  matrix products  8.44 us (8%)
  between operations  3.71 us (4%)
    unnamed x31, local copies, waits for them, and re-layouts  11.6 us
    pallas_call x1, Pallas kernels, contract(): pl.pallas_call(body, out_shape=jax.ShapeDtypeStruct((steps, ri, chunk * r...  11.5 us
    ppermute x4, starting transfers between devices, ring_gather(): ahead = lax.ppermute(ahead, axis, fwd)  8.7 us
    dot_general x2, local copies, waits for them, and re-layouts, on_device(): lax.dot_general(occ_raw, virt_cols, (((0, 1, 2), (1, 2, 3)), ((), ())), p...  6.61 us
    dot_general x1, matrix products, on_device(): lax.dot_general(occ_raw, virt_cols, (((0, 1, 2), (1, 2, 3)), ((), ())), p...  6.14 us
    ppermute x4, waiting for transfers between devices, ring_gather(): ahead = lax.ppermute(ahead, axis, fwd)  4.98 us
    ppermute x2, waiting for transfers between devices, ring_gather(): second = lax.ppermute(behind[rows:], axis, bwd)  4.45 us
    squeeze x2, local copies, waits for them, and re-layouts, on_device(): local_blocks = x_blocks[0]  3.93 us
  transfers between devices with their start and end apart: 15, of which 5 were waited for; matrix products, arithmetic and copies ran while one was open for 42% of the time, Pallas kernels for 0%

profile of v13, /device:TPU:0, one launch (start us, length us, event | category | flops | bytes accessed | tf_op | source)
XLA Modules:
  0.0 100.6 jit_solution(11863964001364776379)
XLA Ops:
  0.0 0.7 convert_bitcast_fusion.2
  0.7 1.8 %squeeze.37 = bf16[4,64,16,64]{3,2,1,0:T(8,128)(2,1)S(1)} reshape(bf16[1,4,64,1024]{3,2,1,0:T(8,128)(2,1)} %param.17) | data formatting | bytes 1048576 | tf_op jit(solution)/shard_map/squeeze | solution.py:113
  2.5 2.2 %copy.210 = bf16[4,64,16,64]{1,0,2,3:T(4,128)(2,1)S(1)} copy(bf16[4,64,16,64]{3,2,1,0:T(8,128)(2,1)S(1)} %squeeze.37) | data formatting | bytes 1048576 | tf_op jit(solution)/shard_map/squeeze | solution.py:113
  5.3 0.6 multiply_bitcast_fusion
  5.9 0.7 copy.211
  6.6 0.8 reshape.266
  7.5 0.8 fusion.11
  8.3 3.0 %collective-permute-start = (bf16[16,16512]{1,0:T(8,128)(2,1)}, bf16[16,16512]{1,0:T(8,128)(2,1)}, u32[]{:S(2)}, u32[]{:S(2)}) collective-permute-start(bf16[16,16512]{1,0:T(8,128)(2,1)} %fusion.11), channel_id=1, source_target_pairs={{0,8},{8,16},{16,24},{24,28},{28,20},{20,12},{12,4},{4,0},{1,9},{9... | collective-permute-start | bytes 1585160 | tf_op jit(solution)/shard_map/ppermute | solution.py:28
  11.3 0.7 reshape.267
  12.1 0.2 copy.212
  12.3 0.9 fusion.40
  13.2 2.0 %collective-permute-start.2 = (bf16[272,1024]{1,0:T(8,128)(2,1)}, bf16[272,1024]{1,0:T(8,128)(2,1)S(1)}, u32[]{:S(2)}, u32[]{:S(2)}) collective-permute-start(bf16[272,1024]{1,0:T(8,128)(2,1)} %get-tuple-element.45), channel_id=1, source_target_pairs={{0,2},{2,3},{3,1},{1,0},{4,6},{6,7},{7,5},{5,4},{8,10},{10,11},{11... | collective-permute-start | bytes 1671176 | tf_op jit(solution)/shard_map/ppermute | solution.py:28
  15.2 0.8 bitcast_dynamic-update-slice_fusion.6
  16.1 0.6 dynamic_slice.34
  16.7 0.7 compare_select_fusion.9
  17.4 0.6 gather_fusion
  18.0 0.6 scatter_custom_fusion
  18.7 0.6 dynamic_slice.36
  19.3 0.7 compare_select_fusion.6
  19.9 0.6 gather_fusion.1
  20.6 0.7 fusion.41
  24.2 1.5 %reshape.354 = bf16[4,128,4,2,64]{4,3,2,1,0:T(2,128)(2,1)} reshape(bf16[512,512]{1,0:T(8,128)(2,1)S(1)} %pad_maximum_fusion.1) | data formatting | bytes 1048576 | tf_op jit(solution)/shard_map/dot_general | solution.py:169
  25.9 2.1 %collective-permute-start.6 = (bf16[16,16512]{1,0:T(8,128)(2,1)}, bf16[16,16512]{1,0:T(8,128)(2,1)S(1)}, u32[]{:S(2)}, u32[]{:S(2)}) collective-permute-start(bf16[16,16512]{1,0:T(8,128)(2,1)} %collective-permute-done), channel_id=1, source_target_pairs={{0,8},{8,16},{16,24},{24,28},{28,20},{20,12},{12,4},{4,0},{1,9},{9... | collective-permute-start | bytes 1585160 | tf_op jit(solution)/shard_map/ppermute | solution.py:28
  28.0 1.9 %bitcast_dynamic-update-slice_fusion.5 = bf16[8,16,16512]{2,1,0:T(8,128)(2,1)} fusion(bf16[8,16,16512]{2,1,0:T(8,128)(2,1)} %bitcast_dynamic-update-slice_fusion.6, bf16[16,16512]{1,0:T(8,128)(2,1)} %collective-permute-done), kind=kLoop, calls=%fused_computation.32 | loop fusion | bytes 1056768
  29.9 1.9 %bitcast_dynamic-update-slice_fusion.4 = bf16[8,16,16512]{2,1,0:T(8,128)(2,1)} fusion(bf16[8,16,16512]{2,1,0:T(8,128)(2,1)} %bitcast_dynamic-update-slice_fusion.5, bf16[16,16512]{1,0:T(8,128)(2,1)} %collective-permute-done.1), kind=kLoop, calls=%fused_computation.31 | loop fusion | bytes 1056768
  32.0 0.8 slice.104
  32.8 0.7 slice.103
  33.5 2.0 %collective-permute-start.4 = (bf16[136,1024]{1,0:T(8,128)(2,1)}, bf16[136,1024]{1,0:T(8,128)(2,1)}, u32[]{:S(2)}, u32[]{:S(2)}) collective-permute-start(bf16[136,1024]{1,0:T(8,128)(2,1)} %slice.103), channel_id=1, source_target_pairs={{0,2},{2,3},{3,1},{1,0},{4,6},{6,7},{7,5},{5,4},{8,10},{10,11},{11... | collective-permute-start | bytes 835592 | tf_op jit(solution)/shard_map/ppermute | solution.py:33
  35.6 0.9 gather_fusion.4
  36.7 0.9 gather_fusion.3
  37.7 4.4 %collective-permute-done.5 = bf16[136,1024]{1,0:T(8,128)(2,1)S(1)} collective-permute-done((bf16[136,1024]{1,0:T(8,128)(2,1)}, bf16[136,1024]{1,0:T(8,128)(2,1)S(1)}, u32[]{:S(2)}, u32[]{:S(2)}) %collective-permute-start.5) | collective-permute-done | bytes 278560 | tf_op jit(solution)/shard_map/ppermute | solution.py:34
  42.3 1.0 maximum_bitcast_fusion
  43.3 0.3 pad_maximum_fusion
  43.6 1.4 %copy-done.3 = bf16[4,272,1024]{2,1,0:T(8,128)(2,1)} copy-done((bf16[4,272,1024]{2,1,0:T(8,128)(2,1)}, bf16[4,272,1024]{2,1,0:T(8,128)(2,1)S(1)}, u32[]{:S(2)}) %copy-start.3) | copy-done | bytes 2228248
  45.2 0.9 gather_fusion.6
  46.1 0.9 gather_fusion.5
  47.0 0.1 select_bitcast_fusion.1
  47.2 0.1 copy.213
  47.4 0.8 copy-done.5
  48.2 0.8 bitcast_dynamic-update-slice_fusion.3
  49.0 1.6 %collective-permute-start.8 = (bf16[16,16512]{1,0:T(8,128)(2,1)}, bf16[16,16512]{1,0:T(8,128)(2,1)S(1)}, u32[]{:S(2)}, u32[]{:S(2)}) collective-permute-start(bf16[16,16512]{1,0:T(8,128)(2,1)} %copy-done.5), channel_id=1, source_target_pairs={{0,8},{8,16},{16,24},{24,28},{28,20},{20,12},{12,4},{4,0},{1,9},{9... | collective-permute-start | bytes 1585160 | tf_op jit(solution)/shard_map/ppermute | solution.py:28
  50.6 0.4 collective-permute-start.9
  51.0 1.9 %bitcast_dynamic-update-slice_fusion.2 = bf16[8,16,16512]{2,1,0:T(8,128)(2,1)} fusion(bf16[8,16,16512]{2,1,0:T(8,128)(2,1)} %bitcast_dynamic-update-slice_fusion.3, bf16[16,16512]{1,0:T(8,128)(2,1)} %collective-permute-done.7), kind=kLoop, calls=%fused_computation.29 | loop fusion | bytes 1056768
  52.9 2.3 %convert_bitcast_fusion = bf16[4,2,1024,128]{2,3,1,0:T(8,128)(2,1)S(1)} fusion(bf16[4,272,1024]{2,1,0:T(8,128)(2,1)} %copy-done.3, bf16[4,2,256]{2,1,0:T(2,128)(2,1)S(1)} %mul.95, bf16[4,256,128]{1,2,0:T(8,128)(2,1)S(1)} %copy.213), kind=kOutput, calls=%fused_computation.13 | convolution fusion | flops 538181632 | bytes 4460544 | tf_op jit(solution)/shard_map/bkr,bhkl->bhrl/dot_general | solution.py:158
  55.2 2.6 %copy.214 = bf16[4,2,1024,128]{3,2,1,0:T(8,128)(2,1)} copy(bf16[4,2,1024,128]{2,3,1,0:T(8,128)(2,1)S(1)} %convert_bitcast_fusion) | data formatting | bytes 4194304 | tf_op jit(solution)/shard_map/convert_element_type | solution.py:160
  57.8 5.0 %collective-permute-done.8 = bf16[16,16512]{1,0:T(8,128)(2,1)S(1)} collective-permute-done((bf16[16,16512]{1,0:T(8,128)(2,1)}, bf16[16,16512]{1,0:T(8,128)(2,1)S(1)}, u32[]{:S(2)}, u32[]{:S(2)}) %collective-permute-start.8) | collective-permute-done | bytes 528416 | tf_op jit(solution)/shard_map/ppermute | solution.py:28
  62.8 0.9 collective-permute-done.9
  63.7 1.0 slice.110
  64.7 1.0 %collective-permute-start.11 = (bf16[8,16512]{1,0:T(8,128)(2,1)S(1)}, bf16[8,16512]{1,0:T(8,128)(2,1)S(1)}, u32[]{:S(2)}, u32[]{:S(2)}) collective-permute-start(bf16[8,16512]{1,0:T(8,128)(2,1)S(1)} %slice.110), channel_id=1, source_target_pairs={{0,4},{8,0},{16,8},{24,16},{28,24},{20,28},{12,20},{4,12},{1,5},{9... | collective-permute-start | bytes 792584 | tf_op jit(solution)/shard_map/ppermute | solution.py:34
  65.7 1.3 %collective-permute-start.10 = (bf16[8,16512]{1,0:T(8,128)(2,1)S(1)}, bf16[8,16512]{1,0:T(8,128)(2,1)S(1)}, u32[]{:S(2)}, u32[]{:S(2)}) collective-permute-start(bf16[8,16512]{1,0:T(8,128)(2,1)S(1)} %slice.109), channel_id=1, source_target_pairs={{0,8},{8,16},{16,24},{24,28},{28,20},{20,12},{12,4},{4,0},{1,9},{9... | collective-permute-start | bytes 792584 | tf_op jit(solution)/shard_map/ppermute | solution.py:33
  67.0 5.1 %copy.216 = bf16[16,128,4,2,64]{4,1,3,2,0:T(8,128)(2,1)} copy(bf16[16,128,4,2,64]{1,0,4,3,2:T(8,128)(2,1)} %bitcast.128) | data formatting | bytes 4194304 | tf_op jit(solution)/shard_map/dot_general | solution.py:169
  72.1 0.8 bitcast_dynamic-update-slice_fusion.1
  72.9 1.9 %bitcast_dynamic-update-slice_fusion = bf16[8,16,16512]{2,1,0:T(8,128)(2,1)} fusion(bf16[8,16,16512]{2,1,0:T(8,128)(2,1)} %bitcast_dynamic-update-slice_fusion.1, bf16[16,16512]{1,0:T(8,128)(2,1)} %collective-permute-done.9), kind=kLoop, calls=%fused_computation.27 | loop fusion | bytes 1056768
  74.8 6.1 %fusion = f32[16,16,8,4,128,1,1]{4,2,6,5,3,1,0:T(8,128)} fusion(bf16[4,128,4,2,64,1,1]{4,3,2,1,0,6,5:T(2,128)(2,1)S(1)} %bitcast.133, bf16[16,128,4,2,64]{4,1,3,2,0:T(8,128)(2,1)} %copy.216), kind=kOutput, calls=%fused_computation.8 | convolution fusion | flops 1073741824 | bytes 6815744 | tf_op jit(solution)/shard_map/dot_general | solution.py:169
  80.9 0.8 fusion.12
  81.8 0.7 slice.111
  82.6 0.7 copy.220.refs_0_
  83.3 11.5 %shard_map.109 = f32[1,16,128]{2,1,0:T(8,128)} custom-call(s32[8,4]{1,0:T(8,128)} %copy.220.refs_0_, f32[8192,128]{1,0:T(8,128)} %bitcast.130, bf16[128,16512]{1,0:T(8,128)(2,1)} %bitcast.129), custom_call_target="tpu_custom_call" | custom-call | tf_op jit(solution)/shard_map/pallas_call | solution.py:106
  94.8 0.8 reshape_reshape_transpose.3
  95.6 0.6 gather_fusion.2
  96.5 0.4 collective-permute-start.12
  96.9 0.8 collective-permute-done.14
  97.7 2.3 %collective-permute-done.13 = f32[4,128]{1,0:T(4,128)S(1)} collective-permute-done((f32[4,128]{1,0:T(4,128)S(1)}, f32[4,128]{1,0:T(4,128)S(1)}, u32[]{:S(2)}, u32[]{:S(2)}) %collective-permute-start.13) | collective-permute-done | bytes 2080 | tf_op jit(solution)/shard_map/ppermute | solution.py:185
  100.0 0.6 fusion.19
  (86 shorter events, 2.1 us)
Async XLA Ops:
  0.0 25.9 %copy-start = (bf16[512,512]{1,0:T(8,128)(2,1)S(1)}, bf16[512,512]{1,0:T(8,128)(2,1)}, u32[]{:S(2)}) copy-start(bf16[512,512]{1,0:T(8,128)(2,1)} %param.20) | copy-start | bytes 1572868
  8.3 17.6 %collective-permute-start = (bf16[16,16512]{1,0:T(8,128)(2,1)}, bf16[16,16512]{1,0:T(8,128)(2,1)}, u32[]{:S(2)}, u32[]{:S(2)}) collective-permute-start(bf16[16,16512]{1,0:T(8,128)(2,1)} %fusion.11), channel_id=1, source_target_pairs={{0,8},{8,16},{16,24},{24,28},{28,20},{20,12},{12,4},{4,0},{1,9},{9... | collective-permute-start | bytes 1585160 | tf_op jit(solution)/shard_map/ppermute | solution.py:28
  11.3 18.6 %collective-permute-start.1 = (bf16[16,16512]{1,0:T(8,128)(2,1)}, bf16[16,16512]{1,0:T(8,128)(2,1)}, u32[]{:S(2)}, u32[]{:S(2)}) collective-permute-start(bf16[16,16512]{1,0:T(8,128)(2,1)} %fusion.11), channel_id=1, source_target_pairs={{0,4},{8,0},{16,8},{24,16},{28,24},{20,28},{12,20},{4,12},{1,5},{9... | collective-permute-start | bytes 1585160 | tf_op jit(solution)/shard_map/ppermute | solution.py:29
  12.0 4.0 %copy-start.7 = (s32[1,1,4]{2,1,0:T(1,128)S(1)}, s32[1,1,4]{2,1,0:T(1,128)}, u32[]{:S(2)}) copy-start(s32[1,1,4]{2,1,0:T(1,128)} %param.18) | copy-start | bytes 52
  12.0 4.1 %copy-start.11 = (s32[8]{0:T(128)S(1)}, s32[8]{0:T(128)}, u32[]{:S(2)}) copy-start(s32[8]{0:T(128)} %constant.213.clone) | copy-start | bytes 100
  12.1 4.6 %copy-start.10 = (s32[8]{0:T(128)S(1)}, s32[8]{0:T(128)}, u32[]{:S(2)}) copy-start(s32[8]{0:T(128)} %constant.215.clone) | copy-start | bytes 100
  12.1 5.3 %copy-start.2 = (s32[8]{0:T(128)S(1)}, s32[8]{0:T(128)}, u32[]{:S(2)}) copy-start(s32[8]{0:T(128)} %constant.214.clone) | copy-start | bytes 100
  12.1 6.6 %copy-start.9 = (s32[4]{0:T(128)S(1)}, s32[4]{0:T(128)}, u32[]{:S(2)}) copy-start(s32[4]{0:T(128)} %constant.210.clone) | copy-start | bytes 52
  12.1 7.2 %copy-start.8 = (s32[4]{0:T(128)S(1)}, s32[4]{0:T(128)}, u32[]{:S(2)}) copy-start(s32[4]{0:T(128)} %constant.212.clone) | copy-start | bytes 52
  12.1 7.8 %copy-start.1 = (s32[4]{0:T(128)S(1)}, s32[4]{0:T(128)}, u32[]{:S(2)}) copy-start(s32[4]{0:T(128)} %constant.211.clone) | copy-start | bytes 52
  13.2 10.8 %copy-start.6 = (bf16[512,512]{1,0:T(8,128)(2,1)S(1)}, bf16[512,512]{1,0:T(8,128)(2,1)}, u32[]{:S(2)}) copy-start(bf16[512,512]{1,0:T(8,128)(2,1)} %param.21) | copy-start | bytes 1572868
  13.2 18.8 %collective-permute-start.3 = (bf16[272,1024]{1,0:T(8,128)(2,1)}, bf16[272,1024]{1,0:T(8,128)(2,1)S(1)}, u32[]{:S(2)}, u32[]{:S(2)}) collective-permute-start(bf16[272,1024]{1,0:T(8,128)(2,1)} %get-tuple-element.45), channel_id=1, source_target_pairs={{0,1},{2,0},{3,2},{1,3},{4,5},{6,4},{7,6},{5,7},{8,9},{10,8},{11,1... | collective-permute-start | bytes 1671176 | tf_op jit(solution)/shard_map/ppermute | solution.py:29
  13.2 18.6 %collective-permute-start.2 = (bf16[272,1024]{1,0:T(8,128)(2,1)}, bf16[272,1024]{1,0:T(8,128)(2,1)S(1)}, u32[]{:S(2)}, u32[]{:S(2)}) collective-permute-start(bf16[272,1024]{1,0:T(8,128)(2,1)} %get-tuple-element.45), channel_id=1, source_target_pairs={{0,2},{2,3},{3,1},{1,0},{4,6},{6,7},{7,5},{5,4},{8,10},{10,11},{11... | collective-permute-start | bytes 1671176 | tf_op jit(solution)/shard_map/ppermute | solution.py:28
  25.9 21.4 %collective-permute-start.6 = (bf16[16,16512]{1,0:T(8,128)(2,1)}, bf16[16,16512]{1,0:T(8,128)(2,1)S(1)}, u32[]{:S(2)}, u32[]{:S(2)}) collective-permute-start(bf16[16,16512]{1,0:T(8,128)(2,1)} %collective-permute-done), channel_id=1, source_target_pairs={{0,8},{8,16},{16,24},{24,28},{28,20},{20,12},{12,4},{4,0},{1,9},{9... | collective-permute-start | bytes 1585160 | tf_op jit(solution)/shard_map/ppermute | solution.py:28
  29.9 17.4 %collective-permute-start.7 = (bf16[16,16512]{1,0:T(8,128)(2,1)}, bf16[16,16512]{1,0:T(8,128)(2,1)}, u32[]{:S(2)}, u32[]{:S(2)}) collective-permute-start(bf16[16,16512]{1,0:T(8,128)(2,1)} %collective-permute-done.1), channel_id=1, source_target_pairs={{0,4},{8,0},{16,8},{24,16},{28,24},{20,28},{12,20},{4,12},{1,5},{9... | collective-permute-start | bytes 1585160 | tf_op jit(solution)/shard_map/ppermute | solution.py:29
  32.8 9.3 %collective-permute-start.5 = (bf16[136,1024]{1,0:T(8,128)(2,1)}, bf16[136,1024]{1,0:T(8,128)(2,1)S(1)}, u32[]{:S(2)}, u32[]{:S(2)}) collective-permute-start(bf16[136,1024]{1,0:T(8,128)(2,1)} %slice.104), channel_id=1, source_target_pairs={{0,1},{2,0},{3,2},{1,3},{4,5},{6,4},{7,6},{5,7},{8,9},{10,8},{11,1... | collective-permute-start | bytes 835592 | tf_op jit(solution)/shard_map/ppermute | solution.py:34
  33.5 8.8 %collective-permute-start.4 = (bf16[136,1024]{1,0:T(8,128)(2,1)}, bf16[136,1024]{1,0:T(8,128)(2,1)}, u32[]{:S(2)}, u32[]{:S(2)}) collective-permute-start(bf16[136,1024]{1,0:T(8,128)(2,1)} %slice.103), channel_id=1, source_target_pairs={{0,2},{2,3},{3,1},{1,0},{4,6},{6,7},{7,5},{5,4},{8,10},{10,11},{11... | collective-permute-start | bytes 835592 | tf_op jit(solution)/shard_map/ppermute | solution.py:33
  43.6 1.4 %copy-start.3 = (bf16[4,272,1024]{2,1,0:T(8,128)(2,1)}, bf16[4,272,1024]{2,1,0:T(8,128)(2,1)S(1)}, u32[]{:S(2)}) copy-start(bf16[4,272,1024]{2,1,0:T(8,128)(2,1)S(1)} %pad_maximum_fusion) | copy-start | bytes 6684676
  47.4 0.8 copy-start.5
  49.0 13.8 %collective-permute-start.8 = (bf16[16,16512]{1,0:T(8,128)(2,1)}, bf16[16,16512]{1,0:T(8,128)(2,1)S(1)}, u32[]{:S(2)}, u32[]{:S(2)}) collective-permute-start(bf16[16,16512]{1,0:T(8,128)(2,1)} %copy-done.5), channel_id=1, source_target_pairs={{0,8},{8,16},{16,24},{24,28},{28,20},{20,12},{12,4},{4,0},{1,9},{9... | collective-permute-start | bytes 1585160 | tf_op jit(solution)/shard_map/ppermute | solution.py:28
  50.6 13.1 %collective-permute-start.9 = (bf16[16,16512]{1,0:T(8,128)(2,1)}, bf16[16,16512]{1,0:T(8,128)(2,1)}, u32[]{:S(2)}, u32[]{:S(2)}) collective-permute-start(bf16[16,16512]{1,0:T(8,128)(2,1)} %collective-permute-done.7), channel_id=1, source_target_pairs={{0,4},{8,0},{16,8},{24,16},{28,24},{20,28},{12,20},{4,12},{1,5},{9... | collective-permute-start | bytes 1585160 | tf_op jit(solution)/shard_map/ppermute | solution.py:29
  64.7 16.3 %collective-permute-start.11 = (bf16[8,16512]{1,0:T(8,128)(2,1)S(1)}, bf16[8,16512]{1,0:T(8,128)(2,1)S(1)}, u32[]{:S(2)}, u32[]{:S(2)}) collective-permute-start(bf16[8,16512]{1,0:T(8,128)(2,1)S(1)} %slice.110), channel_id=1, source_target_pairs={{0,4},{8,0},{16,8},{24,16},{28,24},{20,28},{12,20},{4,12},{1,5},{9... | collective-permute-start | bytes 792584 | tf_op jit(solution)/shard_map/ppermute | solution.py:34
  65.7 15.2 %collective-permute-start.10 = (bf16[8,16512]{1,0:T(8,128)(2,1)S(1)}, bf16[8,16512]{1,0:T(8,128)(2,1)S(1)}, u32[]{:S(2)}, u32[]{:S(2)}) collective-permute-start(bf16[8,16512]{1,0:T(8,128)(2,1)S(1)} %slice.109), channel_id=1, source_target_pairs={{0,8},{8,16},{16,24},{24,28},{28,20},{20,12},{12,4},{4,0},{1,9},{9... | collective-permute-start | bytes 792584 | tf_op jit(solution)/shard_map/ppermute | solution.py:33
  67.0 7.8 %copy-start.4 = (bf16[4,128,4,2,64]{4,3,2,1,0:T(2,128)(2,1)S(1)}, bf16[4,128,4,2,64]{4,3,2,1,0:T(2,128)(2,1)}, u32[]{:S(2)}) copy-start(bf16[4,128,4,2,64]{4,3,2,1,0:T(2,128)(2,1)} %reshape.354) | copy-start | bytes 1572868
  96.3 1.4 %collective-permute-start.14 = (f32[4,128]{1,0:T(4,128)S(1)}, f32[4,128]{1,0:T(4,128)S(1)}, u32[]{:S(2)}, u32[]{:S(2)}) collective-permute-start(f32[4,128]{1,0:T(4,128)S(1)} %get-tuple-element.51), channel_id=1, source_target_pairs={{0,3},{1,0},{2,1},{3,2},{4,7},{5,4},{6,5},{7,6},{8,11},{9,8},{10,9... | collective-permute-start | bytes 6152 | tf_op jit(solution)/shard_map/ppermute | solution.py:185
  96.4 3.7 %collective-permute-start.13 = (f32[4,128]{1,0:T(4,128)S(1)}, f32[4,128]{1,0:T(4,128)S(1)}, u32[]{:S(2)}, u32[]{:S(2)}) collective-permute-start(f32[4,128]{1,0:T(4,128)S(1)} %get-tuple-element.52), channel_id=1, source_target_pairs={{0,2},{1,3},{2,0},{3,1},{4,6},{5,7},{6,4},{7,5},{8,10},{9,11},{10,... | collective-permute-start | bytes 6152 | tf_op jit(solution)/shard_map/ppermute | solution.py:185
  96.5 3.6 %collective-permute-start.12 = (f32[4,128]{1,0:T(4,128)S(1)}, f32[4,128]{1,0:T(4,128)S(1)}, u32[]{:S(2)}, u32[]{:S(2)}) collective-permute-start(f32[4,128]{1,0:T(4,128)S(1)} %get-tuple-element.50), channel_id=1, source_target_pairs={{0,1},{1,2},{2,3},{3,0},{4,5},{5,6},{6,7},{7,4},{8,9},{9,10},{10,1... | collective-permute-start | bytes 6152 | tf_op jit(solution)/shard_map/ppermute | solution.py:185

commit v14 on v12

--- a/solution.py
+++ b/solution.py
@@ -132,6 +132,7 @@
     meta = meta.at[0, :slot_count].set(pair_list.astype(local_blocks.dtype))
     packed = jnp.concatenate([xt, meta], axis=1)
 
+    grp_ids, grp_got = ring_gather(packed, "grp", group_count)
     rows2d = masked.reshape(slot_count, block_size, ri_local, block_size)
     rows2d = jnp.transpose(rows2d, (0, 1, 3, 2)).reshape(slot_count * block_size, ri_cols)
     meta_rows = jnp.zeros((16, ri_cols), local_blocks.dtype)
@@ -141,7 +142,6 @@
     xg = jnp.stack(band_got)
     kdim = slot_count * block_size
     codes_g = xg[:, kdim, :slot_count].astype(jnp.float32).astype(jnp.int32)
-    grp_ids, grp_got = ring_gather(packed, "grp", group_count)
     xg, *early = lax.optimization_barrier([xg] + grp_got[3:5])
     grp_got[3:5] = early
 

time: 97.6 us -> 97.6 us (level)
  no operation moved by 1% of the time
where the time goes in v14:
time: 97.6 us; the launch traced here: 96.9 us
  local copies, waits for them, and re-layouts  38.9 us (40%)
  starting transfers between devices  14.1 us (14%)
  waiting for transfers between devices  12.8 us (13%)
  Pallas kernels  11.5 us (12%)
  matrix products  8.43 us (9%)
  other arithmetic  7.45 us (8%)
  between operations  3.69 us (4%)
    unnamed x29, local copies, waits for them, and re-layouts  11.6 us
    pallas_call x1, Pallas kernels, contract(): pl.pallas_call(body, out_shape=jax.ShapeDtypeStruct((steps, ri, chunk * r...  11.5 us
    ppermute x4, starting transfers between devices, ring_gather(): ahead = lax.ppermute(ahead, axis, fwd)  8.7 us
    dot_general x2, local copies, waits for them, and re-layouts, on_device(): lax.dot_general(occ_raw, virt_cols, (((0, 1, 2), (1, 2, 3)), ((), ())), p...  6.61 us
    dot_general x1, matrix products, on_device(): lax.dot_general(occ_raw, virt_cols, (((0, 1, 2), (1, 2, 3)), ((), ())), p...  6.13 us
    ppermute x2, waiting for transfers between devices, ring_gather(): second = lax.ppermute(behind[rows:], axis, bwd)  4.45 us
    ppermute x4, waiting for transfers between devices, ring_gather(): ahead = lax.ppermute(ahead, axis, fwd)  4.32 us
    squeeze x2, local copies, waits for them, and re-layouts, on_device(): local_blocks = x_blocks[0]  3.93 us
  transfers between devices with their start and end apart: 15, of which 5 were waited for; matrix products, arithmetic and copies ran while one was open for 40% of the time, Pallas kernels for 0%

profile of v14, /device:TPU:0, one launch (start us, length us, event | category | flops | bytes accessed | tf_op | source)
XLA Modules:
  0.0 96.9 jit_solution(4685274487244540803)
XLA Ops:
  0.0 0.7 convert_bitcast_fusion.2
  0.7 1.8 %squeeze.33 = bf16[4,64,16,64]{3,2,1,0:T(8,128)(2,1)S(1)} reshape(bf16[1,4,64,1024]{3,2,1,0:T(8,128)(2,1)} %param.15) | data formatting | bytes 1048576 | tf_op jit(solution)/shard_map/squeeze | solution.py:113
  2.5 2.2 %copy.210 = bf16[4,64,16,64]{1,0,2,3:T(4,128)(2,1)S(1)} copy(bf16[4,64,16,64]{3,2,1,0:T(8,128)(2,1)S(1)} %squeeze.33) | data formatting | bytes 1048576 | tf_op jit(solution)/shard_map/squeeze | solution.py:113
  5.3 0.6 multiply_bitcast_fusion
  5.9 0.7 copy.211
  6.6 0.8 reshape.204
  7.5 0.9 fusion.11
  8.3 3.0 %collective-permute-start = (bf16[16,16512]{1,0:T(8,128)(2,1)}, bf16[16,16512]{1,0:T(8,128)(2,1)}, u32[]{:S(2)}, u32[]{:S(2)}) collective-permute-start(bf16[16,16512]{1,0:T(8,128)(2,1)} %fusion.11), channel_id=1, source_target_pairs={{0,8},{8,16},{16,24},{24,28},{28,20},{20,12},{12,4},{4,0},{1,9},{9... | collective-permute-start | bytes 1585160 | tf_op jit(solution)/shard_map/ppermute | solution.py:28
  11.4 0.7 reshape.205
  12.1 0.2 copy.212
  12.3 0.9 fusion.33
  13.2 2.0 %collective-permute-start.2 = (bf16[272,1024]{1,0:T(8,128)(2,1)}, bf16[272,1024]{1,0:T(8,128)(2,1)S(1)}, u32[]{:S(2)}, u32[]{:S(2)}) collective-permute-start(bf16[272,1024]{1,0:T(8,128)(2,1)} %get-tuple-element.44), channel_id=1, source_target_pairs={{0,2},{2,3},{3,1},{1,0},{4,6},{6,7},{7,5},{5,4},{8,10},{10,11},{11... | collective-permute-start | bytes 1671176 | tf_op jit(solution)/shard_map/ppermute | solution.py:28
  15.3 0.9 bitcast_dynamic-update-slice_fusion.6
  16.1 0.6 dynamic_slice.34
  16.7 0.7 compare_select_fusion.7
  17.4 0.6 gather_fusion
  18.1 0.6 scatter_custom_fusion
  18.7 0.6 dynamic_slice.36
  19.3 0.7 compare_select_fusion.4
  20.0 0.6 gather_fusion.2
  20.6 0.7 fusion.34
  24.0 0.1 constant_dynamic-slice_fusion.7
  24.1 1.5 %reshape.256 = bf16[4,128,4,2,64]{4,3,2,1,0:T(2,128)(2,1)} reshape(bf16[512,512]{1,0:T(8,128)(2,1)S(1)} %pad_maximum_fusion.1) | data formatting | bytes 1048576 | tf_op jit(solution)/shard_map/dot_general | solution.py:166
  25.7 0.1 broadcast_in_dim.43
  25.9 2.1 %collective-permute-start.6 = (bf16[16,16512]{1,0:T(8,128)(2,1)}, bf16[16,16512]{1,0:T(8,128)(2,1)S(1)}, u32[]{:S(2)}, u32[]{:S(2)}) collective-permute-start(bf16[16,16512]{1,0:T(8,128)(2,1)} %collective-permute-done), channel_id=1, source_target_pairs={{0,8},{8,16},{16,24},{24,28},{28,20},{20,12},{12,4},{4,0},{1,9},{9... | collective-permute-start | bytes 1585160 | tf_op jit(solution)/shard_map/ppermute | solution.py:28
  28.0 1.9 %bitcast_dynamic-update-slice_fusion.5 = bf16[8,16,16512]{2,1,0:T(8,128)(2,1)} fusion(bf16[8,16,16512]{2,1,0:T(8,128)(2,1)} %bitcast_dynamic-update-slice_fusion.6, bf16[16,16512]{1,0:T(8,128)(2,1)} %collective-permute-done), kind=kLoop, calls=%fused_computation.29 | loop fusion | bytes 1056768
  30.0 2.0 %collective-permute-start.4 = (bf16[136,1024]{1,0:T(8,128)(2,1)S(1)}, bf16[136,1024]{1,0:T(8,128)(2,1)S(1)}, u32[]{:S(2)}, u32[]{:S(2)}) collective-permute-start(bf16[136,1024]{1,0:T(8,128)(2,1)S(1)} %slice.84), channel_id=1, source_target_pairs={{0,2},{2,3},{3,1},{1,0},{4,6},{6,7},{7,5},{5,4},{8,10},{10,11},{11... | collective-permute-start | bytes 835592 | tf_op jit(solution)/shard_map/ppermute | solution.py:33
  32.0 1.9 %bitcast_dynamic-update-slice_fusion.4 = bf16[8,16,16512]{2,1,0:T(8,128)(2,1)} fusion(bf16[8,16,16512]{2,1,0:T(8,128)(2,1)} %bitcast_dynamic-update-slice_fusion.5, bf16[16,16512]{1,0:T(8,128)(2,1)} %collective-permute-done.1), kind=kLoop, calls=%fused_computation.28 | loop fusion | bytes 1056768
  33.9 4.4 %collective-permute-done.5 = bf16[136,1024]{1,0:T(8,128)(2,1)S(1)} collective-permute-done((bf16[136,1024]{1,0:T(8,128)(2,1)S(1)}, bf16[136,1024]{1,0:T(8,128)(2,1)S(1)}, u32[]{:S(2)}, u32[]{:S(2)}) %collective-permute-start.5) | collective-permute-done | bytes 278560 | tf_op jit(solution)/shard_map/ppermute | solution.py:34
  38.4 0.3 pad_maximum_fusion
  38.7 1.4 %copy-done.3 = bf16[4,272,1024]{2,1,0:T(8,128)(2,1)} copy-done((bf16[4,272,1024]{2,1,0:T(8,128)(2,1)}, bf16[4,272,1024]{2,1,0:T(8,128)(2,1)S(1)}, u32[]{:S(2)}) %copy-start.3) | copy-done | bytes 2228248
  40.2 0.1 add.203
  40.4 0.1 mul.68
  40.6 3.2 %gather_fusion.1 = bf16[1024,128]{1,0:T(8,128)(2,1)S(1)} fusion(bf16[512,128]{1,0:T(8,128)(2,1)S(1)} %constant_dynamic-slice_fusion.8, s32[1024]{0:T(1024)S(1)} %broadcast_clamp_fusion), kind=kCustom, calls=%fused_computation.1 | custom fusion | bytes 528384 | tf_op jit(solution)/shard_map/jit(_take)/gather | solution.py:150
  43.9 0.2 broadcast_select_fusion
  44.1 0.1 copy.213
  44.3 0.8 copy-done.5
  45.0 0.8 bitcast_dynamic-update-slice_fusion.3
  45.9 1.6 %collective-permute-start.8 = (bf16[16,16512]{1,0:T(8,128)(2,1)}, bf16[16,16512]{1,0:T(8,128)(2,1)S(1)}, u32[]{:S(2)}, u32[]{:S(2)}) collective-permute-start(bf16[16,16512]{1,0:T(8,128)(2,1)} %copy-done.5), channel_id=1, source_target_pairs={{0,8},{8,16},{16,24},{24,28},{28,20},{20,12},{12,4},{4,0},{1,9},{9... | collective-permute-start | bytes 1585160 | tf_op jit(solution)/shard_map/ppermute | solution.py:28
  47.4 0.4 collective-permute-start.9
  47.9 1.9 %bitcast_dynamic-update-slice_fusion.2 = bf16[8,16,16512]{2,1,0:T(8,128)(2,1)} fusion(bf16[8,16,16512]{2,1,0:T(8,128)(2,1)} %bitcast_dynamic-update-slice_fusion.3, bf16[16,16512]{1,0:T(8,128)(2,1)} %collective-permute-done.7), kind=kLoop, calls=%fused_computation.26 | loop fusion | bytes 1056768
  49.8 2.3 %convert_bitcast_fusion = bf16[4,2,1024,128]{2,3,1,0:T(8,128)(2,1)S(1)} fusion(bf16[4,272,1024]{2,1,0:T(8,128)(2,1)} %copy-done.3, bf16[4,2,256]{2,1,0:T(2,128)(2,1)S(1)} %mul.68, bf16[4,256,128]{1,2,0:T(8,128)(2,1)S(1)} %copy.213), kind=kOutput, calls=%fused_computation.10 | convolution fusion | flops 538181632 | bytes 4460544 | tf_op jit(solution)/shard_map/bkr,bhkl->bhrl/dot_general | solution.py:155
  52.1 2.6 %copy.214 = bf16[4,2,1024,128]{3,2,1,0:T(8,128)(2,1)} copy(bf16[4,2,1024,128]{2,3,1,0:T(8,128)(2,1)S(1)} %convert_bitcast_fusion) | data formatting | bytes 4194304 | tf_op jit(solution)/shard_map/convert_element_type | solution.py:157
  54.8 4.3 %collective-permute-done.8 = bf16[16,16512]{1,0:T(8,128)(2,1)S(1)} collective-permute-done((bf16[16,16512]{1,0:T(8,128)(2,1)}, bf16[16,16512]{1,0:T(8,128)(2,1)S(1)}, u32[]{:S(2)}, u32[]{:S(2)}) %collective-permute-start.8) | collective-permute-done | bytes 528416 | tf_op jit(solution)/shard_map/ppermute | solution.py:28
  59.1 0.9 collective-permute-done.9
  60.0 1.0 slice.88
  61.0 1.0 %collective-permute-start.11 = (bf16[8,16512]{1,0:T(8,128)(2,1)S(1)}, bf16[8,16512]{1,0:T(8,128)(2,1)S(1)}, u32[]{:S(2)}, u32[]{:S(2)}) collective-permute-start(bf16[8,16512]{1,0:T(8,128)(2,1)S(1)} %slice.88), channel_id=1, source_target_pairs={{0,4},{8,0},{16,8},{24,16},{28,24},{20,28},{12,20},{4,12},{1,5},{9... | collective-permute-start | bytes 792584 | tf_op jit(solution)/shard_map/ppermute | solution.py:34
  62.0 1.3 %collective-permute-start.10 = (bf16[8,16512]{1,0:T(8,128)(2,1)S(1)}, bf16[8,16512]{1,0:T(8,128)(2,1)S(1)}, u32[]{:S(2)}, u32[]{:S(2)}) collective-permute-start(bf16[8,16512]{1,0:T(8,128)(2,1)S(1)} %slice.87), channel_id=1, source_target_pairs={{0,8},{8,16},{16,24},{24,28},{28,20},{20,12},{12,4},{4,0},{1,9},{9... | collective-permute-start | bytes 792584 | tf_op jit(solution)/shard_map/ppermute | solution.py:33
  63.3 5.1 %copy.216 = bf16[16,128,4,2,64]{4,1,3,2,0:T(8,128)(2,1)} copy(bf16[16,128,4,2,64]{1,0,4,3,2:T(8,128)(2,1)} %bitcast.95) | data formatting | bytes 4194304 | tf_op jit(solution)/shard_map/dot_general | solution.py:166
  68.4 0.8 bitcast_dynamic-update-slice_fusion.1
  69.2 1.9 %bitcast_dynamic-update-slice_fusion = bf16[8,16,16512]{2,1,0:T(8,128)(2,1)} fusion(bf16[8,16,16512]{2,1,0:T(8,128)(2,1)} %bitcast_dynamic-update-slice_fusion.1, bf16[16,16512]{1,0:T(8,128)(2,1)} %collective-permute-done.9), kind=kLoop, calls=%fused_computation.24 | loop fusion | bytes 1056768
  71.1 6.1 %fusion = f32[16,16,8,4,128,1,1]{4,2,6,5,3,1,0:T(8,128)} fusion(bf16[4,128,4,2,64,1,1]{4,3,2,1,0,6,5:T(2,128)(2,1)S(1)} %bitcast.101, bf16[16,128,4,2,64]{4,1,3,2,0:T(8,128)(2,1)} %copy.216), kind=kOutput, calls=%fused_computation.5 | convolution fusion | flops 1073741824 | bytes 6815744 | tf_op jit(solution)/shard_map/dot_general | solution.py:166
  77.2 0.8 fusion.12
  78.0 0.7 slice.89
  78.8 0.1 copy.233
  78.9 0.7 copy.220.refs_0_
  79.5 11.5 %shard_map.109 = f32[1,16,128]{2,1,0:T(8,128)} custom-call(s32[8,4]{1,0:T(8,128)} %copy.220.refs_0_, f32[8192,128]{1,0:T(8,128)} %bitcast.97, bf16[128,16512]{1,0:T(8,128)(2,1)} %bitcast.96), custom_call_target="tpu_custom_call" | custom-call | tf_op jit(solution)/shard_map/pallas_call | solution.py:106
  91.1 0.8 reshape_reshape_transpose.3
  91.9 0.6 gather_fusion.3
  92.5 0.1 gather.26
  92.7 0.4 collective-permute-start.12
  93.1 0.8 collective-permute-done.14
  93.9 2.3 %collective-permute-done.13 = f32[4,128]{1,0:T(4,128)S(1)} collective-permute-done((f32[4,128]{1,0:T(4,128)S(1)}, f32[4,128]{1,0:T(4,128)S(1)}, u32[]{:S(2)}, u32[]{:S(2)}) %collective-permute-start.13) | collective-permute-done | bytes 2080 | tf_op jit(solution)/shard_map/ppermute | solution.py:182
  96.3 0.6 fusion.19
  (68 shorter events, 1.1 us)
Async XLA Ops:
  0.0 25.8 %copy-start = (bf16[512,512]{1,0:T(8,128)(2,1)S(1)}, bf16[512,512]{1,0:T(8,128)(2,1)}, u32[]{:S(2)}) copy-start(bf16[512,512]{1,0:T(8,128)(2,1)} %param.18) | copy-start | bytes 1572868
  8.3 17.5 %collective-permute-start = (bf16[16,16512]{1,0:T(8,128)(2,1)}, bf16[16,16512]{1,0:T(8,128)(2,1)}, u32[]{:S(2)}, u32[]{:S(2)}) collective-permute-start(bf16[16,16512]{1,0:T(8,128)(2,1)} %fusion.11), channel_id=1, source_target_pairs={{0,8},{8,16},{16,24},{24,28},{28,20},{20,12},{12,4},{4,0},{1,9},{9... | collective-permute-start | bytes 1585160 | tf_op jit(solution)/shard_map/ppermute | solution.py:28
  11.4 18.5 %collective-permute-start.1 = (bf16[16,16512]{1,0:T(8,128)(2,1)}, bf16[16,16512]{1,0:T(8,128)(2,1)}, u32[]{:S(2)}, u32[]{:S(2)}) collective-permute-start(bf16[16,16512]{1,0:T(8,128)(2,1)} %fusion.11), channel_id=1, source_target_pairs={{0,4},{8,0},{16,8},{24,16},{28,24},{20,28},{12,20},{4,12},{1,5},{9... | collective-permute-start | bytes 1585160 | tf_op jit(solution)/shard_map/ppermute | solution.py:29
  12.0 4.1 %copy-start.10 = (s32[8]{0:T(128)S(1)}, s32[8]{0:T(128)}, u32[]{:S(2)}) copy-start(s32[8]{0:T(128)} %constant.193.clone) | copy-start | bytes 100
  12.1 4.7 %copy-start.9 = (s32[8]{0:T(128)S(1)}, s32[8]{0:T(128)}, u32[]{:S(2)}) copy-start(s32[8]{0:T(128)} %constant.195.clone) | copy-start | bytes 100
  12.1 5.3 %copy-start.2 = (s32[8]{0:T(128)S(1)}, s32[8]{0:T(128)}, u32[]{:S(2)}) copy-start(s32[8]{0:T(128)} %constant.194.clone) | copy-start | bytes 100
  12.1 6.6 %copy-start.8 = (s32[4]{0:T(128)S(1)}, s32[4]{0:T(128)}, u32[]{:S(2)}) copy-start(s32[4]{0:T(128)} %constant.196.clone) | copy-start | bytes 52
  12.1 7.2 %copy-start.7 = (s32[4]{0:T(128)S(1)}, s32[4]{0:T(128)}, u32[]{:S(2)}) copy-start(s32[4]{0:T(128)} %constant.198.clone) | copy-start | bytes 52
  12.1 7.8 %copy-start.1 = (s32[4]{0:T(128)S(1)}, s32[4]{0:T(128)}, u32[]{:S(2)}) copy-start(s32[4]{0:T(128)} %constant.197.clone) | copy-start | bytes 52
  13.2 10.7 %copy-start.6 = (bf16[512,512]{1,0:T(8,128)(2,1)S(1)}, bf16[512,512]{1,0:T(8,128)(2,1)}, u32[]{:S(2)}) copy-start(bf16[512,512]{1,0:T(8,128)(2,1)} %param.19) | copy-start | bytes 1572868
  13.2 16.6 %collective-permute-start.3 = (bf16[272,1024]{1,0:T(8,128)(2,1)}, bf16[272,1024]{1,0:T(8,128)(2,1)S(1)}, u32[]{:S(2)}, u32[]{:S(2)}) collective-permute-start(bf16[272,1024]{1,0:T(8,128)(2,1)} %get-tuple-element.44), channel_id=1, source_target_pairs={{0,1},{2,0},{3,2},{1,3},{4,5},{6,4},{7,6},{5,7},{8,9},{10,8},{11,1... | collective-permute-start | bytes 1671176 | tf_op jit(solution)/shard_map/ppermute | solution.py:29
  13.2 16.7 %collective-permute-start.2 = (bf16[272,1024]{1,0:T(8,128)(2,1)}, bf16[272,1024]{1,0:T(8,128)(2,1)S(1)}, u32[]{:S(2)}, u32[]{:S(2)}) collective-permute-start(bf16[272,1024]{1,0:T(8,128)(2,1)} %get-tuple-element.44), channel_id=1, source_target_pairs={{0,2},{2,3},{3,1},{1,0},{4,6},{6,7},{7,5},{5,4},{8,10},{10,11},{11... | collective-permute-start | bytes 1671176 | tf_op jit(solution)/shard_map/ppermute | solution.py:28
  25.9 18.3 %collective-permute-start.6 = (bf16[16,16512]{1,0:T(8,128)(2,1)}, bf16[16,16512]{1,0:T(8,128)(2,1)S(1)}, u32[]{:S(2)}, u32[]{:S(2)}) collective-permute-start(bf16[16,16512]{1,0:T(8,128)(2,1)} %collective-permute-done), channel_id=1, source_target_pairs={{0,8},{8,16},{16,24},{24,28},{28,20},{20,12},{12,4},{4,0},{1,9},{9... | collective-permute-start | bytes 1585160 | tf_op jit(solution)/shard_map/ppermute | solution.py:28
  29.9 14.4 %collective-permute-start.7 = (bf16[16,16512]{1,0:T(8,128)(2,1)}, bf16[16,16512]{1,0:T(8,128)(2,1)}, u32[]{:S(2)}, u32[]{:S(2)}) collective-permute-start(bf16[16,16512]{1,0:T(8,128)(2,1)} %collective-permute-done.1), channel_id=1, source_target_pairs={{0,4},{8,0},{16,8},{24,16},{28,24},{20,28},{12,20},{4,12},{1,5},{9... | collective-permute-start | bytes 1585160 | tf_op jit(solution)/shard_map/ppermute | solution.py:29
  29.9 8.4 %collective-permute-start.5 = (bf16[136,1024]{1,0:T(8,128)(2,1)S(1)}, bf16[136,1024]{1,0:T(8,128)(2,1)S(1)}, u32[]{:S(2)}, u32[]{:S(2)}) collective-permute-start(bf16[136,1024]{1,0:T(8,128)(2,1)S(1)} %slice.85), channel_id=1, source_target_pairs={{0,1},{2,0},{3,2},{1,3},{4,5},{6,4},{7,6},{5,7},{8,9},{10,8},{11,1... | collective-permute-start | bytes 835592 | tf_op jit(solution)/shard_map/ppermute | solution.py:34
  30.0 8.4 %collective-permute-start.4 = (bf16[136,1024]{1,0:T(8,128)(2,1)S(1)}, bf16[136,1024]{1,0:T(8,128)(2,1)S(1)}, u32[]{:S(2)}, u32[]{:S(2)}) collective-permute-start(bf16[136,1024]{1,0:T(8,128)(2,1)S(1)} %slice.84), channel_id=1, source_target_pairs={{0,2},{2,3},{3,1},{1,0},{4,6},{6,7},{7,5},{5,4},{8,10},{10,11},{11... | collective-permute-start | bytes 835592 | tf_op jit(solution)/shard_map/ppermute | solution.py:33
  38.7 1.4 %copy-start.3 = (bf16[4,272,1024]{2,1,0:T(8,128)(2,1)}, bf16[4,272,1024]{2,1,0:T(8,128)(2,1)S(1)}, u32[]{:S(2)}) copy-start(bf16[4,272,1024]{2,1,0:T(8,128)(2,1)S(1)} %pad_maximum_fusion) | copy-start | bytes 6684676
  44.2 0.8 copy-start.5
  45.9 13.2 %collective-permute-start.8 = (bf16[16,16512]{1,0:T(8,128)(2,1)}, bf16[16,16512]{1,0:T(8,128)(2,1)S(1)}, u32[]{:S(2)}, u32[]{:S(2)}) collective-permute-start(bf16[16,16512]{1,0:T(8,128)(2,1)} %copy-done.5), channel_id=1, source_target_pairs={{0,8},{8,16},{16,24},{24,28},{28,20},{20,12},{12,4},{4,0},{1,9},{9... | collective-permute-start | bytes 1585160 | tf_op jit(solution)/shard_map/ppermute | solution.py:28
  47.4 12.5 %collective-permute-start.9 = (bf16[16,16512]{1,0:T(8,128)(2,1)}, bf16[16,16512]{1,0:T(8,128)(2,1)}, u32[]{:S(2)}, u32[]{:S(2)}) collective-permute-start(bf16[16,16512]{1,0:T(8,128)(2,1)} %collective-permute-done.7), channel_id=1, source_target_pairs={{0,4},{8,0},{16,8},{24,16},{28,24},{20,28},{12,20},{4,12},{1,5},{9... | collective-permute-start | bytes 1585160 | tf_op jit(solution)/shard_map/ppermute | solution.py:29
  61.0 16.3 %collective-permute-start.11 = (bf16[8,16512]{1,0:T(8,128)(2,1)S(1)}, bf16[8,16512]{1,0:T(8,128)(2,1)S(1)}, u32[]{:S(2)}, u32[]{:S(2)}) collective-permute-start(bf16[8,16512]{1,0:T(8,128)(2,1)S(1)} %slice.88), channel_id=1, source_target_pairs={{0,4},{8,0},{16,8},{24,16},{28,24},{20,28},{12,20},{4,12},{1,5},{9... | collective-permute-start | bytes 792584 | tf_op jit(solution)/shard_map/ppermute | solution.py:34
  62.0 15.3 %collective-permute-start.10 = (bf16[8,16512]{1,0:T(8,128)(2,1)S(1)}, bf16[8,16512]{1,0:T(8,128)(2,1)S(1)}, u32[]{:S(2)}, u32[]{:S(2)}) collective-permute-start(bf16[8,16512]{1,0:T(8,128)(2,1)S(1)} %slice.87), channel_id=1, source_target_pairs={{0,8},{8,16},{16,24},{24,28},{28,20},{20,12},{12,4},{4,0},{1,9},{9... | collective-permute-start | bytes 792584 | tf_op jit(solution)/shard_map/ppermute | solution.py:33
  63.3 7.8 %copy-start.4 = (bf16[4,128,4,2,64]{4,3,2,1,0:T(2,128)(2,1)S(1)}, bf16[4,128,4,2,64]{4,3,2,1,0:T(2,128)(2,1)}, u32[]{:S(2)}) copy-start(bf16[4,128,4,2,64]{4,3,2,1,0:T(2,128)(2,1)} %reshape.256) | copy-start | bytes 1572868
  92.6 1.4 %collective-permute-start.14 = (f32[4,128]{1,0:T(4,128)S(1)}, f32[4,128]{1,0:T(4,128)S(1)}, u32[]{:S(2)}, u32[]{:S(2)}) collective-permute-start(f32[4,128]{1,0:T(4,128)S(1)} %get-tuple-element.50), channel_id=1, source_target_pairs={{0,3},{1,0},{2,1},{3,2},{4,7},{5,4},{6,5},{7,6},{8,11},{9,8},{10,9... | collective-permute-start | bytes 6152 | tf_op jit(solution)/shard_map/ppermute | solution.py:182
  92.6 3.7 %collective-permute-start.13 = (f32[4,128]{1,0:T(4,128)S(1)}, f32[4,128]{1,0:T(4,128)S(1)}, u32[]{:S(2)}, u32[]{:S(2)}) collective-permute-start(f32[4,128]{1,0:T(4,128)S(1)} %get-tuple-element.51), channel_id=1, source_target_pairs={{0,2},{1,3},{2,0},{3,1},{4,6},{5,7},{6,4},{7,5},{8,10},{9,11},{10,... | collective-permute-start | bytes 6152 | tf_op jit(solution)/shard_map/ppermute | solution.py:182
  92.7 3.6 %collective-permute-start.12 = (f32[4,128]{1,0:T(4,128)S(1)}, f32[4,128]{1,0:T(4,128)S(1)}, u32[]{:S(2)}, u32[]{:S(2)}) collective-permute-start(f32[4,128]{1,0:T(4,128)S(1)} %get-tuple-element.49), channel_id=1, source_target_pairs={{0,1},{1,2},{2,3},{3,0},{4,5},{5,6},{6,7},{7,4},{8,9},{9,10},{10,1... | collective-permute-start | bytes 6152 | tf_op jit(solution)/shard_map/ppermute | solution.py:182

commit v15 on v14

--- a/solution.py
+++ b/solution.py
@@ -40,8 +40,9 @@
 
 def contract_kernel(codes_ref, table_ref, x_ref, out_ref, both_ref, dense_ref, *, slots, width, ri, chunk, blk):
     step = pl.program_id(0)
+    s = pl.program_id(1)
 
-    @pl.when(step == 0)
+    @pl.when(jnp.logical_and(step == 0, s == 0))
     def split():
         lam_count = 2 * blk
         half = both_ref.shape[0] // (2 * ri)
@@ -61,20 +62,20 @@
                         low = (half + code) * ri
                         both_ref[low:low + ri, j * blk:(j + 1) * blk] = lo[:, u * blk:(u + 1) * blk]
 
-    out_ref[...] = jnp.zeros(out_ref.shape, jnp.float32)
-    for s in range(slots):
-        xs = x_ref[:, s * width:(s + 1) * width]
-        dense = lax.dot_general(
-            both_ref[...], xs, (((1,), (1,)), ((), ())), preferred_element_type=jnp.float32
+    @pl.when(s == 0)
+    def clear():
+        out_ref[...] = jnp.zeros(out_ref.shape, jnp.float32)
+
+    dense_ref[...] = lax.dot_general(
+        both_ref[...], x_ref[...], (((1,), (1,)), ((), ())), preferred_element_type=jnp.float32
+    )
+    for c in range(chunk):
+        code = codes_ref[step * chunk + c, s]
+        start = pl.multiple_of(code * ri, ri)
+        low = pl.multiple_of((code + dense_ref.shape[0] // (2 * ri)) * ri, ri)
+        out_ref[0, :, c * ri:(c + 1) * ri] += (
+            dense_ref[pl.ds(start, ri), c * ri:(c + 1) * ri] + dense_ref[pl.ds(low, ri), c * ri:(c + 1) * ri]
         )
-        dense_ref[...] = dense
-        for c in range(chunk):
-            code = codes_ref[step * chunk + c, s]
-            start = pl.multiple_of(code * ri, ri)
-            low = pl.multiple_of((code + dense_ref.shape[0] // (2 * ri)) * ri, ri)
-            out_ref[0, :, c * ri:(c + 1) * ri] += (
-                dense_ref[pl.ds(start, ri), c * ri:(c + 1) * ri] + dense_ref[pl.ds(low, ri), c * ri:(c + 1) * ri]
-            )
 
 
 def contract(codes, folded, xrows, groups, slots, blk):
@@ -91,12 +92,12 @@
     table2 = jnp.transpose(table2, (0, 1, 3, 2, 4)).reshape(ri * lam_count * tiles, 128)
     grid_spec = pltpu.PrefetchScalarGridSpec(
         num_scalar_prefetch=1,
-        grid=(steps,),
+        grid=(steps, slots),
         in_specs=[
-            pl.BlockSpec(table2.shape, lambda g, c: (0, 0)),
-            pl.BlockSpec((chunk * ri, flat), lambda g, c: (g, 0)),
+            pl.BlockSpec(table2.shape, lambda g, s, c: (0, 0)),
+            pl.BlockSpec((chunk * ri, width), lambda g, s, c: (g, s)),
         ],
-        out_specs=pl.BlockSpec((1, ri, chunk * ri), lambda g, c: (g, 0, 0)),
+        out_specs=pl.BlockSpec((1, ri, chunk * ri), lambda g, s, c: (g, 0, 0)),
         scratch_shapes=[
             pltpu.VMEM((2 * codes_total * ri, width), jnp.bfloat16),
             pltpu.VMEM((2 * codes_total * ri, chunk * ri), jnp.float32),

time: 97.6 us -> 98.4 us (level)
  no operation moved by 1% of the time
where the time goes in v15:
time: 98.4 us; the launch traced here: 97.7 us
  local copies, waits for them, and re-layouts  38.9 us (40%)
  starting transfers between devices  14.1 us (14%)
  waiting for transfers between devices  12.8 us (13%)
  Pallas kernels  12.4 us (13%)
  matrix products  8.43 us (9%)
  other arithmetic  7.45 us (8%)
  between operations  3.69 us (4%)
    pallas_call x1, Pallas kernels, contract(): pl.pallas_call(body, out_shape=jax.ShapeDtypeStruct((steps, ri, chunk * r...  12.4 us
    unnamed x29, local copies, waits for them, and re-layouts  11.6 us
    ppermute x4, starting transfers between devices, ring_gather(): ahead = lax.ppermute(ahead, axis, fwd)  8.7 us
    dot_general x2, local copies, waits for them, and re-layouts, on_device(): lax.dot_general(occ_raw, virt_cols, (((0, 1, 2), (1, 2, 3)), ((), ())), p...  6.61 us
    dot_general x1, matrix products, on_device(): lax.dot_general(occ_raw, virt_cols, (((0, 1, 2), (1, 2, 3)), ((), ())), p...  6.13 us
    ppermute x2, waiting for transfers between devices, ring_gather(): second = lax.ppermute(behind[rows:], axis, bwd)  4.45 us
    ppermute x4, waiting for transfers between devices, ring_gather(): ahead = lax.ppermute(ahead, axis, fwd)  4.32 us
    squeeze x2, local copies, waits for them, and re-layouts, on_device(): local_blocks = x_blocks[0]  3.93 us
  transfers between devices with their start and end apart: 15, of which 5 were waited for; matrix products, arithmetic and copies ran while one was open for 40% of the time, Pallas kernels for 0%

profile of v15, /device:TPU:0, one launch (start us, length us, event | category | flops | bytes accessed | tf_op | source)
XLA Modules:
  0.0 97.7 jit_solution(6073234145742092129)
XLA Ops:
  0.0 0.7 convert_bitcast_fusion.2
  0.7 1.8 %squeeze.33 = bf16[4,64,16,64]{3,2,1,0:T(8,128)(2,1)S(1)} reshape(bf16[1,4,64,1024]{3,2,1,0:T(8,128)(2,1)} %param.15) | data formatting | bytes 1048576 | tf_op jit(solution)/shard_map/squeeze | solution.py:114
  2.5 2.2 %copy.210 = bf16[4,64,16,64]{1,0,2,3:T(4,128)(2,1)S(1)} copy(bf16[4,64,16,64]{3,2,1,0:T(8,128)(2,1)S(1)} %squeeze.33) | data formatting | bytes 1048576 | tf_op jit(solution)/shard_map/squeeze | solution.py:114
  5.3 0.6 multiply_bitcast_fusion
  5.9 0.7 copy.211
  6.6 0.8 reshape.204
  7.5 0.9 fusion.11
  8.3 3.0 %collective-permute-start = (bf16[16,16512]{1,0:T(8,128)(2,1)}, bf16[16,16512]{1,0:T(8,128)(2,1)}, u32[]{:S(2)}, u32[]{:S(2)}) collective-permute-start(bf16[16,16512]{1,0:T(8,128)(2,1)} %fusion.11), channel_id=1, source_target_pairs={{0,8},{8,16},{16,24},{24,28},{28,20},{20,12},{12,4},{4,0},{1,9},{9... | collective-permute-start | bytes 1585160 | tf_op jit(solution)/shard_map/ppermute | solution.py:28
  11.4 0.7 reshape.205
  12.1 0.2 copy.212
  12.3 0.9 fusion.33
  13.2 2.0 %collective-permute-start.2 = (bf16[272,1024]{1,0:T(8,128)(2,1)}, bf16[272,1024]{1,0:T(8,128)(2,1)S(1)}, u32[]{:S(2)}, u32[]{:S(2)}) collective-permute-start(bf16[272,1024]{1,0:T(8,128)(2,1)} %get-tuple-element.44), channel_id=1, source_target_pairs={{0,2},{2,3},{3,1},{1,0},{4,6},{6,7},{7,5},{5,4},{8,10},{10,11},{11... | collective-permute-start | bytes 1671176 | tf_op jit(solution)/shard_map/ppermute | solution.py:28
  15.3 0.9 bitcast_dynamic-update-slice_fusion.6
  16.1 0.6 dynamic_slice.34
  16.7 0.7 compare_select_fusion.7
  17.4 0.6 gather_fusion
  18.1 0.6 scatter_custom_fusion
  18.7 0.6 dynamic_slice.36
  19.3 0.7 compare_select_fusion.4
  20.0 0.6 gather_fusion.2
  20.6 0.7 fusion.34
  24.0 0.1 constant_dynamic-slice_fusion.7
  24.1 1.5 %reshape.256 = bf16[4,128,4,2,64]{4,3,2,1,0:T(2,128)(2,1)} reshape(bf16[512,512]{1,0:T(8,128)(2,1)S(1)} %pad_maximum_fusion.1) | data formatting | bytes 1048576 | tf_op jit(solution)/shard_map/dot_general | solution.py:167
  25.7 0.1 broadcast_in_dim.43
  25.9 2.1 %collective-permute-start.6 = (bf16[16,16512]{1,0:T(8,128)(2,1)}, bf16[16,16512]{1,0:T(8,128)(2,1)S(1)}, u32[]{:S(2)}, u32[]{:S(2)}) collective-permute-start(bf16[16,16512]{1,0:T(8,128)(2,1)} %collective-permute-done), channel_id=1, source_target_pairs={{0,8},{8,16},{16,24},{24,28},{28,20},{20,12},{12,4},{4,0},{1,9},{9... | collective-permute-start | bytes 1585160 | tf_op jit(solution)/shard_map/ppermute | solution.py:28
  28.0 1.9 %bitcast_dynamic-update-slice_fusion.5 = bf16[8,16,16512]{2,1,0:T(8,128)(2,1)} fusion(bf16[8,16,16512]{2,1,0:T(8,128)(2,1)} %bitcast_dynamic-update-slice_fusion.6, bf16[16,16512]{1,0:T(8,128)(2,1)} %collective-permute-done), kind=kLoop, calls=%fused_computation.29 | loop fusion | bytes 1056768
  30.0 2.0 %collective-permute-start.4 = (bf16[136,1024]{1,0:T(8,128)(2,1)S(1)}, bf16[136,1024]{1,0:T(8,128)(2,1)S(1)}, u32[]{:S(2)}, u32[]{:S(2)}) collective-permute-start(bf16[136,1024]{1,0:T(8,128)(2,1)S(1)} %slice.84), channel_id=1, source_target_pairs={{0,2},{2,3},{3,1},{1,0},{4,6},{6,7},{7,5},{5,4},{8,10},{10,11},{11... | collective-permute-start | bytes 835592 | tf_op jit(solution)/shard_map/ppermute | solution.py:33
  32.0 1.9 %bitcast_dynamic-update-slice_fusion.4 = bf16[8,16,16512]{2,1,0:T(8,128)(2,1)} fusion(bf16[8,16,16512]{2,1,0:T(8,128)(2,1)} %bitcast_dynamic-update-slice_fusion.5, bf16[16,16512]{1,0:T(8,128)(2,1)} %collective-permute-done.1), kind=kLoop, calls=%fused_computation.28 | loop fusion | bytes 1056768
  33.9 4.4 %collective-permute-done.5 = bf16[136,1024]{1,0:T(8,128)(2,1)S(1)} collective-permute-done((bf16[136,1024]{1,0:T(8,128)(2,1)S(1)}, bf16[136,1024]{1,0:T(8,128)(2,1)S(1)}, u32[]{:S(2)}, u32[]{:S(2)}) %collective-permute-start.5) | collective-permute-done | bytes 278560 | tf_op jit(solution)/shard_map/ppermute | solution.py:34
  38.4 0.3 pad_maximum_fusion
  38.7 1.4 %copy-done.3 = bf16[4,272,1024]{2,1,0:T(8,128)(2,1)} copy-done((bf16[4,272,1024]{2,1,0:T(8,128)(2,1)}, bf16[4,272,1024]{2,1,0:T(8,128)(2,1)S(1)}, u32[]{:S(2)}) %copy-start.3) | copy-done | bytes 2228248
  40.2 0.1 add.203
  40.4 0.1 mul.68
  40.6 3.2 %gather_fusion.1 = bf16[1024,128]{1,0:T(8,128)(2,1)S(1)} fusion(bf16[512,128]{1,0:T(8,128)(2,1)S(1)} %constant_dynamic-slice_fusion.8, s32[1024]{0:T(1024)S(1)} %broadcast_clamp_fusion), kind=kCustom, calls=%fused_computation.1 | custom fusion | bytes 528384 | tf_op jit(solution)/shard_map/jit(_take)/gather | solution.py:151
  43.9 0.2 broadcast_select_fusion
  44.1 0.1 copy.213
  44.3 0.8 copy-done.5
  45.0 0.8 bitcast_dynamic-update-slice_fusion.3
  45.9 1.6 %collective-permute-start.8 = (bf16[16,16512]{1,0:T(8,128)(2,1)}, bf16[16,16512]{1,0:T(8,128)(2,1)S(1)}, u32[]{:S(2)}, u32[]{:S(2)}) collective-permute-start(bf16[16,16512]{1,0:T(8,128)(2,1)} %copy-done.5), channel_id=1, source_target_pairs={{0,8},{8,16},{16,24},{24,28},{28,20},{20,12},{12,4},{4,0},{1,9},{9... | collective-permute-start | bytes 1585160 | tf_op jit(solution)/shard_map/ppermute | solution.py:28
  47.4 0.4 collective-permute-start.9
  47.9 1.9 %bitcast_dynamic-update-slice_fusion.2 = bf16[8,16,16512]{2,1,0:T(8,128)(2,1)} fusion(bf16[8,16,16512]{2,1,0:T(8,128)(2,1)} %bitcast_dynamic-update-slice_fusion.3, bf16[16,16512]{1,0:T(8,128)(2,1)} %collective-permute-done.7), kind=kLoop, calls=%fused_computation.26 | loop fusion | bytes 1056768
  49.8 2.3 %convert_bitcast_fusion = bf16[4,2,1024,128]{2,3,1,0:T(8,128)(2,1)S(1)} fusion(bf16[4,272,1024]{2,1,0:T(8,128)(2,1)} %copy-done.3, bf16[4,2,256]{2,1,0:T(2,128)(2,1)S(1)} %mul.68, bf16[4,256,128]{1,2,0:T(8,128)(2,1)S(1)} %copy.213), kind=kOutput, calls=%fused_computation.10 | convolution fusion | flops 538181632 | bytes 4460544 | tf_op jit(solution)/shard_map/bkr,bhkl->bhrl/dot_general | solution.py:156
  52.1 2.6 %copy.214 = bf16[4,2,1024,128]{3,2,1,0:T(8,128)(2,1)} copy(bf16[4,2,1024,128]{2,3,1,0:T(8,128)(2,1)S(1)} %convert_bitcast_fusion) | data formatting | bytes 4194304 | tf_op jit(solution)/shard_map/convert_element_type | solution.py:158
  54.8 4.3 %collective-permute-done.8 = bf16[16,16512]{1,0:T(8,128)(2,1)S(1)} collective-permute-done((bf16[16,16512]{1,0:T(8,128)(2,1)}, bf16[16,16512]{1,0:T(8,128)(2,1)S(1)}, u32[]{:S(2)}, u32[]{:S(2)}) %collective-permute-start.8) | collective-permute-done | bytes 528416 | tf_op jit(solution)/shard_map/ppermute | solution.py:28
  59.1 0.9 collective-permute-done.9
  60.0 1.0 slice.88
  61.0 1.0 %collective-permute-start.11 = (bf16[8,16512]{1,0:T(8,128)(2,1)S(1)}, bf16[8,16512]{1,0:T(8,128)(2,1)S(1)}, u32[]{:S(2)}, u32[]{:S(2)}) collective-permute-start(bf16[8,16512]{1,0:T(8,128)(2,1)S(1)} %slice.88), channel_id=1, source_target_pairs={{0,4},{8,0},{16,8},{24,16},{28,24},{20,28},{12,20},{4,12},{1,5},{9... | collective-permute-start | bytes 792584 | tf_op jit(solution)/shard_map/ppermute | solution.py:34
  62.0 1.3 %collective-permute-start.10 = (bf16[8,16512]{1,0:T(8,128)(2,1)S(1)}, bf16[8,16512]{1,0:T(8,128)(2,1)S(1)}, u32[]{:S(2)}, u32[]{:S(2)}) collective-permute-start(bf16[8,16512]{1,0:T(8,128)(2,1)S(1)} %slice.87), channel_id=1, source_target_pairs={{0,8},{8,16},{16,24},{24,28},{28,20},{20,12},{12,4},{4,0},{1,9},{9... | collective-permute-start | bytes 792584 | tf_op jit(solution)/shard_map/ppermute | solution.py:33
  63.3 5.1 %copy.216 = bf16[16,128,4,2,64]{4,1,3,2,0:T(8,128)(2,1)} copy(bf16[16,128,4,2,64]{1,0,4,3,2:T(8,128)(2,1)} %bitcast.95) | data formatting | bytes 4194304 | tf_op jit(solution)/shard_map/dot_general | solution.py:167
  68.4 0.8 bitcast_dynamic-update-slice_fusion.1
  69.2 1.9 %bitcast_dynamic-update-slice_fusion = bf16[8,16,16512]{2,1,0:T(8,128)(2,1)} fusion(bf16[8,16,16512]{2,1,0:T(8,128)(2,1)} %bitcast_dynamic-update-slice_fusion.1, bf16[16,16512]{1,0:T(8,128)(2,1)} %collective-permute-done.9), kind=kLoop, calls=%fused_computation.24 | loop fusion | bytes 1056768
  71.1 6.1 %fusion = f32[16,16,8,4,128,1,1]{4,2,6,5,3,1,0:T(8,128)} fusion(bf16[4,128,4,2,64,1,1]{4,3,2,1,0,6,5:T(2,128)(2,1)S(1)} %bitcast.101, bf16[16,128,4,2,64]{4,1,3,2,0:T(8,128)(2,1)} %copy.216), kind=kOutput, calls=%fused_computation.5 | convolution fusion | flops 1073741824 | bytes 6815744 | tf_op jit(solution)/shard_map/dot_general | solution.py:167
  77.2 0.8 fusion.12
  78.0 0.7 slice.89
  78.8 0.1 copy.233
  78.9 0.7 copy.220.refs_0_
  79.5 12.4 %shard_map.109 = f32[1,16,128]{2,1,0:T(8,128)} custom-call(s32[8,4]{1,0:T(8,128)} %copy.220.refs_0_, f32[8192,128]{1,0:T(8,128)} %bitcast.97, bf16[128,16512]{1,0:T(8,128)(2,1)} %bitcast.96), custom_call_target="tpu_custom_call" | custom-call | tf_op jit(solution)/shard_map/pallas_call | solution.py:107
  91.9 0.8 reshape_reshape_transpose.3
  92.7 0.6 gather_fusion.3
  93.3 0.1 gather.26
  93.6 0.4 collective-permute-start.12
  94.0 0.8 collective-permute-done.14
  94.8 2.3 %collective-permute-done.13 = f32[4,128]{1,0:T(4,128)S(1)} collective-permute-done((f32[4,128]{1,0:T(4,128)S(1)}, f32[4,128]{1,0:T(4,128)S(1)}, u32[]{:S(2)}, u32[]{:S(2)}) %collective-permute-start.13) | collective-permute-done | bytes 2080 | tf_op jit(solution)/shard_map/ppermute | solution.py:183
  97.2 0.6 fusion.19
  (68 shorter events, 1.1 us)
Async XLA Ops:
  0.0 25.8 %copy-start = (bf16[512,512]{1,0:T(8,128)(2,1)S(1)}, bf16[512,512]{1,0:T(8,128)(2,1)}, u32[]{:S(2)}) copy-start(bf16[512,512]{1,0:T(8,128)(2,1)} %param.18) | copy-start | bytes 1572868
  8.3 17.5 %collective-permute-start = (bf16[16,16512]{1,0:T(8,128)(2,1)}, bf16[16,16512]{1,0:T(8,128)(2,1)}, u32[]{:S(2)}, u32[]{:S(2)}) collective-permute-start(bf16[16,16512]{1,0:T(8,128)(2,1)} %fusion.11), channel_id=1, source_target_pairs={{0,8},{8,16},{16,24},{24,28},{28,20},{20,12},{12,4},{4,0},{1,9},{9... | collective-permute-start | bytes 1585160 | tf_op jit(solution)/shard_map/ppermute | solution.py:28
  11.4 18.5 %collective-permute-start.1 = (bf16[16,16512]{1,0:T(8,128)(2,1)}, bf16[16,16512]{1,0:T(8,128)(2,1)}, u32[]{:S(2)}, u32[]{:S(2)}) collective-permute-start(bf16[16,16512]{1,0:T(8,128)(2,1)} %fusion.11), channel_id=1, source_target_pairs={{0,4},{8,0},{16,8},{24,16},{28,24},{20,28},{12,20},{4,12},{1,5},{9... | collective-permute-start | bytes 1585160 | tf_op jit(solution)/shard_map/ppermute | solution.py:29
  12.0 4.1 %copy-start.10 = (s32[8]{0:T(128)S(1)}, s32[8]{0:T(128)}, u32[]{:S(2)}) copy-start(s32[8]{0:T(128)} %constant.193.clone) | copy-start | bytes 100
  12.1 4.7 %copy-start.9 = (s32[8]{0:T(128)S(1)}, s32[8]{0:T(128)}, u32[]{:S(2)}) copy-start(s32[8]{0:T(128)} %constant.195.clone) | copy-start | bytes 100
  12.1 5.3 %copy-start.2 = (s32[8]{0:T(128)S(1)}, s32[8]{0:T(128)}, u32[]{:S(2)}) copy-start(s32[8]{0:T(128)} %constant.194.clone) | copy-start | bytes 100
  12.1 6.6 %copy-start.8 = (s32[4]{0:T(128)S(1)}, s32[4]{0:T(128)}, u32[]{:S(2)}) copy-start(s32[4]{0:T(128)} %constant.196.clone) | copy-start | bytes 52
  12.1 7.2 %copy-start.7 = (s32[4]{0:T(128)S(1)}, s32[4]{0:T(128)}, u32[]{:S(2)}) copy-start(s32[4]{0:T(128)} %constant.198.clone) | copy-start | bytes 52
  12.1 7.8 %copy-start.1 = (s32[4]{0:T(128)S(1)}, s32[4]{0:T(128)}, u32[]{:S(2)}) copy-start(s32[4]{0:T(128)} %constant.197.clone) | copy-start | bytes 52
  13.2 10.7 %copy-start.6 = (bf16[512,512]{1,0:T(8,128)(2,1)S(1)}, bf16[512,512]{1,0:T(8,128)(2,1)}, u32[]{:S(2)}) copy-start(bf16[512,512]{1,0:T(8,128)(2,1)} %param.19) | copy-start | bytes 1572868
  13.2 16.6 %collective-permute-start.3 = (bf16[272,1024]{1,0:T(8,128)(2,1)}, bf16[272,1024]{1,0:T(8,128)(2,1)S(1)}, u32[]{:S(2)}, u32[]{:S(2)}) collective-permute-start(bf16[272,1024]{1,0:T(8,128)(2,1)} %get-tuple-element.44), channel_id=1, source_target_pairs={{0,1},{2,0},{3,2},{1,3},{4,5},{6,4},{7,6},{5,7},{8,9},{10,8},{11,1... | collective-permute-start | bytes 1671176 | tf_op jit(solution)/shard_map/ppermute | solution.py:29
  13.2 16.7 %collective-permute-start.2 = (bf16[272,1024]{1,0:T(8,128)(2,1)}, bf16[272,1024]{1,0:T(8,128)(2,1)S(1)}, u32[]{:S(2)}, u32[]{:S(2)}) collective-permute-start(bf16[272,1024]{1,0:T(8,128)(2,1)} %get-tuple-element.44), channel_id=1, source_target_pairs={{0,2},{2,3},{3,1},{1,0},{4,6},{6,7},{7,5},{5,4},{8,10},{10,11},{11... | collective-permute-start | bytes 1671176 | tf_op jit(solution)/shard_map/ppermute | solution.py:28
  25.9 18.3 %collective-permute-start.6 = (bf16[16,16512]{1,0:T(8,128)(2,1)}, bf16[16,16512]{1,0:T(8,128)(2,1)S(1)}, u32[]{:S(2)}, u32[]{:S(2)}) collective-permute-start(bf16[16,16512]{1,0:T(8,128)(2,1)} %collective-permute-done), channel_id=1, source_target_pairs={{0,8},{8,16},{16,24},{24,28},{28,20},{20,12},{12,4},{4,0},{1,9},{9... | collective-permute-start | bytes 1585160 | tf_op jit(solution)/shard_map/ppermute | solution.py:28
  29.9 14.4 %collective-permute-start.7 = (bf16[16,16512]{1,0:T(8,128)(2,1)}, bf16[16,16512]{1,0:T(8,128)(2,1)}, u32[]{:S(2)}, u32[]{:S(2)}) collective-permute-start(bf16[16,16512]{1,0:T(8,128)(2,1)} %collective-permute-done.1), channel_id=1, source_target_pairs={{0,4},{8,0},{16,8},{24,16},{28,24},{20,28},{12,20},{4,12},{1,5},{9... | collective-permute-start | bytes 1585160 | tf_op jit(solution)/shard_map/ppermute | solution.py:29
  29.9 8.4 %collective-permute-start.5 = (bf16[136,1024]{1,0:T(8,128)(2,1)S(1)}, bf16[136,1024]{1,0:T(8,128)(2,1)S(1)}, u32[]{:S(2)}, u32[]{:S(2)}) collective-permute-start(bf16[136,1024]{1,0:T(8,128)(2,1)S(1)} %slice.85), channel_id=1, source_target_pairs={{0,1},{2,0},{3,2},{1,3},{4,5},{6,4},{7,6},{5,7},{8,9},{10,8},{11,1... | collective-permute-start | bytes 835592 | tf_op jit(solution)/shard_map/ppermute | solution.py:34
  30.0 8.4 %collective-permute-start.4 = (bf16[136,1024]{1,0:T(8,128)(2,1)S(1)}, bf16[136,1024]{1,0:T(8,128)(2,1)S(1)}, u32[]{:S(2)}, u32[]{:S(2)}) collective-permute-start(bf16[136,1024]{1,0:T(8,128)(2,1)S(1)} %slice.84), channel_id=1, source_target_pairs={{0,2},{2,3},{3,1},{1,0},{4,6},{6,7},{7,5},{5,4},{8,10},{10,11},{11... | collective-permute-start | bytes 835592 | tf_op jit(solution)/shard_map/ppermute | solution.py:33
  38.7 1.4 %copy-start.3 = (bf16[4,272,1024]{2,1,0:T(8,128)(2,1)}, bf16[4,272,1024]{2,1,0:T(8,128)(2,1)S(1)}, u32[]{:S(2)}) copy-start(bf16[4,272,1024]{2,1,0:T(8,128)(2,1)S(1)} %pad_maximum_fusion) | copy-start | bytes 6684676
  44.2 0.8 copy-start.5
  45.9 13.2 %collective-permute-start.8 = (bf16[16,16512]{1,0:T(8,128)(2,1)}, bf16[16,16512]{1,0:T(8,128)(2,1)S(1)}, u32[]{:S(2)}, u32[]{:S(2)}) collective-permute-start(bf16[16,16512]{1,0:T(8,128)(2,1)} %copy-done.5), channel_id=1, source_target_pairs={{0,8},{8,16},{16,24},{24,28},{28,20},{20,12},{12,4},{4,0},{1,9},{9... | collective-permute-start | bytes 1585160 | tf_op jit(solution)/shard_map/ppermute | solution.py:28
  47.4 12.5 %collective-permute-start.9 = (bf16[16,16512]{1,0:T(8,128)(2,1)}, bf16[16,16512]{1,0:T(8,128)(2,1)}, u32[]{:S(2)}, u32[]{:S(2)}) collective-permute-start(bf16[16,16512]{1,0:T(8,128)(2,1)} %collective-permute-done.7), channel_id=1, source_target_pairs={{0,4},{8,0},{16,8},{24,16},{28,24},{20,28},{12,20},{4,12},{1,5},{9... | collective-permute-start | bytes 1585160 | tf_op jit(solution)/shard_map/ppermute | solution.py:29
  61.0 16.3 %collective-permute-start.11 = (bf16[8,16512]{1,0:T(8,128)(2,1)S(1)}, bf16[8,16512]{1,0:T(8,128)(2,1)S(1)}, u32[]{:S(2)}, u32[]{:S(2)}) collective-permute-start(bf16[8,16512]{1,0:T(8,128)(2,1)S(1)} %slice.88), channel_id=1, source_target_pairs={{0,4},{8,0},{16,8},{24,16},{28,24},{20,28},{12,20},{4,12},{1,5},{9... | collective-permute-start | bytes 792584 | tf_op jit(solution)/shard_map/ppermute | solution.py:34
  62.0 15.3 %collective-permute-start.10 = (bf16[8,16512]{1,0:T(8,128)(2,1)S(1)}, bf16[8,16512]{1,0:T(8,128)(2,1)S(1)}, u32[]{:S(2)}, u32[]{:S(2)}) collective-permute-start(bf16[8,16512]{1,0:T(8,128)(2,1)S(1)} %slice.87), channel_id=1, source_target_pairs={{0,8},{8,16},{16,24},{24,28},{28,20},{20,12},{12,4},{4,0},{1,9},{9... | collective-permute-start | bytes 792584 | tf_op jit(solution)/shard_map/ppermute | solution.py:33
  63.3 7.8 %copy-start.4 = (bf16[4,128,4,2,64]{4,3,2,1,0:T(2,128)(2,1)S(1)}, bf16[4,128,4,2,64]{4,3,2,1,0:T(2,128)(2,1)}, u32[]{:S(2)}) copy-start(bf16[4,128,4,2,64]{4,3,2,1,0:T(2,128)(2,1)} %reshape.256) | copy-start | bytes 1572868
  93.4 1.4 %collective-permute-start.14 = (f32[4,128]{1,0:T(4,128)S(1)}, f32[4,128]{1,0:T(4,128)S(1)}, u32[]{:S(2)}, u32[]{:S(2)}) collective-permute-start(f32[4,128]{1,0:T(4,128)S(1)} %get-tuple-element.50), channel_id=1, source_target_pairs={{0,3},{1,0},{2,1},{3,2},{4,7},{5,4},{6,5},{7,6},{8,11},{9,8},{10,9... | collective-permute-start | bytes 6152 | tf_op jit(solution)/shard_map/ppermute | solution.py:183
  93.5 3.7 %collective-permute-start.13 = (f32[4,128]{1,0:T(4,128)S(1)}, f32[4,128]{1,0:T(4,128)S(1)}, u32[]{:S(2)}, u32[]{:S(2)}) collective-permute-start(f32[4,128]{1,0:T(4,128)S(1)} %get-tuple-element.51), channel_id=1, source_target_pairs={{0,2},{1,3},{2,0},{3,1},{4,6},{5,7},{6,4},{7,5},{8,10},{9,11},{10,... | collective-permute-start | bytes 6152 | tf_op jit(solution)/shard_map/ppermute | solution.py:183
  93.6 3.6 %collective-permute-start.12 = (f32[4,128]{1,0:T(4,128)S(1)}, f32[4,128]{1,0:T(4,128)S(1)}, u32[]{:S(2)}, u32[]{:S(2)}) collective-permute-start(f32[4,128]{1,0:T(4,128)S(1)} %get-tuple-element.49), channel_id=1, source_target_pairs={{0,1},{1,2},{2,3},{3,0},{4,5},{5,6},{6,7},{7,4},{8,9},{9,10},{10,1... | collective-permute-start | bytes 6152 | tf_op jit(solution)/shard_map/ppermute | solution.py:183

commit v16 on v14

--- a/solution.py
+++ b/solution.py
@@ -29,10 +29,10 @@
         behind = lax.ppermute(behind, axis, bwd)
         got += [ahead, behind]
         shifts += [-step, step]
-    rows = buf.shape[0] // 2
-    first = lax.ppermute(ahead[:rows], axis, fwd)
-    second = lax.ppermute(behind[rows:], axis, bwd)
-    got.append(jnp.concatenate([first, second], axis=0))
+    cols = (buf.shape[1] // 256) * 128
+    first = lax.ppermute(ahead[:, :cols], axis, fwd)
+    second = lax.ppermute(behind[:, cols:], axis, bwd)
+    got.append(jnp.concatenate([first, second], axis=1))
     shifts.append(count // 2)
     sources = order_arr[(pos + jnp.array(shifts, jnp.int32)) % count]
     return sources, got

time: 97.6 us -> 98 us (level)
  transfers between devices with their start and end apart: 15 -> 15, of which waited for: 5 -> 5; matrix products, arithmetic and copies ran while one was open for 40% -> 41% of each run, Pallas kernels for 0% -> 0%
where the time goes in v16:
time: 98 us; the launch traced here: 97.3 us
  local copies, waits for them, and re-layouts  39.4 us (40%)
  starting transfers between devices  14.2 us (14%)
  waiting for transfers between devices  12.6 us (13%)
  Pallas kernels  11.5 us (12%)
  matrix products  8.43 us (9%)
  other arithmetic  7.47 us (8%)
  between operations  3.68 us (4%)
    unnamed x29, local copies, waits for them, and re-layouts  12.1 us
    pallas_call x1, Pallas kernels, contract(): pl.pallas_call(body, out_shape=jax.ShapeDtypeStruct((steps, ri, chunk * r...  11.5 us
    ppermute x4, starting transfers between devices, ring_gather(): ahead = lax.ppermute(ahead, axis, fwd)  8.7 us
    dot_general x2, local copies, waits for them, and re-layouts, on_device(): lax.dot_general(occ_raw, virt_cols, (((0, 1, 2), (1, 2, 3)), ((), ())), p...  6.61 us
    dot_general x1, matrix products, on_device(): lax.dot_general(occ_raw, virt_cols, (((0, 1, 2), (1, 2, 3)), ((), ())), p...  6.13 us
    ppermute x2, waiting for transfers between devices, ring_gather(): second = lax.ppermute(behind[:, cols:], axis, bwd)  4.45 us
    ppermute x4, waiting for transfers between devices, ring_gather(): ahead = lax.ppermute(ahead, axis, fwd)  4.42 us
    squeeze x2, local copies, waits for them, and re-layouts, on_device(): local_blocks = x_blocks[0]  3.93 us
  transfers between devices with their start and end apart: 15, of which 5 were waited for; matrix products, arithmetic and copies ran while one was open for 41% of the time, Pallas kernels for 0%

profile of v16, /device:TPU:0, one launch (start us, length us, event | category | flops | bytes accessed | tf_op | source)
XLA Modules:
  0.0 97.3 jit_solution(2705500281194158452)
XLA Ops:
  0.0 0.7 convert_bitcast_fusion.2
  0.7 1.8 %squeeze.33 = bf16[4,64,16,64]{3,2,1,0:T(8,128)(2,1)S(1)} reshape(bf16[1,4,64,1024]{3,2,1,0:T(8,128)(2,1)} %param.15) | data formatting | bytes 1048576 | tf_op jit(solution)/shard_map/squeeze | solution.py:113
  2.5 2.2 %copy.210 = bf16[4,64,16,64]{1,0,2,3:T(4,128)(2,1)S(1)} copy(bf16[4,64,16,64]{3,2,1,0:T(8,128)(2,1)S(1)} %squeeze.33) | data formatting | bytes 1048576 | tf_op jit(solution)/shard_map/squeeze | solution.py:113
  5.3 0.6 multiply_bitcast_fusion
  5.9 0.7 copy.211
  6.6 0.8 reshape.204
  7.5 0.9 fusion.11
  8.3 3.0 %collective-permute-start = (bf16[16,16512]{1,0:T(8,128)(2,1)}, bf16[16,16512]{1,0:T(8,128)(2,1)}, u32[]{:S(2)}, u32[]{:S(2)}) collective-permute-start(bf16[16,16512]{1,0:T(8,128)(2,1)} %fusion.11), channel_id=1, source_target_pairs={{0,8},{8,16},{16,24},{24,28},{28,20},{20,12},{12,4},{4,0},{1,9},{9... | collective-permute-start | bytes 1585160 | tf_op jit(solution)/shard_map/ppermute | solution.py:28
  11.4 0.7 reshape.205
  12.1 0.2 copy.212
  12.3 0.9 fusion.33
  13.2 2.0 %collective-permute-start.2 = (bf16[272,1024]{1,0:T(8,128)(2,1)}, bf16[272,1024]{1,0:T(8,128)(2,1)S(1)}, u32[]{:S(2)}, u32[]{:S(2)}) collective-permute-start(bf16[272,1024]{1,0:T(8,128)(2,1)} %get-tuple-element.44), channel_id=1, source_target_pairs={{0,2},{2,3},{3,1},{1,0},{4,6},{6,7},{7,5},{5,4},{8,10},{10,11},{11... | collective-permute-start | bytes 1671176 | tf_op jit(solution)/shard_map/ppermute | solution.py:28
  15.3 0.9 bitcast_dynamic-update-slice_fusion.6
  16.1 0.6 dynamic_slice.34
  16.7 0.7 compare_select_fusion.7
  17.4 0.6 gather_fusion
  18.1 0.6 scatter_custom_fusion
  18.7 0.6 dynamic_slice.36
  19.3 0.7 compare_select_fusion.4
  20.0 0.6 gather_fusion.2
  20.6 0.7 fusion.34
  24.0 0.1 constant_dynamic-slice_fusion.7
  24.1 1.5 %reshape.256 = bf16[4,128,4,2,64]{4,3,2,1,0:T(2,128)(2,1)} reshape(bf16[512,512]{1,0:T(8,128)(2,1)S(1)} %pad_maximum_fusion.1) | data formatting | bytes 1048576 | tf_op jit(solution)/shard_map/dot_general | solution.py:166
  25.7 0.1 broadcast_in_dim.43
  25.9 2.1 %collective-permute-start.6 = (bf16[16,16512]{1,0:T(8,128)(2,1)}, bf16[16,16512]{1,0:T(8,128)(2,1)}, u32[]{:S(2)}, u32[]{:S(2)}) collective-permute-start(bf16[16,16512]{1,0:T(8,128)(2,1)} %collective-permute-done), channel_id=1, source_target_pairs={{0,8},{8,16},{16,24},{24,28},{28,20},{20,12},{12,4},{4,0},{1,9},{9... | collective-permute-start | bytes 1585160 | tf_op jit(solution)/shard_map/ppermute | solution.py:28
  28.0 1.9 %bitcast_dynamic-update-slice_fusion.5 = bf16[8,16,16512]{2,1,0:T(8,128)(2,1)} fusion(bf16[8,16,16512]{2,1,0:T(8,128)(2,1)} %bitcast_dynamic-update-slice_fusion.6, bf16[16,16512]{1,0:T(8,128)(2,1)} %collective-permute-done), kind=kLoop, calls=%fused_computation.29 | loop fusion | bytes 1056768
  30.0 2.0 %collective-permute-start.4 = (bf16[272,512]{1,0:T(8,128)(2,1)S(1)}, bf16[272,512]{1,0:T(8,128)(2,1)S(1)}, u32[]{:S(2)}, u32[]{:S(2)}) collective-permute-start(bf16[272,512]{1,0:T(8,128)(2,1)S(1)} %slice.84), channel_id=1, source_target_pairs={{0,2},{2,3},{3,1},{1,0},{4,6},{6,7},{7,5},{5,4},{8,10},{10,11},{11... | collective-permute-start | bytes 835592 | tf_op jit(solution)/shard_map/ppermute | solution.py:33
  32.0 1.9 %bitcast_dynamic-update-slice_fusion.4 = bf16[8,16,16512]{2,1,0:T(8,128)(2,1)} fusion(bf16[8,16,16512]{2,1,0:T(8,128)(2,1)} %bitcast_dynamic-update-slice_fusion.5, bf16[16,16512]{1,0:T(8,128)(2,1)} %collective-permute-done.1), kind=kLoop, calls=%fused_computation.28 | loop fusion | bytes 1056768
  33.9 4.4 %collective-permute-done.5 = bf16[272,512]{1,0:T(8,128)(2,1)S(1)} collective-permute-done((bf16[272,512]{1,0:T(8,128)(2,1)S(1)}, bf16[272,512]{1,0:T(8,128)(2,1)S(1)}, u32[]{:S(2)}, u32[]{:S(2)}) %collective-permute-start.5) | collective-permute-done | bytes 278560 | tf_op jit(solution)/shard_map/ppermute | solution.py:34
  38.4 0.3 pad_maximum_fusion
  38.7 1.4 %copy-done.3 = bf16[4,272,1024]{2,1,0:T(8,128)(2,1)} copy-done((bf16[4,272,1024]{2,1,0:T(8,128)(2,1)}, bf16[4,272,1024]{2,1,0:T(8,128)(2,1)S(1)}, u32[]{:S(2)}) %copy-start.3) | copy-done | bytes 2228248
  40.2 0.1 add.203
  40.4 0.1 mul.68
  40.6 3.2 %gather_fusion.1 = bf16[1024,128]{1,0:T(8,128)(2,1)S(1)} fusion(bf16[512,128]{1,0:T(8,128)(2,1)S(1)} %constant_dynamic-slice_fusion.8, s32[1024]{0:T(1024)S(1)} %broadcast_clamp_fusion), kind=kCustom, calls=%fused_computation.1 | custom fusion | bytes 528384 | tf_op jit(solution)/shard_map/jit(_take)/gather | solution.py:150
  43.9 0.2 broadcast_select_fusion
  44.1 0.1 copy.213
  44.3 2.1 %bitcast_dynamic-update-slice_fusion.3 = bf16[8,16,16512]{2,1,0:T(8,128)(2,1)} fusion(bf16[8,16,16512]{2,1,0:T(8,128)(2,1)} %bitcast_dynamic-update-slice_fusion.4, bf16[16,16512]{1,0:T(8,128)(2,1)} %collective-permute-done.6), kind=kLoop, calls=%fused_computation.27 | loop fusion | bytes 1056768
  46.3 1.6 %collective-permute-start.8 = (bf16[16,16512]{1,0:T(8,128)(2,1)}, bf16[16,16512]{1,0:T(8,128)(2,1)}, u32[]{:S(2)}, u32[]{:S(2)}) collective-permute-start(bf16[16,16512]{1,0:T(8,128)(2,1)} %collective-permute-done.6), channel_id=1, source_target_pairs={{0,8},{8,16},{16,24},{24,28},{28,20},{20,12},{12,4},{4,0},{1,9},{9... | collective-permute-start | bytes 1585160 | tf_op jit(solution)/shard_map/ppermute | solution.py:28
  47.9 0.4 collective-permute-start.9
  48.4 1.9 %bitcast_dynamic-update-slice_fusion.2 = bf16[8,16,16512]{2,1,0:T(8,128)(2,1)} fusion(bf16[8,16,16512]{2,1,0:T(8,128)(2,1)} %bitcast_dynamic-update-slice_fusion.3, bf16[16,16512]{1,0:T(8,128)(2,1)} %copy-done.5), kind=kLoop, calls=%fused_computation.26 | loop fusion | bytes 1056768
  50.3 2.3 %convert_bitcast_fusion = bf16[4,2,1024,128]{2,3,1,0:T(8,128)(2,1)S(1)} fusion(bf16[4,272,1024]{2,1,0:T(8,128)(2,1)} %copy-done.3, bf16[4,2,256]{2,1,0:T(2,128)(2,1)S(1)} %mul.68, bf16[4,256,128]{1,2,0:T(8,128)(2,1)S(1)} %copy.213), kind=kOutput, calls=%fused_computation.10 | convolution fusion | flops 538181632 | bytes 4460544 | tf_op jit(solution)/shard_map/bkr,bhkl->bhrl/dot_general | solution.py:155
  52.6 2.6 %copy.214 = bf16[4,2,1024,128]{3,2,1,0:T(8,128)(2,1)} copy(bf16[4,2,1024,128]{2,3,1,0:T(8,128)(2,1)S(1)} %convert_bitcast_fusion) | data formatting | bytes 4194304 | tf_op jit(solution)/shard_map/convert_element_type | solution.py:157
  55.2 4.4 %collective-permute-done.8 = bf16[16,16512]{1,0:T(8,128)(2,1)} collective-permute-done((bf16[16,16512]{1,0:T(8,128)(2,1)}, bf16[16,16512]{1,0:T(8,128)(2,1)}, u32[]{:S(2)}, u32[]{:S(2)}) %collective-permute-start.8) | collective-permute-done | bytes 528416 | tf_op jit(solution)/shard_map/ppermute | solution.py:28
  59.7 0.7 collective-permute-done.9
  60.4 1.0 %collective-permute-start.11 = (bf16[16,8320]{1,0:T(8,128)(2,1)S(1)}, bf16[16,8320]{1,0:T(8,128)(2,1)S(1)}, u32[]{:S(2)}, u32[]{:S(2)}) collective-permute-start(bf16[16,8320]{1,0:T(8,128)(2,1)S(1)} %slice.88), channel_id=1, source_target_pairs={{0,4},{8,0},{16,8},{24,16},{28,24},{20,28},{12,20},{4,12},{1,5},{9... | collective-permute-start | bytes 798728 | tf_op jit(solution)/shard_map/ppermute | solution.py:34
  61.4 1.0 slice.87
  62.3 1.3 %collective-permute-start.10 = (bf16[16,8192]{1,0:T(8,128)(2,1)S(1)}, bf16[16,8192]{1,0:T(8,128)(2,1)S(1)}, u32[]{:S(2)}, u32[]{:S(2)}) collective-permute-start(bf16[16,8192]{1,0:T(8,128)(2,1)S(1)} %slice.87), channel_id=1, source_target_pairs={{0,8},{8,16},{16,24},{24,28},{28,20},{20,12},{12,4},{4,0},{1,9},{9... | collective-permute-start | bytes 786440 | tf_op jit(solution)/shard_map/ppermute | solution.py:33
  63.7 5.1 %copy.216 = bf16[16,128,4,2,64]{4,1,3,2,0:T(8,128)(2,1)} copy(bf16[16,128,4,2,64]{1,0,4,3,2:T(8,128)(2,1)} %bitcast.95) | data formatting | bytes 4194304 | tf_op jit(solution)/shard_map/dot_general | solution.py:166
  68.7 1.9 %bitcast_dynamic-update-slice_fusion.1 = bf16[8,16,16512]{2,1,0:T(8,128)(2,1)} fusion(bf16[8,16,16512]{2,1,0:T(8,128)(2,1)} %bitcast_dynamic-update-slice_fusion.2, bf16[16,16512]{1,0:T(8,128)(2,1)} %collective-permute-done.8), kind=kLoop, calls=%fused_computation.25 | loop fusion | bytes 1056768
  70.6 0.8 bitcast_dynamic-update-slice_fusion
  71.5 6.1 %fusion = f32[16,16,8,4,128,1,1]{4,2,6,5,3,1,0:T(8,128)} fusion(bf16[4,128,4,2,64,1,1]{4,3,2,1,0,6,5:T(2,128)(2,1)S(1)} %bitcast.101, bf16[16,128,4,2,64]{4,1,3,2,0:T(8,128)(2,1)} %copy.216), kind=kOutput, calls=%fused_computation.5 | convolution fusion | flops 1073741824 | bytes 6815744 | tf_op jit(solution)/shard_map/dot_general | solution.py:166
  77.6 0.8 fusion.12
  78.4 0.7 slice.89
  79.1 0.1 copy.233
  79.3 0.7 copy.220.refs_0_
  79.9 11.5 %shard_map.109 = f32[1,16,128]{2,1,0:T(8,128)} custom-call(s32[8,4]{1,0:T(8,128)} %copy.220.refs_0_, f32[8192,128]{1,0:T(8,128)} %bitcast.97, bf16[128,16512]{1,0:T(8,128)(2,1)} %bitcast.96), custom_call_target="tpu_custom_call" | custom-call | tf_op jit(solution)/shard_map/pallas_call | solution.py:106
  91.5 0.8 reshape_reshape_transpose.3
  92.3 0.6 gather_fusion.3
  92.8 0.1 gather.26
  93.0 0.5 collective-permute-start.13
  93.5 0.2 collective-permute-start.12
  93.7 0.7 collective-permute-done.14
  94.3 2.3 %collective-permute-done.13 = f32[4,128]{1,0:T(4,128)S(1)} collective-permute-done((f32[4,128]{1,0:T(4,128)S(1)}, f32[4,128]{1,0:T(4,128)S(1)}, u32[]{:S(2)}, u32[]{:S(2)}) %collective-permute-start.13) | collective-permute-done | bytes 2080 | tf_op jit(solution)/shard_map/ppermute | solution.py:182
  96.7 0.6 fusion.19
  (68 shorter events, 1.0 us)
Async XLA Ops:
  0.0 25.8 %copy-start = (bf16[512,512]{1,0:T(8,128)(2,1)S(1)}, bf16[512,512]{1,0:T(8,128)(2,1)}, u32[]{:S(2)}) copy-start(bf16[512,512]{1,0:T(8,128)(2,1)} %param.18) | copy-start | bytes 1572868
  8.3 17.5 %collective-permute-start = (bf16[16,16512]{1,0:T(8,128)(2,1)}, bf16[16,16512]{1,0:T(8,128)(2,1)}, u32[]{:S(2)}, u32[]{:S(2)}) collective-permute-start(bf16[16,16512]{1,0:T(8,128)(2,1)} %fusion.11), channel_id=1, source_target_pairs={{0,8},{8,16},{16,24},{24,28},{28,20},{20,12},{12,4},{4,0},{1,9},{9... | collective-permute-start | bytes 1585160 | tf_op jit(solution)/shard_map/ppermute | solution.py:28
  11.4 18.5 %collective-permute-start.1 = (bf16[16,16512]{1,0:T(8,128)(2,1)}, bf16[16,16512]{1,0:T(8,128)(2,1)}, u32[]{:S(2)}, u32[]{:S(2)}) collective-permute-start(bf16[16,16512]{1,0:T(8,128)(2,1)} %fusion.11), channel_id=1, source_target_pairs={{0,4},{8,0},{16,8},{24,16},{28,24},{20,28},{12,20},{4,12},{1,5},{9... | collective-permute-start | bytes 1585160 | tf_op jit(solution)/shard_map/ppermute | solution.py:29
  12.0 4.1 %copy-start.10 = (s32[8]{0:T(128)S(1)}, s32[8]{0:T(128)}, u32[]{:S(2)}) copy-start(s32[8]{0:T(128)} %constant.193.clone) | copy-start | bytes 100
  12.1 4.7 %copy-start.9 = (s32[8]{0:T(128)S(1)}, s32[8]{0:T(128)}, u32[]{:S(2)}) copy-start(s32[8]{0:T(128)} %constant.195.clone) | copy-start | bytes 100
  12.1 5.3 %copy-start.2 = (s32[8]{0:T(128)S(1)}, s32[8]{0:T(128)}, u32[]{:S(2)}) copy-start(s32[8]{0:T(128)} %constant.194.clone) | copy-start | bytes 100
  12.1 6.6 %copy-start.8 = (s32[4]{0:T(128)S(1)}, s32[4]{0:T(128)}, u32[]{:S(2)}) copy-start(s32[4]{0:T(128)} %constant.196.clone) | copy-start | bytes 52
  12.1 7.2 %copy-start.7 = (s32[4]{0:T(128)S(1)}, s32[4]{0:T(128)}, u32[]{:S(2)}) copy-start(s32[4]{0:T(128)} %constant.198.clone) | copy-start | bytes 52
  12.1 7.8 %copy-start.1 = (s32[4]{0:T(128)S(1)}, s32[4]{0:T(128)}, u32[]{:S(2)}) copy-start(s32[4]{0:T(128)} %constant.197.clone) | copy-start | bytes 52
  13.2 10.7 %copy-start.6 = (bf16[512,512]{1,0:T(8,128)(2,1)S(1)}, bf16[512,512]{1,0:T(8,128)(2,1)}, u32[]{:S(2)}) copy-start(bf16[512,512]{1,0:T(8,128)(2,1)} %param.19) | copy-start | bytes 1572868
  13.2 16.6 %collective-permute-start.3 = (bf16[272,1024]{1,0:T(8,128)(2,1)}, bf16[272,1024]{1,0:T(8,128)(2,1)S(1)}, u32[]{:S(2)}, u32[]{:S(2)}) collective-permute-start(bf16[272,1024]{1,0:T(8,128)(2,1)} %get-tuple-element.44), channel_id=1, source_target_pairs={{0,1},{2,0},{3,2},{1,3},{4,5},{6,4},{7,6},{5,7},{8,9},{10,8},{11,1... | collective-permute-start | bytes 1671176 | tf_op jit(solution)/shard_map/ppermute | solution.py:29
  13.2 16.7 %collective-permute-start.2 = (bf16[272,1024]{1,0:T(8,128)(2,1)}, bf16[272,1024]{1,0:T(8,128)(2,1)S(1)}, u32[]{:S(2)}, u32[]{:S(2)}) collective-permute-start(bf16[272,1024]{1,0:T(8,128)(2,1)} %get-tuple-element.44), channel_id=1, source_target_pairs={{0,2},{2,3},{3,1},{1,0},{4,6},{6,7},{7,5},{5,4},{8,10},{10,11},{11... | collective-permute-start | bytes 1671176 | tf_op jit(solution)/shard_map/ppermute | solution.py:28
  25.9 18.4 %collective-permute-start.6 = (bf16[16,16512]{1,0:T(8,128)(2,1)}, bf16[16,16512]{1,0:T(8,128)(2,1)}, u32[]{:S(2)}, u32[]{:S(2)}) collective-permute-start(bf16[16,16512]{1,0:T(8,128)(2,1)} %collective-permute-done), channel_id=1, source_target_pairs={{0,8},{8,16},{16,24},{24,28},{28,20},{20,12},{12,4},{4,0},{1,9},{9... | collective-permute-start | bytes 1585160 | tf_op jit(solution)/shard_map/ppermute | solution.py:28
  29.9 14.4 %collective-permute-start.7 = (bf16[16,16512]{1,0:T(8,128)(2,1)}, bf16[16,16512]{1,0:T(8,128)(2,1)S(1)}, u32[]{:S(2)}, u32[]{:S(2)}) collective-permute-start(bf16[16,16512]{1,0:T(8,128)(2,1)} %collective-permute-done.1), channel_id=1, source_target_pairs={{0,4},{8,0},{16,8},{24,16},{28,24},{20,28},{12,20},{4,12},{1,5},{9... | collective-permute-start | bytes 1585160 | tf_op jit(solution)/shard_map/ppermute | solution.py:29
  29.9 8.4 %collective-permute-start.5 = (bf16[272,512]{1,0:T(8,128)(2,1)S(1)}, bf16[272,512]{1,0:T(8,128)(2,1)S(1)}, u32[]{:S(2)}, u32[]{:S(2)}) collective-permute-start(bf16[272,512]{1,0:T(8,128)(2,1)S(1)} %slice.85), channel_id=1, source_target_pairs={{0,1},{2,0},{3,2},{1,3},{4,5},{6,4},{7,6},{5,7},{8,9},{10,8},{11,1... | collective-permute-start | bytes 835592 | tf_op jit(solution)/shard_map/ppermute | solution.py:34
  30.0 8.4 %collective-permute-start.4 = (bf16[272,512]{1,0:T(8,128)(2,1)S(1)}, bf16[272,512]{1,0:T(8,128)(2,1)S(1)}, u32[]{:S(2)}, u32[]{:S(2)}) collective-permute-start(bf16[272,512]{1,0:T(8,128)(2,1)S(1)} %slice.84), channel_id=1, source_target_pairs={{0,2},{2,3},{3,1},{1,0},{4,6},{6,7},{7,5},{5,4},{8,10},{10,11},{11... | collective-permute-start | bytes 835592 | tf_op jit(solution)/shard_map/ppermute | solution.py:33
  38.7 1.4 %copy-start.3 = (bf16[4,272,1024]{2,1,0:T(8,128)(2,1)}, bf16[4,272,1024]{2,1,0:T(8,128)(2,1)S(1)}, u32[]{:S(2)}) copy-start(bf16[4,272,1024]{2,1,0:T(8,128)(2,1)S(1)} %pad_maximum_fusion) | copy-start | bytes 6684676
  44.3 2.1 %copy-start.5 = (bf16[16,16512]{1,0:T(8,128)(2,1)}, bf16[16,16512]{1,0:T(8,128)(2,1)S(1)}, u32[]{:S(2)}) copy-start(bf16[16,16512]{1,0:T(8,128)(2,1)S(1)} %collective-permute-done.7) | copy-start | bytes 1585156
  46.3 13.3 %collective-permute-start.8 = (bf16[16,16512]{1,0:T(8,128)(2,1)}, bf16[16,16512]{1,0:T(8,128)(2,1)}, u32[]{:S(2)}, u32[]{:S(2)}) collective-permute-start(bf16[16,16512]{1,0:T(8,128)(2,1)} %collective-permute-done.6), channel_id=1, source_target_pairs={{0,8},{8,16},{16,24},{24,28},{28,20},{20,12},{12,4},{4,0},{1,9},{9... | collective-permute-start | bytes 1585160 | tf_op jit(solution)/shard_map/ppermute | solution.py:28
  47.9 12.4 %collective-permute-start.9 = (bf16[16,16512]{1,0:T(8,128)(2,1)}, bf16[16,16512]{1,0:T(8,128)(2,1)S(1)}, u32[]{:S(2)}, u32[]{:S(2)}) collective-permute-start(bf16[16,16512]{1,0:T(8,128)(2,1)} %copy-done.5), channel_id=1, source_target_pairs={{0,4},{8,0},{16,8},{24,16},{28,24},{20,28},{12,20},{4,12},{1,5},{9... | collective-permute-start | bytes 1585160 | tf_op jit(solution)/shard_map/ppermute | solution.py:29
  60.4 17.2 %collective-permute-start.11 = (bf16[16,8320]{1,0:T(8,128)(2,1)S(1)}, bf16[16,8320]{1,0:T(8,128)(2,1)S(1)}, u32[]{:S(2)}, u32[]{:S(2)}) collective-permute-start(bf16[16,8320]{1,0:T(8,128)(2,1)S(1)} %slice.88), channel_id=1, source_target_pairs={{0,4},{8,0},{16,8},{24,16},{28,24},{20,28},{12,20},{4,12},{1,5},{9... | collective-permute-start | bytes 798728 | tf_op jit(solution)/shard_map/ppermute | solution.py:34
  62.3 15.2 %collective-permute-start.10 = (bf16[16,8192]{1,0:T(8,128)(2,1)S(1)}, bf16[16,8192]{1,0:T(8,128)(2,1)S(1)}, u32[]{:S(2)}, u32[]{:S(2)}) collective-permute-start(bf16[16,8192]{1,0:T(8,128)(2,1)S(1)} %slice.87), channel_id=1, source_target_pairs={{0,8},{8,16},{16,24},{24,28},{28,20},{20,12},{12,4},{4,0},{1,9},{9... | collective-permute-start | bytes 786440 | tf_op jit(solution)/shard_map/ppermute | solution.py:33
  63.7 7.8 %copy-start.4 = (bf16[4,128,4,2,64]{4,3,2,1,0:T(2,128)(2,1)S(1)}, bf16[4,128,4,2,64]{4,3,2,1,0:T(2,128)(2,1)}, u32[]{:S(2)}) copy-start(bf16[4,128,4,2,64]{4,3,2,1,0:T(2,128)(2,1)} %reshape.256) | copy-start | bytes 1572868
  93.0 1.4 %collective-permute-start.14 = (f32[4,128]{1,0:T(4,128)S(1)}, f32[4,128]{1,0:T(4,128)S(1)}, u32[]{:S(2)}, u32[]{:S(2)}) collective-permute-start(f32[4,128]{1,0:T(4,128)S(1)} %get-tuple-element.50), channel_id=1, source_target_pairs={{0,3},{1,0},{2,1},{3,2},{4,7},{5,4},{6,5},{7,6},{8,11},{9,8},{10,9... | collective-permute-start | bytes 6152 | tf_op jit(solution)/shard_map/ppermute | solution.py:182
  93.0 3.7 %collective-permute-start.13 = (f32[4,128]{1,0:T(4,128)S(1)}, f32[4,128]{1,0:T(4,128)S(1)}, u32[]{:S(2)}, u32[]{:S(2)}) collective-permute-start(f32[4,128]{1,0:T(4,128)S(1)} %get-tuple-element.51), channel_id=1, source_target_pairs={{0,2},{1,3},{2,0},{3,1},{4,6},{5,7},{6,4},{7,5},{8,10},{9,11},{10,... | collective-permute-start | bytes 6152 | tf_op jit(solution)/shard_map/ppermute | solution.py:182
  93.5 3.2 %collective-permute-start.12 = (f32[4,128]{1,0:T(4,128)S(1)}, f32[4,128]{1,0:T(4,128)S(1)}, u32[]{:S(2)}, u32[]{:S(2)}) collective-permute-start(f32[4,128]{1,0:T(4,128)S(1)} %get-tuple-element.49), channel_id=1, source_target_pairs={{0,1},{1,2},{2,3},{3,0},{4,5},{5,6},{6,7},{7,4},{8,9},{9,10},{10,1... | collective-permute-start | bytes 6152 | tf_op jit(solution)/shard_map/ppermute | solution.py:182

commit v17 on v14

--- a/solution.py
+++ b/solution.py
@@ -29,7 +29,7 @@
         behind = lax.ppermute(behind, axis, bwd)
         got += [ahead, behind]
         shifts += [-step, step]
-    rows = buf.shape[0] // 2
+    rows = (buf.shape[0] // 32) * 16 if buf.shape[0] >= 32 else buf.shape[0] // 2
     first = lax.ppermute(ahead[:rows], axis, fwd)
     second = lax.ppermute(behind[rows:], axis, bwd)
     got.append(jnp.concatenate([first, second], axis=0))

time: 97.6 us -> 97.2 us (level)
    ppermute x2, waiting for transfers between devices: 4.45 us -> 2.24 us  [ring_gather(): second = lax.ppermute(behind[rows:], axis, bwd)]
    ppermute x2, waiting for transfers between devices: 0.01 us -> 2.21 us  [ring_gather(): first = lax.ppermute(ahead[:rows], axis, fwd)]
  transfers between devices with their start and end apart: 15 -> 15, of which waited for: 5 -> 6; matrix products, arithmetic and copies ran while one was open for 40% -> 40% of each run, Pallas kernels for 0% -> 0%
where the time goes in v17:
time: 97.2 us; the launch traced here: 96.5 us
  local copies, waits for them, and re-layouts  38.9 us (40%)
  starting transfers between devices  14.1 us (15%)
  waiting for transfers between devices  12.5 us (13%)
  Pallas kernels  11.5 us (12%)
  matrix products  8.43 us (9%)
  other arithmetic  7.45 us (8%)
  between operations  3.69 us (4%)
    unnamed x29, local copies, waits for them, and re-layouts  11.6 us
    pallas_call x1, Pallas kernels, contract(): pl.pallas_call(body, out_shape=jax.ShapeDtypeStruct((steps, ri, chunk * r...  11.5 us
    ppermute x4, starting transfers between devices, ring_gather(): ahead = lax.ppermute(ahead, axis, fwd)  8.7 us
    dot_general x2, local copies, waits for them, and re-layouts, on_device(): lax.dot_general(occ_raw, virt_cols, (((0, 1, 2), (1, 2, 3)), ((), ())), p...  6.61 us
    dot_general x1, matrix products, on_device(): lax.dot_general(occ_raw, virt_cols, (((0, 1, 2), (1, 2, 3)), ((), ())), p...  6.13 us
    ppermute x4, waiting for transfers between devices, ring_gather(): ahead = lax.ppermute(ahead, axis, fwd)  3.97 us
    squeeze x2, local copies, waits for them, and re-layouts, on_device(): local_blocks = x_blocks[0]  3.93 us
    ppermute x2, starting transfers between devices, ring_gather(): first = lax.ppermute(ahead[:rows], axis, fwd)  3.33 us
  transfers between devices with their start and end apart: 15, of which 6 were waited for; matrix products, arithmetic and copies ran while one was open for 40% of the time, Pallas kernels for 0%

profile of v17, /device:TPU:0, one launch (start us, length us, event | category | flops | bytes accessed | tf_op | source)
XLA Modules:
  0.0 96.5 jit_solution(3363407243930987)
XLA Ops:
  0.0 0.7 convert_bitcast_fusion.2
  0.7 1.8 %squeeze.33 = bf16[4,64,16,64]{3,2,1,0:T(8,128)(2,1)S(1)} reshape(bf16[1,4,64,1024]{3,2,1,0:T(8,128)(2,1)} %param.15) | data formatting | bytes 1048576 | tf_op jit(solution)/shard_map/squeeze | solution.py:113
  2.5 2.2 %copy.210 = bf16[4,64,16,64]{1,0,2,3:T(4,128)(2,1)S(1)} copy(bf16[4,64,16,64]{3,2,1,0:T(8,128)(2,1)S(1)} %squeeze.33) | data formatting | bytes 1048576 | tf_op jit(solution)/shard_map/squeeze | solution.py:113
  5.3 0.6 multiply_bitcast_fusion
  5.9 0.7 copy.211
  6.6 0.8 reshape.204
  7.5 0.9 fusion.11
  8.3 3.0 %collective-permute-start = (bf16[16,16512]{1,0:T(8,128)(2,1)}, bf16[16,16512]{1,0:T(8,128)(2,1)}, u32[]{:S(2)}, u32[]{:S(2)}) collective-permute-start(bf16[16,16512]{1,0:T(8,128)(2,1)} %fusion.11), channel_id=1, source_target_pairs={{0,8},{8,16},{16,24},{24,28},{28,20},{20,12},{12,4},{4,0},{1,9},{9... | collective-permute-start | bytes 1585160 | tf_op jit(solution)/shard_map/ppermute | solution.py:28
  11.4 0.7 reshape.205
  12.1 0.2 copy.212
  12.3 0.9 fusion.33
  13.2 2.0 %collective-permute-start.2 = (bf16[272,1024]{1,0:T(8,128)(2,1)}, bf16[272,1024]{1,0:T(8,128)(2,1)S(1)}, u32[]{:S(2)}, u32[]{:S(2)}) collective-permute-start(bf16[272,1024]{1,0:T(8,128)(2,1)} %get-tuple-element.44), channel_id=1, source_target_pairs={{0,2},{2,3},{3,1},{1,0},{4,6},{6,7},{7,5},{5,4},{8,10},{10,11},{11... | collective-permute-start | bytes 1671176 | tf_op jit(solution)/shard_map/ppermute | solution.py:28
  15.3 0.9 bitcast_dynamic-update-slice_fusion.6
  16.1 0.6 dynamic_slice.34
  16.7 0.7 compare_select_fusion.7
  17.4 0.6 gather_fusion
  18.1 0.6 scatter_custom_fusion
  18.7 0.6 dynamic_slice.36
  19.3 0.7 compare_select_fusion.4
  20.0 0.6 gather_fusion.2
  20.6 0.7 fusion.34
  24.0 0.1 constant_dynamic-slice_fusion.7
  24.1 1.5 %reshape.256 = bf16[4,128,4,2,64]{4,3,2,1,0:T(2,128)(2,1)} reshape(bf16[512,512]{1,0:T(8,128)(2,1)S(1)} %pad_maximum_fusion.1) | data formatting | bytes 1048576 | tf_op jit(solution)/shard_map/dot_general | solution.py:166
  25.7 0.1 broadcast_in_dim.43
  25.9 2.1 %collective-permute-start.6 = (bf16[16,16512]{1,0:T(8,128)(2,1)}, bf16[16,16512]{1,0:T(8,128)(2,1)S(1)}, u32[]{:S(2)}, u32[]{:S(2)}) collective-permute-start(bf16[16,16512]{1,0:T(8,128)(2,1)} %collective-permute-done), channel_id=1, source_target_pairs={{0,8},{8,16},{16,24},{24,28},{28,20},{20,12},{12,4},{4,0},{1,9},{9... | collective-permute-start | bytes 1585160 | tf_op jit(solution)/shard_map/ppermute | solution.py:28
  28.0 1.9 %bitcast_dynamic-update-slice_fusion.5 = bf16[8,16,16512]{2,1,0:T(8,128)(2,1)} fusion(bf16[8,16,16512]{2,1,0:T(8,128)(2,1)} %bitcast_dynamic-update-slice_fusion.6, bf16[16,16512]{1,0:T(8,128)(2,1)} %collective-permute-done), kind=kLoop, calls=%fused_computation.29 | loop fusion | bytes 1056768
  30.0 2.0 %collective-permute-start.4 = (bf16[128,1024]{1,0:T(8,128)(2,1)S(1)}, bf16[128,1024]{1,0:T(8,128)(2,1)S(1)}, u32[]{:S(2)}, u32[]{:S(2)}) collective-permute-start(bf16[128,1024]{1,0:T(8,128)(2,1)S(1)} %slice.84), channel_id=1, source_target_pairs={{0,2},{2,3},{3,1},{1,0},{4,6},{6,7},{7,5},{5,4},{8,10},{10,11},{11... | collective-permute-start | bytes 786440 | tf_op jit(solution)/shard_map/ppermute | solution.py:33
  32.0 1.9 %bitcast_dynamic-update-slice_fusion.4 = bf16[8,16,16512]{2,1,0:T(8,128)(2,1)} fusion(bf16[8,16,16512]{2,1,0:T(8,128)(2,1)} %bitcast_dynamic-update-slice_fusion.5, bf16[16,16512]{1,0:T(8,128)(2,1)} %collective-permute-done.1), kind=kLoop, calls=%fused_computation.28 | loop fusion | bytes 1056768
  33.9 2.2 %collective-permute-done.4 = bf16[128,1024]{1,0:T(8,128)(2,1)S(1)} collective-permute-done((bf16[128,1024]{1,0:T(8,128)(2,1)S(1)}, bf16[128,1024]{1,0:T(8,128)(2,1)S(1)}, u32[]{:S(2)}, u32[]{:S(2)}) %collective-permute-start.4) | collective-permute-done | bytes 262176 | tf_op jit(solution)/shard_map/ppermute | solution.py:33
  36.1 2.2 %collective-permute-done.5 = bf16[144,1024]{1,0:T(8,128)(2,1)S(1)} collective-permute-done((bf16[144,1024]{1,0:T(8,128)(2,1)S(1)}, bf16[144,1024]{1,0:T(8,128)(2,1)S(1)}, u32[]{:S(2)}, u32[]{:S(2)}) %collective-permute-start.5) | collective-permute-done | bytes 294944 | tf_op jit(solution)/shard_map/ppermute | solution.py:34
  38.4 0.3 pad_maximum_fusion
  38.7 1.4 %copy-done.3 = bf16[4,272,1024]{2,1,0:T(8,128)(2,1)} copy-done((bf16[4,272,1024]{2,1,0:T(8,128)(2,1)}, bf16[4,272,1024]{2,1,0:T(8,128)(2,1)S(1)}, u32[]{:S(2)}) %copy-start.3) | copy-done | bytes 2228248
  40.4 0.1 mul.68
  40.6 3.2 %gather_fusion.1 = bf16[1024,128]{1,0:T(8,128)(2,1)S(1)} fusion(bf16[512,128]{1,0:T(8,128)(2,1)S(1)} %constant_dynamic-slice_fusion.8, s32[1024]{0:T(1024)S(1)} %broadcast_clamp_fusion), kind=kCustom, calls=%fused_computation.1 | custom fusion | bytes 528384 | tf_op jit(solution)/shard_map/jit(_take)/gather | solution.py:150
  43.9 0.2 broadcast_select_fusion
  44.1 0.1 copy.213
  44.2 0.8 copy-done.5
  45.0 0.8 bitcast_dynamic-update-slice_fusion.3
  45.9 1.6 %collective-permute-start.8 = (bf16[16,16512]{1,0:T(8,128)(2,1)}, bf16[16,16512]{1,0:T(8,128)(2,1)S(1)}, u32[]{:S(2)}, u32[]{:S(2)}) collective-permute-start(bf16[16,16512]{1,0:T(8,128)(2,1)} %copy-done.5), channel_id=1, source_target_pairs={{0,8},{8,16},{16,24},{24,28},{28,20},{20,12},{12,4},{4,0},{1,9},{9... | collective-permute-start | bytes 1585160 | tf_op jit(solution)/shard_map/ppermute | solution.py:28
  47.4 0.4 collective-permute-start.9
  47.9 1.9 %bitcast_dynamic-update-slice_fusion.2 = bf16[8,16,16512]{2,1,0:T(8,128)(2,1)} fusion(bf16[8,16,16512]{2,1,0:T(8,128)(2,1)} %bitcast_dynamic-update-slice_fusion.3, bf16[16,16512]{1,0:T(8,128)(2,1)} %collective-permute-done.7), kind=kLoop, calls=%fused_computation.26 | loop fusion | bytes 1056768
  49.8 2.3 %convert_bitcast_fusion = bf16[4,2,1024,128]{2,3,1,0:T(8,128)(2,1)S(1)} fusion(bf16[4,272,1024]{2,1,0:T(8,128)(2,1)} %copy-done.3, bf16[4,2,256]{2,1,0:T(2,128)(2,1)S(1)} %mul.68, bf16[4,256,128]{1,2,0:T(8,128)(2,1)S(1)} %copy.213), kind=kOutput, calls=%fused_computation.10 | convolution fusion | flops 538181632 | bytes 4460544 | tf_op jit(solution)/shard_map/bkr,bhkl->bhrl/dot_general | solution.py:155
  52.1 2.6 %copy.214 = bf16[4,2,1024,128]{3,2,1,0:T(8,128)(2,1)} copy(bf16[4,2,1024,128]{2,3,1,0:T(8,128)(2,1)S(1)} %convert_bitcast_fusion) | data formatting | bytes 4194304 | tf_op jit(solution)/shard_map/convert_element_type | solution.py:157
  54.8 4.0 %collective-permute-done.8 = bf16[16,16512]{1,0:T(8,128)(2,1)S(1)} collective-permute-done((bf16[16,16512]{1,0:T(8,128)(2,1)}, bf16[16,16512]{1,0:T(8,128)(2,1)S(1)}, u32[]{:S(2)}, u32[]{:S(2)}) %collective-permute-start.8) | collective-permute-done | bytes 528416 | tf_op jit(solution)/shard_map/ppermute | solution.py:28
  58.7 0.9 collective-permute-done.9
  59.6 1.0 %slice.88 = bf16[8,16512]{1,0:T(8,128)(2,1)S(1)} slice(bf16[16,16512]{1,0:T(8,128)(2,1)} %collective-permute-done.9), slice={[8:16], [0:16512]} | slice | bytes 528384 | tf_op jit(solution)/shard_map/slice | solution.py:34
  60.6 1.0 %collective-permute-start.11 = (bf16[8,16512]{1,0:T(8,128)(2,1)S(1)}, bf16[8,16512]{1,0:T(8,128)(2,1)S(1)}, u32[]{:S(2)}, u32[]{:S(2)}) collective-permute-start(bf16[8,16512]{1,0:T(8,128)(2,1)S(1)} %slice.88), channel_id=1, source_target_pairs={{0,4},{8,0},{16,8},{24,16},{28,24},{20,28},{12,20},{4,12},{1,5},{9... | collective-permute-start | bytes 792584 | tf_op jit(solution)/shard_map/ppermute | solution.py:34
  61.6 1.3 %collective-permute-start.10 = (bf16[8,16512]{1,0:T(8,128)(2,1)S(1)}, bf16[8,16512]{1,0:T(8,128)(2,1)S(1)}, u32[]{:S(2)}, u32[]{:S(2)}) collective-permute-start(bf16[8,16512]{1,0:T(8,128)(2,1)S(1)} %slice.87), channel_id=1, source_target_pairs={{0,8},{8,16},{16,24},{24,28},{28,20},{20,12},{12,4},{4,0},{1,9},{9... | collective-permute-start | bytes 792584 | tf_op jit(solution)/shard_map/ppermute | solution.py:33
  62.9 5.1 %copy.216 = bf16[16,128,4,2,64]{4,1,3,2,0:T(8,128)(2,1)} copy(bf16[16,128,4,2,64]{1,0,4,3,2:T(8,128)(2,1)} %bitcast.95) | data formatting | bytes 4194304 | tf_op jit(solution)/shard_map/dot_general | solution.py:166
  68.0 0.8 bitcast_dynamic-update-slice_fusion.1
  68.8 1.9 %bitcast_dynamic-update-slice_fusion = bf16[8,16,16512]{2,1,0:T(8,128)(2,1)} fusion(bf16[8,16,16512]{2,1,0:T(8,128)(2,1)} %bitcast_dynamic-update-slice_fusion.1, bf16[16,16512]{1,0:T(8,128)(2,1)} %collective-permute-done.9), kind=kLoop, calls=%fused_computation.24 | loop fusion | bytes 1056768
  70.7 6.1 %fusion = f32[16,16,8,4,128,1,1]{4,2,6,5,3,1,0:T(8,128)} fusion(bf16[4,128,4,2,64,1,1]{4,3,2,1,0,6,5:T(2,128)(2,1)S(1)} %bitcast.101, bf16[16,128,4,2,64]{4,1,3,2,0:T(8,128)(2,1)} %copy.216), kind=kOutput, calls=%fused_computation.5 | convolution fusion | flops 1073741824 | bytes 6815744 | tf_op jit(solution)/shard_map/dot_general | solution.py:166
  76.9 0.8 fusion.12
  77.7 0.7 slice.89
  78.4 0.1 copy.233
  78.5 0.7 copy.220.refs_0_
  79.2 11.5 %shard_map.109 = f32[1,16,128]{2,1,0:T(8,128)} custom-call(s32[8,4]{1,0:T(8,128)} %copy.220.refs_0_, f32[8192,128]{1,0:T(8,128)} %bitcast.97, bf16[128,16512]{1,0:T(8,128)(2,1)} %bitcast.96), custom_call_target="tpu_custom_call" | custom-call | tf_op jit(solution)/shard_map/pallas_call | solution.py:106
  90.7 0.8 reshape_reshape_transpose.3
  91.5 0.6 gather_fusion.3
  92.1 0.1 gather.26
  92.4 0.4 collective-permute-start.12
  92.8 0.8 collective-permute-done.14
  93.6 2.3 %collective-permute-done.13 = f32[4,128]{1,0:T(4,128)S(1)} collective-permute-done((f32[4,128]{1,0:T(4,128)S(1)}, f32[4,128]{1,0:T(4,128)S(1)}, u32[]{:S(2)}, u32[]{:S(2)}) %collective-permute-start.13) | collective-permute-done | bytes 2080 | tf_op jit(solution)/shard_map/ppermute | solution.py:182
  95.9 0.6 fusion.19
  (68 shorter events, 1.1 us)
Async XLA Ops:
  0.0 25.8 %copy-start = (bf16[512,512]{1,0:T(8,128)(2,1)S(1)}, bf16[512,512]{1,0:T(8,128)(2,1)}, u32[]{:S(2)}) copy-start(bf16[512,512]{1,0:T(8,128)(2,1)} %param.18) | copy-start | bytes 1572868
  8.3 17.5 %collective-permute-start = (bf16[16,16512]{1,0:T(8,128)(2,1)}, bf16[16,16512]{1,0:T(8,128)(2,1)}, u32[]{:S(2)}, u32[]{:S(2)}) collective-permute-start(bf16[16,16512]{1,0:T(8,128)(2,1)} %fusion.11), channel_id=1, source_target_pairs={{0,8},{8,16},{16,24},{24,28},{28,20},{20,12},{12,4},{4,0},{1,9},{9... | collective-permute-start | bytes 1585160 | tf_op jit(solution)/shard_map/ppermute | solution.py:28
  11.4 18.5 %collective-permute-start.1 = (bf16[16,16512]{1,0:T(8,128)(2,1)}, bf16[16,16512]{1,0:T(8,128)(2,1)}, u32[]{:S(2)}, u32[]{:S(2)}) collective-permute-start(bf16[16,16512]{1,0:T(8,128)(2,1)} %fusion.11), channel_id=1, source_target_pairs={{0,4},{8,0},{16,8},{24,16},{28,24},{20,28},{12,20},{4,12},{1,5},{9... | collective-permute-start | bytes 1585160 | tf_op jit(solution)/shard_map/ppermute | solution.py:29
  12.0 4.1 %copy-start.10 = (s32[8]{0:T(128)S(1)}, s32[8]{0:T(128)}, u32[]{:S(2)}) copy-start(s32[8]{0:T(128)} %constant.193.clone) | copy-start | bytes 100
  12.1 4.7 %copy-start.9 = (s32[8]{0:T(128)S(1)}, s32[8]{0:T(128)}, u32[]{:S(2)}) copy-start(s32[8]{0:T(128)} %constant.195.clone) | copy-start | bytes 100
  12.1 5.3 %copy-start.2 = (s32[8]{0:T(128)S(1)}, s32[8]{0:T(128)}, u32[]{:S(2)}) copy-start(s32[8]{0:T(128)} %constant.194.clone) | copy-start | bytes 100
  12.1 6.6 %copy-start.8 = (s32[4]{0:T(128)S(1)}, s32[4]{0:T(128)}, u32[]{:S(2)}) copy-start(s32[4]{0:T(128)} %constant.196.clone) | copy-start | bytes 52
  12.1 7.2 %copy-start.7 = (s32[4]{0:T(128)S(1)}, s32[4]{0:T(128)}, u32[]{:S(2)}) copy-start(s32[4]{0:T(128)} %constant.198.clone) | copy-start | bytes 52
  12.1 7.8 %copy-start.1 = (s32[4]{0:T(128)S(1)}, s32[4]{0:T(128)}, u32[]{:S(2)}) copy-start(s32[4]{0:T(128)} %constant.197.clone) | copy-start | bytes 52
  13.2 10.7 %copy-start.6 = (bf16[512,512]{1,0:T(8,128)(2,1)S(1)}, bf16[512,512]{1,0:T(8,128)(2,1)}, u32[]{:S(2)}) copy-start(bf16[512,512]{1,0:T(8,128)(2,1)} %param.19) | copy-start | bytes 1572868
  13.2 16.6 %collective-permute-start.3 = (bf16[272,1024]{1,0:T(8,128)(2,1)}, bf16[272,1024]{1,0:T(8,128)(2,1)S(1)}, u32[]{:S(2)}, u32[]{:S(2)}) collective-permute-start(bf16[272,1024]{1,0:T(8,128)(2,1)} %get-tuple-element.44), channel_id=1, source_target_pairs={{0,1},{2,0},{3,2},{1,3},{4,5},{6,4},{7,6},{5,7},{8,9},{10,8},{11,1... | collective-permute-start | bytes 1671176 | tf_op jit(solution)/shard_map/ppermute | solution.py:29
  13.2 16.7 %collective-permute-start.2 = (bf16[272,1024]{1,0:T(8,128)(2,1)}, bf16[272,1024]{1,0:T(8,128)(2,1)S(1)}, u32[]{:S(2)}, u32[]{:S(2)}) collective-permute-start(bf16[272,1024]{1,0:T(8,128)(2,1)} %get-tuple-element.44), channel_id=1, source_target_pairs={{0,2},{2,3},{3,1},{1,0},{4,6},{6,7},{7,5},{5,4},{8,10},{10,11},{11... | collective-permute-start | bytes 1671176 | tf_op jit(solution)/shard_map/ppermute | solution.py:28
  25.9 18.3 %collective-permute-start.6 = (bf16[16,16512]{1,0:T(8,128)(2,1)}, bf16[16,16512]{1,0:T(8,128)(2,1)S(1)}, u32[]{:S(2)}, u32[]{:S(2)}) collective-permute-start(bf16[16,16512]{1,0:T(8,128)(2,1)} %collective-permute-done), channel_id=1, source_target_pairs={{0,8},{8,16},{16,24},{24,28},{28,20},{20,12},{12,4},{4,0},{1,9},{9... | collective-permute-start | bytes 1585160 | tf_op jit(solution)/shard_map/ppermute | solution.py:28
  29.9 14.4 %collective-permute-start.7 = (bf16[16,16512]{1,0:T(8,128)(2,1)}, bf16[16,16512]{1,0:T(8,128)(2,1)}, u32[]{:S(2)}, u32[]{:S(2)}) collective-permute-start(bf16[16,16512]{1,0:T(8,128)(2,1)} %collective-permute-done.1), channel_id=1, source_target_pairs={{0,4},{8,0},{16,8},{24,16},{28,24},{20,28},{12,20},{4,12},{1,5},{9... | collective-permute-start | bytes 1585160 | tf_op jit(solution)/shard_map/ppermute | solution.py:29
  29.9 8.4 %collective-permute-start.5 = (bf16[144,1024]{1,0:T(8,128)(2,1)S(1)}, bf16[144,1024]{1,0:T(8,128)(2,1)S(1)}, u32[]{:S(2)}, u32[]{:S(2)}) collective-permute-start(bf16[144,1024]{1,0:T(8,128)(2,1)S(1)} %slice.85), channel_id=1, source_target_pairs={{0,1},{2,0},{3,2},{1,3},{4,5},{6,4},{7,6},{5,7},{8,9},{10,8},{11,1... | collective-permute-start | bytes 884744 | tf_op jit(solution)/shard_map/ppermute | solution.py:34
  30.0 6.1 %collective-permute-start.4 = (bf16[128,1024]{1,0:T(8,128)(2,1)S(1)}, bf16[128,1024]{1,0:T(8,128)(2,1)S(1)}, u32[]{:S(2)}, u32[]{:S(2)}) collective-permute-start(bf16[128,1024]{1,0:T(8,128)(2,1)S(1)} %slice.84), channel_id=1, source_target_pairs={{0,2},{2,3},{3,1},{1,0},{4,6},{6,7},{7,5},{5,4},{8,10},{10,11},{11... | collective-permute-start | bytes 786440 | tf_op jit(solution)/shard_map/ppermute | solution.py:33
  38.7 1.4 %copy-start.3 = (bf16[4,272,1024]{2,1,0:T(8,128)(2,1)}, bf16[4,272,1024]{2,1,0:T(8,128)(2,1)S(1)}, u32[]{:S(2)}) copy-start(bf16[4,272,1024]{2,1,0:T(8,128)(2,1)S(1)} %pad_maximum_fusion) | copy-start | bytes 6684676
  44.2 0.8 copy-start.5
  45.9 12.9 %collective-permute-start.8 = (bf16[16,16512]{1,0:T(8,128)(2,1)}, bf16[16,16512]{1,0:T(8,128)(2,1)S(1)}, u32[]{:S(2)}, u32[]{:S(2)}) collective-permute-start(bf16[16,16512]{1,0:T(8,128)(2,1)} %copy-done.5), channel_id=1, source_target_pairs={{0,8},{8,16},{16,24},{24,28},{28,20},{20,12},{12,4},{4,0},{1,9},{9... | collective-permute-start | bytes 1585160 | tf_op jit(solution)/shard_map/ppermute | solution.py:28
  47.4 12.2 %collective-permute-start.9 = (bf16[16,16512]{1,0:T(8,128)(2,1)}, bf16[16,16512]{1,0:T(8,128)(2,1)}, u32[]{:S(2)}, u32[]{:S(2)}) collective-permute-start(bf16[16,16512]{1,0:T(8,128)(2,1)} %collective-permute-done.7), channel_id=1, source_target_pairs={{0,4},{8,0},{16,8},{24,16},{28,24},{20,28},{12,20},{4,12},{1,5},{9... | collective-permute-start | bytes 1585160 | tf_op jit(solution)/shard_map/ppermute | solution.py:29
  60.6 16.3 %collective-permute-start.11 = (bf16[8,16512]{1,0:T(8,128)(2,1)S(1)}, bf16[8,16512]{1,0:T(8,128)(2,1)S(1)}, u32[]{:S(2)}, u32[]{:S(2)}) collective-permute-start(bf16[8,16512]{1,0:T(8,128)(2,1)S(1)} %slice.88), channel_id=1, source_target_pairs={{0,4},{8,0},{16,8},{24,16},{28,24},{20,28},{12,20},{4,12},{1,5},{9... | collective-permute-start | bytes 792584 | tf_op jit(solution)/shard_map/ppermute | solution.py:34
  61.6 15.2 %collective-permute-start.10 = (bf16[8,16512]{1,0:T(8,128)(2,1)S(1)}, bf16[8,16512]{1,0:T(8,128)(2,1)S(1)}, u32[]{:S(2)}, u32[]{:S(2)}) collective-permute-start(bf16[8,16512]{1,0:T(8,128)(2,1)S(1)} %slice.87), channel_id=1, source_target_pairs={{0,8},{8,16},{16,24},{24,28},{28,20},{20,12},{12,4},{4,0},{1,9},{9... | collective-permute-start | bytes 792584 | tf_op jit(solution)/shard_map/ppermute | solution.py:33
  62.9 7.8 %copy-start.4 = (bf16[4,128,4,2,64]{4,3,2,1,0:T(2,128)(2,1)S(1)}, bf16[4,128,4,2,64]{4,3,2,1,0:T(2,128)(2,1)}, u32[]{:S(2)}) copy-start(bf16[4,128,4,2,64]{4,3,2,1,0:T(2,128)(2,1)} %reshape.256) | copy-start | bytes 1572868
  92.2 1.4 %collective-permute-start.14 = (f32[4,128]{1,0:T(4,128)S(1)}, f32[4,128]{1,0:T(4,128)S(1)}, u32[]{:S(2)}, u32[]{:S(2)}) collective-permute-start(f32[4,128]{1,0:T(4,128)S(1)} %get-tuple-element.50), channel_id=1, source_target_pairs={{0,3},{1,0},{2,1},{3,2},{4,7},{5,4},{6,5},{7,6},{8,11},{9,8},{10,9... | collective-permute-start | bytes 6152 | tf_op jit(solution)/shard_map/ppermute | solution.py:182
  92.3 3.7 %collective-permute-start.13 = (f32[4,128]{1,0:T(4,128)S(1)}, f32[4,128]{1,0:T(4,128)S(1)}, u32[]{:S(2)}, u32[]{:S(2)}) collective-permute-start(f32[4,128]{1,0:T(4,128)S(1)} %get-tuple-element.51), channel_id=1, source_target_pairs={{0,2},{1,3},{2,0},{3,1},{4,6},{5,7},{6,4},{7,5},{8,10},{9,11},{10,... | collective-permute-start | bytes 6152 | tf_op jit(solution)/shard_map/ppermute | solution.py:182
  92.4 3.6 %collective-permute-start.12 = (f32[4,128]{1,0:T(4,128)S(1)}, f32[4,128]{1,0:T(4,128)S(1)}, u32[]{:S(2)}, u32[]{:S(2)}) collective-permute-start(f32[4,128]{1,0:T(4,128)S(1)} %get-tuple-element.49), channel_id=1, source_target_pairs={{0,1},{1,2},{2,3},{3,0},{4,5},{5,6},{6,7},{7,4},{8,9},{9,10},{10,1... | collective-permute-start | bytes 6152 | tf_op jit(solution)/shard_map/ppermute | solution.py:182
